TPU v7x, 512 devices: a whole 4x4x16 slice. The times are simulated.
512 devices in a mesh: space: 256 (over z, y, x), vec: 2 (over core).
Axes of the slice: x: 4, y: 4, z: 16, core: 2. Of those that a mesh axis runs over, the one named last changes fastest.
Arguments:
- vectors: bfloat16 [262144, 256], P('space', 'vec'), may hold values from -6 to 6
- points: float32 [3, 262144], P(None, 'space'), may hold values from 0 to 1024, as said below
- near_index: int32 [4096, 3], P('space'), may hold values from -1 to 4095, as said below
- leaf_basis: bfloat16 [32, 262144], P(None, 'space'), may hold values from -0.75 to 0.75
- transfer: bfloat16 [256, 15, 32, 64], P('space'), may hold values from -0.875 to 0.875
- coupling: bfloat16 [256, 31, 32, 96], P('space'), may hold values from -0.1875 to 0.1875
- upper_transfer: bfloat16 [256, 32, 64], P('space'), may hold values from -0.875 to 0.875
- upper_coupling: bfloat16 [256, 32, 96], P('space'), may hold values from -0.1875 to 0.1875
Outputs:
- covariance_product: bfloat16 [262144, 256], P('space', 'vec')
Inputs may be any that keep to these rules, and one draw needn't show every extreme that they name: `near_index`: entry 0 of row t is t; entry 1 is t - 1 or -1, entry 2 is t + 1 or -1; -1 marks an absent block, and it stands in entry 1 of row 0 and entry 2 of row 4095; entry 1 of a row t > 0 that is a multiple of 16 is t - 1, and entry 2 of a row t < 4095 with t + 1 a multiple of 16 is t + 1. `points`: the first coordinate of a point of leaf t lies in [t / 4, (t + 1) / 4], the other two in [0, 1/4].
All inputs are finite; a program needn't handle non-finite values.
Results may differ from a plain program's by a relative error of at most 0.005.
Values may be sent and summed in bfloat16 or wider, within the bound.
No kernel may reach another device: no remote copies, remote signals or barrier semaphores. Data moves between devices by JAX's collectives and lax.ppermute only.
A program may use at most 64 MiB of HBM per device.

v0:
```python
import jax
import jax.numpy as jnp
import numpy as np
from jax import lax
from jax.sharding import PartitionSpec as P

LEAF = 64
RANK = 32


SCALE_A = 2.0 * 3.0**0.5
VARIANCE = 0.0625
NUGGET = 0.5
HIGHEST = lax.Precision.HIGHEST


def passed_along(block, axis, distance):
    devices = range(lax.axis_size(axis))
    route = [(i - distance, i) for i in devices if i - distance in devices]
    return lax.ppermute(block, axis, route)


def extended_2(cells, sides, width):
    for axis, dim in sides:
        count = lax.axis_size(axis)
        ends = count - 1
        head = lax.slice_in_dim(cells, 0, width, axis=dim)
        tail = lax.slice_in_dim(cells, cells.shape[dim] - width, cells.shape[dim], axis=dim)
        cells = jnp.concatenate(
            [
                lax.ppermute(tail, axis, [(i, (i + 1) % count) for i in range(ends)]),
                cells,
                lax.ppermute(head, axis, [((i + 1) % count, i) for i in range(ends)]),
            ],
            axis=dim,
        )
    return cells


def matern(own_points, other_points):
    difference = own_points[:, :, None, :, None] - other_points[:, :, :, None, :]
    distance = jnp.sqrt(jnp.sum(difference * difference, axis=0))
    return (VARIANCE * (1.0 + SCALE_A * distance) * jnp.exp(-SCALE_A * distance)).astype(
        jnp.bfloat16
    )


def near_field(source, extended_points, index_rows, first_leaf, leaf_zero, leaf_count):
    block_count = index_rows.shape[0]
    col_width = source.shape[1]
    group_size = min(8, block_count)
    source_leaves = source.reshape(leaf_count + 2, LEAF, col_width)
    point_leaves = extended_points.reshape(3, leaf_count + 2, LEAF)
    present = (index_rows >= 0).astype(jnp.bfloat16)
    located = jnp.where(index_rows >= 0, index_rows - leaf_zero + 1, 0)

    def one_group(first_row):
        own_points = lax.dynamic_slice_in_dim(
            point_leaves, first_row + first_leaf + 1, group_size, 1
        )
        blocks = matern(own_points, point_leaves[:, located]) * present[:, :, None, None]
        return jnp.einsum(
            "gkij,gkjv->giv", blocks, source_leaves[located], preferred_element_type=jnp.float32
        )

    starts = jnp.arange(block_count // group_size, dtype=jnp.int32) * group_size
    return lax.map(one_group, starts).reshape(block_count * LEAF, col_width)


def partner_table(cluster_count):
    base = np.arange(cluster_count)
    odd_mask = base % 2 == 1
    return (
        np.stack(
            [np.where(odd_mask, -3, -2), np.where(odd_mask, -2, 2), np.where(odd_mask, 2, 3)], 1
        )
        + base[:, None]
    )


def as_float(matrix):
    return matrix.astype(jnp.float32)


def product(matrix, operand):
    return jnp.dot(matrix, operand, precision=HIGHEST)


def move_cluster(operand, amount):
    return passed_along(operand, "space", amount)


def child_steps(height):
    if height == 1:
        return (1, 0)
    return (2 ** (height - 2), 2 ** (height - 2))


def pick_three(parity, far_left, near_left, near_right, far_right):
    odd_mask = parity == 1
    return jnp.concatenate(
        [
            jnp.where(odd_mask, far_left, near_left),
            jnp.where(odd_mask, near_left, near_right),
            jnp.where(odd_mask, near_right, far_right),
        ],
        0,
    )


def chain_partners(operand, spacing, parity):
    return pick_three(
        parity,
        move_cluster(operand, 3 * spacing),
        move_cluster(operand, 2 * spacing),
        move_cluster(operand, -2 * spacing),
        move_cluster(operand, -3 * spacing),
    )


def chain_tree(device_coef, device_coupling, upper_transfer, upper_coupling, position, space_bits):
    lift_mats = as_float(upper_transfer[0])
    mixers = as_float(upper_coupling[0])
    summit = space_bits - 2
    fields = [product(device_coupling, chain_partners(device_coef, 1, position % 2))]
    current = device_coef
    for height in range(1, summit + 1):
        step_left, step_right = child_steps(height)
        holder = position % 2**height == 2 ** (height - 1)
        left_child = move_cluster(current, step_left)
        right_child = current if step_right == 0 else move_cluster(current, -step_right)
        lifted = product(lift_mats[:, :RANK], left_child) + product(
            lift_mats[:, RANK:], right_child
        )
        current = jnp.where(holder, lifted, 0.0)
        parity = position // 2**height % 2
        fields.append(
            jnp.where(holder, product(mixers, chain_partners(current, 2**height, parity)), 0.0)
        )
    downward = fields[summit]
    for height in range(summit - 1, -1, -1):
        step_left, step_right = child_steps(height + 1)
        to_left = product(lift_mats[:, :RANK].T, downward)
        to_right = product(lift_mats[:, RANK:].T, downward)
        from_left = move_cluster(to_left, -step_left)
        from_right = to_right if step_right == 0 else move_cluster(to_right, step_right)
        parity = position // 2**height % 2
        downward = fields[height] + jnp.where(parity == 1, from_right, from_left)
        if height > 0:
            holder = position % 2**height == 2 ** (height - 1)
            downward = jnp.where(holder, downward, 0.0)
    return downward


def local(
    vectors, points, near_index, leaf_basis, transfer, coupling, upper_transfer, upper_coupling
):
    row_count, columns = vectors.shape
    leaf_count = row_count // LEAF
    depth_local = leaf_count.bit_length() - 1
    space_bits = lax.axis_size("space").bit_length() - 1
    position = lax.axis_index("space")
    leaf_zero = position * leaf_count
    vector_rims = extended_2(vectors, (("space", 0),), LEAF)
    point_rims = extended_2(points, (("space", 1),), LEAF)
    lane_count = lax.axis_size("vec")
    lane_leaves = leaf_count // lane_count
    first_leaf = lax.axis_index("vec") * lane_leaves
    all_columns = lax.all_gather(vector_rims, "vec", axis=1, tiled=True)
    own_rows = lax.dynamic_slice_in_dim(near_index, first_leaf, lane_leaves, 0)
    half_near = near_field(all_columns, point_rims, own_rows, first_leaf, leaf_zero, leaf_count)
    nearby = lax.all_to_all(half_near, "vec", split_axis=1, concat_axis=0, tiled=True)
    basis_leaves = leaf_basis.reshape(RANK, leaf_count, LEAF)
    leaf_vectors = vectors.reshape(leaf_count, LEAF, columns)
    coefficients = [
        jnp.einsum("rlp,lpv->lrv", basis_leaves, leaf_vectors, preferred_element_type=jnp.float32)
    ]
    for height in range(1, depth_local + 1):
        cluster_count = leaf_count >> height
        first_slot = leaf_count - (2 * leaf_count >> height)
        lift_mats = as_float(transfer[0, first_slot : first_slot + cluster_count])
        children = coefficients[-1].reshape(cluster_count, 2 * RANK, columns)
        coefficients.append(jnp.einsum("cra,cav->crv", lift_mats, children, precision=HIGHEST))
    edge_coefs = jnp.stack(
        [
            jnp.concatenate([coefficients[height][:2], coefficients[height][-2:]], 0)
            for height in range(depth_local)
        ],
        0,
    )
    wide_edges = extended_2(edge_coefs.astype(jnp.bfloat16), (("space", 1),), 2).astype(
        edge_coefs.dtype
    )
    fields = []
    for height in range(depth_local):
        cluster_count = leaf_count >> height
        first_slot = 2 * leaf_count - (2 * leaf_count >> height)
        extended = jnp.concatenate(
            [wide_edges[height, :2], coefficients[height], wide_edges[height, 6:]], 0
        )
        stacked = extended[partner_table(cluster_count) + 2].reshape(
            cluster_count, 3 * RANK, columns
        )
        mixers = as_float(coupling[0, first_slot : first_slot + cluster_count])
        fields.append(jnp.einsum("cra,cav->crv", mixers, stacked, precision=HIGHEST))
    device_coupling = as_float(coupling[0, 2 * leaf_count - 2])
    device_coef = coefficients[depth_local][0]
    downward = chain_tree(
        device_coef, device_coupling, upper_transfer, upper_coupling, position, space_bits
    )
    downward = downward[None]
    for height in range(depth_local - 1, -1, -1):
        cluster_count = leaf_count >> height + 1
        first_slot = leaf_count - (2 * leaf_count >> height + 1)
        lift_mats = as_float(transfer[0, first_slot : first_slot + cluster_count])
        spread = jnp.einsum("cra,crv->cav", lift_mats, downward, precision=HIGHEST)
        downward = fields[height] + spread.reshape(2 * cluster_count, RANK, columns)
    far_field = jnp.einsum(
        "rlp,lrv->lpv", as_float(basis_leaves), downward, precision=HIGHEST
    ).reshape(row_count, columns)
    return (nearby + NUGGET * vectors.astype(jnp.float32) + far_field).astype(jnp.bfloat16)


def solution(mesh):
    return jax.shard_map(
        local,
        mesh=mesh,
        in_specs=(
            P("space", "vec"),
            P(None, "space"),
            P("space", None),
            P(None, "space"),
            P("space", None, None, None),
            P("space", None, None, None),
            P("space", None, None),
            P("space", None, None),
        ),
        out_specs=P("space", "vec"),
        check_vma=False,
    )
```

profile of v0, /device:TPU:30, one launch (start us, length us, event | category | flops | bytes accessed | tf_op | source)
XLA Modules:
  0.0 297.5 jit_solution(1354133993385652370)
XLA Ops:
  3.0 3.4 %collective-permute-start.10 = (f32[32,128]{1,0:T(8,128)S(1)}, f32[32,128]{1,0:T(8,128)S(1)}, u32[]{:S(2)}, u32[]{:S(2)}) collective-permute-start(f32[32,128]{1,0:T(8,128)S(1)} %bitcast.305), channel_id=1, source_target_pairs={{0,2},{2,4},{4,6},{6,8},{8,10},{10,12},{12,14},{14,16},{16,18},{18... | collective-permute-start | bytes 49160 | tf_op jit(solution)/shard_map/ppermute | solution.py:20
  6.4 2.4 collective-permute-start.9
  8.8 4.2 %collective-permute-start.8 = (f32[32,128]{1,0:T(8,128)S(1)}, f32[32,128]{1,0:T(8,128)S(1)}, u32[]{:S(2)}, u32[]{:S(2)}) collective-permute-start(f32[32,128]{1,0:T(8,128)S(1)} %bitcast.307), channel_id=1, source_target_pairs={{4,0},{6,2},{8,4},{10,6},{12,8},{14,10},{16,12},{18,14},{20,16},{2... | collective-permute-start | bytes 49160 | tf_op jit(solution)/shard_map/ppermute | solution.py:20
  13.1 2.1 collective-permute-start.1
  15.3 7.9 %collective-permute-start = (f32[3,64]{1,0:T(4,128)S(1)}, f32[3,64]{1,0:T(4,128)S(1)}, u32[]{:S(2)}, u32[]{:S(2)}) collective-permute-start(f32[3,64]{1,0:T(4,128)S(1)} %get-tuple-element.45), channel_id=1, source_target_pairs={{0,2},{2,4},{4,6},{6,8},{8,10},{10,12},{12,14},{14,16},{16,18},{18... | collective-permute-start | bytes 2312 | tf_op jit(solution)/shard_map/ppermute | solution.py:31
  24.5 2.5 collective-permute-start.2
  27.0 3.3 %collective-permute-start.3 = (bf16[64,128]{1,0:T(8,128)(2,1)S(1)}, bf16[64,128]{1,0:T(8,128)(2,1)S(1)}, u32[]{:S(2)}, u32[]{:S(2)}) collective-permute-start(bf16[64,128]{1,0:T(8,128)(2,1)S(1)} %get-tuple-element.20), channel_id=1, source_target_pairs={{2,0},{4,2},{6,4},{8,6},{10,8},{12,10},{14,12},{16,14},{18,16},{20... | collective-permute-start | bytes 49160 | tf_op jit(solution)/shard_map/ppermute | solution.py:33
  31.6 5.9 %collective-permute-start.7 = (f32[32,128]{1,0:T(8,128)S(1)}, f32[32,128]{1,0:T(8,128)S(1)}, u32[]{:S(2)}, u32[]{:S(2)}) collective-permute-start(f32[32,128]{1,0:T(8,128)S(1)} %bitcast.308), channel_id=1, source_target_pairs={{0,4},{2,6},{4,8},{6,10},{8,12},{10,14},{12,16},{14,18},{16,20},{1... | collective-permute-start | bytes 49160 | tf_op jit(solution)/shard_map/ppermute | solution.py:20
  37.5 2.5 collective-permute-start.6
  40.0 2.2 all_gather.3
  42.3 1.5 gather_fusion.1
  43.8 1.7 convolution_bitcast_fusion
  46.6 3.5 %all-to-all-start = ((f32[512,2,128]{2,0,1:T(8,128)}), f32[512,2,128]{2,0,1:T(8,128)S(1)}, u32[]{:S(2)}, u32[]{:S(2)}) async-start(f32[512,2,128]{2,0,1:T(8,128)} %copy.49), calls=%async_computation | async-start | bytes 1048576 | tf_op jit(solution)/shard_map/all_to_all | solution.py:172
  50.1 3.2 %collective-permute-start.4 = (bf16[4,2,32,128]{3,2,1,0:T(8,128)(2,1)S(1)}, bf16[4,2,32,128]{3,2,1,0:T(8,128)(2,1)S(1)}, u32[]{:S(2)}, u32[]{:S(2)}) collective-permute-start(bf16[4,2,32,128]{3,2,1,0:T(8,128)(2,1)S(1)} %get-tuple-element.38), channel_id=1, source_target_pairs={{0,2},{2,4},{4,6},{6,8},{8,10},{10,12},{12,14},{14,16},{16,18},{18... | collective-permute-start | bytes 196616 | tf_op jit(solution)/shard_map/ppermute | solution.py:31
  53.4 2.7 collective-permute-start.16
  56.1 7.4 %collective-permute-start.15 = (f32[32,128]{1,0:T(8,128)S(1)}, f32[32,128]{1,0:T(8,128)S(1)}, u32[]{:S(2)}, u32[]{:S(2)}) collective-permute-start(f32[32,128]{1,0:T(8,128)S(1)} %fusion.31), channel_id=1, source_target_pairs={{0,2},{2,4},{4,6},{6,8},{8,10},{10,12},{12,14},{14,16},{16,18},{18... | collective-permute-start | bytes 49160 | tf_op jit(solution)/shard_map/ppermute | solution.py:20
  63.5 1.9 collective-permute-start.14
  65.5 2.7 collective-permute-start.13
  68.2 5.3 %collective-permute-start.12 = (f32[32,128]{1,0:T(8,128)S(1)}, f32[32,128]{1,0:T(8,128)S(1)}, u32[]{:S(2)}, u32[]{:S(2)}) collective-permute-start(f32[32,128]{1,0:T(8,128)S(1)} %fusion.31), channel_id=1, source_target_pairs={{0,8},{2,10},{4,12},{6,14},{8,16},{10,18},{12,20},{14,22},{16,24},... | collective-permute-start | bytes 49160 | tf_op jit(solution)/shard_map/ppermute | solution.py:20
  73.7 6.6 %collective-permute-start.11 = (f32[32,128]{1,0:T(8,128)S(1)}, f32[32,128]{1,0:T(8,128)S(1)}, u32[]{:S(2)}, u32[]{:S(2)}) collective-permute-start(f32[32,128]{1,0:T(8,128)S(1)} %fusion.31), channel_id=1, source_target_pairs={{0,12},{2,14},{4,16},{6,18},{8,20},{10,22},{12,24},{14,26},{16,28}... | collective-permute-start | bytes 49160 | tf_op jit(solution)/shard_map/ppermute | solution.py:20
  80.4 2.1 collective-permute-start.22
  82.5 8.4 %collective-permute-start.21 = (f32[32,128]{1,0:T(8,128)S(1)}, f32[32,128]{1,0:T(8,128)S(1)}, u32[]{:S(2)}, u32[]{:S(2)}) collective-permute-start(f32[32,128]{1,0:T(8,128)S(1)} %fusion.26), channel_id=1, source_target_pairs={{0,4},{2,6},{4,8},{6,10},{8,12},{10,14},{12,16},{14,18},{16,20},{1... | collective-permute-start | bytes 49160 | tf_op jit(solution)/shard_map/ppermute | solution.py:20
  91.0 1.9 collective-permute-start.20
  92.9 1.9 collective-permute-start.19
  94.9 6.3 %collective-permute-start.18 = (f32[32,128]{1,0:T(8,128)S(1)}, f32[32,128]{1,0:T(8,128)S(1)}, u32[]{:S(2)}, u32[]{:S(2)}) collective-permute-start(f32[32,128]{1,0:T(8,128)S(1)} %fusion.26), channel_id=1, source_target_pairs={{0,16},{2,18},{4,20},{6,22},{8,24},{10,26},{12,28},{14,30},{16,32}... | collective-permute-start | bytes 49160 | tf_op jit(solution)/shard_map/ppermute | solution.py:20
  101.4 4.8 %collective-permute-start.17 = (f32[32,128]{1,0:T(8,128)S(1)}, f32[32,128]{1,0:T(8,128)S(1)}, u32[]{:S(2)}, u32[]{:S(2)}) collective-permute-start(f32[32,128]{1,0:T(8,128)S(1)} %fusion.26), channel_id=1, source_target_pairs={{0,24},{2,26},{4,28},{6,30},{8,32},{10,34},{12,36},{14,38},{16,40}... | collective-permute-start | bytes 49160 | tf_op jit(solution)/shard_map/ppermute | solution.py:20
  106.4 1.9 collective-permute-start.5
  108.3 1.9 collective-permute-start.28
  110.2 6.0 %collective-permute-start.27 = (f32[32,128]{1,0:T(8,128)S(1)}, f32[32,128]{1,0:T(8,128)S(1)}, u32[]{:S(2)}, u32[]{:S(2)}) collective-permute-start(f32[32,128]{1,0:T(8,128)S(1)} %fusion.21), channel_id=1, source_target_pairs={{0,8},{2,10},{4,12},{6,14},{8,16},{10,18},{12,20},{14,22},{16,24},... | collective-permute-start | bytes 49160 | tf_op jit(solution)/shard_map/ppermute | solution.py:20
  116.3 1.3 collective-permute-start.26
  117.6 1.3 collective-permute-start.25
  119.1 5.1 %collective-permute-start.24 = (f32[32,128]{1,0:T(8,128)S(1)}, f32[32,128]{1,0:T(8,128)S(1)}, u32[]{:S(2)}, u32[]{:S(2)}) collective-permute-start(f32[32,128]{1,0:T(8,128)S(1)} %fusion.21), channel_id=1, source_target_pairs={{0,32},{2,34},{4,36},{6,38},{8,40},{10,42},{12,44},{14,46},{16,48}... | collective-permute-start | bytes 49160 | tf_op jit(solution)/shard_map/ppermute | solution.py:20
  124.4 9.2 %collective-permute-start.23 = (f32[32,128]{1,0:T(8,128)S(1)}, f32[32,128]{1,0:T(8,128)S(1)}, u32[]{:S(2)}, u32[]{:S(2)}) collective-permute-start(f32[32,128]{1,0:T(8,128)S(1)} %fusion.21), channel_id=1, source_target_pairs={{0,48},{2,50},{4,52},{6,54},{8,56},{10,58},{12,60},{14,62},{16,64}... | collective-permute-start | bytes 49160 | tf_op jit(solution)/shard_map/ppermute | solution.py:20
  133.6 4.0 %collective-permute-start.34 = (f32[32,128]{1,0:T(8,128)S(1)}, f32[32,128]{1,0:T(8,128)S(1)}, u32[]{:S(2)}, u32[]{:S(2)}) collective-permute-start(f32[32,128]{1,0:T(8,128)S(1)} %fusion.16), channel_id=1, source_target_pairs={{16,0},{18,2},{20,4},{22,6},{24,8},{26,10},{28,12},{30,14},{32,16}... | collective-permute-start | bytes 49160 | tf_op jit(solution)/shard_map/ppermute | solution.py:20
  138.2 6.1 %collective-permute-done.34 = f32[32,128]{1,0:T(8,128)S(1)} collective-permute-done((f32[32,128]{1,0:T(8,128)S(1)}, f32[32,128]{1,0:T(8,128)S(1)}, u32[]{:S(2)}, u32[]{:S(2)}) %collective-permute-start.34) | collective-permute-done | bytes 16416 | tf_op jit(solution)/shard_map/ppermute | solution.py:20
  144.2 5.4 %collective-permute-start.33 = (f32[32,128]{1,0:T(8,128)S(1)}, f32[32,128]{1,0:T(8,128)S(1)}, u32[]{:S(2)}, u32[]{:S(2)}) collective-permute-start(f32[32,128]{1,0:T(8,128)S(1)} %fusion.16), channel_id=1, source_target_pairs={{0,16},{2,18},{4,20},{6,22},{8,24},{10,26},{12,28},{14,30},{16,32}... | collective-permute-start | bytes 49160 | tf_op jit(solution)/shard_map/ppermute | solution.py:20
  149.9 1.5 collective-permute-done.33
  151.5 1.3 collective-permute-start.40
  153.0 5.4 %collective-permute-done.40 = f32[32,128]{1,0:T(8,128)S(1)} collective-permute-done((f32[32,128]{1,0:T(8,128)S(1)}, f32[32,128]{1,0:T(8,128)S(1)}, u32[]{:S(2)}, u32[]{:S(2)}) %collective-permute-start.40) | collective-permute-done | bytes 16416 | tf_op jit(solution)/shard_map/ppermute | solution.py:20
  158.4 7.1 %collective-permute-start.39 = (f32[32,128]{1,0:T(8,128)S(1)}, f32[32,128]{1,0:T(8,128)S(1)}, u32[]{:S(2)}, u32[]{:S(2)}) collective-permute-start(f32[32,128]{1,0:T(8,128)S(1)} %fusion.11), channel_id=1, source_target_pairs={{0,32},{2,34},{4,36},{6,38},{8,40},{10,42},{12,44},{14,46},{16,48}... | collective-permute-start | bytes 49160 | tf_op jit(solution)/shard_map/ppermute | solution.py:20
  168.4 1.3 collective-permute-start.44
  169.7 1.3 collective-permute-start.43
  171.0 16.8 %collective-permute-start.42 = (f32[32,128]{1,0:T(8,128)S(1)}, f32[32,128]{1,0:T(8,128)S(1)}, u32[]{:S(2)}, u32[]{:S(2)}) collective-permute-start(f32[32,128]{1,0:T(8,128)S(1)} %fusion.6), channel_id=1, source_target_pairs={{0,256},{2,258},{4,260},{6,262},{8,264},{10,266},{12,268},{14,270}... | collective-permute-start | bytes 49160 | tf_op jit(solution)/shard_map/ppermute | solution.py:20
  189.2 1.3 collective-permute-start.38
  190.5 1.3 collective-permute-start.37
  191.8 8.5 %collective-permute-start.36 = (f32[32,128]{1,0:T(8,128)S(1)}, f32[32,128]{1,0:T(8,128)S(1)}, u32[]{:S(2)}, u32[]{:S(2)}) collective-permute-start(f32[32,128]{1,0:T(8,128)S(1)} %fusion.11), channel_id=1, source_target_pairs={{0,128},{2,130},{4,132},{6,134},{8,136},{10,138},{12,140},{14,142}... | collective-permute-start | bytes 49160 | tf_op jit(solution)/shard_map/ppermute | solution.py:20
  200.3 10.9 %collective-permute-start.35 = (f32[32,128]{1,0:T(8,128)S(1)}, f32[32,128]{1,0:T(8,128)S(1)}, u32[]{:S(2)}, u32[]{:S(2)}) collective-permute-start(f32[32,128]{1,0:T(8,128)S(1)} %fusion.11), channel_id=1, source_target_pairs={{0,192},{2,194},{4,196},{6,198},{8,200},{10,202},{12,204},{14,206}... | collective-permute-start | bytes 49160 | tf_op jit(solution)/shard_map/ppermute | solution.py:20
  213.1 7.5 %collective-permute-start.30 = (f32[32,128]{1,0:T(8,128)S(1)}, f32[32,128]{1,0:T(8,128)S(1)}, u32[]{:S(2)}, u32[]{:S(2)}) collective-permute-start(f32[32,128]{1,0:T(8,128)S(1)} %fusion.16), channel_id=1, source_target_pairs={{0,64},{2,66},{4,68},{6,70},{8,72},{10,74},{12,76},{14,78},{16,80}... | collective-permute-start | bytes 49160 | tf_op jit(solution)/shard_map/ppermute | solution.py:20
  220.6 4.0 %collective-permute-start.45 = (f32[32,128]{1,0:T(8,128)S(1)}, f32[32,128]{1,0:T(8,128)S(1)}, u32[]{:S(2)}, u32[]{:S(2)}) collective-permute-start(f32[32,128]{1,0:T(8,128)S(1)} %convolution_bitcast_fusion.17), channel_id=1, source_target_pairs={{0,32},{2,34},{4,36},{6,38},{8,40},{10,42},{12,44},{14,46},{16,48}... | collective-permute-start | bytes 49160 | tf_op jit(solution)/shard_map/ppermute | solution.py:20
  226.1 8.0 %collective-permute-start.29 = (f32[32,128]{1,0:T(8,128)S(1)}, f32[32,128]{1,0:T(8,128)S(1)}, u32[]{:S(2)}, u32[]{:S(2)}) collective-permute-start(f32[32,128]{1,0:T(8,128)S(1)} %fusion.16), channel_id=1, source_target_pairs={{0,96},{2,98},{4,100},{6,102},{8,104},{10,106},{12,108},{14,110},{... | collective-permute-start | bytes 49160 | tf_op jit(solution)/shard_map/ppermute | solution.py:20
  234.7 2.3 collective-permute-start.47
  237.1 5.0 %collective-permute-start.48 = (f32[32,128]{1,0:T(8,128)S(1)}, f32[32,128]{1,0:T(8,128)S(1)}, u32[]{:S(2)}, u32[]{:S(2)}) collective-permute-start(f32[32,128]{1,0:T(8,128)S(1)} %convolution_bitcast_fusion.14), channel_id=1, source_target_pairs={{16,0},{18,2},{20,4},{22,6},{24,8},{26,10},{28,12},{30,14},{32,16}... | collective-permute-start | bytes 49160 | tf_op jit(solution)/shard_map/ppermute | solution.py:20
  242.2 2.9 collective-permute-done.48
  245.7 1.9 collective-permute-start.49
  247.6 3.9 %collective-permute-start.50 = (f32[32,128]{1,0:T(8,128)S(1)}, f32[32,128]{1,0:T(8,128)S(1)}, u32[]{:S(2)}, u32[]{:S(2)}) collective-permute-start(f32[32,128]{1,0:T(8,128)S(1)} %convolution_bitcast_fusion.12), channel_id=1, source_target_pairs={{8,0},{10,2},{12,4},{14,6},{16,8},{18,10},{20,12},{22,14},{24,16},... | collective-permute-start | bytes 49160 | tf_op jit(solution)/shard_map/ppermute | solution.py:20
  251.6 3.8 %collective-permute-done.50 = f32[32,128]{1,0:T(8,128)S(1)} collective-permute-done((f32[32,128]{1,0:T(8,128)S(1)}, f32[32,128]{1,0:T(8,128)S(1)}, u32[]{:S(2)}, u32[]{:S(2)}) %collective-permute-start.50) | collective-permute-done | bytes 16416 | tf_op jit(solution)/shard_map/ppermute | solution.py:20
  256.0 1.9 collective-permute-start.51
  257.9 5.4 %collective-permute-start.52 = (f32[32,128]{1,0:T(8,128)S(1)}, f32[32,128]{1,0:T(8,128)S(1)}, u32[]{:S(2)}, u32[]{:S(2)}) collective-permute-start(f32[32,128]{1,0:T(8,128)S(1)} %convolution_bitcast_fusion.10), channel_id=1, source_target_pairs={{4,0},{6,2},{8,4},{10,6},{12,8},{14,10},{16,12},{18,14},{20,16},{2... | collective-permute-start | bytes 49160 | tf_op jit(solution)/shard_map/ppermute | solution.py:20
  263.4 4.7 %collective-permute-done.52 = f32[32,128]{1,0:T(8,128)S(1)} collective-permute-done((f32[32,128]{1,0:T(8,128)S(1)}, f32[32,128]{1,0:T(8,128)S(1)}, u32[]{:S(2)}, u32[]{:S(2)}) %collective-permute-start.52) | collective-permute-done | bytes 16416 | tf_op jit(solution)/shard_map/ppermute | solution.py:20
  268.7 5.1 %collective-permute-start.53 = (f32[32,128]{1,0:T(8,128)S(1)}, f32[32,128]{1,0:T(8,128)S(1)}, u32[]{:S(2)}, u32[]{:S(2)}) collective-permute-start(f32[32,128]{1,0:T(8,128)S(1)} %convolution_bitcast_fusion.9), channel_id=1, source_target_pairs={{0,2},{2,4},{4,6},{6,8},{8,10},{10,12},{12,14},{14,16},{16,18},{18... | collective-permute-start | bytes 49160 | tf_op jit(solution)/shard_map/ppermute | solution.py:20
  273.8 3.0 %collective-permute-start.54 = (f32[32,128]{1,0:T(8,128)S(1)}, f32[32,128]{1,0:T(8,128)S(1)}, u32[]{:S(2)}, u32[]{:S(2)}) collective-permute-start(f32[32,128]{1,0:T(8,128)S(1)} %convolution_bitcast_fusion.8), channel_id=1, source_target_pairs={{2,0},{4,2},{6,4},{8,6},{10,8},{12,10},{14,12},{16,14},{18,16},{20... | collective-permute-start | bytes 49160 | tf_op jit(solution)/shard_map/ppermute | solution.py:20
  276.9 6.8 %collective-permute-done.54 = f32[32,128]{1,0:T(8,128)S(1)} collective-permute-done((f32[32,128]{1,0:T(8,128)S(1)}, f32[32,128]{1,0:T(8,128)S(1)}, u32[]{:S(2)}, u32[]{:S(2)}) %collective-permute-start.54) | collective-permute-done | bytes 16416 | tf_op jit(solution)/shard_map/ppermute | solution.py:20
  284.0 1.9 collective-permute-start.55
  287.7 6.1 %collective-permute-done.55 = f32[32,128]{1,0:T(8,128)S(1)} collective-permute-done((f32[32,128]{1,0:T(8,128)S(1)}, f32[32,128]{1,0:T(8,128)S(1)}, u32[]{:S(2)}, u32[]{:S(2)}) %collective-permute-start.55) | collective-permute-done | bytes 16416 | tf_op jit(solution)/shard_map/ppermute | solution.py:20
  (171 shorter events, 24.1 us)
Async XLA Ops:
  0.0 211.2 %copy-start = (bf16[1,32,96]{2,1,0:T(8,128)(2,1)S(1)}, bf16[1,32,96]{2,1,0:T(8,128)(2,1)}, u32[]{:S(2)}) copy-start(bf16[1,32,96]{2,1,0:T(8,128)(2,1)} %param.23) | copy-start | bytes 18436
  2.2 21.6 %copy-start.10 = (s32[48]{0:T(128)S(1)}, s32[48]{0:T(128)}, u32[]{:S(2)}) copy-start(s32[48]{0:T(128)} %constant.268) | copy-start | bytes 580
  2.2 21.6 %copy-start.9 = (s32[24]{0:T(128)S(1)}, s32[24]{0:T(128)}, u32[]{:S(2)}) copy-start(s32[24]{0:T(128)} %constant.269) | copy-start | bytes 292
  2.2 21.7 %copy-start.8 = (s32[12]{0:T(128)S(1)}, s32[12]{0:T(128)}, u32[]{:S(2)}) copy-start(s32[12]{0:T(128)} %constant.270) | copy-start | bytes 148
  2.3 21.7 %copy-start.7 = (s32[6]{0:T(128)S(1)}, s32[6]{0:T(128)}, u32[]{:S(2)}) copy-start(s32[6]{0:T(128)} %constant.271) | copy-start | bytes 76
  2.3 21.7 %copy-start.2 = (bf16[1,32,64]{2,1,0:T(8,128)(2,1)S(1)}, bf16[1,32,64]{2,1,0:T(8,128)(2,1)}, u32[]{:S(2)}) copy-start(bf16[1,32,64]{2,1,0:T(8,128)(2,1)} %param.22) | copy-start | bytes 12292
  3.0 47.1 %collective-permute-start.10 = (f32[32,128]{1,0:T(8,128)S(1)}, f32[32,128]{1,0:T(8,128)S(1)}, u32[]{:S(2)}, u32[]{:S(2)}) collective-permute-start(f32[32,128]{1,0:T(8,128)S(1)} %bitcast.305), channel_id=1, source_target_pairs={{0,2},{2,4},{4,6},{6,8},{8,10},{10,12},{12,14},{14,16},{16,18},{18... | collective-permute-start | bytes 49160 | tf_op jit(solution)/shard_map/ppermute | solution.py:20
  6.4 47.0 %collective-permute-start.9 = (f32[32,128]{1,0:T(8,128)S(1)}, f32[32,128]{1,0:T(8,128)S(1)}, u32[]{:S(2)}, u32[]{:S(2)}) collective-permute-start(f32[32,128]{1,0:T(8,128)S(1)} %bitcast.306), channel_id=1, source_target_pairs={{6,0},{8,2},{10,4},{12,6},{14,8},{16,10},{18,12},{20,14},{22,16},{... | collective-permute-start | bytes 49160 | tf_op jit(solution)/shard_map/ppermute | solution.py:20
  8.8 47.3 %collective-permute-start.8 = (f32[32,128]{1,0:T(8,128)S(1)}, f32[32,128]{1,0:T(8,128)S(1)}, u32[]{:S(2)}, u32[]{:S(2)}) collective-permute-start(f32[32,128]{1,0:T(8,128)S(1)} %bitcast.307), channel_id=1, source_target_pairs={{4,0},{6,2},{8,4},{10,6},{12,8},{14,10},{16,12},{18,14},{20,16},{2... | collective-permute-start | bytes 49160 | tf_op jit(solution)/shard_map/ppermute | solution.py:20
  13.1 11.4 %collective-permute-start.1 = (f32[3,64]{1,0:T(4,128)S(1)}, f32[3,64]{1,0:T(4,128)S(1)}, u32[]{:S(2)}, u32[]{:S(2)}) collective-permute-start(f32[3,64]{1,0:T(4,128)S(1)} %get-tuple-element.44), channel_id=1, source_target_pairs={{2,0},{4,2},{6,4},{8,6},{10,8},{12,10},{14,12},{16,14},{18,16},{20... | collective-permute-start | bytes 2312 | tf_op jit(solution)/shard_map/ppermute | solution.py:33
  15.3 11.7 %collective-permute-start = (f32[3,64]{1,0:T(4,128)S(1)}, f32[3,64]{1,0:T(4,128)S(1)}, u32[]{:S(2)}, u32[]{:S(2)}) collective-permute-start(f32[3,64]{1,0:T(4,128)S(1)} %get-tuple-element.45), channel_id=1, source_target_pairs={{0,2},{2,4},{4,6},{6,8},{8,10},{10,12},{12,14},{14,16},{16,18},{18... | collective-permute-start | bytes 2312 | tf_op jit(solution)/shard_map/ppermute | solution.py:31
  24.5 7.1 %collective-permute-start.2 = (bf16[64,128]{1,0:T(8,128)(2,1)S(1)}, bf16[64,128]{1,0:T(8,128)(2,1)S(1)}, u32[]{:S(2)}, u32[]{:S(2)}) collective-permute-start(bf16[64,128]{1,0:T(8,128)(2,1)S(1)} %get-tuple-element.19), channel_id=1, source_target_pairs={{0,2},{2,4},{4,6},{6,8},{8,10},{10,12},{12,14},{14,16},{16,18},{18... | collective-permute-start | bytes 49160 | tf_op jit(solution)/shard_map/ppermute | solution.py:31
  27.0 10.5 %collective-permute-start.3 = (bf16[64,128]{1,0:T(8,128)(2,1)S(1)}, bf16[64,128]{1,0:T(8,128)(2,1)S(1)}, u32[]{:S(2)}, u32[]{:S(2)}) collective-permute-start(bf16[64,128]{1,0:T(8,128)(2,1)S(1)} %get-tuple-element.20), channel_id=1, source_target_pairs={{2,0},{4,2},{6,4},{8,6},{10,8},{12,10},{14,12},{16,14},{18,16},{20... | collective-permute-start | bytes 49160 | tf_op jit(solution)/shard_map/ppermute | solution.py:33
  31.6 31.9 %collective-permute-start.7 = (f32[32,128]{1,0:T(8,128)S(1)}, f32[32,128]{1,0:T(8,128)S(1)}, u32[]{:S(2)}, u32[]{:S(2)}) collective-permute-start(f32[32,128]{1,0:T(8,128)S(1)} %bitcast.308), channel_id=1, source_target_pairs={{0,4},{2,6},{4,8},{6,10},{8,12},{10,14},{12,16},{14,18},{16,20},{1... | collective-permute-start | bytes 49160 | tf_op jit(solution)/shard_map/ppermute | solution.py:20
  37.5 27.9 %collective-permute-start.6 = (f32[32,128]{1,0:T(8,128)S(1)}, f32[32,128]{1,0:T(8,128)S(1)}, u32[]{:S(2)}, u32[]{:S(2)}) collective-permute-start(f32[32,128]{1,0:T(8,128)S(1)} %bitcast.309), channel_id=1, source_target_pairs={{0,6},{2,8},{4,10},{6,12},{8,14},{10,16},{12,18},{14,20},{16,22},{... | collective-permute-start | bytes 49160 | tf_op jit(solution)/shard_map/ppermute | solution.py:20
  46.6 250.1 %all-to-all-start = ((f32[512,2,128]{2,0,1:T(8,128)}), f32[512,2,128]{2,0,1:T(8,128)S(1)}, u32[]{:S(2)}, u32[]{:S(2)}) async-start(f32[512,2,128]{2,0,1:T(8,128)} %copy.49), calls=%async_computation | async-start | bytes 1048576 | tf_op jit(solution)/shard_map/all_to_all | solution.py:172
  50.1 74.2 %collective-permute-start.4 = (bf16[4,2,32,128]{3,2,1,0:T(8,128)(2,1)S(1)}, bf16[4,2,32,128]{3,2,1,0:T(8,128)(2,1)S(1)}, u32[]{:S(2)}, u32[]{:S(2)}) collective-permute-start(bf16[4,2,32,128]{3,2,1,0:T(8,128)(2,1)S(1)} %get-tuple-element.38), channel_id=1, source_target_pairs={{0,2},{2,4},{4,6},{6,8},{8,10},{10,12},{12,14},{14,16},{16,18},{18... | collective-permute-start | bytes 196616 | tf_op jit(solution)/shard_map/ppermute | solution.py:31
  53.4 14.7 %collective-permute-start.16 = (f32[32,128]{1,0:T(8,128)S(1)}, f32[32,128]{1,0:T(8,128)S(1)}, u32[]{:S(2)}, u32[]{:S(2)}) collective-permute-start(f32[32,128]{1,0:T(8,128)S(1)} %fusion.31), channel_id=1, source_target_pairs={{2,0},{4,2},{6,4},{8,6},{10,8},{12,10},{14,12},{16,14},{18,16},{20... | collective-permute-start | bytes 49160 | tf_op jit(solution)/shard_map/ppermute | solution.py:20
  56.1 17.5 %collective-permute-start.15 = (f32[32,128]{1,0:T(8,128)S(1)}, f32[32,128]{1,0:T(8,128)S(1)}, u32[]{:S(2)}, u32[]{:S(2)}) collective-permute-start(f32[32,128]{1,0:T(8,128)S(1)} %fusion.31), channel_id=1, source_target_pairs={{0,2},{2,4},{4,6},{6,8},{8,10},{10,12},{12,14},{14,16},{16,18},{18... | collective-permute-start | bytes 49160 | tf_op jit(solution)/shard_map/ppermute | solution.py:20
  63.5 16.9 %collective-permute-start.14 = (f32[32,128]{1,0:T(8,128)S(1)}, f32[32,128]{1,0:T(8,128)S(1)}, u32[]{:S(2)}, u32[]{:S(2)}) collective-permute-start(f32[32,128]{1,0:T(8,128)S(1)} %fusion.31), channel_id=1, source_target_pairs={{12,0},{14,2},{16,4},{18,6},{20,8},{22,10},{24,12},{26,14},{28,16}... | collective-permute-start | bytes 49160 | tf_op jit(solution)/shard_map/ppermute | solution.py:20
  65.5 17.0 %collective-permute-start.13 = (f32[32,128]{1,0:T(8,128)S(1)}, f32[32,128]{1,0:T(8,128)S(1)}, u32[]{:S(2)}, u32[]{:S(2)}) collective-permute-start(f32[32,128]{1,0:T(8,128)S(1)} %fusion.31), channel_id=1, source_target_pairs={{8,0},{10,2},{12,4},{14,6},{16,8},{18,10},{20,12},{22,14},{24,16},... | collective-permute-start | bytes 49160 | tf_op jit(solution)/shard_map/ppermute | solution.py:20
  68.2 22.8 %collective-permute-start.12 = (f32[32,128]{1,0:T(8,128)S(1)}, f32[32,128]{1,0:T(8,128)S(1)}, u32[]{:S(2)}, u32[]{:S(2)}) collective-permute-start(f32[32,128]{1,0:T(8,128)S(1)} %fusion.31), channel_id=1, source_target_pairs={{0,8},{2,10},{4,12},{6,14},{8,16},{10,18},{12,20},{14,22},{16,24},... | collective-permute-start | bytes 49160 | tf_op jit(solution)/shard_map/ppermute | solution.py:20
  73.7 19.2 %collective-permute-start.11 = (f32[32,128]{1,0:T(8,128)S(1)}, f32[32,128]{1,0:T(8,128)S(1)}, u32[]{:S(2)}, u32[]{:S(2)}) collective-permute-start(f32[32,128]{1,0:T(8,128)S(1)} %fusion.31), channel_id=1, source_target_pairs={{0,12},{2,14},{4,16},{6,18},{8,20},{10,22},{12,24},{14,26},{16,28}... | collective-permute-start | bytes 49160 | tf_op jit(solution)/shard_map/ppermute | solution.py:20
  80.4 72.4 %copy-start.4 = (bf16[1,31,32,96]{3,2,1,0:T(8,128)(2,1)S(1)}, bf16[1,31,32,96]{3,2,1,0:T(8,128)(2,1)}, u32[]{:S(2)}) copy-start(bf16[1,31,32,96]{3,2,1,0:T(8,128)(2,1)} %param.21) | copy-start | bytes 571396
  80.4 14.4 %collective-permute-start.22 = (f32[32,128]{1,0:T(8,128)S(1)}, f32[32,128]{1,0:T(8,128)S(1)}, u32[]{:S(2)}, u32[]{:S(2)}) collective-permute-start(f32[32,128]{1,0:T(8,128)S(1)} %fusion.26), channel_id=1, source_target_pairs={{4,0},{6,2},{8,4},{10,6},{12,8},{14,10},{16,12},{18,14},{20,16},{2... | collective-permute-start | bytes 49160 | tf_op jit(solution)/shard_map/ppermute | solution.py:20
  82.5 18.9 %collective-permute-start.21 = (f32[32,128]{1,0:T(8,128)S(1)}, f32[32,128]{1,0:T(8,128)S(1)}, u32[]{:S(2)}, u32[]{:S(2)}) collective-permute-start(f32[32,128]{1,0:T(8,128)S(1)} %fusion.26), channel_id=1, source_target_pairs={{0,4},{2,6},{4,8},{6,10},{8,12},{10,14},{12,16},{14,18},{16,20},{1... | collective-permute-start | bytes 49160 | tf_op jit(solution)/shard_map/ppermute | solution.py:20
  91.0 15.4 %collective-permute-start.20 = (f32[32,128]{1,0:T(8,128)S(1)}, f32[32,128]{1,0:T(8,128)S(1)}, u32[]{:S(2)}, u32[]{:S(2)}) collective-permute-start(f32[32,128]{1,0:T(8,128)S(1)} %fusion.26), channel_id=1, source_target_pairs={{24,0},{26,2},{28,4},{30,6},{32,8},{34,10},{36,12},{38,14},{40,16}... | collective-permute-start | bytes 49160 | tf_op jit(solution)/shard_map/ppermute | solution.py:20
  92.9 15.4 %collective-permute-start.19 = (f32[32,128]{1,0:T(8,128)S(1)}, f32[32,128]{1,0:T(8,128)S(1)}, u32[]{:S(2)}, u32[]{:S(2)}) collective-permute-start(f32[32,128]{1,0:T(8,128)S(1)} %fusion.26), channel_id=1, source_target_pairs={{16,0},{18,2},{20,4},{22,6},{24,8},{26,10},{28,12},{30,14},{32,16}... | collective-permute-start | bytes 49160 | tf_op jit(solution)/shard_map/ppermute | solution.py:20
  94.9 15.4 %collective-permute-start.18 = (f32[32,128]{1,0:T(8,128)S(1)}, f32[32,128]{1,0:T(8,128)S(1)}, u32[]{:S(2)}, u32[]{:S(2)}) collective-permute-start(f32[32,128]{1,0:T(8,128)S(1)} %fusion.26), channel_id=1, source_target_pairs={{0,16},{2,18},{4,20},{6,22},{8,24},{10,26},{12,28},{14,30},{16,32}... | collective-permute-start | bytes 49160 | tf_op jit(solution)/shard_map/ppermute | solution.py:20
  101.4 14.9 %collective-permute-start.17 = (f32[32,128]{1,0:T(8,128)S(1)}, f32[32,128]{1,0:T(8,128)S(1)}, u32[]{:S(2)}, u32[]{:S(2)}) collective-permute-start(f32[32,128]{1,0:T(8,128)S(1)} %fusion.26), channel_id=1, source_target_pairs={{0,24},{2,26},{4,28},{6,30},{8,32},{10,34},{12,36},{14,38},{16,40}... | collective-permute-start | bytes 49160 | tf_op jit(solution)/shard_map/ppermute | solution.py:20
  106.4 27.2 %collective-permute-start.5 = (bf16[4,2,32,128]{3,2,1,0:T(8,128)(2,1)S(1)}, bf16[4,2,32,128]{3,2,1,0:T(8,128)(2,1)S(1)}, u32[]{:S(2)}, u32[]{:S(2)}) collective-permute-start(bf16[4,2,32,128]{3,2,1,0:T(8,128)(2,1)S(1)} %get-tuple-element.39), channel_id=1, source_target_pairs={{2,0},{4,2},{6,4},{8,6},{10,8},{12,10},{14,12},{16,14},{18,16},{20... | collective-permute-start | bytes 196616 | tf_op jit(solution)/shard_map/ppermute | solution.py:33
  108.3 9.3 %collective-permute-start.28 = (f32[32,128]{1,0:T(8,128)S(1)}, f32[32,128]{1,0:T(8,128)S(1)}, u32[]{:S(2)}, u32[]{:S(2)}) collective-permute-start(f32[32,128]{1,0:T(8,128)S(1)} %fusion.21), channel_id=1, source_target_pairs={{8,0},{10,2},{12,4},{14,6},{16,8},{18,10},{20,12},{22,14},{24,16},... | collective-permute-start | bytes 49160 | tf_op jit(solution)/shard_map/ppermute | solution.py:20
  110.2 8.9 %collective-permute-start.27 = (f32[32,128]{1,0:T(8,128)S(1)}, f32[32,128]{1,0:T(8,128)S(1)}, u32[]{:S(2)}, u32[]{:S(2)}) collective-permute-start(f32[32,128]{1,0:T(8,128)S(1)} %fusion.21), channel_id=1, source_target_pairs={{0,8},{2,10},{4,12},{6,14},{8,16},{10,18},{12,20},{14,22},{16,24},... | collective-permute-start | bytes 49160 | tf_op jit(solution)/shard_map/ppermute | solution.py:20
  116.3 52.1 %collective-permute-start.26 = (f32[32,128]{1,0:T(8,128)S(1)}, f32[32,128]{1,0:T(8,128)S(1)}, u32[]{:S(2)}, u32[]{:S(2)}) collective-permute-start(f32[32,128]{1,0:T(8,128)S(1)} %fusion.21), channel_id=1, source_target_pairs={{48,0},{50,2},{52,4},{54,6},{56,8},{58,10},{60,12},{62,14},{64,16}... | collective-permute-start | bytes 49160 | tf_op jit(solution)/shard_map/ppermute | solution.py:20
  117.6 52.1 %collective-permute-start.25 = (f32[32,128]{1,0:T(8,128)S(1)}, f32[32,128]{1,0:T(8,128)S(1)}, u32[]{:S(2)}, u32[]{:S(2)}) collective-permute-start(f32[32,128]{1,0:T(8,128)S(1)} %fusion.21), channel_id=1, source_target_pairs={{32,0},{34,2},{36,4},{38,6},{40,8},{42,10},{44,12},{46,14},{48,16}... | collective-permute-start | bytes 49160 | tf_op jit(solution)/shard_map/ppermute | solution.py:20
  119.1 51.9 %collective-permute-start.24 = (f32[32,128]{1,0:T(8,128)S(1)}, f32[32,128]{1,0:T(8,128)S(1)}, u32[]{:S(2)}, u32[]{:S(2)}) collective-permute-start(f32[32,128]{1,0:T(8,128)S(1)} %fusion.21), channel_id=1, source_target_pairs={{0,32},{2,34},{4,36},{6,38},{8,40},{10,42},{12,44},{14,46},{16,48}... | collective-permute-start | bytes 49160 | tf_op jit(solution)/shard_map/ppermute | solution.py:20
  124.4 63.5 %collective-permute-start.23 = (f32[32,128]{1,0:T(8,128)S(1)}, f32[32,128]{1,0:T(8,128)S(1)}, u32[]{:S(2)}, u32[]{:S(2)}) collective-permute-start(f32[32,128]{1,0:T(8,128)S(1)} %fusion.21), channel_id=1, source_target_pairs={{0,48},{2,50},{4,52},{6,54},{8,56},{10,58},{12,60},{14,62},{16,64}... | collective-permute-start | bytes 49160 | tf_op jit(solution)/shard_map/ppermute | solution.py:20
  133.6 10.7 %collective-permute-start.34 = (f32[32,128]{1,0:T(8,128)S(1)}, f32[32,128]{1,0:T(8,128)S(1)}, u32[]{:S(2)}, u32[]{:S(2)}) collective-permute-start(f32[32,128]{1,0:T(8,128)S(1)} %fusion.16), channel_id=1, source_target_pairs={{16,0},{18,2},{20,4},{22,6},{24,8},{26,10},{28,12},{30,14},{32,16}... | collective-permute-start | bytes 49160 | tf_op jit(solution)/shard_map/ppermute | solution.py:20
  144.2 7.1 %collective-permute-start.33 = (f32[32,128]{1,0:T(8,128)S(1)}, f32[32,128]{1,0:T(8,128)S(1)}, u32[]{:S(2)}, u32[]{:S(2)}) collective-permute-start(f32[32,128]{1,0:T(8,128)S(1)} %fusion.16), channel_id=1, source_target_pairs={{0,16},{2,18},{4,20},{6,22},{8,24},{10,26},{12,28},{14,30},{16,32}... | collective-permute-start | bytes 49160 | tf_op jit(solution)/shard_map/ppermute | solution.py:20
  151.5 6.9 %collective-permute-start.40 = (f32[32,128]{1,0:T(8,128)S(1)}, f32[32,128]{1,0:T(8,128)S(1)}, u32[]{:S(2)}, u32[]{:S(2)}) collective-permute-start(f32[32,128]{1,0:T(8,128)S(1)} %fusion.11), channel_id=1, source_target_pairs={{32,0},{34,2},{36,4},{38,6},{40,8},{42,10},{44,12},{46,14},{48,16}... | collective-permute-start | bytes 49160 | tf_op jit(solution)/shard_map/ppermute | solution.py:20
  158.4 8.6 %collective-permute-start.39 = (f32[32,128]{1,0:T(8,128)S(1)}, f32[32,128]{1,0:T(8,128)S(1)}, u32[]{:S(2)}, u32[]{:S(2)}) collective-permute-start(f32[32,128]{1,0:T(8,128)S(1)} %fusion.11), channel_id=1, source_target_pairs={{0,32},{2,34},{4,36},{6,38},{8,40},{10,42},{12,44},{14,46},{16,48}... | collective-permute-start | bytes 49160 | tf_op jit(solution)/shard_map/ppermute | solution.py:20
  167.0 70.1 %collective-permute-start.32 = (f32[32,128]{1,0:T(8,128)S(1)}, f32[32,128]{1,0:T(8,128)S(1)}, u32[]{:S(2)}, u32[]{:S(2)}) collective-permute-start(f32[32,128]{1,0:T(8,128)S(1)} %fusion.16), channel_id=1, source_target_pairs={{96,0},{98,2},{100,4},{102,6},{104,8},{106,10},{108,12},{110,14},{... | collective-permute-start | bytes 49160 | tf_op jit(solution)/shard_map/ppermute | solution.py:20
  168.4 20.8 %collective-permute-start.44 = (f32[32,128]{1,0:T(8,128)S(1)}, f32[32,128]{1,0:T(8,128)S(1)}, u32[]{:S(2)}, u32[]{:S(2)}) collective-permute-start(f32[32,128]{1,0:T(8,128)S(1)} %fusion.6), channel_id=1, source_target_pairs={{384,0},{386,2},{388,4},{390,6},{392,8},{394,10},{396,12},{398,14}... | collective-permute-start | bytes 49160 | tf_op jit(solution)/shard_map/ppermute | solution.py:20
  169.7 20.8 %collective-permute-start.43 = (f32[32,128]{1,0:T(8,128)S(1)}, f32[32,128]{1,0:T(8,128)S(1)}, u32[]{:S(2)}, u32[]{:S(2)}) collective-permute-start(f32[32,128]{1,0:T(8,128)S(1)} %fusion.6), channel_id=1, source_target_pairs={{256,0},{258,2},{260,4},{262,6},{264,8},{266,10},{268,12},{270,14}... | collective-permute-start | bytes 49160 | tf_op jit(solution)/shard_map/ppermute | solution.py:20
  171.0 20.8 %collective-permute-start.42 = (f32[32,128]{1,0:T(8,128)S(1)}, f32[32,128]{1,0:T(8,128)S(1)}, u32[]{:S(2)}, u32[]{:S(2)}) collective-permute-start(f32[32,128]{1,0:T(8,128)S(1)} %fusion.6), channel_id=1, source_target_pairs={{0,256},{2,258},{4,260},{6,262},{8,264},{10,266},{12,268},{14,270}... | collective-permute-start | bytes 49160 | tf_op jit(solution)/shard_map/ppermute | solution.py:20
  187.9 12.4 %collective-permute-start.41 = (f32[32,128]{1,0:T(8,128)S(1)}, f32[32,128]{1,0:T(8,128)S(1)}, u32[]{:S(2)}, u32[]{:S(2)}) collective-permute-start(f32[32,128]{1,0:T(8,128)S(1)} %fusion.6), channel_id=1, source_target_pairs={{0,384},{2,386},{4,388},{6,390},{8,392},{10,394},{12,396},{14,398}... | collective-permute-start | bytes 49160 | tf_op jit(solution)/shard_map/ppermute | solution.py:20
  189.2 22.6 %collective-permute-start.38 = (f32[32,128]{1,0:T(8,128)S(1)}, f32[32,128]{1,0:T(8,128)S(1)}, u32[]{:S(2)}, u32[]{:S(2)}) collective-permute-start(f32[32,128]{1,0:T(8,128)S(1)} %fusion.11), channel_id=1, source_target_pairs={{192,0},{194,2},{196,4},{198,6},{200,8},{202,10},{204,12},{206,14}... | collective-permute-start | bytes 49160 | tf_op jit(solution)/shard_map/ppermute | solution.py:20
  190.5 22.6 %collective-permute-start.37 = (f32[32,128]{1,0:T(8,128)S(1)}, f32[32,128]{1,0:T(8,128)S(1)}, u32[]{:S(2)}, u32[]{:S(2)}) collective-permute-start(f32[32,128]{1,0:T(8,128)S(1)} %fusion.11), channel_id=1, source_target_pairs={{128,0},{130,2},{132,4},{134,6},{136,8},{138,10},{140,12},{142,14}... | collective-permute-start | bytes 49160 | tf_op jit(solution)/shard_map/ppermute | solution.py:20
  191.8 28.8 %collective-permute-start.36 = (f32[32,128]{1,0:T(8,128)S(1)}, f32[32,128]{1,0:T(8,128)S(1)}, u32[]{:S(2)}, u32[]{:S(2)}) collective-permute-start(f32[32,128]{1,0:T(8,128)S(1)} %fusion.11), channel_id=1, source_target_pairs={{0,128},{2,130},{4,132},{6,134},{8,136},{10,138},{12,140},{14,142}... | collective-permute-start | bytes 49160 | tf_op jit(solution)/shard_map/ppermute | solution.py:20
  200.3 24.4 %collective-permute-start.35 = (f32[32,128]{1,0:T(8,128)S(1)}, f32[32,128]{1,0:T(8,128)S(1)}, u32[]{:S(2)}, u32[]{:S(2)}) collective-permute-start(f32[32,128]{1,0:T(8,128)S(1)} %fusion.11), channel_id=1, source_target_pairs={{0,192},{2,194},{4,196},{6,198},{8,200},{10,202},{12,204},{14,206}... | collective-permute-start | bytes 49160 | tf_op jit(solution)/shard_map/ppermute | solution.py:20
  211.8 30.3 %collective-permute-start.31 = (f32[32,128]{1,0:T(8,128)S(1)}, f32[32,128]{1,0:T(8,128)S(1)}, u32[]{:S(2)}, u32[]{:S(2)}) collective-permute-start(f32[32,128]{1,0:T(8,128)S(1)} %fusion.16), channel_id=1, source_target_pairs={{64,0},{66,2},{68,4},{70,6},{72,8},{74,10},{76,12},{78,14},{80,16}... | collective-permute-start | bytes 49160 | tf_op jit(solution)/shard_map/ppermute | solution.py:20
  213.1 29.0 %collective-permute-start.30 = (f32[32,128]{1,0:T(8,128)S(1)}, f32[32,128]{1,0:T(8,128)S(1)}, u32[]{:S(2)}, u32[]{:S(2)}) collective-permute-start(f32[32,128]{1,0:T(8,128)S(1)} %fusion.16), channel_id=1, source_target_pairs={{0,64},{2,66},{4,68},{6,70},{8,72},{10,74},{12,76},{14,78},{16,80}... | collective-permute-start | bytes 49160 | tf_op jit(solution)/shard_map/ppermute | solution.py:20
  220.6 5.4 %collective-permute-start.45 = (f32[32,128]{1,0:T(8,128)S(1)}, f32[32,128]{1,0:T(8,128)S(1)}, u32[]{:S(2)}, u32[]{:S(2)}) collective-permute-start(f32[32,128]{1,0:T(8,128)S(1)} %convolution_bitcast_fusion.17), channel_id=1, source_target_pairs={{0,32},{2,34},{4,36},{6,38},{8,40},{10,42},{12,44},{14,46},{16,48}... | collective-permute-start | bytes 49160 | tf_op jit(solution)/shard_map/ppermute | solution.py:20
  224.7 9.5 %collective-permute-start.46 = (f32[32,128]{1,0:T(8,128)S(1)}, f32[32,128]{1,0:T(8,128)S(1)}, u32[]{:S(2)}, u32[]{:S(2)}) collective-permute-start(f32[32,128]{1,0:T(8,128)S(1)} %convolution_bitcast_fusion.16), channel_id=1, source_target_pairs={{32,0},{34,2},{36,4},{38,6},{40,8},{42,10},{44,12},{46,14},{48,16}... | collective-permute-start | bytes 49160 | tf_op jit(solution)/shard_map/ppermute | solution.py:20
  226.1 16.1 %collective-permute-start.29 = (f32[32,128]{1,0:T(8,128)S(1)}, f32[32,128]{1,0:T(8,128)S(1)}, u32[]{:S(2)}, u32[]{:S(2)}) collective-permute-start(f32[32,128]{1,0:T(8,128)S(1)} %fusion.16), channel_id=1, source_target_pairs={{0,96},{2,98},{4,100},{6,102},{8,104},{10,106},{12,108},{14,110},{... | collective-permute-start | bytes 49160 | tf_op jit(solution)/shard_map/ppermute | solution.py:20
  234.7 7.4 %collective-permute-start.47 = (f32[32,128]{1,0:T(8,128)S(1)}, f32[32,128]{1,0:T(8,128)S(1)}, u32[]{:S(2)}, u32[]{:S(2)}) collective-permute-start(f32[32,128]{1,0:T(8,128)S(1)} %convolution_bitcast_fusion.15), channel_id=1, source_target_pairs={{0,16},{2,18},{4,20},{6,22},{8,24},{10,26},{12,28},{14,30},{16,32}... | collective-permute-start | bytes 49160 | tf_op jit(solution)/shard_map/ppermute | solution.py:20
  237.1 8.0 %collective-permute-start.48 = (f32[32,128]{1,0:T(8,128)S(1)}, f32[32,128]{1,0:T(8,128)S(1)}, u32[]{:S(2)}, u32[]{:S(2)}) collective-permute-start(f32[32,128]{1,0:T(8,128)S(1)} %convolution_bitcast_fusion.14), channel_id=1, source_target_pairs={{16,0},{18,2},{20,4},{22,6},{24,8},{26,10},{28,12},{30,14},{32,16}... | collective-permute-start | bytes 49160 | tf_op jit(solution)/shard_map/ppermute | solution.py:20
  245.7 5.9 %collective-permute-start.49 = (f32[32,128]{1,0:T(8,128)S(1)}, f32[32,128]{1,0:T(8,128)S(1)}, u32[]{:S(2)}, u32[]{:S(2)}) collective-permute-start(f32[32,128]{1,0:T(8,128)S(1)} %convolution_bitcast_fusion.13), channel_id=1, source_target_pairs={{0,8},{2,10},{4,12},{6,14},{8,16},{10,18},{12,20},{14,22},{16,24},... | collective-permute-start | bytes 49160 | tf_op jit(solution)/shard_map/ppermute | solution.py:20
  247.6 7.7 %collective-permute-start.50 = (f32[32,128]{1,0:T(8,128)S(1)}, f32[32,128]{1,0:T(8,128)S(1)}, u32[]{:S(2)}, u32[]{:S(2)}) collective-permute-start(f32[32,128]{1,0:T(8,128)S(1)} %convolution_bitcast_fusion.12), channel_id=1, source_target_pairs={{8,0},{10,2},{12,4},{14,6},{16,8},{18,10},{20,12},{22,14},{24,16},... | collective-permute-start | bytes 49160 | tf_op jit(solution)/shard_map/ppermute | solution.py:20
  256.0 7.4 %collective-permute-start.51 = (f32[32,128]{1,0:T(8,128)S(1)}, f32[32,128]{1,0:T(8,128)S(1)}, u32[]{:S(2)}, u32[]{:S(2)}) collective-permute-start(f32[32,128]{1,0:T(8,128)S(1)} %convolution_bitcast_fusion.11), channel_id=1, source_target_pairs={{0,4},{2,6},{4,8},{6,10},{8,12},{10,14},{12,16},{14,18},{16,20},{1... | collective-permute-start | bytes 49160 | tf_op jit(solution)/shard_map/ppermute | solution.py:20
  257.9 10.1 %collective-permute-start.52 = (f32[32,128]{1,0:T(8,128)S(1)}, f32[32,128]{1,0:T(8,128)S(1)}, u32[]{:S(2)}, u32[]{:S(2)}) collective-permute-start(f32[32,128]{1,0:T(8,128)S(1)} %convolution_bitcast_fusion.10), channel_id=1, source_target_pairs={{4,0},{6,2},{8,4},{10,6},{12,8},{14,10},{16,12},{18,14},{20,16},{2... | collective-permute-start | bytes 49160 | tf_op jit(solution)/shard_map/ppermute | solution.py:20
  268.7 8.2 %collective-permute-start.53 = (f32[32,128]{1,0:T(8,128)S(1)}, f32[32,128]{1,0:T(8,128)S(1)}, u32[]{:S(2)}, u32[]{:S(2)}) collective-permute-start(f32[32,128]{1,0:T(8,128)S(1)} %convolution_bitcast_fusion.9), channel_id=1, source_target_pairs={{0,2},{2,4},{4,6},{6,8},{8,10},{10,12},{12,14},{14,16},{16,18},{18... | collective-permute-start | bytes 49160 | tf_op jit(solution)/shard_map/ppermute | solution.py:20
  273.8 9.9 %collective-permute-start.54 = (f32[32,128]{1,0:T(8,128)S(1)}, f32[32,128]{1,0:T(8,128)S(1)}, u32[]{:S(2)}, u32[]{:S(2)}) collective-permute-start(f32[32,128]{1,0:T(8,128)S(1)} %convolution_bitcast_fusion.8), channel_id=1, source_target_pairs={{2,0},{4,2},{6,4},{8,6},{10,8},{12,10},{14,12},{16,14},{18,16},{20... | collective-permute-start | bytes 49160 | tf_op jit(solution)/shard_map/ppermute | solution.py:20
  284.0 9.9 %collective-permute-start.55 = (f32[32,128]{1,0:T(8,128)S(1)}, f32[32,128]{1,0:T(8,128)S(1)}, u32[]{:S(2)}, u32[]{:S(2)}) collective-permute-start(f32[32,128]{1,0:T(8,128)S(1)} %convolution_bitcast_fusion.6), channel_id=1, source_target_pairs={{2,0},{4,2},{6,4},{8,6},{10,8},{12,10},{14,12},{16,14},{18,16},{20... | collective-permute-start | bytes 49160 | tf_op jit(solution)/shard_map/ppermute | solution.py:20
  (4 other events, 56.8 us)
where the time goes:
time: 300 us; the launch traced here: 297 us
  starting transfers between devices  234 us (78%)
  waiting for transfers between devices  38.8 us (13%)
  matrix products  11.7 us (4%)
  local copies, waits for them, and re-layouts  7.32 us (2%)
    ppermute x50, starting transfers between devices, passed_along(): return lax.ppermute(block, axis, route)  210 us
    ppermute x50, waiting for transfers between devices, passed_along(): return lax.ppermute(block, axis, route)  38.8 us
    ppermute x3, starting transfers between devices, extended_2(): lax.ppermute(tail, axis, [(i, (i + 1) % count) for i in range(ends)])  13.6 us
    ppermute x3, starting transfers between devices, extended_2(): lax.ppermute(head, axis, [((i + 1) % count, i) for i in range(ends)])  7.38 us
  transfers between devices with their start and end apart: 57, of which 10 were waited for; matrix products, arithmetic and copies ran while one was open for 6% of the time, Pallas kernels for 0%

commit v1 on v0

--- a/solution.py
+++ b/solution.py
@@ -12,12 +12,6 @@
 VARIANCE = 0.0625
 NUGGET = 0.5
 HIGHEST = lax.Precision.HIGHEST
-
-
-def passed_along(block, axis, distance):
-    devices = range(lax.axis_size(axis))
-    route = [(i - distance, i) for i in devices if i - distance in devices]
-    return lax.ppermute(block, axis, route)
 
 
 def extended_2(cells, sides, width):
@@ -86,69 +80,46 @@
     return jnp.dot(matrix, operand, precision=HIGHEST)
 
 
-def move_cluster(operand, amount):
-    return passed_along(operand, "space", amount)
-
-
-def child_steps(height):
-    if height == 1:
-        return (1, 0)
-    return (2 ** (height - 2), 2 ** (height - 2))
-
-
-def pick_three(parity, far_left, near_left, near_right, far_right):
-    odd_mask = parity == 1
-    return jnp.concatenate(
-        [
-            jnp.where(odd_mask, far_left, near_left),
-            jnp.where(odd_mask, near_left, near_right),
-            jnp.where(odd_mask, near_right, far_right),
-        ],
-        0,
-    )
-
-
-def chain_partners(operand, spacing, parity):
-    return pick_three(
-        parity,
-        move_cluster(operand, 3 * spacing),
-        move_cluster(operand, 2 * spacing),
-        move_cluster(operand, -2 * spacing),
-        move_cluster(operand, -3 * spacing),
-    )
-
-
-def chain_tree(device_coef, device_coupling, upper_transfer, upper_coupling, position, space_bits):
-    lift_mats = as_float(upper_transfer[0])
-    mixers = as_float(upper_coupling[0])
+def neighbours(coefs, cluster):
+    padded = jnp.pad(coefs, ((3, 3), (0, 0), (0, 0)))
+    odd_mask = cluster % 2 == 1
+    offsets = (
+        jnp.where(odd_mask, -3, -2),
+        jnp.where(odd_mask, -2, 2),
+        jnp.where(odd_mask, 2, 3),
+    )
+    picked = [lax.dynamic_index_in_dim(padded, cluster + 3 + step, 0, False) for step in offsets]
+    return jnp.concatenate(picked, 0)
+
+
+def upper_tree(device_coef, device_coupling, upper_transfer, upper_coupling, position, space_bits):
+    count = 2**space_bits
     summit = space_bits - 2
-    fields = [product(device_coupling, chain_partners(device_coef, 1, position % 2))]
-    current = device_coef
+    level_coefs = [lax.all_gather(device_coef, "space")]
+    lift_all = as_float(lax.all_gather(upper_transfer[0], "space"))
+    mix_all = as_float(lax.all_gather(upper_coupling[0], "space"))
     for height in range(1, summit + 1):
-        step_left, step_right = child_steps(height)
-        holder = position % 2**height == 2 ** (height - 1)
-        left_child = move_cluster(current, step_left)
-        right_child = current if step_right == 0 else move_cluster(current, -step_right)
-        lifted = product(lift_mats[:, :RANK], left_child) + product(
-            lift_mats[:, RANK:], right_child
-        )
-        current = jnp.where(holder, lifted, 0.0)
-        parity = position // 2**height % 2
-        fields.append(
-            jnp.where(holder, product(mixers, chain_partners(current, 2**height, parity)), 0.0)
-        )
-    downward = fields[summit]
+        cluster_count = count >> height
+        lift_mats = lift_all[2 ** (height - 1) :: 2**height]
+        children = level_coefs[-1].reshape(cluster_count, 2 * RANK, -1)
+        level_coefs.append(jnp.einsum("cra,cav->crv", lift_mats, children, precision=HIGHEST))
+
+    def field(height, cluster):
+        if height == 0:
+            mixer = device_coupling
+        else:
+            mixer = lax.dynamic_index_in_dim(
+                mix_all, cluster * 2**height + 2 ** (height - 1), 0, False
+            )
+        return product(mixer, neighbours(level_coefs[height], cluster))
+
+    downward = field(summit, position >> summit)
     for height in range(summit - 1, -1, -1):
-        step_left, step_right = child_steps(height + 1)
-        to_left = product(lift_mats[:, :RANK].T, downward)
-        to_right = product(lift_mats[:, RANK:].T, downward)
-        from_left = move_cluster(to_left, -step_left)
-        from_right = to_right if step_right == 0 else move_cluster(to_right, step_right)
-        parity = position // 2**height % 2
-        downward = fields[height] + jnp.where(parity == 1, from_right, from_left)
-        if height > 0:
-            holder = position % 2**height == 2 ** (height - 1)
-            downward = jnp.where(holder, downward, 0.0)
+        cluster = position >> height
+        parent = cluster >> 1
+        lift = lax.dynamic_index_in_dim(lift_all, parent * 2 ** (height + 1) + 2**height, 0, False)
+        half = jnp.where(cluster % 2 == 1, lift[:, RANK:], lift[:, :RANK])
+        downward = field(height, cluster) + product(half.T, downward)
     return downward
 
 
@@ -205,7 +176,7 @@
         fields.append(jnp.einsum("cra,cav->crv", mixers, stacked, precision=HIGHEST))
     device_coupling = as_float(coupling[0, 2 * leaf_count - 2])
     device_coef = coefficients[depth_local][0]
-    downward = chain_tree(
+    downward = upper_tree(
         device_coef, device_coupling, upper_transfer, upper_coupling, position, space_bits
     )
     downward = downward[None]

time: 300 us -> 643 us (2.14)
  the two profiles are of different devices: /device:TPU:30 before, /device:TPU:6 now
where the time goes in v1:
time: 643 us; the launch traced here: 640 us
  waiting for transfers between devices  536 us (83%)
  matrix products  33.4 us (5%)
  starting transfers between devices  28.1 us (4%)
  local copies, waits for them, and re-layouts  18.9 us (3%)
  between operations  13.9 us (2%)
  other arithmetic  7.55 us (1%)
    all_gather x1, waiting for transfers between devices, upper_tree(): level_coefs = [lax.all_gather(device_coef, 'space')]  209 us
    all_gather x1, waiting for transfers between devices, upper_tree(): mix_all = as_float(lax.all_gather(upper_coupling[0], 'space'))  178 us
    all_gather x1, waiting for transfers between devices, upper_tree(): lift_all = as_float(lax.all_gather(upper_transfer[0], 'space'))  149 us
    ppermute x3, starting transfers between devices, extended_2(): lax.ppermute(tail, axis, [(i, (i + 1) % count) for i in range(ends)])  17.3 us
  transfers between devices with their start and end apart: 10, of which 4 were waited for; matrix products, arithmetic and copies ran while one was open for 8% of the time, Pallas kernels for 0%

profile of v1, /device:TPU:6, one launch (start us, length us, event | category | flops | bytes accessed | tf_op | source)
XLA Modules:
  0.0 640.4 jit_solution(15796708810521620030)
XLA Ops:
  6.6 0.7 all-gather.5.cloned.1.call-update
  7.4 1.0 reshape.92
  8.4 1.1 fusion.163
  9.5 1.1 bitcast_convert_fusion.1
  10.6 0.9 fusion.81
  11.5 0.9 bitcast_convert_fusion
  12.4 1.4 convolution_bitcast_fusion.8
  14.0 0.7 fusion.159
  14.7 2.7 collective-permute-start.5
  17.4 5.2 collective-permute-start.4
  22.7 1.9 collective-permute-start.3
  24.7 6.0 collective-permute-start
  30.7 1.9 collective-permute-start.1
  32.8 0.7 slice_bitcast_fusion
  33.6 0.6 pad_clamp_fusion
  34.1 0.7 copy.51
  35.2 0.6 copy.48
  35.9 6.0 collective-permute-start.2
  42.1 0.6 gather_fusion
  43.3 2.2 all_gather.12
  45.6 0.6 gather_fusion.1
  46.2 2.0 convolution_bitcast_fusion
  48.1 1.3 all_to_all.14
  49.4 0.9 copy.49
  50.3 4.2 all-to-all-start
  54.5 0.7 convert_bitcast_fusion.4
  55.3 0.8 convert_bitcast_fusion.6
  56.0 0.7 gather_fusion.5
  56.7 0.7 convert_bitcast_fusion.5
  57.5 1.2 gather_fusion.4
  58.7 1.4 gather_fusion.3
  60.1 1.5 gather_fusion.2
  61.6 1.5 convolution_bitcast_fusion.6
  63.1 148.8 %all-gather.5.cloned.1.call-done = bf16[256,32,64]{2,1,0:T(8,128)(2,1)} async-done(((bf16[1,32,64]{2,1,0:T(8,128)(2,1)}), bf16[256,32,64]{2,1,0:T(8,128)(2,1)}) %all-gather.5.cloned.1.call-update) | async-done | bytes 1048592 | tf_op jit(solution)/shard_map/all_gather | solution.py:99
  211.9 2.2 convert_element_type.32
  214.1 0.6 dynamic-slice_bitcast_fusion.5
  214.7 208.8 %all-gather.9.cloned.1.call-done = f32[8192,128]{1,0:T(8,128)} async-done(((f32[32,128]{1,0:T(8,128)}), f32[8192,128]{1,0:T(8,128)}) %all-gather.9.cloned.1.call-update) | async-done | bytes 4194320 | tf_op jit(solution)/shard_map/all_gather | solution.py:98
  423.6 0.9 fusion.117
  424.5 1.3 copy-done
  425.8 3.4 fusion.5
  429.1 2.2 fusion.8
  431.3 1.6 fusion.16
  432.9 0.8 copy-done.1
  433.7 2.0 fusion.20
  435.7 1.2 fusion.32
  436.9 0.6 fusion.90
  437.5 0.9 convolution_bitcast_fusion.3
  438.4 0.6 fusion.87
  439.1 1.4 convolution_bitcast_fusion.7
  440.5 177.7 %all-gather.7.cloned.1.call-done = bf16[256,32,96]{2,1,0:T(8,128)(2,1)} async-done(((bf16[1,32,96]{2,1,0:T(8,128)(2,1)}), bf16[256,32,96]{2,1,0:T(8,128)(2,1)}) %all-gather.7.cloned.1.call-update) | async-done | bytes 1572880 | tf_op jit(solution)/shard_map/all_gather | solution.py:100
  618.2 0.9 fusion.66
  619.2 0.9 fusion.72
  620.1 1.1 convolution_add_fusion.5
  621.2 0.8 fusion.105
  621.9 0.8 fusion.60
  622.8 1.1 convolution_add_fusion.4
  623.9 0.8 fusion.108
  624.7 0.9 fusion.54
  625.6 1.1 convolution_add_fusion.3
  626.8 0.9 fusion.48
  628.0 0.9 fusion.42
  631.0 0.5 fusion
  631.5 0.4 fusion.23
  632.0 1.9 fusion.7
  (86 shorter events, 3.9 us)
Async XLA Ops:
  6.5 27.0 %copy-start.18 = (s32[6]{0:T(128)S(1)}, s32[6]{0:T(128)}, u32[]{:S(2)}) copy-start(s32[6]{0:T(128)} %constant.279) | copy-start | bytes 76
  6.5 28.3 %copy-start.17 = (s32[12]{0:T(128)S(1)}, s32[12]{0:T(128)}, u32[]{:S(2)}) copy-start(s32[12]{0:T(128)} %constant.278) | copy-start | bytes 148
  6.5 28.3 %copy-start.16 = (s32[24]{0:T(128)S(1)}, s32[24]{0:T(128)}, u32[]{:S(2)}) copy-start(s32[24]{0:T(128)} %constant.277) | copy-start | bytes 292
  6.5 28.3 %copy-start.15 = (s32[48]{0:T(128)S(1)}, s32[48]{0:T(128)}, u32[]{:S(2)}) copy-start(s32[48]{0:T(128)} %constant.276) | copy-start | bytes 580
  6.5 16.1 %copy-start.3 = (bf16[1024,128]{1,0:T(8,128)(2,1)S(1)}, bf16[1024,128]{1,0:T(8,128)(2,1)}, u32[]{:S(2)}) copy-start(bf16[1024,128]{1,0:T(8,128)(2,1)} %param.16) | copy-start | bytes 786436
  6.6 18.1 %copy-start.13 = (f32[3,1024]{1,0:T(4,128)S(1)}, f32[3,1024]{1,0:T(4,128)}, u32[]{:S(2)}) copy-start(f32[3,1024]{1,0:T(4,128)} %param.17) | copy-start | bytes 36868
  6.6 28.3 %copy-start.14 = (s32[16,3]{0,1:T(4,128)S(1)}, s32[16,3]{0,1:T(4,128)}, u32[]{:S(2)}) copy-start(s32[16,3]{0,1:T(4,128)} %param.18) | copy-start | bytes 580
  6.6 205.3 %all-gather.5.cloned.1.call-start = ((), (), s32[]{:S(2)}) async-start(), calls=%async_computation.1 | async-start | bytes 2105344 | tf_op jit(solution)/shard_map/all_gather | solution.py:99
  7.3 416.3 %all-gather.9.cloned.1.call-start = ((), (), s32[]{:S(2)}) async-start(), calls=%async_computation.3 | async-start | bytes 4210688 | tf_op jit(solution)/shard_map/all_gather | solution.py:98
  13.9 604.4 %all-gather.7.cloned.1.call-start = ((), (), s32[]{:S(2)}) async-start(), calls=%async_computation.2 | async-start | bytes 2105344 | tf_op jit(solution)/shard_map/all_gather | solution.py:100
  14.7 39.8 %collective-permute-start.5 = (bf16[4,2,32,128]{3,2,1,0:T(8,128)(2,1)}, bf16[4,2,32,128]{3,2,1,0:T(8,128)(2,1)S(1)}, u32[]{:S(2)}, u32[]{:S(2)}) collective-permute-start(bf16[4,2,32,128]{3,2,1,0:T(8,128)(2,1)} %get-tuple-element.63), channel_id=1, source_target_pairs={{2,0},{4,2},{6,4},{8,6},{10,8},{12,10},{14,12},{16,14},{18,16},{20... | collective-permute-start | bytes 196616 | tf_op jit(solution)/shard_map/ppermute | solution.py:27
  17.4 37.1 %collective-permute-start.4 = (bf16[4,2,32,128]{3,2,1,0:T(8,128)(2,1)}, bf16[4,2,32,128]{3,2,1,0:T(8,128)(2,1)}, u32[]{:S(2)}, u32[]{:S(2)}) collective-permute-start(bf16[4,2,32,128]{3,2,1,0:T(8,128)(2,1)} %get-tuple-element.62), channel_id=1, source_target_pairs={{0,2},{2,4},{4,6},{6,8},{8,10},{10,12},{12,14},{14,16},{16,18},{18... | collective-permute-start | bytes 196616 | tf_op jit(solution)/shard_map/ppermute | solution.py:25
  22.7 20.5 %collective-permute-start.3 = (bf16[64,128]{1,0:T(8,128)(2,1)S(1)}, bf16[64,128]{1,0:T(8,128)(2,1)S(1)}, u32[]{:S(2)}, u32[]{:S(2)}) collective-permute-start(bf16[64,128]{1,0:T(8,128)(2,1)S(1)} %get-tuple-element.47), channel_id=1, source_target_pairs={{2,0},{4,2},{6,4},{8,6},{10,8},{12,10},{14,12},{16,14},{18,16},{20... | collective-permute-start | bytes 49160 | tf_op jit(solution)/shard_map/ppermute | solution.py:27
  24.7 11.2 %collective-permute-start = (f32[3,64]{1,0:T(4,128)S(1)}, f32[3,64]{1,0:T(4,128)S(1)}, u32[]{:S(2)}, u32[]{:S(2)}) collective-permute-start(f32[3,64]{1,0:T(4,128)S(1)} %get-tuple-element.72), channel_id=1, source_target_pairs={{0,2},{2,4},{4,6},{6,8},{8,10},{10,12},{12,14},{14,16},{16,18},{18... | collective-permute-start | bytes 2312 | tf_op jit(solution)/shard_map/ppermute | solution.py:25
  30.7 11.2 %collective-permute-start.1 = (f32[3,64]{1,0:T(4,128)S(1)}, f32[3,64]{1,0:T(4,128)S(1)}, u32[]{:S(2)}, u32[]{:S(2)}) collective-permute-start(f32[3,64]{1,0:T(4,128)S(1)} %get-tuple-element.71), channel_id=1, source_target_pairs={{2,0},{4,2},{6,4},{8,6},{10,8},{12,10},{14,12},{16,14},{18,16},{20... | collective-permute-start | bytes 2312 | tf_op jit(solution)/shard_map/ppermute | solution.py:27
  35.9 7.4 %collective-permute-start.2 = (bf16[64,128]{1,0:T(8,128)(2,1)S(1)}, bf16[64,128]{1,0:T(8,128)(2,1)S(1)}, u32[]{:S(2)}, u32[]{:S(2)}) collective-permute-start(bf16[64,128]{1,0:T(8,128)(2,1)S(1)} %get-tuple-element.46), channel_id=1, source_target_pairs={{0,2},{2,4},{4,6},{6,8},{8,10},{10,12},{12,14},{14,16},{16,18},{18... | collective-permute-start | bytes 49160 | tf_op jit(solution)/shard_map/ppermute | solution.py:25
  50.3 581.7 %all-to-all-start = ((f32[512,2,128]{2,0,1:T(8,128)}), f32[512,2,128]{2,0,1:T(8,128)}, u32[]{:S(2)}, u32[]{:S(2)}) async-start(f32[512,2,128]{2,0,1:T(8,128)} %copy.49), calls=%async_computation | async-start | bytes 1048576 | tf_op jit(solution)/shard_map/all_to_all | solution.py:143
  423.6 2.2 copy-start
  432.9 0.8 copy-start.1
  618.2 9.4 %copy-start.10 = (f32[32,64]{1,0:T(8,128)S(1)}, f32[32,64]{1,0:T(8,128)}, u32[]{:S(2)}) copy-start(f32[32,64]{1,0:T(8,128)} %get-tuple-element.32) | copy-start | bytes 24580
  623.9 5.0 copy-start.9
  623.9 5.3 copy-start.12
  623.9 5.6 copy-start.8
  623.9 5.6 copy-start.11
  623.9 5.8 copy-start.6
  624.7 5.2 copy-start.5
  624.7 5.2 copy-start.7
  626.7 3.7 copy-start.4
  628.0 3.1 copy-start.2
Sparse Core Ops, SparseCore 0:
  11.7 200.1 all-gather.4
  216.4 207.1 all-gather.8
  427.8 190.3 all-gather.6

commit v2 on v1

--- a/solution.py
+++ b/solution.py
@@ -80,8 +80,12 @@
     return jnp.dot(matrix, operand, precision=HIGHEST)
 
 
-def neighbours(coefs, cluster):
-    padded = jnp.pad(coefs, ((3, 3), (0, 0), (0, 0)))
+SPACE = ("z", "y", "x")
+PLANE = ("y", "x")
+CUTS = (16, 4, 4)
+
+
+def neighbours(padded, cluster):
     odd_mask = cluster % 2 == 1
     offsets = (
         jnp.where(odd_mask, -3, -2),
@@ -92,34 +96,77 @@
     return jnp.concatenate(picked, 0)
 
 
-def upper_tree(device_coef, device_coupling, upper_transfer, upper_coupling, position, space_bits):
-    count = 2**space_bits
-    summit = space_bits - 2
-    level_coefs = [lax.all_gather(device_coef, "space")]
-    lift_all = as_float(lax.all_gather(upper_transfer[0], "space"))
-    mix_all = as_float(lax.all_gather(upper_coupling[0], "space"))
-    for height in range(1, summit + 1):
-        cluster_count = count >> height
-        lift_mats = lift_all[2 ** (height - 1) :: 2**height]
-        children = level_coefs[-1].reshape(cluster_count, 2 * RANK, -1)
-        level_coefs.append(jnp.einsum("cra,cav->crv", lift_mats, children, precision=HIGHEST))
-
-    def field(height, cluster):
+def pick(stack, index):
+    return lax.dynamic_index_in_dim(stack, index, 0, False)
+
+
+def lift_up(lift_mats, coefs):
+    children = coefs.reshape(lift_mats.shape[0], 2 * RANK, coefs.shape[-1])
+    return jnp.einsum("cra,cav->crv", lift_mats, children, precision=HIGHEST)
+
+
+def rims(own, left_tail, right_head):
+    zeros = jnp.zeros((3 - left_tail.shape[0],) + own.shape[1:], own.dtype)
+    return jnp.concatenate([zeros, left_tail, own, right_head, zeros], 0)
+
+
+def upper_tree(device_coef, device_coupling, upper_transfer, upper_coupling):
+    planes = lax.axis_size("z")
+    plane_bits = lax.axis_size(PLANE).bit_length() - 1
+    plane = lax.axis_index("z")
+    seat = lax.axis_index(PLANE)
+    plane_lift_held = lax.all_gather(upper_transfer[0], PLANE)
+    plane_mix_held = lax.all_gather(upper_coupling[0], PLANE)
+    plane_lift = as_float(plane_lift_held)
+    plane_mix = as_float(plane_mix_held)
+    inner = [lax.all_gather(device_coef, PLANE)]
+    for height in range(1, plane_bits + 1):
+        inner.append(lift_up(plane_lift[2 ** (height - 1) :: 2**height], inner[-1]))
+    tails = jnp.concatenate([level[-3:] for level in inner[:plane_bits]], 0)
+    heads = jnp.concatenate([level[:3] for level in inner[:plane_bits]], 0)
+    from_left = lax.ppermute(tails, "z", [(i, i + 1) for i in range(planes - 1)])
+    from_right = lax.ppermute(heads, "z", [(i + 1, i) for i in range(planes - 1)])
+    summary = lax.all_gather(inner[plane_bits][0], "z")
+    outer_lift = as_float(lax.all_gather(plane_lift_held[0], "z"))
+    outer_mix = as_float(lax.all_gather(plane_mix_held[0], "z"))
+    outer = [summary]
+    for height in range(1, (planes.bit_length() - 1) - 1):
+        outer.append(lift_up(outer_lift[2 ** (height - 1) :: 2**height], outer[-1]))
+    summit = plane_bits + len(outer) - 1
+    fields = []
+    lifts = []
+    done = 0
+    for height in range(plane_bits):
+        width = min(3, inner[height].shape[0])
+        extended = rims(
+            inner[height], from_left[done : done + width], from_right[done : done + width]
+        )
+        done += width
+        cluster = seat >> height
         if height == 0:
             mixer = device_coupling
         else:
-            mixer = lax.dynamic_index_in_dim(
-                mix_all, cluster * 2**height + 2 ** (height - 1), 0, False
-            )
-        return product(mixer, neighbours(level_coefs[height], cluster))
-
-    downward = field(summit, position >> summit)
+            mixer = pick(plane_mix, cluster * 2**height + 2 ** (height - 1))
+        fields.append(product(mixer, neighbours(extended, cluster)))
+        parent = cluster >> 1
+        lifts.append((cluster, pick(plane_lift, parent * 2 ** (height + 1) + 2**height)))
+    for level, coefs in enumerate(outer):
+        height = plane_bits + level
+        cluster = plane >> level
+        if level == 0:
+            mixer = pick(plane_mix, 2 ** (height - 1))
+        else:
+            mixer = pick(outer_mix, cluster * 2**level + 2 ** (level - 1))
+        padded = jnp.pad(coefs, ((3, 3), (0, 0), (0, 0)))
+        fields.append(product(mixer, neighbours(padded, cluster)))
+        if height < summit:
+            parent = cluster >> 1
+            lifts.append((cluster, pick(outer_lift, parent * 2 ** (level + 1) + 2**level)))
+    downward = fields[summit]
     for height in range(summit - 1, -1, -1):
-        cluster = position >> height
-        parent = cluster >> 1
-        lift = lax.dynamic_index_in_dim(lift_all, parent * 2 ** (height + 1) + 2**height, 0, False)
+        cluster, lift = lifts[height]
         half = jnp.where(cluster % 2 == 1, lift[:, RANK:], lift[:, :RANK])
-        downward = field(height, cluster) + product(half.T, downward)
+        downward = fields[height] + product(half.T, downward)
     return downward
 
 
@@ -129,11 +176,10 @@
     row_count, columns = vectors.shape
     leaf_count = row_count // LEAF
     depth_local = leaf_count.bit_length() - 1
-    space_bits = lax.axis_size("space").bit_length() - 1
-    position = lax.axis_index("space")
+    position = lax.axis_index(SPACE)
     leaf_zero = position * leaf_count
-    vector_rims = extended_2(vectors, (("space", 0),), LEAF)
-    point_rims = extended_2(points, (("space", 1),), LEAF)
+    vector_rims = extended_2(vectors, ((SPACE, 0),), LEAF)
+    point_rims = extended_2(points, ((SPACE, 1),), LEAF)
     lane_count = lax.axis_size("vec")
     lane_leaves = leaf_count // lane_count
     first_leaf = lax.axis_index("vec") * lane_leaves
@@ -159,7 +205,7 @@
         ],
         0,
     )
-    wide_edges = extended_2(edge_coefs.astype(jnp.bfloat16), (("space", 1),), 2).astype(
+    wide_edges = extended_2(edge_coefs.astype(jnp.bfloat16), ((SPACE, 1),), 2).astype(
         edge_coefs.dtype
     )
     fields = []
@@ -176,9 +222,7 @@
         fields.append(jnp.einsum("cra,cav->crv", mixers, stacked, precision=HIGHEST))
     device_coupling = as_float(coupling[0, 2 * leaf_count - 2])
     device_coef = coefficients[depth_local][0]
-    downward = upper_tree(
-        device_coef, device_coupling, upper_transfer, upper_coupling, position, space_bits
-    )
+    downward = upper_tree(device_coef, device_coupling, upper_transfer, upper_coupling)
     downward = downward[None]
     for height in range(depth_local - 1, -1, -1):
         cluster_count = leaf_count >> height + 1
@@ -193,19 +237,21 @@
 
 
 def solution(mesh):
+    devices = mesh.devices.reshape(CUTS + (mesh.shape["vec"],))
+    split_mesh = jax.sharding.Mesh(devices, SPACE + ("vec",))
     return jax.shard_map(
         local,
-        mesh=mesh,
+        mesh=split_mesh,
         in_specs=(
-            P("space", "vec"),
-            P(None, "space"),
-            P("space", None),
-            P(None, "space"),
-            P("space", None, None, None),
-            P("space", None, None, None),
-            P("space", None, None),
-            P("space", None, None),
+            P(SPACE, "vec"),
+            P(None, SPACE),
+            P(SPACE, None),
+            P(None, SPACE),
+            P(SPACE, None, None, None),
+            P(SPACE, None, None, None),
+            P(SPACE, None, None),
+            P(SPACE, None, None),
         ),
-        out_specs=P("space", "vec"),
+        out_specs=P(SPACE, "vec"),
         check_vma=False,
     )

time: 643 us -> 239 us (0.37)
  waiting for transfers between devices: 536 us -> 0.02 us
  blocking collectives: 2.23 us -> 172 us
  matrix products: 33.4 us -> 12.6 us
  between operations: 13.9 us -> 0.87 us
    all_gather x3 -> x0, waiting for transfers between devices: 535 us -> none  [the longest x1 209 us: upper_tree(): level_coefs = [lax.all_gather(device_coef, 'space')]]
    all_gather x0 -> x6, blocking collectives: none -> 170 us  [the longest x1 40.8 us: upper_tree(): summary = lax.all_gather(inner[plane_bits][0], 'z')]
    dot_general x6, matrix products: 11.2 us -> 1.12 us  [lift_up(): return jnp.einsum('cra,cav->crv', lift_mats, children, precision=HIGHEST)]
  transfers between devices with their start and end apart: 10 -> 9, of which waited for: 4 -> 0; matrix products, arithmetic and copies ran while one was open for 8% -> 11% of each run, Pallas kernels for 0% -> 0%
where the time goes in v2:
time: 239 us; the launch traced here: 237 us
  blocking collectives  172 us (72%)
  starting transfers between devices  31.1 us (13%)
  local copies, waits for them, and re-layouts  16.6 us (7%)
  matrix products  12.6 us (5%)
  other arithmetic  3.55 us (1%)
    all_gather x1, blocking collectives, upper_tree(): summary = lax.all_gather(inner[plane_bits][0], 'z')  40.8 us
    all_gather x1, blocking collectives, upper_tree(): outer_lift = as_float(lax.all_gather(plane_lift_held[0], 'z'))  29.5 us
    all_gather x1, blocking collectives, upper_tree(): outer_mix = as_float(lax.all_gather(plane_mix_held[0], 'z'))  26.6 us
    all_gather x1, blocking collectives, upper_tree(): plane_mix_held = lax.all_gather(upper_coupling[0], PLANE)  26.5 us
    all_gather x1, blocking collectives, upper_tree(): inner = [lax.all_gather(device_coef, PLANE)]  25.8 us
    all_gather x1, blocking collectives, upper_tree(): plane_lift_held = lax.all_gather(upper_transfer[0], PLANE)  20.6 us
    ppermute x3, starting transfers between devices, extended_2(): lax.ppermute(tail, axis, [(i, (i + 1) % count) for i in range(ends)])  14.6 us
    ppermute x3, starting transfers between devices, extended_2(): lax.ppermute(head, axis, [((i + 1) % count, i) for i in range(ends)])  7.09 us
  transfers between devices with their start and end apart: 9, of which 0 were waited for; matrix products, arithmetic and copies ran while one was open for 11% of the time, Pallas kernels for 0%

profile of v2, /device:TPU:6, one launch (start us, length us, event | category | flops | bytes accessed | tf_op | source)
XLA Modules:
  0.0 236.7 jit_solution(10833344965487202321)
XLA Ops:
  0.0 1.0 reshape.98
  1.0 1.1 fusion.151
  2.2 0.2 bitcast_convert_fusion.1
  2.5 0.2 fusion.74
  2.9 0.7 fusion.146
  3.5 2.7 %collective-permute-start.5 = (bf16[4,2,32,128]{3,2,1,0:T(8,128)(2,1)}, bf16[4,2,32,128]{3,2,1,0:T(8,128)(2,1)S(1)}, u32[]{:S(2)}, u32[]{:S(2)}) collective-permute-start(bf16[4,2,32,128]{3,2,1,0:T(8,128)(2,1)} %get-tuple-element.73), channel_id=1, source_target_pairs={{2,0},{4,2},{6,4},{8,6},{10,8},{12,10},{14,12},{16,14},{18,16},{20... | collective-permute-start | bytes 196616 | tf_op jit(solution)/shard_map/ppermute | solution.py:27
  6.3 5.2 %collective-permute-start.4 = (bf16[4,2,32,128]{3,2,1,0:T(8,128)(2,1)}, bf16[4,2,32,128]{3,2,1,0:T(8,128)(2,1)S(1)}, u32[]{:S(2)}, u32[]{:S(2)}) collective-permute-start(bf16[4,2,32,128]{3,2,1,0:T(8,128)(2,1)} %get-tuple-element.72), channel_id=1, source_target_pairs={{0,2},{2,4},{4,6},{6,8},{8,10},{10,12},{12,14},{14,16},{16,18},{18... | collective-permute-start | bytes 196616 | tf_op jit(solution)/shard_map/ppermute | solution.py:25
  11.6 25.8 %all-gather = f32[512,128]{1,0:T(8,128)S(1)} all-gather(f32[32,128]{1,0:T(8,128)S(1)} %convolution_bitcast_fusion.10), channel_id=2, replica_groups=mesh['z'=16,'y'=4,'x'=4,'vec'=2] {'y','x'}, dimensions={0}, use_global_device_ids=true | all-gather | bytes 278528 | tf_op jit(solution)/shard_map/all_gather | solution.py:122
  37.4 20.6 %all_gather.23 = bf16[16,32,64]{2,1,0:T(8,128)(2,1)S(1)} all-gather(bf16[1,32,64]{2,1,0:T(8,128)(2,1)S(1)} %copy-done.14), channel_id=1, replica_groups=mesh['z'=16,'y'=4,'x'=4,'vec'=2] {'y','x'}, dimensions={0}, use_global_device_ids=true | all-gather | bytes 69632 | tf_op jit(solution)/shard_map/all_gather | solution.py:118
  58.1 0.2 fusion.26
  58.7 0.8 pad_maximum_fusion.4
  59.5 1.3 collective-permute-start.7
  60.8 3.4 %collective-permute-start = (f32[3,64]{1,0:T(4,128)S(1)}, f32[3,64]{1,0:T(4,128)S(1)}, u32[]{:S(2)}, u32[]{:S(2)}) collective-permute-start(f32[3,64]{1,0:T(4,128)S(1)} %get-tuple-element.86), channel_id=1, source_target_pairs={{0,2},{2,4},{4,6},{6,8},{8,10},{10,12},{12,14},{14,16},{16,18},{18... | collective-permute-start | bytes 2312 | tf_op jit(solution)/shard_map/ppermute | solution.py:25
  64.2 2.5 %collective-permute-start.1 = (f32[3,64]{1,0:T(4,128)S(1)}, f32[3,64]{1,0:T(4,128)S(1)}, u32[]{:S(2)}, u32[]{:S(2)}) collective-permute-start(f32[3,64]{1,0:T(4,128)S(1)} %get-tuple-element.85), channel_id=1, source_target_pairs={{2,0},{4,2},{6,4},{8,6},{10,8},{12,10},{14,12},{16,14},{18,16},{20... | collective-permute-start | bytes 2312 | tf_op jit(solution)/shard_map/ppermute | solution.py:27
  66.8 0.6 constant_dynamic-update-slice_fusion.2
  67.4 26.5 %all_gather.24 = bf16[16,32,96]{2,1,0:T(8,128)(2,1)S(1)} all-gather(bf16[1,32,96]{2,1,0:T(8,128)(2,1)S(1)} %copy-done.15), channel_id=1, replica_groups=mesh['z'=16,'y'=4,'x'=4,'vec'=2] {'y','x'}, dimensions={0}, use_global_device_ids=true | all-gather | bytes 104448 | tf_op jit(solution)/shard_map/all_gather | solution.py:119
  94.1 40.8 %all-gather.1 = f32[512,128]{1,0:T(8,128)S(1)} all-gather(f32[32,128]{1,0:T(8,128)S(1)} %convolution_bitcast_fusion.8), channel_id=3, replica_groups=mesh['z'=16,'y'=4,'x'=4,'vec'=2] {'z'}, dimensions={0}, use_global_device_ids=true | all-gather | bytes 278528 | tf_op jit(solution)/shard_map/all_gather | solution.py:129
  134.9 29.5 %all_gather.26 = bf16[16,32,64]{2,1,0:T(8,128)(2,1)S(1)} all-gather(bf16[1,32,64]{2,1,0:T(8,128)(2,1)S(1)} %slice.300), channel_id=1, replica_groups=mesh['z'=16,'y'=4,'x'=4,'vec'=2] {'z'}, dimensions={0}, use_global_device_ids=true | all-gather | bytes 69632 | tf_op jit(solution)/shard_map/all_gather | solution.py:130
  164.4 0.2 fusion.24
  164.7 26.6 %all_gather.27 = bf16[16,32,96]{2,1,0:T(8,128)(2,1)S(1)} all-gather(bf16[1,32,96]{2,1,0:T(8,128)(2,1)S(1)} %slice.303), channel_id=1, replica_groups=mesh['z'=16,'y'=4,'x'=4,'vec'=2] {'z'}, dimensions={0}, use_global_device_ids=true | all-gather | bytes 104448 | tf_op jit(solution)/shard_map/all_gather | solution.py:131
  191.9 0.7 copy.48
  192.6 0.6 pad_clamp_fusion
  193.2 0.6 pad_clamp_fusion.2
  194.3 0.3 convolution_add_fusion.5
  194.6 0.3 convolution_add_fusion.4
  194.9 0.6 dynamic-slice_bitcast_fusion.14
  195.5 1.9 collective-permute-start.3
  197.5 6.0 %collective-permute-start.2 = (bf16[64,128]{1,0:T(8,128)(2,1)S(1)}, bf16[64,128]{1,0:T(8,128)(2,1)S(1)}, u32[]{:S(2)}, u32[]{:S(2)}) collective-permute-start(bf16[64,128]{1,0:T(8,128)(2,1)S(1)} %get-tuple-element.30), channel_id=1, source_target_pairs={{0,2},{2,4},{4,6},{6,8},{8,10},{10,12},{12,14},{14,16},{16,18},{18... | collective-permute-start | bytes 49160 | tf_op jit(solution)/shard_map/ppermute | solution.py:25
  203.7 0.6 gather_fusion
  204.4 0.4 multiply_reduce_fusion
  204.8 4.6 %collective-permute-start.6 = (f32[11,32,128]{2,1,0:T(8,128)}, f32[11,32,128]{2,1,0:T(8,128)}, u32[]{:S(2)}, u32[]{:S(2)}) collective-permute-start(f32[11,32,128]{2,1,0:T(8,128)} %get-tuple-element.83), channel_id=1, source_target_pairs={{0,32},{32,64},{64,96},{96,128},{128,160},{160,192},{192,224},{224... | collective-permute-start | bytes 540680 | tf_op jit(solution)/shard_map/ppermute | solution.py:127
  209.4 2.2 all_gather.21
  211.6 1.5 gather_fusion.1
  213.2 1.7 convolution_bitcast_fusion
  214.8 0.3 all_to_all.14
  215.1 0.8 copy.49
  216.0 3.5 %all-to-all-start = ((f32[512,2,128]{2,0,1:T(8,128)}), f32[512,2,128]{2,0,1:T(8,128)S(1)}, u32[]{:S(2)}, u32[]{:S(2)}) async-start(f32[512,2,128]{2,0,1:T(8,128)} %copy.49), calls=%async_computation | async-start | bytes 1048576 | tf_op jit(solution)/shard_map/all_to_all | solution.py:189
  219.5 1.3 gather_fusion.5
  220.9 1.2 gather_fusion.4
  222.1 0.6 gather_fusion.3
  222.8 0.6 gather_fusion.2
  223.4 0.3 copy-done.4
  223.7 0.9 convolution_bitcast_fusion.6
  224.6 0.8 slice_dynamic-update-slice_fusion.1
  225.4 0.8 slice_dynamic-update-slice_fusion
  226.2 0.9 fusion.144
  227.1 0.9 fusion.143
  228.1 0.8 copy-done.5
  229.0 0.8 dynamic-slice_bitcast_fusion.5
  229.8 0.8 fusion.48
  230.6 0.3 convolution_add_fusion.3
  230.9 0.8 fusion.42
  231.8 0.3 convolution_add_fusion.2
  232.1 0.8 fusion.36
  233.0 0.3 convolution_add_fusion.1
  233.2 0.3 fusion.4
  233.7 0.2 fusion.95
  233.9 0.2 fusion.2
  234.1 0.3 fusion.72
  234.4 0.3 fusion.1
  234.7 0.3 fusion.20
  235.0 0.5 fusion
  235.5 0.4 fusion.15
  235.9 0.8 fusion.5
  (108 shorter events, 3.0 us)
Async XLA Ops:
  0.0 2.2 copy-start.2
  2.4 35.0 %copy-start.14 = (bf16[1,32,64]{2,1,0:T(8,128)(2,1)S(1)}, bf16[1,32,64]{2,1,0:T(8,128)(2,1)}, u32[]{:S(2)}) copy-start(bf16[1,32,64]{2,1,0:T(8,128)(2,1)} %param.22) | copy-start | bytes 12292
  3.5 215.9 %collective-permute-start.5 = (bf16[4,2,32,128]{3,2,1,0:T(8,128)(2,1)}, bf16[4,2,32,128]{3,2,1,0:T(8,128)(2,1)S(1)}, u32[]{:S(2)}, u32[]{:S(2)}) collective-permute-start(bf16[4,2,32,128]{3,2,1,0:T(8,128)(2,1)} %get-tuple-element.73), channel_id=1, source_target_pairs={{2,0},{4,2},{6,4},{8,6},{10,8},{12,10},{14,12},{16,14},{18,16},{20... | collective-permute-start | bytes 196616 | tf_op jit(solution)/shard_map/ppermute | solution.py:27
  6.3 213.2 %collective-permute-start.4 = (bf16[4,2,32,128]{3,2,1,0:T(8,128)(2,1)}, bf16[4,2,32,128]{3,2,1,0:T(8,128)(2,1)S(1)}, u32[]{:S(2)}, u32[]{:S(2)}) collective-permute-start(bf16[4,2,32,128]{3,2,1,0:T(8,128)(2,1)} %get-tuple-element.72), channel_id=1, source_target_pairs={{0,2},{2,4},{4,6},{6,8},{8,10},{10,12},{12,14},{14,16},{16,18},{18... | collective-permute-start | bytes 196616 | tf_op jit(solution)/shard_map/ppermute | solution.py:25
  58.3 2.5 %copy-start.13 = (f32[3,1024]{1,0:T(4,128)S(1)}, f32[3,1024]{1,0:T(4,128)}, u32[]{:S(2)}) copy-start(f32[3,1024]{1,0:T(4,128)} %param.17) | copy-start | bytes 36868
  58.7 8.7 %copy-start = (bf16[1024,128]{1,0:T(8,128)(2,1)S(1)}, bf16[1024,128]{1,0:T(8,128)(2,1)}, u32[]{:S(2)}) copy-start(bf16[1024,128]{1,0:T(8,128)(2,1)} %param.16) | copy-start | bytes 786436
  58.7 8.7 %copy-start.15 = (bf16[1,32,96]{2,1,0:T(8,128)(2,1)S(1)}, bf16[1,32,96]{2,1,0:T(8,128)(2,1)}, u32[]{:S(2)}) copy-start(bf16[1,32,96]{2,1,0:T(8,128)(2,1)} %param.23) | copy-start | bytes 18436
  59.5 165.9 %collective-permute-start.7 = (f32[11,32,128]{2,1,0:T(8,128)}, f32[11,32,128]{2,1,0:T(8,128)}, u32[]{:S(2)}, u32[]{:S(2)}) collective-permute-start(f32[11,32,128]{2,1,0:T(8,128)} %get-tuple-element.84), channel_id=1, source_target_pairs={{32,0},{64,32},{96,64},{128,96},{160,128},{192,160},{224,192},{256... | collective-permute-start | bytes 540680 | tf_op jit(solution)/shard_map/ppermute | solution.py:128
  60.8 134.7 %collective-permute-start = (f32[3,64]{1,0:T(4,128)S(1)}, f32[3,64]{1,0:T(4,128)S(1)}, u32[]{:S(2)}, u32[]{:S(2)}) collective-permute-start(f32[3,64]{1,0:T(4,128)S(1)} %get-tuple-element.86), channel_id=1, source_target_pairs={{0,2},{2,4},{4,6},{6,8},{8,10},{10,12},{12,14},{14,16},{16,18},{18... | collective-permute-start | bytes 2312 | tf_op jit(solution)/shard_map/ppermute | solution.py:25
  64.2 133.2 %collective-permute-start.1 = (f32[3,64]{1,0:T(4,128)S(1)}, f32[3,64]{1,0:T(4,128)S(1)}, u32[]{:S(2)}, u32[]{:S(2)}) collective-permute-start(f32[3,64]{1,0:T(4,128)S(1)} %get-tuple-element.85), channel_id=1, source_target_pairs={{2,0},{4,2},{6,4},{8,6},{10,8},{12,10},{14,12},{16,14},{18,16},{20... | collective-permute-start | bytes 2312 | tf_op jit(solution)/shard_map/ppermute | solution.py:27
  94.0 99.8 %copy-start.6 = (bf16[16,32,96]{2,1,0:T(8,128)(2,1)}, bf16[16,32,96]{2,1,0:T(8,128)(2,1)S(1)}, u32[]{:S(2)}) copy-start(bf16[16,32,96]{2,1,0:T(8,128)(2,1)S(1)} %all_gather.24) | copy-start | bytes 294916
  94.1 97.5 %copy-start.16 = (s32[16,3]{0,1:T(4,128)S(1)}, s32[16,3]{0,1:T(4,128)}, u32[]{:S(2)}) copy-start(s32[16,3]{0,1:T(4,128)} %param.18) | copy-start | bytes 580
  134.9 57.7 %copy-start.20 = (s32[6]{0:T(128)S(1)}, s32[6]{0:T(128)}, u32[]{:S(2)}) copy-start(s32[6]{0:T(128)} %constant.262) | copy-start | bytes 76
  134.9 57.7 %copy-start.21 = (s32[12]{0:T(128)S(1)}, s32[12]{0:T(128)}, u32[]{:S(2)}) copy-start(s32[12]{0:T(128)} %constant.261) | copy-start | bytes 148
  134.9 58.3 %copy-start.18 = (s32[24]{0:T(128)S(1)}, s32[24]{0:T(128)}, u32[]{:S(2)}) copy-start(s32[24]{0:T(128)} %constant.260) | copy-start | bytes 292
  134.9 58.3 %copy-start.19 = (s32[48]{0:T(128)S(1)}, s32[48]{0:T(128)}, u32[]{:S(2)}) copy-start(s32[48]{0:T(128)} %constant.259) | copy-start | bytes 580
  195.5 9.2 %collective-permute-start.3 = (bf16[64,128]{1,0:T(8,128)(2,1)S(1)}, bf16[64,128]{1,0:T(8,128)(2,1)S(1)}, u32[]{:S(2)}, u32[]{:S(2)}) collective-permute-start(bf16[64,128]{1,0:T(8,128)(2,1)S(1)} %get-tuple-element.32), channel_id=1, source_target_pairs={{2,0},{4,2},{6,4},{8,6},{10,8},{12,10},{14,12},{16,14},{18,16},{20... | collective-permute-start | bytes 49160 | tf_op jit(solution)/shard_map/ppermute | solution.py:27
  197.5 11.9 %collective-permute-start.2 = (bf16[64,128]{1,0:T(8,128)(2,1)S(1)}, bf16[64,128]{1,0:T(8,128)(2,1)S(1)}, u32[]{:S(2)}, u32[]{:S(2)}) collective-permute-start(bf16[64,128]{1,0:T(8,128)(2,1)S(1)} %get-tuple-element.30), channel_id=1, source_target_pairs={{0,2},{2,4},{4,6},{6,8},{8,10},{10,12},{12,14},{14,16},{16,18},{18... | collective-permute-start | bytes 49160 | tf_op jit(solution)/shard_map/ppermute | solution.py:25
  204.8 19.8 %collective-permute-start.6 = (f32[11,32,128]{2,1,0:T(8,128)}, f32[11,32,128]{2,1,0:T(8,128)}, u32[]{:S(2)}, u32[]{:S(2)}) collective-permute-start(f32[11,32,128]{2,1,0:T(8,128)} %get-tuple-element.83), channel_id=1, source_target_pairs={{0,32},{32,64},{64,96},{96,128},{128,160},{160,192},{192,224},{224... | collective-permute-start | bytes 540680 | tf_op jit(solution)/shard_map/ppermute | solution.py:127
  211.6 1.5 copy-start.17
  216.0 20.0 %all-to-all-start = ((f32[512,2,128]{2,0,1:T(8,128)}), f32[512,2,128]{2,0,1:T(8,128)S(1)}, u32[]{:S(2)}, u32[]{:S(2)}) async-start(f32[512,2,128]{2,0,1:T(8,128)} %copy.49), calls=%async_computation | async-start | bytes 1048576 | tf_op jit(solution)/shard_map/all_to_all | solution.py:189
  222.1 0.7 copy-start.10
  222.8 0.9 copy-start.4
  222.8 1.8 copy-start.11
  226.1 1.8 copy-start.12
  227.9 1.0 copy-start.5
  228.0 2.7 %copy-start.9 = (f32[32,64]{1,0:T(8,128)S(1)}, f32[32,64]{1,0:T(8,128)}, u32[]{:S(2)}) copy-start(f32[32,64]{1,0:T(8,128)} %get-tuple-element.42) | copy-start | bytes 24580
  228.0 3.8 %copy-start.8 = (f32[32,64]{1,0:T(8,128)S(1)}, f32[32,64]{1,0:T(8,128)}, u32[]{:S(2)}) copy-start(f32[32,64]{1,0:T(8,128)} %get-tuple-element.43) | copy-start | bytes 24580
  228.0 4.9 %copy-start.7 = (f32[32,64]{1,0:T(8,128)S(1)}, f32[32,64]{1,0:T(8,128)}, u32[]{:S(2)}) copy-start(f32[32,64]{1,0:T(8,128)} %get-tuple-element.44) | copy-start | bytes 24580
  228.0 5.7 %copy-start.3 = (bf16[1,15,32,64]{3,2,1,0:T(8,128)(2,1)S(1)}, bf16[1,15,32,64]{3,2,1,0:T(8,128)(2,1)}, u32[]{:S(2)}) copy-start(bf16[1,15,32,64]{3,2,1,0:T(8,128)(2,1)} %param.20) | copy-start | bytes 184324
  228.0 5.9 %copy-start.1 = (f32[12,32,128]{2,1,0:T(8,128)S(1)}, f32[12,32,128]{2,1,0:T(8,128)}, u32[]{:S(2)}) copy-start(f32[12,32,128]{2,1,0:T(8,128)} %gather_fusion.4) | copy-start | bytes 589828

commit v3 on v2

--- a/solution.py
+++ b/solution.py
@@ -110,25 +110,44 @@
     return jnp.concatenate([zeros, left_tail, own, right_head, zeros], 0)
 
 
+def doubling_gather(block, axis):
+    count = lax.axis_size(axis)
+    index = lax.axis_index(axis)
+    gathered = block[None]
+    step = 1
+    while step < count:
+        received = lax.ppermute(gathered, axis, [(i, i ^ step) for i in range(count)])
+        upper = (index & step) != 0
+        gathered = jnp.where(
+            upper,
+            jnp.concatenate([received, gathered], 0),
+            jnp.concatenate([gathered, received], 0),
+        )
+        step *= 2
+    return gathered
+
+
 def upper_tree(device_coef, device_coupling, upper_transfer, upper_coupling):
     planes = lax.axis_size("z")
     plane_bits = lax.axis_size(PLANE).bit_length() - 1
     plane = lax.axis_index("z")
     seat = lax.axis_index(PLANE)
-    plane_lift_held = lax.all_gather(upper_transfer[0], PLANE)
-    plane_mix_held = lax.all_gather(upper_coupling[0], PLANE)
+    matrices = doubling_gather(jnp.concatenate([upper_transfer[0], upper_coupling[0]], 1), PLANE)
+    plane_lift_held = matrices[:, :, : 2 * RANK]
+    plane_mix_held = matrices[:, :, 2 * RANK :]
     plane_lift = as_float(plane_lift_held)
     plane_mix = as_float(plane_mix_held)
-    inner = [lax.all_gather(device_coef, PLANE)]
+    inner = [doubling_gather(device_coef, PLANE)]
     for height in range(1, plane_bits + 1):
         inner.append(lift_up(plane_lift[2 ** (height - 1) :: 2**height], inner[-1]))
     tails = jnp.concatenate([level[-3:] for level in inner[:plane_bits]], 0)
     heads = jnp.concatenate([level[:3] for level in inner[:plane_bits]], 0)
     from_left = lax.ppermute(tails, "z", [(i, i + 1) for i in range(planes - 1)])
     from_right = lax.ppermute(heads, "z", [(i + 1, i) for i in range(planes - 1)])
-    summary = lax.all_gather(inner[plane_bits][0], "z")
-    outer_lift = as_float(lax.all_gather(plane_lift_held[0], "z"))
-    outer_mix = as_float(lax.all_gather(plane_mix_held[0], "z"))
+    summary = doubling_gather(inner[plane_bits][0], "z")
+    outer_matrices = as_float(doubling_gather(matrices[0], "z"))
+    outer_lift = outer_matrices[:, :, : 2 * RANK]
+    outer_mix = outer_matrices[:, :, 2 * RANK :]
     outer = [summary]
     for height in range(1, (planes.bit_length() - 1) - 1):
         outer.append(lift_up(outer_lift[2 ** (height - 1) :: 2**height], outer[-1]))

time: 239 us -> 176 us (0.74)
  blocking collectives: 172 us -> 2.23 us
  starting transfers between devices: 31.1 us -> 111 us
  waiting for transfers between devices: 0.02 us -> 35.3 us
  local copies, waits for them, and re-layouts: 16.6 us -> 9.65 us
  matrix products: 12.6 us -> 10.2 us
    all_gather x6 -> x0, blocking collectives: 170 us -> none  [the longest x1 40.8 us: upper_tree(): summary = lax.all_gather(inner[plane_bits][0], 'z')]
    ppermute x0 -> x16, starting transfers between devices: none -> 78.9 us  [doubling_gather(): lax.ppermute(gathered, axis, [(i, i ^ step) for i in range(count)])]
    ppermute x0 -> x16, waiting for transfers between devices: none -> 35.2 us  [doubling_gather(): lax.ppermute(gathered, axis, [(i, i ^ step) for i in range(count)])]
  transfers between devices with their start and end apart: 9 -> 25, of which waited for: 0 -> 6; matrix products, arithmetic and copies ran while one was open for 11% -> 11% of each run, Pallas kernels for 0% -> 0%
where the time goes in v3:
time: 176 us; the launch traced here: 175 us
  starting transfers between devices  111 us (63%)
  waiting for transfers between devices  35.3 us (20%)
  matrix products  10.2 us (6%)
  local copies, waits for them, and re-layouts  9.65 us (5%)
  other arithmetic  5.19 us (3%)
  blocking collectives  2.23 us (1%)
    ppermute x16, starting transfers between devices, doubling_gather(): lax.ppermute(gathered, axis, [(i, i ^ step) for i in range(count)])  78.9 us
    ppermute x16, waiting for transfers between devices, doubling_gather(): lax.ppermute(gathered, axis, [(i, i ^ step) for i in range(count)])  35.2 us
    ppermute x3, starting transfers between devices, extended_2(): lax.ppermute(tail, axis, [(i, (i + 1) % count) for i in range(ends)])  14 us
    ppermute x3, starting transfers between devices, extended_2(): lax.ppermute(head, axis, [((i + 1) % count, i) for i in range(ends)])  7.72 us
    ppermute x1, starting transfers between devices, upper_tree(): lax.ppermute(tails, 'z', [(i, i + 1) for i in range(planes - 1)])  5.5 us
  transfers between devices with their start and end apart: 25, of which 6 were waited for; matrix products, arithmetic and copies ran while one was open for 11% of the time, Pallas kernels for 0%

profile of v3, /device:TPU:6, one launch (start us, length us, event | category | flops | bytes accessed | tf_op | source)
XLA Modules:
  0.0 174.6 jit_solution(2148258806957014178)
XLA Ops:
  0.0 1.0 reshape.102
  1.0 1.1 fusion.153
  3.0 0.7 fusion.148
  3.6 2.7 %collective-permute-start.5 = (bf16[4,2,32,128]{3,2,1,0:T(8,128)(2,1)}, bf16[4,2,32,128]{3,2,1,0:T(8,128)(2,1)S(1)}, u32[]{:S(2)}, u32[]{:S(2)}) collective-permute-start(bf16[4,2,32,128]{3,2,1,0:T(8,128)(2,1)} %get-tuple-element.77), channel_id=1, source_target_pairs={{2,0},{4,2},{6,4},{8,6},{10,8},{12,10},{14,12},{16,14},{18,16},{20... | collective-permute-start | bytes 196616 | tf_op jit(solution)/shard_map/ppermute | solution.py:27
  6.4 5.2 %collective-permute-start.4 = (bf16[4,2,32,128]{3,2,1,0:T(8,128)(2,1)}, bf16[4,2,32,128]{3,2,1,0:T(8,128)(2,1)S(1)}, u32[]{:S(2)}, u32[]{:S(2)}) collective-permute-start(bf16[4,2,32,128]{3,2,1,0:T(8,128)(2,1)} %get-tuple-element.76), channel_id=1, source_target_pairs={{0,2},{2,4},{4,6},{6,8},{8,10},{10,12},{12,14},{14,16},{16,18},{18... | collective-permute-start | bytes 196616 | tf_op jit(solution)/shard_map/ppermute | solution.py:25
  11.7 1.9 %collective-permute-start.6 = (f32[1,32,128]{2,1,0:T(8,128)S(1)}, f32[1,32,128]{2,1,0:T(8,128)S(1)}, u32[]{:S(2)}, u32[]{:S(2)}) collective-permute-start(f32[1,32,128]{2,1,0:T(8,128)S(1)} %convolution_bitcast_fusion.8), channel_id=1, source_target_pairs={{0,2},{2,0},{4,6},{6,4},{8,10},{10,8},{12,14},{14,12},{16,18},{18,... | collective-permute-start | bytes 49160 | tf_op jit(solution)/shard_map/ppermute | solution.py:119
  13.7 2.8 %collective-permute-start = (f32[3,64]{1,0:T(4,128)S(1)}, f32[3,64]{1,0:T(4,128)S(1)}, u32[]{:S(2)}, u32[]{:S(2)}) collective-permute-start(f32[3,64]{1,0:T(4,128)S(1)} %get-tuple-element.90), channel_id=1, source_target_pairs={{0,2},{2,4},{4,6},{6,8},{8,10},{10,12},{12,14},{14,16},{16,18},{18... | collective-permute-start | bytes 2312 | tf_op jit(solution)/shard_map/ppermute | solution.py:25
  16.5 3.1 %collective-permute-start.1 = (f32[3,64]{1,0:T(4,128)S(1)}, f32[3,64]{1,0:T(4,128)S(1)}, u32[]{:S(2)}, u32[]{:S(2)}) collective-permute-start(f32[3,64]{1,0:T(4,128)S(1)} %get-tuple-element.89), channel_id=1, source_target_pairs={{2,0},{4,2},{6,4},{8,6},{10,8},{12,10},{14,12},{16,14},{18,16},{20... | collective-permute-start | bytes 2312 | tf_op jit(solution)/shard_map/ppermute | solution.py:27
  19.7 0.6 constant_dynamic-update-slice_fusion.2
  20.8 0.7 copy.48
  21.4 0.6 pad_clamp_fusion
  22.1 0.6 pad_clamp_fusion.2
  22.7 5.0 %collective-permute-start.10 = (bf16[1,32,160]{2,1,0:T(8,128)(2,1)S(1)}, bf16[1,32,160]{2,1,0:T(8,128)(2,1)S(1)}, u32[]{:S(2)}, u32[]{:S(2)}) collective-permute-start(bf16[1,32,160]{2,1,0:T(8,128)(2,1)S(1)} %maximum_bitcast_fusion.3), channel_id=1, source_target_pairs={{0,2},{2,0},{4,6},{6,4},{8,10},{10,8},{12,14},{14,12},{16,18},{18,... | collective-permute-start | bytes 30728 | tf_op jit(solution)/shard_map/ppermute | solution.py:119
  27.8 1.9 %collective-permute-start.3 = (bf16[64,128]{1,0:T(8,128)(2,1)S(1)}, bf16[64,128]{1,0:T(8,128)(2,1)S(1)}, u32[]{:S(2)}, u32[]{:S(2)}) collective-permute-start(bf16[64,128]{1,0:T(8,128)(2,1)S(1)} %get-tuple-element.32), channel_id=1, source_target_pairs={{2,0},{4,2},{6,4},{8,6},{10,8},{12,10},{14,12},{16,14},{18,16},{20... | collective-permute-start | bytes 49160 | tf_op jit(solution)/shard_map/ppermute | solution.py:27
  29.9 0.6 gather_fusion
  30.6 0.4 multiply_reduce_fusion
  31.0 6.0 %collective-permute-start.2 = (bf16[64,128]{1,0:T(8,128)(2,1)S(1)}, bf16[64,128]{1,0:T(8,128)(2,1)S(1)}, u32[]{:S(2)}, u32[]{:S(2)}) collective-permute-start(bf16[64,128]{1,0:T(8,128)(2,1)S(1)} %get-tuple-element.30), channel_id=1, source_target_pairs={{0,2},{2,4},{4,6},{6,8},{8,10},{10,12},{12,14},{14,16},{16,18},{18... | collective-permute-start | bytes 49160 | tf_op jit(solution)/shard_map/ppermute | solution.py:25
  37.0 1.9 %collective-permute-start.11 = (bf16[2,32,160]{2,1,0:T(8,128)(2,1)S(1)}, bf16[2,32,160]{2,1,0:T(8,128)(2,1)S(1)}, u32[]{:S(2)}, u32[]{:S(2)}) collective-permute-start(bf16[2,32,160]{2,1,0:T(8,128)(2,1)S(1)} %maximum_select_fusion.13), channel_id=1, source_target_pairs={{0,4},{2,6},{4,0},{6,2},{8,12},{10,14},{12,8},{14,10},{16,20},{18,... | collective-permute-start | bytes 61448 | tf_op jit(solution)/shard_map/ppermute | solution.py:119
  39.0 5.4 %collective-permute-start.7 = (f32[2,32,128]{2,1,0:T(8,128)S(1)}, f32[2,32,128]{2,1,0:T(8,128)}, u32[]{:S(2)}, u32[]{:S(2)}) collective-permute-start(f32[2,32,128]{2,1,0:T(8,128)S(1)} %maximum_select_fusion.12), channel_id=1, source_target_pairs={{0,4},{2,6},{4,0},{6,2},{8,12},{10,14},{12,8},{14,10},{16,20},{18,... | collective-permute-start | bytes 98312 | tf_op jit(solution)/shard_map/ppermute | solution.py:119
  44.5 2.2 %all_gather.3 = bf16[1152,256]{1,0:T(8,128)(2,1)S(1)} all-gather(bf16[1152,128]{1,0:T(8,128)(2,1)S(1)} %pad_maximum_fusion.2), channel_id=1, replica_groups=mesh['z'=16,'y'=4,'x'=4,'vec'=2] {'vec'}, dimensions={1}, use_global_device_ids=true | all-gather | bytes 884736 | tf_op jit(solution)/shard_map/all_gather | solution.py:205
  46.7 0.6 gather_fusion.1
  47.3 1.2 convolution_bitcast_fusion
  48.5 0.3 all_to_all.14
  48.8 0.8 copy.49
  49.7 3.5 %all-to-all-start = ((f32[512,2,128]{2,0,1:T(8,128)}), f32[512,2,128]{2,0,1:T(8,128)S(1)}, u32[]{:S(2)}, u32[]{:S(2)}) async-start(f32[512,2,128]{2,0,1:T(8,128)} %copy.49), calls=%async_computation | async-start | bytes 1048576 | tf_op jit(solution)/shard_map/all_to_all | solution.py:208
  53.2 2.4 %collective-permute-start.12 = (bf16[4,32,160]{2,1,0:T(8,128)(2,1)S(1)}, bf16[4,32,160]{2,1,0:T(8,128)(2,1)S(1)}, u32[]{:S(2)}, u32[]{:S(2)}) collective-permute-start(bf16[4,32,160]{2,1,0:T(8,128)(2,1)S(1)} %maximum_select_fusion.9), channel_id=1, source_target_pairs={{0,8},{2,10},{4,12},{6,14},{8,0},{10,2},{12,4},{14,6},{16,24},{18,... | collective-permute-start | bytes 122888 | tf_op jit(solution)/shard_map/ppermute | solution.py:119
  55.6 0.8 maximum_select_fusion.8
  56.4 3.5 %collective-permute-start.8 = (f32[4,32,128]{2,1,0:T(8,128)S(1)}, f32[4,32,128]{2,1,0:T(8,128)}, u32[]{:S(2)}, u32[]{:S(2)}) collective-permute-start(f32[4,32,128]{2,1,0:T(8,128)S(1)} %maximum_select_fusion.8), channel_id=1, source_target_pairs={{0,8},{2,10},{4,12},{6,14},{8,0},{10,2},{12,4},{14,6},{16,24},{18,... | collective-permute-start | bytes 196616 | tf_op jit(solution)/shard_map/ppermute | solution.py:119
  60.0 0.7 gather_fusion.5
  60.7 0.9 convolution_bitcast_fusion.5
  61.7 0.6 gather_fusion.4
  62.2 0.6 gather_fusion.3
  62.9 7.5 %collective-permute-start.13 = (bf16[8,32,160]{2,1,0:T(8,128)(2,1)S(1)}, bf16[8,32,160]{2,1,0:T(8,128)(2,1)S(1)}, u32[]{:S(2)}, u32[]{:S(2)}) collective-permute-start(bf16[8,32,160]{2,1,0:T(8,128)(2,1)S(1)} %maximum_select_fusion.5), channel_id=1, source_target_pairs={{0,16},{2,18},{4,20},{6,22},{8,24},{10,26},{12,28},{14,30},{16,0},... | collective-permute-start | bytes 245768 | tf_op jit(solution)/shard_map/ppermute | solution.py:119
  70.4 0.6 gather_fusion.2
  71.0 3.2 %collective-permute-done.13 = bf16[8,32,160]{2,1,0:T(8,128)(2,1)S(1)} collective-permute-done((bf16[8,32,160]{2,1,0:T(8,128)(2,1)S(1)}, bf16[8,32,160]{2,1,0:T(8,128)(2,1)S(1)}, u32[]{:S(2)}, u32[]{:S(2)}) %collective-permute-start.13) | collective-permute-done | bytes 81952 | tf_op jit(solution)/shard_map/ppermute | solution.py:119
  74.3 3.8 %collective-permute-start.20 = (bf16[1,32,160]{2,1,0:T(8,128)(2,1)S(1)}, bf16[1,32,160]{2,1,0:T(8,128)(2,1)S(1)}, u32[]{:S(2)}, u32[]{:S(2)}) collective-permute-start(bf16[1,32,160]{2,1,0:T(8,128)(2,1)S(1)} %slice.318), channel_id=1, source_target_pairs={{0,32},{32,0},{64,96},{96,64},{128,160},{160,128},{192,224},{224,1... | collective-permute-start | bytes 30728 | tf_op jit(solution)/shard_map/ppermute | solution.py:119
  78.2 0.9 maximum_select_fusion.4
  79.1 5.1 %collective-permute-start.9 = (f32[8,32,128]{2,1,0:T(8,128)S(1)}, f32[8,32,128]{2,1,0:T(8,128)S(1)}, u32[]{:S(2)}, u32[]{:S(2)}) collective-permute-start(f32[8,32,128]{2,1,0:T(8,128)S(1)} %maximum_select_fusion.4), channel_id=1, source_target_pairs={{0,16},{2,18},{4,20},{6,22},{8,24},{10,26},{12,28},{14,30},{16,0},... | collective-permute-start | bytes 393224 | tf_op jit(solution)/shard_map/ppermute | solution.py:119
  84.3 7.6 %collective-permute-start.21 = (bf16[2,32,160]{2,1,0:T(8,128)(2,1)S(1)}, bf16[2,32,160]{2,1,0:T(8,128)(2,1)S(1)}, u32[]{:S(2)}, u32[]{:S(2)}) collective-permute-start(bf16[2,32,160]{2,1,0:T(8,128)(2,1)S(1)} %maximum_select_fusion.15), channel_id=1, source_target_pairs={{0,64},{32,96},{64,0},{96,32},{128,192},{160,224},{192,128},{224,1... | collective-permute-start | bytes 61448 | tf_op jit(solution)/shard_map/ppermute | solution.py:119
  92.0 1.8 %collective-permute-done.21 = bf16[2,32,160]{2,1,0:T(8,128)(2,1)S(1)} collective-permute-done((bf16[2,32,160]{2,1,0:T(8,128)(2,1)S(1)}, bf16[2,32,160]{2,1,0:T(8,128)(2,1)S(1)}, u32[]{:S(2)}, u32[]{:S(2)}) %collective-permute-start.21) | collective-permute-done | bytes 20512 | tf_op jit(solution)/shard_map/ppermute | solution.py:119
  93.8 9.1 %collective-permute-start.22 = (bf16[4,32,160]{2,1,0:T(8,128)(2,1)S(1)}, bf16[4,32,160]{2,1,0:T(8,128)(2,1)S(1)}, u32[]{:S(2)}, u32[]{:S(2)}) collective-permute-start(bf16[4,32,160]{2,1,0:T(8,128)(2,1)S(1)} %maximum_select_fusion.11), channel_id=1, source_target_pairs={{0,128},{32,160},{64,192},{96,224},{128,0},{160,32},{192,64},{224,... | collective-permute-start | bytes 122888 | tf_op jit(solution)/shard_map/ppermute | solution.py:119
  103.1 4.7 %collective-permute-done.22 = bf16[4,32,160]{2,1,0:T(8,128)(2,1)S(1)} collective-permute-done((bf16[4,32,160]{2,1,0:T(8,128)(2,1)S(1)}, bf16[4,32,160]{2,1,0:T(8,128)(2,1)S(1)}, u32[]{:S(2)}, u32[]{:S(2)}) %collective-permute-start.22) | collective-permute-done | bytes 40992 | tf_op jit(solution)/shard_map/ppermute | solution.py:119
  107.8 10.1 %collective-permute-start.23 = (bf16[8,32,160]{2,1,0:T(8,128)(2,1)S(1)}, bf16[8,32,160]{2,1,0:T(8,128)(2,1)S(1)}, u32[]{:S(2)}, u32[]{:S(2)}) collective-permute-start(bf16[8,32,160]{2,1,0:T(8,128)(2,1)S(1)} %maximum_select_fusion.7), channel_id=1, source_target_pairs={{0,256},{32,288},{64,320},{96,352},{128,384},{160,416},{192,448},{... | collective-permute-start | bytes 245768 | tf_op jit(solution)/shard_map/ppermute | solution.py:119
  118.7 1.9 %collective-permute-start.16 = (f32[1,32,128]{2,1,0:T(8,128)S(1)}, f32[1,32,128]{2,1,0:T(8,128)S(1)}, u32[]{:S(2)}, u32[]{:S(2)}) collective-permute-start(f32[1,32,128]{2,1,0:T(8,128)S(1)} %convolution_bitcast_fusion.6), channel_id=1, source_target_pairs={{0,32},{32,0},{64,96},{96,64},{128,160},{160,128},{192,224},{224,1... | collective-permute-start | bytes 49160 | tf_op jit(solution)/shard_map/ppermute | solution.py:119
  120.6 6.6 %collective-permute-done.16 = f32[1,32,128]{2,1,0:T(8,128)S(1)} collective-permute-done((f32[1,32,128]{2,1,0:T(8,128)S(1)}, f32[1,32,128]{2,1,0:T(8,128)S(1)}, u32[]{:S(2)}, u32[]{:S(2)}) %collective-permute-start.16) | collective-permute-done | bytes 16416 | tf_op jit(solution)/shard_map/ppermute | solution.py:119
  127.3 2.4 %collective-permute-start.17 = (f32[2,32,128]{2,1,0:T(8,128)S(1)}, f32[2,32,128]{2,1,0:T(8,128)S(1)}, u32[]{:S(2)}, u32[]{:S(2)}) collective-permute-start(f32[2,32,128]{2,1,0:T(8,128)S(1)} %maximum_select_fusion.14), channel_id=1, source_target_pairs={{0,64},{32,96},{64,0},{96,32},{128,192},{160,224},{192,128},{224,1... | collective-permute-start | bytes 98312 | tf_op jit(solution)/shard_map/ppermute | solution.py:119
  129.7 1.3 collective-permute-start.15
  131.0 5.5 %collective-permute-start.14 = (f32[11,32,128]{2,1,0:T(8,128)S(1)}, f32[11,32,128]{2,1,0:T(8,128)S(1)}, u32[]{:S(2)}, u32[]{:S(2)}) collective-permute-start(f32[11,32,128]{2,1,0:T(8,128)S(1)} %get-tuple-element.87), channel_id=1, source_target_pairs={{0,32},{32,64},{64,96},{96,128},{128,160},{160,192},{192,224},{224... | collective-permute-start | bytes 540680 | tf_op jit(solution)/shard_map/ppermute | solution.py:145
  136.6 5.4 %collective-permute-start.18 = (f32[4,32,128]{2,1,0:T(8,128)S(1)}, f32[4,32,128]{2,1,0:T(8,128)S(1)}, u32[]{:S(2)}, u32[]{:S(2)}) collective-permute-start(f32[4,32,128]{2,1,0:T(8,128)S(1)} %maximum_select_fusion.10), channel_id=1, source_target_pairs={{0,128},{32,160},{64,192},{96,224},{128,0},{160,32},{192,64},{224,... | collective-permute-start | bytes 196616 | tf_op jit(solution)/shard_map/ppermute | solution.py:119
  142.3 4.4 %collective-permute-done.18 = f32[4,32,128]{2,1,0:T(8,128)S(1)} collective-permute-done((f32[4,32,128]{2,1,0:T(8,128)S(1)}, f32[4,32,128]{2,1,0:T(8,128)S(1)}, u32[]{:S(2)}, u32[]{:S(2)}) %collective-permute-start.18) | collective-permute-done | bytes 65568 | tf_op jit(solution)/shard_map/ppermute | solution.py:119
  146.8 5.7 %collective-permute-start.19 = (f32[8,32,128]{2,1,0:T(8,128)S(1)}, f32[8,32,128]{2,1,0:T(8,128)S(1)}, u32[]{:S(2)}, u32[]{:S(2)}) collective-permute-start(f32[8,32,128]{2,1,0:T(8,128)S(1)} %maximum_select_fusion.6), channel_id=1, source_target_pairs={{0,256},{32,288},{64,320},{96,352},{128,384},{160,416},{192,448},{... | collective-permute-start | bytes 393224 | tf_op jit(solution)/shard_map/ppermute | solution.py:119
  152.8 0.8 copy-done.2
  154.2 14.4 %collective-permute-done.19 = f32[8,32,128]{2,1,0:T(8,128)S(1)} collective-permute-done((f32[8,32,128]{2,1,0:T(8,128)S(1)}, f32[8,32,128]{2,1,0:T(8,128)S(1)}, u32[]{:S(2)}, u32[]{:S(2)}) %collective-permute-start.19) | collective-permute-done | bytes 131104 | tf_op jit(solution)/shard_map/ppermute | solution.py:119
  169.7 0.3 convolution_add_fusion.5
  170.0 0.3 convolution_add_fusion.4
  170.3 0.3 convolution_add_fusion.3
  170.6 0.3 convolution_add_fusion.2
  170.9 0.3 convolution_add_fusion.1
  171.2 0.3 fusion.4
  172.3 0.3 fusion.1
  172.6 0.3 fusion.20
  172.9 0.5 fusion
  173.4 0.4 fusion.15
  173.8 0.8 fusion.5
  (137 shorter events, 5.9 us)
Async XLA Ops:
  0.0 2.2 %copy-start.1 = (bf16[1,15,32,64]{3,2,1,0:T(8,128)(2,1)S(1)}, bf16[1,15,32,64]{3,2,1,0:T(8,128)(2,1)}, u32[]{:S(2)}) copy-start(bf16[1,15,32,64]{3,2,1,0:T(8,128)(2,1)} %param.20) | copy-start | bytes 184324
  2.4 11.2 %copy-start.4 = (f32[3,1024]{1,0:T(4,128)S(1)}, f32[3,1024]{1,0:T(4,128)}, u32[]{:S(2)}) copy-start(f32[3,1024]{1,0:T(4,128)} %param.17) | copy-start | bytes 36868
  2.6 17.6 %copy-start = (bf16[1024,128]{1,0:T(8,128)(2,1)S(1)}, bf16[1024,128]{1,0:T(8,128)(2,1)}, u32[]{:S(2)}) copy-start(bf16[1024,128]{1,0:T(8,128)(2,1)} %param.16) | copy-start | bytes 786436
  2.8 17.6 %copy-start.7 = (s32[16,3]{0,1:T(4,128)S(1)}, s32[16,3]{0,1:T(4,128)}, u32[]{:S(2)}) copy-start(s32[16,3]{0,1:T(4,128)} %param.18) | copy-start | bytes 580
  2.8 18.6 %copy-start.12 = (s32[6]{0:T(128)S(1)}, s32[6]{0:T(128)}, u32[]{:S(2)}) copy-start(s32[6]{0:T(128)} %constant.262) | copy-start | bytes 76
  2.9 18.6 %copy-start.13 = (s32[12]{0:T(128)S(1)}, s32[12]{0:T(128)}, u32[]{:S(2)}) copy-start(s32[12]{0:T(128)} %constant.261) | copy-start | bytes 148
  2.9 19.2 %copy-start.8 = (bf16[1,32,96]{2,1,0:T(8,128)(2,1)S(1)}, bf16[1,32,96]{2,1,0:T(8,128)(2,1)}, u32[]{:S(2)}) copy-start(bf16[1,32,96]{2,1,0:T(8,128)(2,1)} %param.23) | copy-start | bytes 18436
  2.9 19.2 %copy-start.9 = (bf16[1,32,64]{2,1,0:T(8,128)(2,1)S(1)}, bf16[1,32,64]{2,1,0:T(8,128)(2,1)}, u32[]{:S(2)}) copy-start(bf16[1,32,64]{2,1,0:T(8,128)(2,1)} %param.22) | copy-start | bytes 12292
  2.9 19.2 %copy-start.10 = (s32[24]{0:T(128)S(1)}, s32[24]{0:T(128)}, u32[]{:S(2)}) copy-start(s32[24]{0:T(128)} %constant.260) | copy-start | bytes 292
  2.9 19.2 %copy-start.11 = (s32[48]{0:T(128)S(1)}, s32[48]{0:T(128)}, u32[]{:S(2)}) copy-start(s32[48]{0:T(128)} %constant.259) | copy-start | bytes 580
  3.6 56.3 %collective-permute-start.5 = (bf16[4,2,32,128]{3,2,1,0:T(8,128)(2,1)}, bf16[4,2,32,128]{3,2,1,0:T(8,128)(2,1)S(1)}, u32[]{:S(2)}, u32[]{:S(2)}) collective-permute-start(bf16[4,2,32,128]{3,2,1,0:T(8,128)(2,1)} %get-tuple-element.77), channel_id=1, source_target_pairs={{2,0},{4,2},{6,4},{8,6},{10,8},{12,10},{14,12},{16,14},{18,16},{20... | collective-permute-start | bytes 196616 | tf_op jit(solution)/shard_map/ppermute | solution.py:27
  6.4 53.5 %collective-permute-start.4 = (bf16[4,2,32,128]{3,2,1,0:T(8,128)(2,1)}, bf16[4,2,32,128]{3,2,1,0:T(8,128)(2,1)S(1)}, u32[]{:S(2)}, u32[]{:S(2)}) collective-permute-start(bf16[4,2,32,128]{3,2,1,0:T(8,128)(2,1)} %get-tuple-element.76), channel_id=1, source_target_pairs={{0,2},{2,4},{4,6},{6,8},{8,10},{10,12},{12,14},{14,16},{16,18},{18... | collective-permute-start | bytes 196616 | tf_op jit(solution)/shard_map/ppermute | solution.py:25
  11.7 25.3 %collective-permute-start.6 = (f32[1,32,128]{2,1,0:T(8,128)S(1)}, f32[1,32,128]{2,1,0:T(8,128)S(1)}, u32[]{:S(2)}, u32[]{:S(2)}) collective-permute-start(f32[1,32,128]{2,1,0:T(8,128)S(1)} %convolution_bitcast_fusion.8), channel_id=1, source_target_pairs={{0,2},{2,0},{4,6},{6,4},{8,10},{10,8},{12,14},{14,12},{16,18},{18,... | collective-permute-start | bytes 49160 | tf_op jit(solution)/shard_map/ppermute | solution.py:119
  13.7 9.0 %collective-permute-start = (f32[3,64]{1,0:T(4,128)S(1)}, f32[3,64]{1,0:T(4,128)S(1)}, u32[]{:S(2)}, u32[]{:S(2)}) collective-permute-start(f32[3,64]{1,0:T(4,128)S(1)} %get-tuple-element.90), channel_id=1, source_target_pairs={{0,2},{2,4},{4,6},{6,8},{8,10},{10,12},{12,14},{14,16},{16,18},{18... | collective-permute-start | bytes 2312 | tf_op jit(solution)/shard_map/ppermute | solution.py:25
  16.5 11.3 %collective-permute-start.1 = (f32[3,64]{1,0:T(4,128)S(1)}, f32[3,64]{1,0:T(4,128)S(1)}, u32[]{:S(2)}, u32[]{:S(2)}) collective-permute-start(f32[3,64]{1,0:T(4,128)S(1)} %get-tuple-element.89), channel_id=1, source_target_pairs={{2,0},{4,2},{6,4},{8,6},{10,8},{12,10},{14,12},{16,14},{18,16},{20... | collective-permute-start | bytes 2312 | tf_op jit(solution)/shard_map/ppermute | solution.py:27
  22.7 8.2 %collective-permute-start.10 = (bf16[1,32,160]{2,1,0:T(8,128)(2,1)S(1)}, bf16[1,32,160]{2,1,0:T(8,128)(2,1)S(1)}, u32[]{:S(2)}, u32[]{:S(2)}) collective-permute-start(bf16[1,32,160]{2,1,0:T(8,128)(2,1)S(1)} %maximum_bitcast_fusion.3), channel_id=1, source_target_pairs={{0,2},{2,0},{4,6},{6,4},{8,10},{10,8},{12,14},{14,12},{16,18},{18,... | collective-permute-start | bytes 30728 | tf_op jit(solution)/shard_map/ppermute | solution.py:119
  27.8 11.2 %collective-permute-start.3 = (bf16[64,128]{1,0:T(8,128)(2,1)S(1)}, bf16[64,128]{1,0:T(8,128)(2,1)S(1)}, u32[]{:S(2)}, u32[]{:S(2)}) collective-permute-start(bf16[64,128]{1,0:T(8,128)(2,1)S(1)} %get-tuple-element.32), channel_id=1, source_target_pairs={{2,0},{4,2},{6,4},{8,6},{10,8},{12,10},{14,12},{16,14},{18,16},{20... | collective-permute-start | bytes 49160 | tf_op jit(solution)/shard_map/ppermute | solution.py:27
  31.0 13.5 %collective-permute-start.2 = (bf16[64,128]{1,0:T(8,128)(2,1)S(1)}, bf16[64,128]{1,0:T(8,128)(2,1)S(1)}, u32[]{:S(2)}, u32[]{:S(2)}) collective-permute-start(bf16[64,128]{1,0:T(8,128)(2,1)S(1)} %get-tuple-element.30), channel_id=1, source_target_pairs={{0,2},{2,4},{4,6},{6,8},{8,10},{10,12},{12,14},{14,16},{16,18},{18... | collective-permute-start | bytes 49160 | tf_op jit(solution)/shard_map/ppermute | solution.py:25
  37.0 16.1 %collective-permute-start.11 = (bf16[2,32,160]{2,1,0:T(8,128)(2,1)S(1)}, bf16[2,32,160]{2,1,0:T(8,128)(2,1)S(1)}, u32[]{:S(2)}, u32[]{:S(2)}) collective-permute-start(bf16[2,32,160]{2,1,0:T(8,128)(2,1)S(1)} %maximum_select_fusion.13), channel_id=1, source_target_pairs={{0,4},{2,6},{4,0},{6,2},{8,12},{10,14},{12,8},{14,10},{16,20},{18,... | collective-permute-start | bytes 61448 | tf_op jit(solution)/shard_map/ppermute | solution.py:119
  39.0 16.6 %collective-permute-start.7 = (f32[2,32,128]{2,1,0:T(8,128)S(1)}, f32[2,32,128]{2,1,0:T(8,128)}, u32[]{:S(2)}, u32[]{:S(2)}) collective-permute-start(f32[2,32,128]{2,1,0:T(8,128)S(1)} %maximum_select_fusion.12), channel_id=1, source_target_pairs={{0,4},{2,6},{4,0},{6,2},{8,12},{10,14},{12,8},{14,10},{16,20},{18,... | collective-permute-start | bytes 98312 | tf_op jit(solution)/shard_map/ppermute | solution.py:119
  49.7 124.2 %all-to-all-start = ((f32[512,2,128]{2,0,1:T(8,128)}), f32[512,2,128]{2,0,1:T(8,128)S(1)}, u32[]{:S(2)}, u32[]{:S(2)}) async-start(f32[512,2,128]{2,0,1:T(8,128)} %copy.49), calls=%async_computation | async-start | bytes 1048576 | tf_op jit(solution)/shard_map/all_to_all | solution.py:208
  53.2 9.6 %collective-permute-start.12 = (bf16[4,32,160]{2,1,0:T(8,128)(2,1)S(1)}, bf16[4,32,160]{2,1,0:T(8,128)(2,1)S(1)}, u32[]{:S(2)}, u32[]{:S(2)}) collective-permute-start(bf16[4,32,160]{2,1,0:T(8,128)(2,1)S(1)} %maximum_select_fusion.9), channel_id=1, source_target_pairs={{0,8},{2,10},{4,12},{6,14},{8,0},{10,2},{12,4},{14,6},{16,24},{18,... | collective-permute-start | bytes 122888 | tf_op jit(solution)/shard_map/ppermute | solution.py:119
  56.4 21.7 %collective-permute-start.8 = (f32[4,32,128]{2,1,0:T(8,128)S(1)}, f32[4,32,128]{2,1,0:T(8,128)}, u32[]{:S(2)}, u32[]{:S(2)}) collective-permute-start(f32[4,32,128]{2,1,0:T(8,128)S(1)} %maximum_select_fusion.8), channel_id=1, source_target_pairs={{0,8},{2,10},{4,12},{6,14},{8,0},{10,2},{12,4},{14,6},{16,24},{18,... | collective-permute-start | bytes 196616 | tf_op jit(solution)/shard_map/ppermute | solution.py:119
  60.0 1.7 copy-start.6
  60.7 1.5 copy-start.5
  62.9 11.3 %collective-permute-start.13 = (bf16[8,32,160]{2,1,0:T(8,128)(2,1)S(1)}, bf16[8,32,160]{2,1,0:T(8,128)(2,1)S(1)}, u32[]{:S(2)}, u32[]{:S(2)}) collective-permute-start(bf16[8,32,160]{2,1,0:T(8,128)(2,1)S(1)} %maximum_select_fusion.5), channel_id=1, source_target_pairs={{0,16},{2,18},{4,20},{6,22},{8,24},{10,26},{12,28},{14,30},{16,0},... | collective-permute-start | bytes 245768 | tf_op jit(solution)/shard_map/ppermute | solution.py:119
  74.3 9.9 %collective-permute-start.20 = (bf16[1,32,160]{2,1,0:T(8,128)(2,1)S(1)}, bf16[1,32,160]{2,1,0:T(8,128)(2,1)S(1)}, u32[]{:S(2)}, u32[]{:S(2)}) collective-permute-start(bf16[1,32,160]{2,1,0:T(8,128)(2,1)S(1)} %slice.318), channel_id=1, source_target_pairs={{0,32},{32,0},{64,96},{96,64},{128,160},{160,128},{192,224},{224,1... | collective-permute-start | bytes 30728 | tf_op jit(solution)/shard_map/ppermute | solution.py:119
  79.1 38.8 %collective-permute-start.9 = (f32[8,32,128]{2,1,0:T(8,128)S(1)}, f32[8,32,128]{2,1,0:T(8,128)S(1)}, u32[]{:S(2)}, u32[]{:S(2)}) collective-permute-start(f32[8,32,128]{2,1,0:T(8,128)S(1)} %maximum_select_fusion.4), channel_id=1, source_target_pairs={{0,16},{2,18},{4,20},{6,22},{8,24},{10,26},{12,28},{14,30},{16,0},... | collective-permute-start | bytes 393224 | tf_op jit(solution)/shard_map/ppermute | solution.py:119
  84.3 9.5 %collective-permute-start.21 = (bf16[2,32,160]{2,1,0:T(8,128)(2,1)S(1)}, bf16[2,32,160]{2,1,0:T(8,128)(2,1)S(1)}, u32[]{:S(2)}, u32[]{:S(2)}) collective-permute-start(bf16[2,32,160]{2,1,0:T(8,128)(2,1)S(1)} %maximum_select_fusion.15), channel_id=1, source_target_pairs={{0,64},{32,96},{64,0},{96,32},{128,192},{160,224},{192,128},{224,1... | collective-permute-start | bytes 61448 | tf_op jit(solution)/shard_map/ppermute | solution.py:119
  93.8 13.9 %collective-permute-start.22 = (bf16[4,32,160]{2,1,0:T(8,128)(2,1)S(1)}, bf16[4,32,160]{2,1,0:T(8,128)(2,1)S(1)}, u32[]{:S(2)}, u32[]{:S(2)}) collective-permute-start(bf16[4,32,160]{2,1,0:T(8,128)(2,1)S(1)} %maximum_select_fusion.11), channel_id=1, source_target_pairs={{0,128},{32,160},{64,192},{96,224},{128,0},{160,32},{192,64},{224,... | collective-permute-start | bytes 122888 | tf_op jit(solution)/shard_map/ppermute | solution.py:119
  107.8 34.3 %collective-permute-start.23 = (bf16[8,32,160]{2,1,0:T(8,128)(2,1)S(1)}, bf16[8,32,160]{2,1,0:T(8,128)(2,1)S(1)}, u32[]{:S(2)}, u32[]{:S(2)}) collective-permute-start(bf16[8,32,160]{2,1,0:T(8,128)(2,1)S(1)} %maximum_select_fusion.7), channel_id=1, source_target_pairs={{0,256},{32,288},{64,320},{96,352},{128,384},{160,416},{192,448},{... | collective-permute-start | bytes 245768 | tf_op jit(solution)/shard_map/ppermute | solution.py:119
  118.7 8.6 %collective-permute-start.16 = (f32[1,32,128]{2,1,0:T(8,128)S(1)}, f32[1,32,128]{2,1,0:T(8,128)S(1)}, u32[]{:S(2)}, u32[]{:S(2)}) collective-permute-start(f32[1,32,128]{2,1,0:T(8,128)S(1)} %convolution_bitcast_fusion.6), channel_id=1, source_target_pairs={{0,32},{32,0},{64,96},{96,64},{128,160},{160,128},{192,224},{224,1... | collective-permute-start | bytes 49160 | tf_op jit(solution)/shard_map/ppermute | solution.py:119
  127.3 9.3 %collective-permute-start.17 = (f32[2,32,128]{2,1,0:T(8,128)S(1)}, f32[2,32,128]{2,1,0:T(8,128)S(1)}, u32[]{:S(2)}, u32[]{:S(2)}) collective-permute-start(f32[2,32,128]{2,1,0:T(8,128)S(1)} %maximum_select_fusion.14), channel_id=1, source_target_pairs={{0,64},{32,96},{64,0},{96,32},{128,192},{160,224},{192,128},{224,1... | collective-permute-start | bytes 98312 | tf_op jit(solution)/shard_map/ppermute | solution.py:119
  129.7 22.8 %collective-permute-start.15 = (f32[11,32,128]{2,1,0:T(8,128)S(1)}, f32[11,32,128]{2,1,0:T(8,128)S(1)}, u32[]{:S(2)}, u32[]{:S(2)}) collective-permute-start(f32[11,32,128]{2,1,0:T(8,128)S(1)} %get-tuple-element.88), channel_id=1, source_target_pairs={{32,0},{64,32},{96,64},{128,96},{160,128},{192,160},{224,192},{256... | collective-permute-start | bytes 540680 | tf_op jit(solution)/shard_map/ppermute | solution.py:146
  131.0 21.5 %collective-permute-start.14 = (f32[11,32,128]{2,1,0:T(8,128)S(1)}, f32[11,32,128]{2,1,0:T(8,128)S(1)}, u32[]{:S(2)}, u32[]{:S(2)}) collective-permute-start(f32[11,32,128]{2,1,0:T(8,128)S(1)} %get-tuple-element.87), channel_id=1, source_target_pairs={{0,32},{32,64},{64,96},{96,128},{128,160},{160,192},{192,224},{224... | collective-permute-start | bytes 540680 | tf_op jit(solution)/shard_map/ppermute | solution.py:145
  136.6 16.0 %copy-start.3 = (f32[8,32,128]{2,1,0:T(8,128)S(1)}, f32[8,32,128]{2,1,0:T(8,128)}, u32[]{:S(2)}) copy-start(f32[8,32,128]{2,1,0:T(8,128)} %constant_dynamic-update-slice_fusion.2) | copy-start | bytes 393220
  136.6 10.2 %collective-permute-start.18 = (f32[4,32,128]{2,1,0:T(8,128)S(1)}, f32[4,32,128]{2,1,0:T(8,128)S(1)}, u32[]{:S(2)}, u32[]{:S(2)}) collective-permute-start(f32[4,32,128]{2,1,0:T(8,128)S(1)} %maximum_select_fusion.10), channel_id=1, source_target_pairs={{0,128},{32,160},{64,192},{96,224},{128,0},{160,32},{192,64},{224,... | collective-permute-start | bytes 196616 | tf_op jit(solution)/shard_map/ppermute | solution.py:119
  146.8 21.9 %collective-permute-start.19 = (f32[8,32,128]{2,1,0:T(8,128)S(1)}, f32[8,32,128]{2,1,0:T(8,128)S(1)}, u32[]{:S(2)}, u32[]{:S(2)}) collective-permute-start(f32[8,32,128]{2,1,0:T(8,128)S(1)} %maximum_select_fusion.6), channel_id=1, source_target_pairs={{0,256},{32,288},{64,320},{96,352},{128,384},{160,416},{192,448},{... | collective-permute-start | bytes 393224 | tf_op jit(solution)/shard_map/ppermute | solution.py:119
  152.7 1.0 copy-start.2

commit v4 on v3

--- a/solution.py
+++ b/solution.py
@@ -42,7 +42,7 @@
 def near_field(source, extended_points, index_rows, first_leaf, leaf_zero, leaf_count):
     block_count = index_rows.shape[0]
     col_width = source.shape[1]
-    group_size = min(8, block_count)
+    group_size = block_count
     source_leaves = source.reshape(leaf_count + 2, LEAF, col_width)
     point_leaves = extended_points.reshape(3, leaf_count + 2, LEAF)
     present = (index_rows >= 0).astype(jnp.bfloat16)
@@ -132,22 +132,24 @@
     plane_bits = lax.axis_size(PLANE).bit_length() - 1
     plane = lax.axis_index("z")
     seat = lax.axis_index(PLANE)
-    matrices = doubling_gather(jnp.concatenate([upper_transfer[0], upper_coupling[0]], 1), PLANE)
-    plane_lift_held = matrices[:, :, : 2 * RANK]
-    plane_mix_held = matrices[:, :, 2 * RANK :]
-    plane_lift = as_float(plane_lift_held)
-    plane_mix = as_float(plane_mix_held)
-    inner = [doubling_gather(device_coef, PLANE)]
+    matrices = as_float(jnp.concatenate([upper_transfer[0], upper_coupling[0]], 1))
+    columns = device_coef.shape[1]
+    plane_held = doubling_gather(jnp.concatenate([device_coef, matrices], 1), PLANE)
+    plane_lift = plane_held[:, :, columns : columns + 2 * RANK]
+    plane_mix = plane_held[:, :, columns + 2 * RANK :]
+    inner = [plane_held[:, :, :columns]]
     for height in range(1, plane_bits + 1):
         inner.append(lift_up(plane_lift[2 ** (height - 1) :: 2**height], inner[-1]))
     tails = jnp.concatenate([level[-3:] for level in inner[:plane_bits]], 0)
     heads = jnp.concatenate([level[:3] for level in inner[:plane_bits]], 0)
     from_left = lax.ppermute(tails, "z", [(i, i + 1) for i in range(planes - 1)])
     from_right = lax.ppermute(heads, "z", [(i + 1, i) for i in range(planes - 1)])
-    summary = doubling_gather(inner[plane_bits][0], "z")
-    outer_matrices = as_float(doubling_gather(matrices[0], "z"))
-    outer_lift = outer_matrices[:, :, : 2 * RANK]
-    outer_mix = outer_matrices[:, :, 2 * RANK :]
+    outer_held = doubling_gather(
+        jnp.concatenate([inner[plane_bits][0], plane_held[0, :, columns:]], 1), "z"
+    )
+    summary = outer_held[:, :, :columns]
+    outer_lift = outer_held[:, :, columns : columns + 2 * RANK]
+    outer_mix = outer_held[:, :, columns + 2 * RANK :]
     outer = [summary]
     for height in range(1, (planes.bit_length() - 1) - 1):
         outer.append(lift_up(outer_lift[2 ** (height - 1) :: 2**height], outer[-1]))
@@ -199,13 +201,7 @@
     leaf_zero = position * leaf_count
     vector_rims = extended_2(vectors, ((SPACE, 0),), LEAF)
     point_rims = extended_2(points, ((SPACE, 1),), LEAF)
-    lane_count = lax.axis_size("vec")
-    lane_leaves = leaf_count // lane_count
-    first_leaf = lax.axis_index("vec") * lane_leaves
-    all_columns = lax.all_gather(vector_rims, "vec", axis=1, tiled=True)
-    own_rows = lax.dynamic_slice_in_dim(near_index, first_leaf, lane_leaves, 0)
-    half_near = near_field(all_columns, point_rims, own_rows, first_leaf, leaf_zero, leaf_count)
-    nearby = lax.all_to_all(half_near, "vec", split_axis=1, concat_axis=0, tiled=True)
+    nearby = near_field(vector_rims, point_rims, near_index, 0, leaf_zero, leaf_count)
     basis_leaves = leaf_basis.reshape(RANK, leaf_count, LEAF)
     leaf_vectors = vectors.reshape(leaf_count, LEAF, columns)
     coefficients = [

time: 176 us -> 177 us (level)
  the two profiles are of different devices: /device:TPU:6 before, /device:TPU:16 now
where the time goes in v4:
time: 177 us; the launch traced here: 176 us
  starting transfers between devices  96.8 us (55%)
  waiting for transfers between devices  47.8 us (27%)
  matrix products  14.5 us (8%)
  local copies, waits for them, and re-layouts  9.54 us (5%)
  other arithmetic  5.92 us (3%)
    ppermute x8, starting transfers between devices, doubling_gather(): lax.ppermute(gathered, axis, [(i, i ^ step) for i in range(count)])  70.7 us
    ppermute x8, waiting for transfers between devices, doubling_gather(): lax.ppermute(gathered, axis, [(i, i ^ step) for i in range(count)])  44.4 us
    ppermute x3, starting transfers between devices, extended_2(): lax.ppermute(head, axis, [((i + 1) % count, i) for i in range(ends)])  12.5 us
    ppermute x3, starting transfers between devices, extended_2(): lax.ppermute(tail, axis, [(i, (i + 1) % count) for i in range(ends)])  7.75 us
    ppermute x1, starting transfers between devices, upper_tree(): lax.ppermute(tails, 'z', [(i, i + 1) for i in range(planes - 1)])  4.56 us
    dot_general x4, matrix products, local(): jnp.einsum('cra,cav->crv', lift_mats, children, precision=HIGHEST)  3.75 us
  transfers between devices with their start and end apart: 16, of which 7 were waited for; matrix products, arithmetic and copies ran while one was open for 9% of the time, Pallas kernels for 0%

profile of v4, /device:TPU:16, one launch (start us, length us, event | category | flops | bytes accessed | tf_op | source)
XLA Modules:
  0.0 175.7 jit_solution(18142618559426605177)
XLA Ops:
  0.0 1.0 reshape.99
  1.1 1.2 fusion.154
  2.3 1.1 bitcast_convert_fusion.1
  3.4 0.9 fusion.76
  4.4 0.9 bitcast_convert_fusion
  5.3 0.7 fusion.149
  6.0 4.5 %collective-permute-start.5 = (bf16[4,2,32,128]{3,2,1,0:T(8,128)(2,1)}, bf16[4,2,32,128]{3,2,1,0:T(8,128)(2,1)S(1)}, u32[]{:S(2)}, u32[]{:S(2)}) collective-permute-start(bf16[4,2,32,128]{3,2,1,0:T(8,128)(2,1)} %get-tuple-element.68), channel_id=1, source_target_pairs={{2,0},{4,2},{6,4},{8,6},{10,8},{12,10},{14,12},{16,14},{18,16},{20... | collective-permute-start | bytes 196616 | tf_op jit(solution)/shard_map/ppermute | solution.py:27
  10.5 1.9 %collective-permute-start.4 = (bf16[4,2,32,128]{3,2,1,0:T(8,128)(2,1)}, bf16[4,2,32,128]{3,2,1,0:T(8,128)(2,1)S(1)}, u32[]{:S(2)}, u32[]{:S(2)}) collective-permute-start(bf16[4,2,32,128]{3,2,1,0:T(8,128)(2,1)} %get-tuple-element.67), channel_id=1, source_target_pairs={{0,2},{2,4},{4,6},{6,8},{8,10},{10,12},{12,14},{14,16},{16,18},{18... | collective-permute-start | bytes 196616 | tf_op jit(solution)/shard_map/ppermute | solution.py:25
  12.5 0.8 convolution_bitcast_fusion.6
  13.4 0.6 maximum_bitcast_fusion
  14.0 2.8 %collective-permute-start.6 = (f32[1,32,288]{2,1,0:T(8,128)}, f32[1,32,288]{2,1,0:T(8,128)}, u32[]{:S(2)}, u32[]{:S(2)}) collective-permute-start(f32[1,32,288]{2,1,0:T(8,128)} %maximum_bitcast_fusion), channel_id=1, source_target_pairs={{0,2},{2,0},{4,6},{6,4},{8,10},{10,8},{12,14},{14,12},{16,18},{18,... | collective-permute-start | bytes 110600 | tf_op jit(solution)/shard_map/ppermute | solution.py:119
  16.9 3.1 %collective-permute-start = (f32[3,64]{1,0:T(4,128)S(1)}, f32[3,64]{1,0:T(4,128)S(1)}, u32[]{:S(2)}, u32[]{:S(2)}) collective-permute-start(f32[3,64]{1,0:T(4,128)S(1)} %get-tuple-element.81), channel_id=1, source_target_pairs={{0,2},{2,4},{4,6},{6,8},{8,10},{10,12},{12,14},{14,16},{16,18},{18... | collective-permute-start | bytes 2312 | tf_op jit(solution)/shard_map/ppermute | solution.py:25
  19.9 4.9 %collective-permute-start.1 = (f32[3,64]{1,0:T(4,128)S(1)}, f32[3,64]{1,0:T(4,128)S(1)}, u32[]{:S(2)}, u32[]{:S(2)}) collective-permute-start(f32[3,64]{1,0:T(4,128)S(1)} %get-tuple-element.80), channel_id=1, source_target_pairs={{2,0},{4,2},{6,4},{8,6},{10,8},{12,10},{14,12},{16,14},{18,16},{20... | collective-permute-start | bytes 2312 | tf_op jit(solution)/shard_map/ppermute | solution.py:27
  24.9 0.6 constant_dynamic-update-slice_fusion.2
  25.5 0.7 slice_bitcast_fusion.5
  26.5 0.7 copy.37
  27.2 0.6 pad_clamp_fusion
  27.8 0.6 pad_clamp_fusion.2
  28.4 3.1 %collective-permute-start.3 = (bf16[64,128]{1,0:T(8,128)(2,1)S(1)}, bf16[64,128]{1,0:T(8,128)(2,1)S(1)}, u32[]{:S(2)}, u32[]{:S(2)}) collective-permute-start(bf16[64,128]{1,0:T(8,128)(2,1)S(1)} %get-tuple-element.29), channel_id=1, source_target_pairs={{2,0},{4,2},{6,4},{8,6},{10,8},{12,10},{14,12},{16,14},{18,16},{20... | collective-permute-start | bytes 49160 | tf_op jit(solution)/shard_map/ppermute | solution.py:27
  31.5 2.8 %collective-permute-start.2 = (bf16[64,128]{1,0:T(8,128)(2,1)S(1)}, bf16[64,128]{1,0:T(8,128)(2,1)S(1)}, u32[]{:S(2)}, u32[]{:S(2)}) collective-permute-start(bf16[64,128]{1,0:T(8,128)(2,1)S(1)} %get-tuple-element.28), channel_id=1, source_target_pairs={{0,2},{2,4},{4,6},{6,8},{8,10},{10,12},{12,14},{14,16},{16,18},{18... | collective-permute-start | bytes 49160 | tf_op jit(solution)/shard_map/ppermute | solution.py:25
  34.5 0.6 gather_fusion
  35.2 0.7 multiply_reduce_fusion
  35.9 3.4 %collective-permute-done.2 = bf16[64,128]{1,0:T(8,128)(2,1)S(1)} collective-permute-done((bf16[64,128]{1,0:T(8,128)(2,1)S(1)}, bf16[64,128]{1,0:T(8,128)(2,1)S(1)}, u32[]{:S(2)}, u32[]{:S(2)}) %collective-permute-start.2) | collective-permute-done | bytes 16416 | tf_op jit(solution)/shard_map/ppermute | solution.py:25
  39.3 1.6 gather_fusion.1
  40.9 2.1 %fusion.6 = f32[16,64,128,1]{2,1,3,0:T(8,128)S(1)} fusion(bf16[16,3,64,128]{3,2,1,0:T(8,128)(2,1)} %bitcast.267, f32[16,3,64,64]{3,2,1,0:T(8,128)S(1)} %multiply_reduce_fusion, bf16[16,3]{1,0:T(8,128)(2,1)} %copy.37), kind=kOutput, calls=%fused_computation.29 | convolution fusion | flops 51707904 | bytes 2097248 | tf_op jit(solution)/shard_map/while/body/eval_jaxpr/gkij,gkjv->giv/dot_general | solution.py:56
  43.0 0.9 maximum_select_fusion.6
  43.9 1.9 %collective-permute-start.7 = (f32[2,32,288]{2,1,0:T(8,128)S(1)}, f32[2,32,288]{2,1,0:T(8,128)S(1)}, u32[]{:S(2)}, u32[]{:S(2)}) collective-permute-start(f32[2,32,288]{2,1,0:T(8,128)S(1)} %maximum_select_fusion.6), channel_id=1, source_target_pairs={{0,4},{2,6},{4,0},{6,2},{8,12},{10,14},{12,8},{14,10},{16,20},{18,... | collective-permute-start | bytes 221192 | tf_op jit(solution)/shard_map/ppermute | solution.py:119
  45.9 6.0 %collective-permute-done.7 = f32[2,32,288]{2,1,0:T(8,128)S(1)} collective-permute-done((f32[2,32,288]{2,1,0:T(8,128)S(1)}, f32[2,32,288]{2,1,0:T(8,128)S(1)}, u32[]{:S(2)}, u32[]{:S(2)}) %collective-permute-start.7) | collective-permute-done | bytes 73760 | tf_op jit(solution)/shard_map/ppermute | solution.py:119
  51.9 3.5 %collective-permute-start.8 = (f32[4,32,288]{2,1,0:T(8,128)S(1)}, f32[4,32,288]{2,1,0:T(8,128)S(1)}, u32[]{:S(2)}, u32[]{:S(2)}) collective-permute-start(f32[4,32,288]{2,1,0:T(8,128)S(1)} %maximum_select_fusion.4), channel_id=1, source_target_pairs={{0,8},{2,10},{4,12},{6,14},{8,0},{10,2},{12,4},{14,6},{16,24},{18,... | collective-permute-start | bytes 442376 | tf_op jit(solution)/shard_map/ppermute | solution.py:119
  55.4 0.7 gather_fusion.5
  56.1 0.6 gather_fusion.4
  56.7 0.6 gather_fusion.3
  57.3 3.0 %collective-permute-done.8 = f32[4,32,288]{2,1,0:T(8,128)S(1)} collective-permute-done((f32[4,32,288]{2,1,0:T(8,128)S(1)}, f32[4,32,288]{2,1,0:T(8,128)S(1)}, u32[]{:S(2)}, u32[]{:S(2)}) %collective-permute-start.8) | collective-permute-done | bytes 147488 | tf_op jit(solution)/shard_map/ppermute | solution.py:119
  60.4 1.9 %collective-permute-start.9 = (f32[8,32,288]{2,1,0:T(8,128)S(1)}, f32[8,32,288]{2,1,0:T(8,128)}, u32[]{:S(2)}, u32[]{:S(2)}) collective-permute-start(f32[8,32,288]{2,1,0:T(8,128)S(1)} %maximum_select_fusion.2), channel_id=1, source_target_pairs={{0,16},{2,18},{4,20},{6,22},{8,24},{10,26},{12,28},{14,30},{16,0},... | collective-permute-start | bytes 884744 | tf_op jit(solution)/shard_map/ppermute | solution.py:119
  62.4 0.6 gather_fusion.2
  63.0 0.9 convolution_bitcast_fusion.4
  63.9 7.8 %collective-permute-done.9 = f32[8,32,288]{2,1,0:T(8,128)} collective-permute-done((f32[8,32,288]{2,1,0:T(8,128)S(1)}, f32[8,32,288]{2,1,0:T(8,128)}, u32[]{:S(2)}, u32[]{:S(2)}) %collective-permute-start.9) | collective-permute-done | bytes 294944 | tf_op jit(solution)/shard_map/ppermute | solution.py:119
  71.7 1.2 maximum_select_fusion
  73.0 0.4 fusion.13
  73.3 0.2 fusion.27
  73.9 8.0 %collective-permute-start.12 = (f32[1,32,288]{2,1,0:T(8,128)S(1)}, f32[1,32,288]{2,1,0:T(8,128)S(1)}, u32[]{:S(2)}, u32[]{:S(2)}) collective-permute-start(f32[1,32,288]{2,1,0:T(8,128)S(1)} %maximum_bitcast_fusion.1), channel_id=1, source_target_pairs={{0,32},{32,0},{64,96},{96,64},{128,160},{160,128},{192,224},{224,1... | collective-permute-start | bytes 110600 | tf_op jit(solution)/shard_map/ppermute | solution.py:119
  82.1 1.3 collective-permute-start.11
  83.4 4.6 %collective-permute-start.10 = (f32[11,32,128]{2,1,0:T(8,128)S(1)}, f32[11,32,128]{2,1,0:T(8,128)S(1)}, u32[]{:S(2)}, u32[]{:S(2)}) collective-permute-start(f32[11,32,128]{2,1,0:T(8,128)S(1)} %get-tuple-element.78), channel_id=1, source_target_pairs={{0,32},{32,64},{64,96},{96,128},{128,160},{160,192},{192,224},{224... | collective-permute-start | bytes 540680 | tf_op jit(solution)/shard_map/ppermute | solution.py:145
  88.0 5.2 %collective-permute-start.13 = (f32[2,32,288]{2,1,0:T(8,128)S(1)}, f32[2,32,288]{2,1,0:T(8,128)S(1)}, u32[]{:S(2)}, u32[]{:S(2)}) collective-permute-start(f32[2,32,288]{2,1,0:T(8,128)S(1)} %maximum_select_fusion.7), channel_id=1, source_target_pairs={{0,64},{32,96},{64,0},{96,32},{128,192},{160,224},{192,128},{224,1... | collective-permute-start | bytes 221192 | tf_op jit(solution)/shard_map/ppermute | solution.py:119
  93.2 2.6 %collective-permute-done.13 = f32[2,32,288]{2,1,0:T(8,128)S(1)} collective-permute-done((f32[2,32,288]{2,1,0:T(8,128)S(1)}, f32[2,32,288]{2,1,0:T(8,128)S(1)}, u32[]{:S(2)}, u32[]{:S(2)}) %collective-permute-start.13) | collective-permute-done | bytes 73760 | tf_op jit(solution)/shard_map/ppermute | solution.py:119
  95.8 12.6 %collective-permute-start.14 = (f32[4,32,288]{2,1,0:T(8,128)S(1)}, f32[4,32,288]{2,1,0:T(8,128)S(1)}, u32[]{:S(2)}, u32[]{:S(2)}) collective-permute-start(f32[4,32,288]{2,1,0:T(8,128)S(1)} %maximum_select_fusion.5), channel_id=1, source_target_pairs={{0,128},{32,160},{64,192},{96,224},{128,0},{160,32},{192,64},{224,... | collective-permute-start | bytes 442376 | tf_op jit(solution)/shard_map/ppermute | solution.py:119
  109.0 8.3 %collective-permute-done.14 = f32[4,32,288]{2,1,0:T(8,128)S(1)} collective-permute-done((f32[4,32,288]{2,1,0:T(8,128)S(1)}, f32[4,32,288]{2,1,0:T(8,128)S(1)}, u32[]{:S(2)}, u32[]{:S(2)}) %collective-permute-start.14) | collective-permute-done | bytes 147488 | tf_op jit(solution)/shard_map/ppermute | solution.py:119
  117.4 34.9 %collective-permute-start.15 = (f32[8,32,288]{2,1,0:T(8,128)S(1)}, f32[8,32,288]{2,1,0:T(8,128)S(1)}, u32[]{:S(2)}, u32[]{:S(2)}) collective-permute-start(f32[8,32,288]{2,1,0:T(8,128)S(1)} %maximum_select_fusion.3), channel_id=1, source_target_pairs={{0,256},{32,288},{64,320},{96,352},{128,384},{160,416},{192,448},{... | collective-permute-start | bytes 884744 | tf_op jit(solution)/shard_map/ppermute | solution.py:119
  152.6 16.7 %collective-permute-done.15 = f32[8,32,288]{2,1,0:T(8,128)S(1)} collective-permute-done((f32[8,32,288]{2,1,0:T(8,128)S(1)}, f32[8,32,288]{2,1,0:T(8,128)S(1)}, u32[]{:S(2)}, u32[]{:S(2)}) %collective-permute-start.15) | collective-permute-done | bytes 294944 | tf_op jit(solution)/shard_map/ppermute | solution.py:119
  169.5 0.4 fusion.11
  169.9 0.2 fusion.25
  170.8 0.3 convolution_add_fusion.5
  171.1 0.3 convolution_add_fusion.4
  171.4 0.3 convolution_add_fusion.3
  171.7 0.3 convolution_add_fusion.2
  172.0 0.3 convolution_add_fusion.1
  172.2 0.3 fusion.4
  172.7 0.2 fusion.102
  173.1 0.3 fusion.74
  173.4 0.3 fusion.1
  173.7 0.3 fusion.21
  174.0 0.5 fusion
  174.5 0.4 fusion.16
  174.9 0.8 fusion.8
  (113 shorter events, 3.6 us)
Async XLA Ops:
  0.0 13.3 %copy-start.9 = (bf16[1,32,96]{2,1,0:T(8,128)(2,1)S(1)}, bf16[1,32,96]{2,1,0:T(8,128)(2,1)}, u32[]{:S(2)}) copy-start(bf16[1,32,96]{2,1,0:T(8,128)(2,1)} %param.23) | copy-start | bytes 18436
  0.0 13.3 %copy-start.10 = (bf16[1,32,64]{2,1,0:T(8,128)(2,1)S(1)}, bf16[1,32,64]{2,1,0:T(8,128)(2,1)}, u32[]{:S(2)}) copy-start(bf16[1,32,64]{2,1,0:T(8,128)(2,1)} %param.22) | copy-start | bytes 12292
  0.0 16.8 %copy-start.5 = (f32[3,1024]{1,0:T(4,128)S(1)}, f32[3,1024]{1,0:T(4,128)}, u32[]{:S(2)}) copy-start(f32[3,1024]{1,0:T(4,128)} %param.17) | copy-start | bytes 36868
  1.1 25.2 %copy-start = (bf16[1024,128]{1,0:T(8,128)(2,1)S(1)}, bf16[1024,128]{1,0:T(8,128)(2,1)}, u32[]{:S(2)}) copy-start(bf16[1024,128]{1,0:T(8,128)(2,1)} %param.16) | copy-start | bytes 786436
  1.1 25.3 %copy-start.8 = (s32[16,3]{0,1:T(4,128)S(1)}, s32[16,3]{0,1:T(4,128)}, u32[]{:S(2)}) copy-start(s32[16,3]{0,1:T(4,128)} %param.18) | copy-start | bytes 580
  1.1 26.1 %copy-start.13 = (s32[6]{0:T(128)S(1)}, s32[6]{0:T(128)}, u32[]{:S(2)}) copy-start(s32[6]{0:T(128)} %constant.263) | copy-start | bytes 76
  1.1 26.1 %copy-start.14 = (s32[12]{0:T(128)S(1)}, s32[12]{0:T(128)}, u32[]{:S(2)}) copy-start(s32[12]{0:T(128)} %constant.262) | copy-start | bytes 148
  2.3 25.6 %copy-start.11 = (s32[24]{0:T(128)S(1)}, s32[24]{0:T(128)}, u32[]{:S(2)}) copy-start(s32[24]{0:T(128)} %constant.261) | copy-start | bytes 292
  2.3 25.5 %copy-start.12 = (s32[48]{0:T(128)S(1)}, s32[48]{0:T(128)}, u32[]{:S(2)}) copy-start(s32[48]{0:T(128)} %constant.260) | copy-start | bytes 580
  6.0 39.8 %collective-permute-start.5 = (bf16[4,2,32,128]{3,2,1,0:T(8,128)(2,1)}, bf16[4,2,32,128]{3,2,1,0:T(8,128)(2,1)S(1)}, u32[]{:S(2)}, u32[]{:S(2)}) collective-permute-start(bf16[4,2,32,128]{3,2,1,0:T(8,128)(2,1)} %get-tuple-element.68), channel_id=1, source_target_pairs={{2,0},{4,2},{6,4},{8,6},{10,8},{12,10},{14,12},{16,14},{18,16},{20... | collective-permute-start | bytes 196616 | tf_op jit(solution)/shard_map/ppermute | solution.py:27
  10.5 35.3 %collective-permute-start.4 = (bf16[4,2,32,128]{3,2,1,0:T(8,128)(2,1)}, bf16[4,2,32,128]{3,2,1,0:T(8,128)(2,1)S(1)}, u32[]{:S(2)}, u32[]{:S(2)}) collective-permute-start(bf16[4,2,32,128]{3,2,1,0:T(8,128)(2,1)} %get-tuple-element.67), channel_id=1, source_target_pairs={{0,2},{2,4},{4,6},{6,8},{8,10},{10,12},{12,14},{14,16},{16,18},{18... | collective-permute-start | bytes 196616 | tf_op jit(solution)/shard_map/ppermute | solution.py:25
  14.0 28.9 %collective-permute-start.6 = (f32[1,32,288]{2,1,0:T(8,128)}, f32[1,32,288]{2,1,0:T(8,128)}, u32[]{:S(2)}, u32[]{:S(2)}) collective-permute-start(f32[1,32,288]{2,1,0:T(8,128)} %maximum_bitcast_fusion), channel_id=1, source_target_pairs={{0,2},{2,0},{4,6},{6,4},{8,10},{10,8},{12,14},{14,12},{16,18},{18,... | collective-permute-start | bytes 110600 | tf_op jit(solution)/shard_map/ppermute | solution.py:119
  16.9 11.6 %collective-permute-start = (f32[3,64]{1,0:T(4,128)S(1)}, f32[3,64]{1,0:T(4,128)S(1)}, u32[]{:S(2)}, u32[]{:S(2)}) collective-permute-start(f32[3,64]{1,0:T(4,128)S(1)} %get-tuple-element.81), channel_id=1, source_target_pairs={{0,2},{2,4},{4,6},{6,8},{8,10},{10,12},{12,14},{14,16},{16,18},{18... | collective-permute-start | bytes 2312 | tf_op jit(solution)/shard_map/ppermute | solution.py:25
  19.9 11.6 %collective-permute-start.1 = (f32[3,64]{1,0:T(4,128)S(1)}, f32[3,64]{1,0:T(4,128)S(1)}, u32[]{:S(2)}, u32[]{:S(2)}) collective-permute-start(f32[3,64]{1,0:T(4,128)S(1)} %get-tuple-element.80), channel_id=1, source_target_pairs={{2,0},{4,2},{6,4},{8,6},{10,8},{12,10},{14,12},{16,14},{18,16},{20... | collective-permute-start | bytes 2312 | tf_op jit(solution)/shard_map/ppermute | solution.py:27
  28.4 7.4 %collective-permute-start.3 = (bf16[64,128]{1,0:T(8,128)(2,1)S(1)}, bf16[64,128]{1,0:T(8,128)(2,1)S(1)}, u32[]{:S(2)}, u32[]{:S(2)}) collective-permute-start(bf16[64,128]{1,0:T(8,128)(2,1)S(1)} %get-tuple-element.29), channel_id=1, source_target_pairs={{2,0},{4,2},{6,4},{8,6},{10,8},{12,10},{14,12},{16,14},{18,16},{20... | collective-permute-start | bytes 49160 | tf_op jit(solution)/shard_map/ppermute | solution.py:27
  31.5 7.7 %collective-permute-start.2 = (bf16[64,128]{1,0:T(8,128)(2,1)S(1)}, bf16[64,128]{1,0:T(8,128)(2,1)S(1)}, u32[]{:S(2)}, u32[]{:S(2)}) collective-permute-start(bf16[64,128]{1,0:T(8,128)(2,1)S(1)} %get-tuple-element.28), channel_id=1, source_target_pairs={{0,2},{2,4},{4,6},{6,8},{8,10},{10,12},{12,14},{14,16},{16,18},{18... | collective-permute-start | bytes 49160 | tf_op jit(solution)/shard_map/ppermute | solution.py:25
  43.0 13.2 %copy-start.7 = (s32[1024]{0:T(1024)S(1)}, s32[1024]{0:T(1024)}, u32[]{:S(2)}) copy-start(s32[1024]{0:T(1024)} %get-tuple-element.93) | copy-start | bytes 12292
  43.0 13.8 %copy-start.6 = (s32[1024]{0:T(1024)S(1)}, s32[1024]{0:T(1024)}, u32[]{:S(2)}) copy-start(s32[1024]{0:T(1024)} %get-tuple-element.94) | copy-start | bytes 12292
  43.9 8.0 %collective-permute-start.7 = (f32[2,32,288]{2,1,0:T(8,128)S(1)}, f32[2,32,288]{2,1,0:T(8,128)S(1)}, u32[]{:S(2)}, u32[]{:S(2)}) collective-permute-start(f32[2,32,288]{2,1,0:T(8,128)S(1)} %maximum_select_fusion.6), channel_id=1, source_target_pairs={{0,4},{2,6},{4,0},{6,2},{8,12},{10,14},{12,8},{14,10},{16,20},{18,... | collective-permute-start | bytes 221192 | tf_op jit(solution)/shard_map/ppermute | solution.py:119
  51.9 8.4 %collective-permute-start.8 = (f32[4,32,288]{2,1,0:T(8,128)S(1)}, f32[4,32,288]{2,1,0:T(8,128)S(1)}, u32[]{:S(2)}, u32[]{:S(2)}) collective-permute-start(f32[4,32,288]{2,1,0:T(8,128)S(1)} %maximum_select_fusion.4), channel_id=1, source_target_pairs={{0,8},{2,10},{4,12},{6,14},{8,0},{10,2},{12,4},{14,6},{16,24},{18,... | collective-permute-start | bytes 442376 | tf_op jit(solution)/shard_map/ppermute | solution.py:119
  55.4 6.9 %copy-start.3 = (s32[1024]{0:T(1024)S(1)}, s32[1024]{0:T(1024)}, u32[]{:S(2)}) copy-start(s32[1024]{0:T(1024)} %get-tuple-element.95) | copy-start | bytes 12292
  60.4 11.3 %collective-permute-start.9 = (f32[8,32,288]{2,1,0:T(8,128)S(1)}, f32[8,32,288]{2,1,0:T(8,128)}, u32[]{:S(2)}, u32[]{:S(2)}) collective-permute-start(f32[8,32,288]{2,1,0:T(8,128)S(1)} %maximum_select_fusion.2), channel_id=1, source_target_pairs={{0,16},{2,18},{4,20},{6,22},{8,24},{10,26},{12,28},{14,30},{16,0},... | collective-permute-start | bytes 884744 | tf_op jit(solution)/shard_map/ppermute | solution.py:119
  73.3 35.1 %copy-start.4 = (f32[8,32,128]{2,1,0:T(8,128)S(1)}, f32[8,32,128]{2,1,0:T(8,128)}, u32[]{:S(2)}) copy-start(f32[8,32,128]{2,1,0:T(8,128)} %constant_dynamic-update-slice_fusion.2) | copy-start | bytes 393220
  73.9 14.1 %collective-permute-start.12 = (f32[1,32,288]{2,1,0:T(8,128)S(1)}, f32[1,32,288]{2,1,0:T(8,128)S(1)}, u32[]{:S(2)}, u32[]{:S(2)}) collective-permute-start(f32[1,32,288]{2,1,0:T(8,128)S(1)} %maximum_bitcast_fusion.1), channel_id=1, source_target_pairs={{0,32},{32,0},{64,96},{96,64},{128,160},{160,128},{192,224},{224,1... | collective-permute-start | bytes 110600 | tf_op jit(solution)/shard_map/ppermute | solution.py:119
  82.1 26.3 %collective-permute-start.11 = (f32[11,32,128]{2,1,0:T(8,128)S(1)}, f32[11,32,128]{2,1,0:T(8,128)S(1)}, u32[]{:S(2)}, u32[]{:S(2)}) collective-permute-start(f32[11,32,128]{2,1,0:T(8,128)S(1)} %get-tuple-element.79), channel_id=1, source_target_pairs={{32,0},{64,32},{96,64},{128,96},{160,128},{192,160},{224,192},{256... | collective-permute-start | bytes 540680 | tf_op jit(solution)/shard_map/ppermute | solution.py:146
  83.4 24.9 %collective-permute-start.10 = (f32[11,32,128]{2,1,0:T(8,128)S(1)}, f32[11,32,128]{2,1,0:T(8,128)S(1)}, u32[]{:S(2)}, u32[]{:S(2)}) collective-permute-start(f32[11,32,128]{2,1,0:T(8,128)S(1)} %get-tuple-element.78), channel_id=1, source_target_pairs={{0,32},{32,64},{64,96},{96,128},{128,160},{160,192},{192,224},{224... | collective-permute-start | bytes 540680 | tf_op jit(solution)/shard_map/ppermute | solution.py:145
  88.0 7.8 %collective-permute-start.13 = (f32[2,32,288]{2,1,0:T(8,128)S(1)}, f32[2,32,288]{2,1,0:T(8,128)S(1)}, u32[]{:S(2)}, u32[]{:S(2)}) collective-permute-start(f32[2,32,288]{2,1,0:T(8,128)S(1)} %maximum_select_fusion.7), channel_id=1, source_target_pairs={{0,64},{32,96},{64,0},{96,32},{128,192},{160,224},{192,128},{224,1... | collective-permute-start | bytes 221192 | tf_op jit(solution)/shard_map/ppermute | solution.py:119
  95.8 21.5 %collective-permute-start.14 = (f32[4,32,288]{2,1,0:T(8,128)S(1)}, f32[4,32,288]{2,1,0:T(8,128)S(1)}, u32[]{:S(2)}, u32[]{:S(2)}) collective-permute-start(f32[4,32,288]{2,1,0:T(8,128)S(1)} %maximum_select_fusion.5), channel_id=1, source_target_pairs={{0,128},{32,160},{64,192},{96,224},{128,0},{160,32},{192,64},{224,... | collective-permute-start | bytes 442376 | tf_op jit(solution)/shard_map/ppermute | solution.py:119
  108.5 43.9 %copy-start.2 = (bf16[1,31,32,96]{3,2,1,0:T(8,128)(2,1)S(1)}, bf16[1,31,32,96]{3,2,1,0:T(8,128)(2,1)}, u32[]{:S(2)}) copy-start(bf16[1,31,32,96]{3,2,1,0:T(8,128)(2,1)} %param.21) | copy-start | bytes 571396
  117.4 51.9 %collective-permute-start.15 = (f32[8,32,288]{2,1,0:T(8,128)S(1)}, f32[8,32,288]{2,1,0:T(8,128)S(1)}, u32[]{:S(2)}, u32[]{:S(2)}) collective-permute-start(f32[8,32,288]{2,1,0:T(8,128)S(1)} %maximum_select_fusion.3), channel_id=1, source_target_pairs={{0,256},{32,288},{64,320},{96,352},{128,384},{160,416},{192,448},{... | collective-permute-start | bytes 884744 | tf_op jit(solution)/shard_map/ppermute | solution.py:119
  169.4 3.3 %copy-start.1 = (bf16[1,15,32,64]{3,2,1,0:T(8,128)(2,1)S(1)}, bf16[1,15,32,64]{3,2,1,0:T(8,128)(2,1)}, u32[]{:S(2)}) copy-start(bf16[1,15,32,64]{3,2,1,0:T(8,128)(2,1)} %param.20) | copy-start | bytes 184324

commit v5 on v4

--- a/solution.py
+++ b/solution.py
@@ -114,8 +114,8 @@
     count = lax.axis_size(axis)
     index = lax.axis_index(axis)
     gathered = block[None]
-    step = 1
-    while step < count:
+    step = count // 2
+    while step >= 1:
         received = lax.ppermute(gathered, axis, [(i, i ^ step) for i in range(count)])
         upper = (index & step) != 0
         gathered = jnp.where(
@@ -123,8 +123,10 @@
             jnp.concatenate([received, gathered], 0),
             jnp.concatenate([gathered, received], 0),
         )
-        step *= 2
-    return gathered
+        step //= 2
+    bits = count.bit_length() - 1
+    order = [int(format(i, f"0{bits}b")[::-1], 2) for i in range(count)]
+    return jnp.take(gathered, np.array(order), axis=0)
 
 
 def upper_tree(device_coef, device_coupling, upper_transfer, upper_coupling):

time: 177 us -> 142 us (0.80)
  the two profiles are of different devices: /device:TPU:16 before, /device:TPU:32 now
where the time goes in v5:
time: 142 us; the launch traced here: 141 us
  starting transfers between devices  66.6 us (47%)
  waiting for transfers between devices  40.1 us (28%)
  matrix products  18.5 us (13%)
  local copies, waits for them, and re-layouts  12.2 us (9%)
  other arithmetic  2.09 us (1%)
    ppermute x8, starting transfers between devices, doubling_gather(): lax.ppermute(gathered, axis, [(i, i ^ step) for i in range(count)])  35.8 us
    ppermute x8, waiting for transfers between devices, doubling_gather(): lax.ppermute(gathered, axis, [(i, i ^ step) for i in range(count)])  34.8 us
    ppermute x3, starting transfers between devices, extended_2(): lax.ppermute(head, axis, [((i + 1) % count, i) for i in range(ends)])  16.8 us
    ppermute x3, starting transfers between devices, extended_2(): lax.ppermute(tail, axis, [(i, (i + 1) % count) for i in range(ends)])  7.67 us
    dot_general x13, matrix products, product(): return jnp.dot(matrix, operand, precision=HIGHEST)  5.34 us
    ppermute x3, waiting for transfers between devices, extended_2(): lax.ppermute(tail, axis, [(i, (i + 1) % count) for i in range(ends)])  5.28 us
    ppermute x1, starting transfers between devices, upper_tree(): lax.ppermute(heads, 'z', [(i + 1, i) for i in range(planes - 1)])  4.44 us
    dot_general x4, matrix products, local(): jnp.einsum('cra,cav->crv', lift_mats, children, precision=HIGHEST)  3.75 us
  transfers between devices with their start and end apart: 16, of which 7 were waited for; matrix products, arithmetic and copies ran while one was open for 13% of the time, Pallas kernels for 0%

profile of v5, /device:TPU:32, one launch (start us, length us, event | category | flops | bytes accessed | tf_op | source)
XLA Modules:
  0.0 140.8 jit_solution(13098187862336868196)
XLA Ops:
  0.0 1.0 reshape.104
  1.1 1.2 fusion.154
  2.3 1.1 bitcast_convert_fusion.1
  3.4 0.9 fusion.76
  4.4 0.9 bitcast_convert_fusion
  5.4 6.7 %collective-permute-start.5 = (bf16[4,2,32,128]{3,2,1,0:T(8,128)(2,1)S(1)}, bf16[4,2,32,128]{3,2,1,0:T(8,128)(2,1)S(1)}, u32[]{:S(2)}, u32[]{:S(2)}) collective-permute-start(bf16[4,2,32,128]{3,2,1,0:T(8,128)(2,1)S(1)} %get-tuple-element.69), channel_id=1, source_target_pairs={{2,0},{4,2},{6,4},{8,6},{10,8},{12,10},{14,12},{16,14},{18,16},{20... | collective-permute-start | bytes 196616 | tf_op jit(solution)/shard_map/ppermute | solution.py:27
  12.0 1.9 %collective-permute-start.4 = (bf16[4,2,32,128]{3,2,1,0:T(8,128)(2,1)S(1)}, bf16[4,2,32,128]{3,2,1,0:T(8,128)(2,1)S(1)}, u32[]{:S(2)}, u32[]{:S(2)}) collective-permute-start(bf16[4,2,32,128]{3,2,1,0:T(8,128)(2,1)S(1)} %get-tuple-element.68), channel_id=1, source_target_pairs={{0,2},{2,4},{4,6},{6,8},{8,10},{10,12},{12,14},{14,16},{16,18},{18... | collective-permute-start | bytes 196616 | tf_op jit(solution)/shard_map/ppermute | solution.py:25
  14.0 0.8 convolution_bitcast_fusion.6
  14.9 3.0 %collective-permute-start.6 = (f32[1,32,288]{2,1,0:T(8,128)S(1)}, f32[1,32,288]{2,1,0:T(8,128)S(1)}, u32[]{:S(2)}, u32[]{:S(2)}) collective-permute-start(f32[1,32,288]{2,1,0:T(8,128)S(1)} %maximum_bitcast_fusion), channel_id=1, source_target_pairs={{0,16},{2,18},{4,20},{6,22},{8,24},{10,26},{12,28},{14,30},{16,0},... | collective-permute-start | bytes 110600 | tf_op jit(solution)/shard_map/ppermute | solution.py:119
  18.0 2.8 %collective-permute-start = (f32[3,64]{1,0:T(4,128)S(1)}, f32[3,64]{1,0:T(4,128)S(1)}, u32[]{:S(2)}, u32[]{:S(2)}) collective-permute-start(f32[3,64]{1,0:T(4,128)S(1)} %get-tuple-element.82), channel_id=1, source_target_pairs={{0,2},{2,4},{4,6},{6,8},{8,10},{10,12},{12,14},{14,16},{16,18},{18... | collective-permute-start | bytes 2312 | tf_op jit(solution)/shard_map/ppermute | solution.py:25
  20.8 7.3 %collective-permute-start.1 = (f32[3,64]{1,0:T(4,128)S(1)}, f32[3,64]{1,0:T(4,128)S(1)}, u32[]{:S(2)}, u32[]{:S(2)}) collective-permute-start(f32[3,64]{1,0:T(4,128)S(1)} %get-tuple-element.81), channel_id=1, source_target_pairs={{2,0},{4,2},{6,4},{8,6},{10,8},{12,10},{14,12},{16,14},{18,16},{20... | collective-permute-start | bytes 2312 | tf_op jit(solution)/shard_map/ppermute | solution.py:27
  28.1 0.6 constant_dynamic-update-slice_fusion.2
  28.7 0.7 slice_bitcast_fusion.5
  29.5 0.7 copy.41
  30.5 2.8 %collective-permute-start.3 = (bf16[64,128]{1,0:T(8,128)(2,1)S(1)}, bf16[64,128]{1,0:T(8,128)(2,1)S(1)}, u32[]{:S(2)}, u32[]{:S(2)}) collective-permute-start(bf16[64,128]{1,0:T(8,128)(2,1)S(1)} %get-tuple-element.30), channel_id=1, source_target_pairs={{2,0},{4,2},{6,4},{8,6},{10,8},{12,10},{14,12},{16,14},{18,16},{20... | collective-permute-start | bytes 49160 | tf_op jit(solution)/shard_map/ppermute | solution.py:27
  33.4 3.0 %collective-permute-start.2 = (bf16[64,128]{1,0:T(8,128)(2,1)S(1)}, bf16[64,128]{1,0:T(8,128)(2,1)S(1)}, u32[]{:S(2)}, u32[]{:S(2)}) collective-permute-start(bf16[64,128]{1,0:T(8,128)(2,1)S(1)} %get-tuple-element.29), channel_id=1, source_target_pairs={{0,2},{2,4},{4,6},{6,8},{8,10},{10,12},{12,14},{14,16},{16,18},{18... | collective-permute-start | bytes 49160 | tf_op jit(solution)/shard_map/ppermute | solution.py:25
  36.6 0.6 gather_fusion
  37.3 0.7 multiply_reduce_fusion
  38.0 5.3 %collective-permute-done.2 = bf16[64,128]{1,0:T(8,128)(2,1)S(1)} collective-permute-done((bf16[64,128]{1,0:T(8,128)(2,1)S(1)}, bf16[64,128]{1,0:T(8,128)(2,1)S(1)}, u32[]{:S(2)}, u32[]{:S(2)}) %collective-permute-start.2) | collective-permute-done | bytes 16416 | tf_op jit(solution)/shard_map/ppermute | solution.py:25
  43.3 1.6 %gather_fusion.1 = bf16[48,64,128]{2,1,0:T(8,128)(2,1)} fusion(bf16[18,64,128]{2,1,0:T(8,128)(2,1)S(1)} %bitcast.252, s32[1024]{0:T(1024)S(1)} %pad_clamp_fusion.5), kind=kCustom, calls=%fused_computation.3 | custom fusion | bytes 1573056 | tf_op jit(solution)/shard_map/while/body/eval_jaxpr/gather | solution.py:57
  44.9 2.9 %fusion.6 = f32[16,64,128,1]{2,1,3,0:T(8,128)} fusion(bf16[16,3,64,128]{3,2,1,0:T(8,128)(2,1)} %bitcast.267, f32[16,3,64,64]{3,2,1,0:T(8,128)S(1)} %multiply_reduce_fusion, bf16[16,3]{1,0:T(8,128)(2,1)S(1)} %copy.39), kind=kOutput, calls=%fused_computation.31 | convolution fusion | flops 51707904 | bytes 2097248 | tf_op jit(solution)/shard_map/while/body/eval_jaxpr/gkij,gkjv->giv/dot_general | solution.py:56
  47.8 1.9 %collective-permute-start.7 = (f32[2,32,288]{2,1,0:T(8,128)S(1)}, f32[2,32,288]{2,1,0:T(8,128)S(1)}, u32[]{:S(2)}, u32[]{:S(2)}) collective-permute-start(f32[2,32,288]{2,1,0:T(8,128)S(1)} %maximum_select_fusion.6), channel_id=1, source_target_pairs={{0,8},{2,10},{4,12},{6,14},{8,0},{10,2},{12,4},{14,6},{16,24},{18,... | collective-permute-start | bytes 221192 | tf_op jit(solution)/shard_map/ppermute | solution.py:119
  49.8 4.5 %collective-permute-done.7 = f32[2,32,288]{2,1,0:T(8,128)S(1)} collective-permute-done((f32[2,32,288]{2,1,0:T(8,128)S(1)}, f32[2,32,288]{2,1,0:T(8,128)S(1)}, u32[]{:S(2)}, u32[]{:S(2)}) %collective-permute-start.7) | collective-permute-done | bytes 73760 | tf_op jit(solution)/shard_map/ppermute | solution.py:119
  54.3 1.9 %collective-permute-start.8 = (f32[4,32,288]{2,1,0:T(8,128)S(1)}, f32[4,32,288]{2,1,0:T(8,128)S(1)}, u32[]{:S(2)}, u32[]{:S(2)}) collective-permute-start(f32[4,32,288]{2,1,0:T(8,128)S(1)} %maximum_select_fusion.4), channel_id=1, source_target_pairs={{0,4},{2,6},{4,0},{6,2},{8,12},{10,14},{12,8},{14,10},{16,20},{18,... | collective-permute-start | bytes 442376 | tf_op jit(solution)/shard_map/ppermute | solution.py:119
  56.3 0.6 gather_fusion.5
  56.8 1.2 gather_fusion.4
  58.1 1.3 gather_fusion.3
  59.4 5.8 %collective-permute-done.8 = f32[4,32,288]{2,1,0:T(8,128)S(1)} collective-permute-done((f32[4,32,288]{2,1,0:T(8,128)S(1)}, f32[4,32,288]{2,1,0:T(8,128)S(1)}, u32[]{:S(2)}, u32[]{:S(2)}) %collective-permute-start.8) | collective-permute-done | bytes 147488 | tf_op jit(solution)/shard_map/ppermute | solution.py:119
  65.2 1.9 %collective-permute-start.9 = (f32[8,32,288]{2,1,0:T(8,128)S(1)}, f32[8,32,288]{2,1,0:T(8,128)S(1)}, u32[]{:S(2)}, u32[]{:S(2)}) collective-permute-start(f32[8,32,288]{2,1,0:T(8,128)S(1)} %maximum_select_fusion.2), channel_id=1, source_target_pairs={{0,2},{2,0},{4,6},{6,4},{8,10},{10,8},{12,14},{14,12},{16,18},{18,... | collective-permute-start | bytes 884744 | tf_op jit(solution)/shard_map/ppermute | solution.py:119
  67.2 0.6 gather_fusion.2
  67.8 1.5 %convolution_bitcast_fusion.4 = f32[2,32,128]{2,1,0:T(8,128)} fusion(f32[2,96,128]{2,1,0:T(8,128)S(1)} %bitcast.271, bf16[1,31,32,96]{3,2,1,0:T(8,128)(2,1)} %param.25), kind=kOutput, calls=%fused_computation.18 | convolution fusion | flops 9437184 | bytes 147456 | tf_op jit(solution)/shard_map/cra,cav->crv/dot_general | solution.py:239
  69.3 5.6 %collective-permute-done.9 = f32[8,32,288]{2,1,0:T(8,128)S(1)} collective-permute-done((f32[8,32,288]{2,1,0:T(8,128)S(1)}, f32[8,32,288]{2,1,0:T(8,128)S(1)}, u32[]{:S(2)}, u32[]{:S(2)}) %collective-permute-start.9) | collective-permute-done | bytes 294944 | tf_op jit(solution)/shard_map/ppermute | solution.py:119
  75.0 0.6 gather_fusion.6
  75.7 0.3 fusion.13
  76.0 0.2 fusion.27
  76.7 15.7 %collective-permute-start.12 = (f32[1,32,288]{2,1,0:T(8,128)S(1)}, f32[1,32,288]{2,1,0:T(8,128)S(1)}, u32[]{:S(2)}, u32[]{:S(2)}) collective-permute-start(f32[1,32,288]{2,1,0:T(8,128)S(1)} %maximum_bitcast_fusion.1), channel_id=1, source_target_pairs={{0,256},{32,288},{64,320},{96,352},{128,384},{160,416},{192,448},{... | collective-permute-start | bytes 110600 | tf_op jit(solution)/shard_map/ppermute | solution.py:119
  92.6 4.4 %collective-permute-start.11 = (f32[11,32,128]{2,1,0:T(8,128)S(1)}, f32[11,32,128]{2,1,0:T(8,128)S(1)}, u32[]{:S(2)}, u32[]{:S(2)}) collective-permute-start(f32[11,32,128]{2,1,0:T(8,128)S(1)} %get-tuple-element.80), channel_id=1, source_target_pairs={{32,0},{64,32},{96,64},{128,96},{160,128},{192,160},{224,192},{256... | collective-permute-start | bytes 540680 | tf_op jit(solution)/shard_map/ppermute | solution.py:148
  97.0 1.9 %collective-permute-start.10 = (f32[11,32,128]{2,1,0:T(8,128)S(1)}, f32[11,32,128]{2,1,0:T(8,128)S(1)}, u32[]{:S(2)}, u32[]{:S(2)}) collective-permute-start(f32[11,32,128]{2,1,0:T(8,128)S(1)} %get-tuple-element.79), channel_id=1, source_target_pairs={{0,32},{32,64},{64,96},{96,128},{128,160},{160,192},{192,224},{224... | collective-permute-start | bytes 540680 | tf_op jit(solution)/shard_map/ppermute | solution.py:147
  99.0 6.4 %collective-permute-start.13 = (f32[2,32,288]{2,1,0:T(8,128)S(1)}, f32[2,32,288]{2,1,0:T(8,128)S(1)}, u32[]{:S(2)}, u32[]{:S(2)}) collective-permute-start(f32[2,32,288]{2,1,0:T(8,128)S(1)} %maximum_select_fusion.7), channel_id=1, source_target_pairs={{0,128},{32,160},{64,192},{96,224},{128,0},{160,32},{192,64},{224,... | collective-permute-start | bytes 221192 | tf_op jit(solution)/shard_map/ppermute | solution.py:119
  105.4 0.6 dynamic-slice_bitcast_fusion.14
  106.0 7.0 %collective-permute-done.13 = f32[2,32,288]{2,1,0:T(8,128)S(1)} collective-permute-done((f32[2,32,288]{2,1,0:T(8,128)S(1)}, f32[2,32,288]{2,1,0:T(8,128)S(1)}, u32[]{:S(2)}, u32[]{:S(2)}) %collective-permute-start.13) | collective-permute-done | bytes 73760 | tf_op jit(solution)/shard_map/ppermute | solution.py:119
  113.1 3.0 %collective-permute-start.14 = (f32[4,32,288]{2,1,0:T(8,128)S(1)}, f32[4,32,288]{2,1,0:T(8,128)S(1)}, u32[]{:S(2)}, u32[]{:S(2)}) collective-permute-start(f32[4,32,288]{2,1,0:T(8,128)S(1)} %maximum_select_fusion.5), channel_id=1, source_target_pairs={{0,64},{32,96},{64,0},{96,32},{128,192},{160,224},{192,128},{224,1... | collective-permute-start | bytes 442376 | tf_op jit(solution)/shard_map/ppermute | solution.py:119
  116.5 0.8 fusion.43
  117.3 6.4 %collective-permute-done.14 = f32[4,32,288]{2,1,0:T(8,128)S(1)} collective-permute-done((f32[4,32,288]{2,1,0:T(8,128)S(1)}, f32[4,32,288]{2,1,0:T(8,128)S(1)}, u32[]{:S(2)}, u32[]{:S(2)}) %collective-permute-start.14) | collective-permute-done | bytes 147488 | tf_op jit(solution)/shard_map/ppermute | solution.py:119
  123.7 1.9 %collective-permute-start.15 = (f32[8,32,288]{2,1,0:T(8,128)S(1)}, f32[8,32,288]{2,1,0:T(8,128)S(1)}, u32[]{:S(2)}, u32[]{:S(2)}) collective-permute-start(f32[8,32,288]{2,1,0:T(8,128)S(1)} %maximum_select_fusion.3), channel_id=1, source_target_pairs={{0,32},{32,0},{64,96},{96,64},{128,160},{160,128},{192,224},{224,1... | collective-permute-start | bytes 884744 | tf_op jit(solution)/shard_map/ppermute | solution.py:119
  125.6 0.8 fusion.49
  126.3 1.4 %convolution_bitcast_fusion.5 = f32[32,128]{1,0:T(8,128)} fusion(f32[32,128]{1,0:T(8,128)S(1)} %get-tuple-element.26, f32[32,128]{1,0:T(8,128)S(1)} %get-tuple-element.28, f32[32,128]{1,0:T(8,128)S(1)} %get-tuple-element.24, bf16[1,31,32,96]{3,2,1,0:T(8,128)(2,1)} %param.25), kind=kOutput, calls=%fused_computation.26 | convolution fusion | flops 4743168 | bytes 73728 | tf_op jit(solution)/shard_map/dot_general | solution.py:80
  127.8 5.5 %collective-permute-done.15 = f32[8,32,288]{2,1,0:T(8,128)S(1)} collective-permute-done((f32[8,32,288]{2,1,0:T(8,128)S(1)}, f32[8,32,288]{2,1,0:T(8,128)S(1)}, u32[]{:S(2)}, u32[]{:S(2)}) %collective-permute-start.15) | collective-permute-done | bytes 294944 | tf_op jit(solution)/shard_map/ppermute | solution.py:119
  133.4 0.7 gather_fusion.7
  134.5 0.4 fusion.11
  134.8 0.2 fusion.25
  135.7 0.3 convolution_add_fusion.5
  136.0 0.3 convolution_add_fusion.4
  136.3 0.3 convolution_add_fusion.3
  136.6 0.3 convolution_add_fusion.2
  136.9 0.3 convolution_add_fusion.1
  137.2 0.3 fusion.4
  137.7 0.2 fusion.102
  138.1 0.3 fusion.74
  138.4 0.3 fusion.1
  138.7 0.3 fusion.21
  139.0 0.5 fusion
  139.5 0.4 fusion.16
  140.0 0.8 fusion.8
  (138 shorter events, 3.2 us)
Async XLA Ops:
  0.0 14.8 %copy-start.18 = (bf16[1,32,96]{2,1,0:T(8,128)(2,1)S(1)}, bf16[1,32,96]{2,1,0:T(8,128)(2,1)}, u32[]{:S(2)}) copy-start(bf16[1,32,96]{2,1,0:T(8,128)(2,1)} %param.27) | copy-start | bytes 18436
  0.0 14.8 %copy-start.19 = (bf16[1,32,64]{2,1,0:T(8,128)(2,1)S(1)}, bf16[1,32,64]{2,1,0:T(8,128)(2,1)}, u32[]{:S(2)}) copy-start(bf16[1,32,64]{2,1,0:T(8,128)(2,1)} %param.26) | copy-start | bytes 12292
  0.0 17.9 %copy-start.16 = (f32[3,1024]{1,0:T(4,128)S(1)}, f32[3,1024]{1,0:T(4,128)}, u32[]{:S(2)}) copy-start(f32[3,1024]{1,0:T(4,128)} %param.21) | copy-start | bytes 36868
  1.1 28.4 %copy-start = (bf16[1024,128]{1,0:T(8,128)(2,1)S(1)}, bf16[1024,128]{1,0:T(8,128)(2,1)}, u32[]{:S(2)}) copy-start(bf16[1024,128]{1,0:T(8,128)(2,1)} %param.20) | copy-start | bytes 786436
  1.1 28.4 %copy-start.25 = (s32[16]{0:T(128)S(1)}, s32[16]{0:T(128)}, u32[]{:S(2)}) copy-start(s32[16]{0:T(128)} %constant.295) | copy-start | bytes 196
  1.1 29.1 %copy-start.17 = (s32[16,3]{0,1:T(4,128)S(1)}, s32[16,3]{0,1:T(4,128)}, u32[]{:S(2)}) copy-start(s32[16,3]{0,1:T(4,128)} %param.22) | copy-start | bytes 580
  2.3 28.2 %copy-start.23 = (s32[6]{0:T(128)S(1)}, s32[6]{0:T(128)}, u32[]{:S(2)}) copy-start(s32[6]{0:T(128)} %constant.292) | copy-start | bytes 76
  2.3 28.2 %copy-start.24 = (s32[12]{0:T(128)S(1)}, s32[12]{0:T(128)}, u32[]{:S(2)}) copy-start(s32[12]{0:T(128)} %constant.291) | copy-start | bytes 148
  2.3 28.2 %copy-start.21 = (s32[24]{0:T(128)S(1)}, s32[24]{0:T(128)}, u32[]{:S(2)}) copy-start(s32[24]{0:T(128)} %constant.290) | copy-start | bytes 292
  2.3 28.2 %copy-start.22 = (s32[48]{0:T(128)S(1)}, s32[48]{0:T(128)}, u32[]{:S(2)}) copy-start(s32[48]{0:T(128)} %constant.289) | copy-start | bytes 580
  5.4 44.4 %collective-permute-start.5 = (bf16[4,2,32,128]{3,2,1,0:T(8,128)(2,1)S(1)}, bf16[4,2,32,128]{3,2,1,0:T(8,128)(2,1)S(1)}, u32[]{:S(2)}, u32[]{:S(2)}) collective-permute-start(bf16[4,2,32,128]{3,2,1,0:T(8,128)(2,1)S(1)} %get-tuple-element.69), channel_id=1, source_target_pairs={{2,0},{4,2},{6,4},{8,6},{10,8},{12,10},{14,12},{16,14},{18,16},{20... | collective-permute-start | bytes 196616 | tf_op jit(solution)/shard_map/ppermute | solution.py:27
  12.0 37.7 %collective-permute-start.4 = (bf16[4,2,32,128]{3,2,1,0:T(8,128)(2,1)S(1)}, bf16[4,2,32,128]{3,2,1,0:T(8,128)(2,1)S(1)}, u32[]{:S(2)}, u32[]{:S(2)}) collective-permute-start(bf16[4,2,32,128]{3,2,1,0:T(8,128)(2,1)S(1)} %get-tuple-element.68), channel_id=1, source_target_pairs={{0,2},{2,4},{4,6},{6,8},{8,10},{10,12},{12,14},{14,16},{16,18},{18... | collective-permute-start | bytes 196616 | tf_op jit(solution)/shard_map/ppermute | solution.py:25
  14.9 32.9 %collective-permute-start.6 = (f32[1,32,288]{2,1,0:T(8,128)S(1)}, f32[1,32,288]{2,1,0:T(8,128)S(1)}, u32[]{:S(2)}, u32[]{:S(2)}) collective-permute-start(f32[1,32,288]{2,1,0:T(8,128)S(1)} %maximum_bitcast_fusion), channel_id=1, source_target_pairs={{0,16},{2,18},{4,20},{6,22},{8,24},{10,26},{12,28},{14,30},{16,0},... | collective-permute-start | bytes 110600 | tf_op jit(solution)/shard_map/ppermute | solution.py:119
  18.0 12.5 %collective-permute-start = (f32[3,64]{1,0:T(4,128)S(1)}, f32[3,64]{1,0:T(4,128)S(1)}, u32[]{:S(2)}, u32[]{:S(2)}) collective-permute-start(f32[3,64]{1,0:T(4,128)S(1)} %get-tuple-element.82), channel_id=1, source_target_pairs={{0,2},{2,4},{4,6},{6,8},{8,10},{10,12},{12,14},{14,16},{16,18},{18... | collective-permute-start | bytes 2312 | tf_op jit(solution)/shard_map/ppermute | solution.py:25
  20.8 12.6 %collective-permute-start.1 = (f32[3,64]{1,0:T(4,128)S(1)}, f32[3,64]{1,0:T(4,128)S(1)}, u32[]{:S(2)}, u32[]{:S(2)}) collective-permute-start(f32[3,64]{1,0:T(4,128)S(1)} %get-tuple-element.81), channel_id=1, source_target_pairs={{2,0},{4,2},{6,4},{8,6},{10,8},{12,10},{14,12},{16,14},{18,16},{20... | collective-permute-start | bytes 2312 | tf_op jit(solution)/shard_map/ppermute | solution.py:27
  29.5 45.5 %copy-start.20 = (s32[1024]{0:T(1024)}, s32[1024]{0:T(1024)S(1)}, u32[]{:S(2)}) copy-start(s32[1024]{0:T(1024)S(1)} %pad_clamp_fusion) | copy-start | bytes 12292
  30.5 7.4 %collective-permute-start.3 = (bf16[64,128]{1,0:T(8,128)(2,1)S(1)}, bf16[64,128]{1,0:T(8,128)(2,1)S(1)}, u32[]{:S(2)}, u32[]{:S(2)}) collective-permute-start(bf16[64,128]{1,0:T(8,128)(2,1)S(1)} %get-tuple-element.30), channel_id=1, source_target_pairs={{2,0},{4,2},{6,4},{8,6},{10,8},{12,10},{14,12},{16,14},{18,16},{20... | collective-permute-start | bytes 49160 | tf_op jit(solution)/shard_map/ppermute | solution.py:27
  33.4 9.9 %collective-permute-start.2 = (bf16[64,128]{1,0:T(8,128)(2,1)S(1)}, bf16[64,128]{1,0:T(8,128)(2,1)S(1)}, u32[]{:S(2)}, u32[]{:S(2)}) collective-permute-start(bf16[64,128]{1,0:T(8,128)(2,1)S(1)} %get-tuple-element.29), channel_id=1, source_target_pairs={{0,2},{2,4},{4,6},{6,8},{8,10},{10,12},{12,14},{14,16},{16,18},{18... | collective-permute-start | bytes 49160 | tf_op jit(solution)/shard_map/ppermute | solution.py:25
  47.8 6.5 %collective-permute-start.7 = (f32[2,32,288]{2,1,0:T(8,128)S(1)}, f32[2,32,288]{2,1,0:T(8,128)S(1)}, u32[]{:S(2)}, u32[]{:S(2)}) collective-permute-start(f32[2,32,288]{2,1,0:T(8,128)S(1)} %maximum_select_fusion.6), channel_id=1, source_target_pairs={{0,8},{2,10},{4,12},{6,14},{8,0},{10,2},{12,4},{14,6},{16,24},{18,... | collective-permute-start | bytes 221192 | tf_op jit(solution)/shard_map/ppermute | solution.py:119
  54.3 10.9 %collective-permute-start.8 = (f32[4,32,288]{2,1,0:T(8,128)S(1)}, f32[4,32,288]{2,1,0:T(8,128)S(1)}, u32[]{:S(2)}, u32[]{:S(2)}) collective-permute-start(f32[4,32,288]{2,1,0:T(8,128)S(1)} %maximum_select_fusion.4), channel_id=1, source_target_pairs={{0,4},{2,6},{4,0},{6,2},{8,12},{10,14},{12,8},{14,10},{16,20},{18,... | collective-permute-start | bytes 442376 | tf_op jit(solution)/shard_map/ppermute | solution.py:119
  65.2 9.7 %collective-permute-start.9 = (f32[8,32,288]{2,1,0:T(8,128)S(1)}, f32[8,32,288]{2,1,0:T(8,128)S(1)}, u32[]{:S(2)}, u32[]{:S(2)}) collective-permute-start(f32[8,32,288]{2,1,0:T(8,128)S(1)} %maximum_select_fusion.2), channel_id=1, source_target_pairs={{0,2},{2,0},{4,6},{6,4},{8,10},{10,8},{12,14},{14,12},{16,18},{18,... | collective-permute-start | bytes 884744 | tf_op jit(solution)/shard_map/ppermute | solution.py:119
  76.0 40.0 %copy-start.15 = (f32[8,32,128]{2,1,0:T(8,128)S(1)}, f32[8,32,128]{2,1,0:T(8,128)}, u32[]{:S(2)}) copy-start(f32[8,32,128]{2,1,0:T(8,128)} %constant_dynamic-update-slice_fusion.2) | copy-start | bytes 393220
  76.7 22.3 %collective-permute-start.12 = (f32[1,32,288]{2,1,0:T(8,128)S(1)}, f32[1,32,288]{2,1,0:T(8,128)S(1)}, u32[]{:S(2)}, u32[]{:S(2)}) collective-permute-start(f32[1,32,288]{2,1,0:T(8,128)S(1)} %maximum_bitcast_fusion.1), channel_id=1, source_target_pairs={{0,256},{32,288},{64,320},{96,352},{128,384},{160,416},{192,448},{... | collective-permute-start | bytes 110600 | tf_op jit(solution)/shard_map/ppermute | solution.py:119
  92.6 23.6 %collective-permute-start.11 = (f32[11,32,128]{2,1,0:T(8,128)S(1)}, f32[11,32,128]{2,1,0:T(8,128)S(1)}, u32[]{:S(2)}, u32[]{:S(2)}) collective-permute-start(f32[11,32,128]{2,1,0:T(8,128)S(1)} %get-tuple-element.80), channel_id=1, source_target_pairs={{32,0},{64,32},{96,64},{128,96},{160,128},{192,160},{224,192},{256... | collective-permute-start | bytes 540680 | tf_op jit(solution)/shard_map/ppermute | solution.py:148
  97.0 19.1 %collective-permute-start.10 = (f32[11,32,128]{2,1,0:T(8,128)S(1)}, f32[11,32,128]{2,1,0:T(8,128)S(1)}, u32[]{:S(2)}, u32[]{:S(2)}) collective-permute-start(f32[11,32,128]{2,1,0:T(8,128)S(1)} %get-tuple-element.79), channel_id=1, source_target_pairs={{0,32},{32,64},{64,96},{96,128},{128,160},{160,192},{192,224},{224... | collective-permute-start | bytes 540680 | tf_op jit(solution)/shard_map/ppermute | solution.py:147
  99.0 14.1 %collective-permute-start.13 = (f32[2,32,288]{2,1,0:T(8,128)S(1)}, f32[2,32,288]{2,1,0:T(8,128)S(1)}, u32[]{:S(2)}, u32[]{:S(2)}) collective-permute-start(f32[2,32,288]{2,1,0:T(8,128)S(1)} %maximum_select_fusion.7), channel_id=1, source_target_pairs={{0,128},{32,160},{64,192},{96,224},{128,0},{160,32},{192,64},{224,... | collective-permute-start | bytes 221192 | tf_op jit(solution)/shard_map/ppermute | solution.py:119
  113.1 10.6 %collective-permute-start.14 = (f32[4,32,288]{2,1,0:T(8,128)S(1)}, f32[4,32,288]{2,1,0:T(8,128)S(1)}, u32[]{:S(2)}, u32[]{:S(2)}) collective-permute-start(f32[4,32,288]{2,1,0:T(8,128)S(1)} %maximum_select_fusion.5), channel_id=1, source_target_pairs={{0,64},{32,96},{64,0},{96,32},{128,192},{160,224},{192,128},{224,1... | collective-permute-start | bytes 442376 | tf_op jit(solution)/shard_map/ppermute | solution.py:119
  123.7 9.7 %collective-permute-start.15 = (f32[8,32,288]{2,1,0:T(8,128)S(1)}, f32[8,32,288]{2,1,0:T(8,128)S(1)}, u32[]{:S(2)}, u32[]{:S(2)}) collective-permute-start(f32[8,32,288]{2,1,0:T(8,128)S(1)} %maximum_select_fusion.3), channel_id=1, source_target_pairs={{0,32},{32,0},{64,96},{96,64},{128,160},{160,128},{192,224},{224,1... | collective-permute-start | bytes 884744 | tf_op jit(solution)/shard_map/ppermute | solution.py:119
  134.2 2.1 %copy-start.8 = (f32[32,128]{1,0:T(8,128)S(1)}, f32[32,128]{1,0:T(8,128)}, u32[]{:S(2)}) copy-start(f32[32,128]{1,0:T(8,128)} %fusion.49) | copy-start | bytes 49156
  134.2 2.1 %copy-start.14 = (f32[32,64]{1,0:T(8,128)S(1)}, f32[32,64]{1,0:T(8,128)}, u32[]{:S(2)}) copy-start(f32[32,64]{1,0:T(8,128)} %get-tuple-element.40) | copy-start | bytes 24580
  134.2 2.4 %copy-start.7 = (f32[32,128]{1,0:T(8,128)S(1)}, f32[32,128]{1,0:T(8,128)}, u32[]{:S(2)}) copy-start(f32[32,128]{1,0:T(8,128)} %fusion.43) | copy-start | bytes 49156
  134.2 2.4 %copy-start.13 = (f32[32,64]{1,0:T(8,128)S(1)}, f32[32,64]{1,0:T(8,128)}, u32[]{:S(2)}) copy-start(f32[32,64]{1,0:T(8,128)} %get-tuple-element.41) | copy-start | bytes 24580
  134.2 2.7 %copy-start.12 = (f32[32,64]{1,0:T(8,128)S(1)}, f32[32,64]{1,0:T(8,128)}, u32[]{:S(2)}) copy-start(f32[32,64]{1,0:T(8,128)} %get-tuple-element.42) | copy-start | bytes 24580
  134.2 3.0 %copy-start.10 = (f32[32,128]{1,0:T(8,128)S(1)}, f32[32,128]{1,0:T(8,128)}, u32[]{:S(2)}) copy-start(f32[32,128]{1,0:T(8,128)} %convolution_bitcast_fusion.5) | copy-start | bytes 49156
  134.2 3.0 %copy-start.11 = (f32[32,64]{1,0:T(8,128)S(1)}, f32[32,64]{1,0:T(8,128)}, u32[]{:S(2)}) copy-start(f32[32,64]{1,0:T(8,128)} %get-tuple-element.39) | copy-start | bytes 24580
  134.2 3.3 %copy-start.6 = (f32[2,32,128]{2,1,0:T(8,128)S(1)}, f32[2,32,128]{2,1,0:T(8,128)}, u32[]{:S(2)}) copy-start(f32[2,32,128]{2,1,0:T(8,128)} %convolution_bitcast_fusion.4) | copy-start | bytes 98308
  134.2 3.3 %copy-start.9 = (bf16[64,32]{1,0:T(8,128)(2,1)S(1)}, bf16[64,32]{1,0:T(8,128)(2,1)}, u32[]{:S(2)}) copy-start(bf16[64,32]{1,0:T(8,128)(2,1)} %copy.41) | copy-start | bytes 12292
  134.2 3.4 %copy-start.4 = (bf16[1,15,32,64]{3,2,1,0:T(8,128)(2,1)S(1)}, bf16[1,15,32,64]{3,2,1,0:T(8,128)(2,1)}, u32[]{:S(2)}) copy-start(bf16[1,15,32,64]{3,2,1,0:T(8,128)(2,1)} %param.24) | copy-start | bytes 184324
  134.3 3.7 %copy-start.2 = (f32[12,32,128]{2,1,0:T(8,128)S(1)}, f32[12,32,128]{2,1,0:T(8,128)}, u32[]{:S(2)}) copy-start(f32[12,32,128]{2,1,0:T(8,128)} %gather_fusion.4) | copy-start | bytes 589828
  134.3 3.7 %copy-start.5 = (bf16[1,31,32,96]{3,2,1,0:T(8,128)(2,1)S(1)}, bf16[1,31,32,96]{3,2,1,0:T(8,128)(2,1)}, u32[]{:S(2)}) copy-start(bf16[1,31,32,96]{3,2,1,0:T(8,128)(2,1)} %param.25) | copy-start | bytes 571396
  134.4 4.0 %copy-start.1 = (f32[24,32,128]{2,1,0:T(8,128)S(1)}, f32[24,32,128]{2,1,0:T(8,128)}, u32[]{:S(2)}) copy-start(f32[24,32,128]{2,1,0:T(8,128)} %gather_fusion.3) | copy-start | bytes 1179652
  138.7 1.2 copy-start.3

commit v6 on v5

--- a/solution.py
+++ b/solution.py
@@ -12,23 +12,6 @@
 VARIANCE = 0.0625
 NUGGET = 0.5
 HIGHEST = lax.Precision.HIGHEST
-
-
-def extended_2(cells, sides, width):
-    for axis, dim in sides:
-        count = lax.axis_size(axis)
-        ends = count - 1
-        head = lax.slice_in_dim(cells, 0, width, axis=dim)
-        tail = lax.slice_in_dim(cells, cells.shape[dim] - width, cells.shape[dim], axis=dim)
-        cells = jnp.concatenate(
-            [
-                lax.ppermute(tail, axis, [(i, (i + 1) % count) for i in range(ends)]),
-                cells,
-                lax.ppermute(head, axis, [((i + 1) % count, i) for i in range(ends)]),
-            ],
-            axis=dim,
-        )
-    return cells
 
 
 def matern(own_points, other_points):
@@ -201,9 +184,6 @@
     depth_local = leaf_count.bit_length() - 1
     position = lax.axis_index(SPACE)
     leaf_zero = position * leaf_count
-    vector_rims = extended_2(vectors, ((SPACE, 0),), LEAF)
-    point_rims = extended_2(points, ((SPACE, 1),), LEAF)
-    nearby = near_field(vector_rims, point_rims, near_index, 0, leaf_zero, leaf_count)
     basis_leaves = leaf_basis.reshape(RANK, leaf_count, LEAF)
     leaf_vectors = vectors.reshape(leaf_count, LEAF, columns)
     coefficients = [
@@ -215,23 +195,41 @@
         lift_mats = as_float(transfer[0, first_slot : first_slot + cluster_count])
         children = coefficients[-1].reshape(cluster_count, 2 * RANK, columns)
         coefficients.append(jnp.einsum("cra,cav->crv", lift_mats, children, precision=HIGHEST))
-    edge_coefs = jnp.stack(
-        [
-            jnp.concatenate([coefficients[height][:2], coefficients[height][-2:]], 0)
-            for height in range(depth_local)
-        ],
-        0,
-    )
-    wide_edges = extended_2(edge_coefs.astype(jnp.bfloat16), ((SPACE, 1),), 2).astype(
-        edge_coefs.dtype
-    )
+    def rim(rows, clusters):
+        edges = jnp.stack([coefficients[height][clusters] for height in range(depth_local)], 0)
+        parts = [
+            vectors[rows].astype(jnp.float32),
+            points[:, rows],
+            edges.astype(jnp.bfloat16).astype(jnp.float32),
+        ]
+        return jnp.concatenate([part.reshape(-1) for part in parts]), [p.shape for p in parts]
+
+    head, shapes = rim(slice(0, LEAF), slice(0, 2))
+    tail, _ = rim(slice(row_count - LEAF, row_count), slice(-2, None))
+    count = lax.axis_size(SPACE)
+    from_left = lax.ppermute(tail, SPACE, [(i, i + 1) for i in range(count - 1)])
+    from_right = lax.ppermute(head, SPACE, [(i + 1, i) for i in range(count - 1)])
+
+    def unpack(flat):
+        pieces, done = [], 0
+        for shape in shapes:
+            size = int(np.prod(shape))
+            pieces.append(flat[done : done + size].reshape(shape))
+            done += size
+        return pieces
+
+    left_vectors, left_points, left_edges = unpack(from_left)
+    right_vectors, right_points, right_edges = unpack(from_right)
+    vector_rims = jnp.concatenate(
+        [left_vectors.astype(vectors.dtype), vectors, right_vectors.astype(vectors.dtype)], 0
+    )
+    point_rims = jnp.concatenate([left_points, points, right_points], 1)
+    nearby = near_field(vector_rims, point_rims, near_index, 0, leaf_zero, leaf_count)
     fields = []
     for height in range(depth_local):
         cluster_count = leaf_count >> height
         first_slot = 2 * leaf_count - (2 * leaf_count >> height)
-        extended = jnp.concatenate(
-            [wide_edges[height, :2], coefficients[height], wide_edges[height, 6:]], 0
-        )
+        extended = jnp.concatenate([left_edges[height], coefficients[height], right_edges[height]], 0)
         stacked = extended[partner_table(cluster_count) + 2].reshape(
             cluster_count, 3 * RANK, columns
         )

time: 142 us -> 119 us (0.84)
  the two profiles are of different devices: /device:TPU:32 before, /device:TPU:6 now
where the time goes in v6:
time: 119 us; the launch traced here: 118 us
  starting transfers between devices  56.6 us (48%)
  waiting for transfers between devices  29.3 us (25%)
  matrix products  15.1 us (13%)
  local copies, waits for them, and re-layouts  12.1 us (10%)
  other arithmetic  3.84 us (3%)
  between operations  1.36 us (1%)
    ppermute x8, starting transfers between devices, doubling_gather(): lax.ppermute(gathered, axis, [(i, i ^ step) for i in range(count)])  42.8 us
    ppermute x8, waiting for transfers between devices, doubling_gather(): lax.ppermute(gathered, axis, [(i, i ^ step) for i in range(count)])  29.3 us
    dot_general x13, matrix products, product(): return jnp.dot(matrix, operand, precision=HIGHEST)  5.35 us
    ppermute x1, starting transfers between devices, local(): lax.ppermute(tail, SPACE, [(i, i + 1) for i in range(count - 1)])  5.22 us
    ppermute x1, starting transfers between devices, upper_tree(): lax.ppermute(tails, 'z', [(i, i + 1) for i in range(planes - 1)])  4.56 us
    gather x4, local copies, waits for them, and re-layouts, local(): extended[partner_table(cluster_count) + 2]  3.72 us
    ppermute x1, starting transfers between devices, local(): lax.ppermute(head, SPACE, [(i + 1, i) for i in range(count - 1)])  2.74 us
    dot_general x4, matrix products, local(): jnp.einsum('cra,cav->crv', mixers, stacked, precision=HIGHEST)  2.49 us
  transfers between devices with their start and end apart: 12, of which 6 were waited for; matrix products, arithmetic and copies ran while one was open for 13% of the time, Pallas kernels for 0%

profile of v6, /device:TPU:6, one launch (start us, length us, event | category | flops | bytes accessed | tf_op | source)
XLA Modules:
  0.0 118.3 jit_solution(6423386340160799434)
XLA Ops:
  0.0 0.8 bitcast_convert_fusion.1
  0.8 0.8 fusion.153
  1.6 1.0 reshape.192
  2.7 1.1 fusion.154
  3.9 1.1 bitcast_convert_fusion.3
  5.0 0.2 bitcast_convert_fusion.2
  5.2 0.2 fusion.106
  5.5 2.7 %collective-permute-start.1 = (f32[41152]{0:T(1024)S(1)}, f32[41152]{0:T(1024)S(1)}, u32[]{:S(2)}, u32[]{:S(2)}) collective-permute-start(f32[41152]{0:T(1024)S(1)} %concatenate.121), channel_id=1, source_target_pairs={{2,0},{4,2},{6,4},{8,6},{10,8},{12,10},{14,12},{16,14},{18,16},{20... | collective-permute-start | bytes 493832 | tf_op jit(solution)/shard_map/ppermute | solution.py:211
  8.5 5.2 %collective-permute-start = (f32[41152]{0:T(1024)S(1)}, f32[41152]{0:T(1024)S(1)}, u32[]{:S(2)}, u32[]{:S(2)}) collective-permute-start(f32[41152]{0:T(1024)S(1)} %concatenate.120), channel_id=1, source_target_pairs={{0,2},{2,4},{4,6},{6,8},{8,10},{10,12},{12,14},{14,16},{16,18},{18... | collective-permute-start | bytes 493832 | tf_op jit(solution)/shard_map/ppermute | solution.py:210
  14.0 5.1 %collective-permute-start.2 = (f32[1,32,288]{2,1,0:T(8,128)S(1)}, f32[1,32,288]{2,1,0:T(8,128)S(1)}, u32[]{:S(2)}, u32[]{:S(2)}) collective-permute-start(f32[1,32,288]{2,1,0:T(8,128)S(1)} %maximum_bitcast_fusion), channel_id=1, source_target_pairs={{0,16},{2,18},{4,20},{6,22},{8,24},{10,26},{12,28},{14,30},{16,0},... | collective-permute-start | bytes 110600 | tf_op jit(solution)/shard_map/ppermute | solution.py:102
  19.1 0.6 constant_dynamic-update-slice_fusion.2
  20.0 1.5 %collective-permute-done.2 = f32[1,32,288]{2,1,0:T(8,128)S(1)} collective-permute-done((f32[1,32,288]{2,1,0:T(8,128)S(1)}, f32[1,32,288]{2,1,0:T(8,128)S(1)}, u32[]{:S(2)}, u32[]{:S(2)}) %collective-permute-start.2) | collective-permute-done | bytes 36896 | tf_op jit(solution)/shard_map/ppermute | solution.py:102
  21.5 4.4 %collective-permute-start.3 = (f32[2,32,288]{2,1,0:T(8,128)S(1)}, f32[2,32,288]{2,1,0:T(8,128)S(1)}, u32[]{:S(2)}, u32[]{:S(2)}) collective-permute-start(f32[2,32,288]{2,1,0:T(8,128)S(1)} %maximum_select_fusion.6), channel_id=1, source_target_pairs={{0,8},{2,10},{4,12},{6,14},{8,0},{10,2},{12,4},{14,6},{16,24},{18,... | collective-permute-start | bytes 221192 | tf_op jit(solution)/shard_map/ppermute | solution.py:102
  26.0 0.7 copy.41
  26.8 1.6 %collective-permute-done.3 = f32[2,32,288]{2,1,0:T(8,128)S(1)} collective-permute-done((f32[2,32,288]{2,1,0:T(8,128)S(1)}, f32[2,32,288]{2,1,0:T(8,128)S(1)}, u32[]{:S(2)}, u32[]{:S(2)}) %collective-permute-start.3) | collective-permute-done | bytes 73760 | tf_op jit(solution)/shard_map/ppermute | solution.py:102
  28.5 4.6 %collective-permute-start.4 = (f32[4,32,288]{2,1,0:T(8,128)S(1)}, f32[4,32,288]{2,1,0:T(8,128)}, u32[]{:S(2)}, u32[]{:S(2)}) collective-permute-start(f32[4,32,288]{2,1,0:T(8,128)S(1)} %maximum_select_fusion.4), channel_id=1, source_target_pairs={{0,4},{2,6},{4,0},{6,2},{8,12},{10,14},{12,8},{14,10},{16,20},{18,... | collective-permute-start | bytes 442376 | tf_op jit(solution)/shard_map/ppermute | solution.py:102
  33.6 0.7 gather_fusion.1
  34.3 0.6 gather_fusion
  35.2 0.6 gather_fusion.5
  35.8 1.5 %convolution_bitcast_fusion.4 = f32[2,32,128]{2,1,0:T(8,128)} fusion(f32[2,96,128]{2,1,0:T(8,128)S(1)} %bitcast.287, bf16[1,31,32,96]{3,2,1,0:T(8,128)(2,1)} %param.25), kind=kOutput, calls=%fused_computation.18 | convolution fusion | flops 9437184 | bytes 147456 | tf_op jit(solution)/shard_map/cra,cav->crv/dot_general | solution.py:237
  37.3 1.2 %gather_fusion.4 = f32[12,32,128]{2,1,0:T(8,128)} fusion(f32[8,32,128]{2,1,0:T(8,128)S(1)} %pad_maximum_fusion.8, s32[1024]{0:T(1024)S(1)} %get-tuple-element.94), kind=kCustom, calls=%fused_computation.6 | custom fusion | bytes 393264 | tf_op jit(solution)/shard_map/gather | solution.py:233
  38.5 1.3 %gather_fusion.3 = f32[24,32,128]{2,1,0:T(8,128)} fusion(f32[12,32,128]{2,1,0:T(8,128)S(1)} %pad_maximum_fusion.6, s32[1024]{0:T(1024)S(1)} %get-tuple-element.95), kind=kCustom, calls=%fused_computation.5 | custom fusion | bytes 786528 | tf_op jit(solution)/shard_map/gather | solution.py:233
  39.9 0.6 gather_fusion.2
  40.5 0.7 multiply_reduce_fusion
  41.2 1.1 maximum_select_fusion.2
  42.2 3.3 %collective-permute-start.5 = (f32[8,32,288]{2,1,0:T(8,128)S(1)}, f32[8,32,288]{2,1,0:T(8,128)S(1)}, u32[]{:S(2)}, u32[]{:S(2)}) collective-permute-start(f32[8,32,288]{2,1,0:T(8,128)S(1)} %maximum_select_fusion.2), channel_id=1, source_target_pairs={{0,2},{2,0},{4,6},{6,4},{8,10},{10,8},{12,14},{14,12},{16,18},{18,... | collective-permute-start | bytes 884744 | tf_op jit(solution)/shard_map/ppermute | solution.py:102
  45.6 1.8 %fusion.6 = f32[16,64,128,1]{2,1,3,0:T(8,128)} fusion(bf16[16,3,64,128]{3,2,1,0:T(8,128)(2,1)S(1)} %bitcast.277, f32[16,3,64,64]{3,2,1,0:T(8,128)S(1)} %multiply_reduce_fusion, bf16[16,3]{1,0:T(8,128)(2,1)S(1)} %copy.40), kind=kOutput, calls=%fused_computation.31 | convolution fusion | flops 51707904 | bytes 2097248 | tf_op jit(solution)/shard_map/while/body/eval_jaxpr/gkij,gkjv->giv/dot_general | solution.py:39
  47.3 4.6 %collective-permute-done.5 = f32[8,32,288]{2,1,0:T(8,128)S(1)} collective-permute-done((f32[8,32,288]{2,1,0:T(8,128)S(1)}, f32[8,32,288]{2,1,0:T(8,128)S(1)}, u32[]{:S(2)}, u32[]{:S(2)}) %collective-permute-start.5) | collective-permute-done | bytes 294944 | tf_op jit(solution)/shard_map/ppermute | solution.py:102
  52.0 0.6 gather_fusion.6
  52.7 0.3 fusion.13
  53.0 0.2 fusion.27
  53.3 0.2 fusion.78
  53.6 16.9 %collective-permute-start.8 = (f32[1,32,288]{2,1,0:T(8,128)S(1)}, f32[1,32,288]{2,1,0:T(8,128)S(1)}, u32[]{:S(2)}, u32[]{:S(2)}) collective-permute-start(f32[1,32,288]{2,1,0:T(8,128)S(1)} %maximum_bitcast_fusion.1), channel_id=1, source_target_pairs={{0,256},{32,288},{64,320},{96,352},{128,384},{160,416},{192,448},{... | collective-permute-start | bytes 110600 | tf_op jit(solution)/shard_map/ppermute | solution.py:102
  70.8 1.3 %collective-permute-start.7 = (f32[11,32,128]{2,1,0:T(8,128)S(1)}, f32[11,32,128]{2,1,0:T(8,128)S(1)}, u32[]{:S(2)}, u32[]{:S(2)}) collective-permute-start(f32[11,32,128]{2,1,0:T(8,128)S(1)} %get-tuple-element.78), channel_id=1, source_target_pairs={{32,0},{64,32},{96,64},{128,96},{160,128},{192,160},{224,192},{256... | collective-permute-start | bytes 540680 | tf_op jit(solution)/shard_map/ppermute | solution.py:131
  72.1 4.6 %collective-permute-start.6 = (f32[11,32,128]{2,1,0:T(8,128)S(1)}, f32[11,32,128]{2,1,0:T(8,128)S(1)}, u32[]{:S(2)}, u32[]{:S(2)}) collective-permute-start(f32[11,32,128]{2,1,0:T(8,128)S(1)} %get-tuple-element.77), channel_id=1, source_target_pairs={{0,32},{32,64},{64,96},{96,128},{128,160},{160,192},{192,224},{224... | collective-permute-start | bytes 540680 | tf_op jit(solution)/shard_map/ppermute | solution.py:130
  76.7 4.5 %collective-permute-start.9 = (f32[2,32,288]{2,1,0:T(8,128)S(1)}, f32[2,32,288]{2,1,0:T(8,128)S(1)}, u32[]{:S(2)}, u32[]{:S(2)}) collective-permute-start(f32[2,32,288]{2,1,0:T(8,128)S(1)} %maximum_select_fusion.7), channel_id=1, source_target_pairs={{0,128},{32,160},{64,192},{96,224},{128,0},{160,32},{192,64},{224,... | collective-permute-start | bytes 221192 | tf_op jit(solution)/shard_map/ppermute | solution.py:102
  81.2 0.6 dynamic-slice_bitcast_fusion.14
  81.9 8.4 %collective-permute-done.9 = f32[2,32,288]{2,1,0:T(8,128)S(1)} collective-permute-done((f32[2,32,288]{2,1,0:T(8,128)S(1)}, f32[2,32,288]{2,1,0:T(8,128)S(1)}, u32[]{:S(2)}, u32[]{:S(2)}) %collective-permute-start.9) | collective-permute-done | bytes 73760 | tf_op jit(solution)/shard_map/ppermute | solution.py:102
  90.3 1.9 %collective-permute-start.10 = (f32[4,32,288]{2,1,0:T(8,128)S(1)}, f32[4,32,288]{2,1,0:T(8,128)S(1)}, u32[]{:S(2)}, u32[]{:S(2)}) collective-permute-start(f32[4,32,288]{2,1,0:T(8,128)S(1)} %maximum_select_fusion.5), channel_id=1, source_target_pairs={{0,64},{32,96},{64,0},{96,32},{128,192},{160,224},{192,128},{224,1... | collective-permute-start | bytes 442376 | tf_op jit(solution)/shard_map/ppermute | solution.py:102
  92.6 0.8 fusion.43
  93.4 6.2 %collective-permute-done.10 = f32[4,32,288]{2,1,0:T(8,128)S(1)} collective-permute-done((f32[4,32,288]{2,1,0:T(8,128)S(1)}, f32[4,32,288]{2,1,0:T(8,128)S(1)}, u32[]{:S(2)}, u32[]{:S(2)}) %collective-permute-start.10) | collective-permute-done | bytes 147488 | tf_op jit(solution)/shard_map/ppermute | solution.py:102
  99.7 1.9 %collective-permute-start.11 = (f32[8,32,288]{2,1,0:T(8,128)S(1)}, f32[8,32,288]{2,1,0:T(8,128)S(1)}, u32[]{:S(2)}, u32[]{:S(2)}) collective-permute-start(f32[8,32,288]{2,1,0:T(8,128)S(1)} %maximum_select_fusion.3), channel_id=1, source_target_pairs={{0,32},{32,0},{64,96},{96,64},{128,160},{160,128},{192,224},{224,1... | collective-permute-start | bytes 884744 | tf_op jit(solution)/shard_map/ppermute | solution.py:102
  101.6 0.8 fusion.49
  102.4 1.4 %convolution_bitcast_fusion.5 = f32[32,128]{1,0:T(8,128)} fusion(f32[32,128]{1,0:T(8,128)S(1)} %get-tuple-element.26, f32[32,128]{1,0:T(8,128)S(1)} %get-tuple-element.28, f32[32,128]{1,0:T(8,128)S(1)} %get-tuple-element.24, bf16[1,31,32,96]{3,2,1,0:T(8,128)(2,1)} %param.25), kind=kOutput, calls=%fused_computation.26 | convolution fusion | flops 4743168 | bytes 73728 | tf_op jit(solution)/shard_map/dot_general | solution.py:63
  103.8 7.0 %collective-permute-done.11 = f32[8,32,288]{2,1,0:T(8,128)S(1)} collective-permute-done((f32[8,32,288]{2,1,0:T(8,128)S(1)}, f32[8,32,288]{2,1,0:T(8,128)S(1)}, u32[]{:S(2)}, u32[]{:S(2)}) %collective-permute-start.11) | collective-permute-done | bytes 294944 | tf_op jit(solution)/shard_map/ppermute | solution.py:102
  110.9 0.7 gather_fusion.7
  112.0 0.4 fusion.11
  112.3 0.2 fusion.25
  112.6 0.2 fusion.55
  113.0 0.2 fusion.67
  113.2 0.3 convolution_add_fusion.5
  113.5 0.3 convolution_add_fusion.4
  113.8 0.3 convolution_add_fusion.3
  114.1 0.3 convolution_add_fusion.2
  114.4 0.3 convolution_add_fusion.1
  114.7 0.3 fusion.4
  115.2 0.2 fusion.104
  115.4 0.2 fusion.2
  115.7 0.3 fusion.74
  115.9 0.3 fusion.1
  116.2 0.3 fusion.21
  116.6 0.5 fusion
  117.0 0.4 fusion.16
  117.5 0.8 fusion.8
  (138 shorter events, 3.2 us)
Async XLA Ops:
  0.0 5.0 %copy-start.4 = (bf16[1,15,32,64]{3,2,1,0:T(8,128)(2,1)S(1)}, bf16[1,15,32,64]{3,2,1,0:T(8,128)(2,1)}, u32[]{:S(2)}) copy-start(bf16[1,15,32,64]{3,2,1,0:T(8,128)(2,1)} %param.24) | copy-start | bytes 184324
  0.0 13.9 %copy-start.19 = (bf16[1,32,96]{2,1,0:T(8,128)(2,1)S(1)}, bf16[1,32,96]{2,1,0:T(8,128)(2,1)}, u32[]{:S(2)}) copy-start(bf16[1,32,96]{2,1,0:T(8,128)(2,1)} %param.27) | copy-start | bytes 18436
  0.0 13.9 %copy-start.20 = (bf16[1,32,64]{2,1,0:T(8,128)(2,1)S(1)}, bf16[1,32,64]{2,1,0:T(8,128)(2,1)}, u32[]{:S(2)}) copy-start(bf16[1,32,64]{2,1,0:T(8,128)(2,1)} %param.26) | copy-start | bytes 12292
  1.6 18.1 %copy-start.18 = (s32[16,3]{0,1:T(4,128)S(1)}, s32[16,3]{0,1:T(4,128)}, u32[]{:S(2)}) copy-start(s32[16,3]{0,1:T(4,128)} %param.22) | copy-start | bytes 580
  1.6 18.1 %copy-start.25 = (s32[6]{0:T(128)S(1)}, s32[6]{0:T(128)}, u32[]{:S(2)}) copy-start(s32[6]{0:T(128)} %constant.292) | copy-start | bytes 76
  1.6 18.1 %copy-start.26 = (s32[12]{0:T(128)S(1)}, s32[12]{0:T(128)}, u32[]{:S(2)}) copy-start(s32[12]{0:T(128)} %constant.291) | copy-start | bytes 148
  2.7 17.1 %copy-start.23 = (s32[24]{0:T(128)S(1)}, s32[24]{0:T(128)}, u32[]{:S(2)}) copy-start(s32[24]{0:T(128)} %constant.290) | copy-start | bytes 292
  2.7 17.1 %copy-start.24 = (s32[48]{0:T(128)S(1)}, s32[48]{0:T(128)}, u32[]{:S(2)}) copy-start(s32[48]{0:T(128)} %constant.289) | copy-start | bytes 580
  2.7 17.1 %copy-start.22 = (s32[16]{0:T(128)S(1)}, s32[16]{0:T(128)}, u32[]{:S(2)}) copy-start(s32[16]{0:T(128)} %constant.295) | copy-start | bytes 196
  5.0 28.3 %copy-start.17 = (f32[3,1024]{1,0:T(4,128)S(1)}, f32[3,1024]{1,0:T(4,128)}, u32[]{:S(2)}) copy-start(f32[3,1024]{1,0:T(4,128)} %param.21) | copy-start | bytes 36868
  5.0 28.6 %copy-start = (bf16[1024,128]{1,0:T(8,128)(2,1)S(1)}, bf16[1024,128]{1,0:T(8,128)(2,1)}, u32[]{:S(2)}) copy-start(bf16[1024,128]{1,0:T(8,128)(2,1)} %param.20) | copy-start | bytes 786436
  5.5 27.7 %collective-permute-start.1 = (f32[41152]{0:T(1024)S(1)}, f32[41152]{0:T(1024)S(1)}, u32[]{:S(2)}, u32[]{:S(2)}) collective-permute-start(f32[41152]{0:T(1024)S(1)} %concatenate.121), channel_id=1, source_target_pairs={{2,0},{4,2},{6,4},{8,6},{10,8},{12,10},{14,12},{16,14},{18,16},{20... | collective-permute-start | bytes 493832 | tf_op jit(solution)/shard_map/ppermute | solution.py:211
  8.5 24.6 %collective-permute-start = (f32[41152]{0:T(1024)S(1)}, f32[41152]{0:T(1024)S(1)}, u32[]{:S(2)}, u32[]{:S(2)}) collective-permute-start(f32[41152]{0:T(1024)S(1)} %concatenate.120), channel_id=1, source_target_pairs={{0,2},{2,4},{4,6},{6,8},{8,10},{10,12},{12,14},{14,16},{16,18},{18... | collective-permute-start | bytes 493832 | tf_op jit(solution)/shard_map/ppermute | solution.py:210
  14.0 7.5 %collective-permute-start.2 = (f32[1,32,288]{2,1,0:T(8,128)S(1)}, f32[1,32,288]{2,1,0:T(8,128)S(1)}, u32[]{:S(2)}, u32[]{:S(2)}) collective-permute-start(f32[1,32,288]{2,1,0:T(8,128)S(1)} %maximum_bitcast_fusion), channel_id=1, source_target_pairs={{0,16},{2,18},{4,20},{6,22},{8,24},{10,26},{12,28},{14,30},{16,0},... | collective-permute-start | bytes 110600 | tf_op jit(solution)/shard_map/ppermute | solution.py:102
  19.8 32.2 %copy-start.21 = (s32[1024]{0:T(1024)}, s32[1024]{0:T(1024)S(1)}, u32[]{:S(2)}) copy-start(s32[1024]{0:T(1024)S(1)} %pad_clamp_fusion) | copy-start | bytes 12292
  21.5 7.0 %collective-permute-start.3 = (f32[2,32,288]{2,1,0:T(8,128)S(1)}, f32[2,32,288]{2,1,0:T(8,128)S(1)}, u32[]{:S(2)}, u32[]{:S(2)}) collective-permute-start(f32[2,32,288]{2,1,0:T(8,128)S(1)} %maximum_select_fusion.6), channel_id=1, source_target_pairs={{0,8},{2,10},{4,12},{6,14},{8,0},{10,2},{12,4},{14,6},{16,24},{18,... | collective-permute-start | bytes 221192 | tf_op jit(solution)/shard_map/ppermute | solution.py:102
  28.5 12.7 %collective-permute-start.4 = (f32[4,32,288]{2,1,0:T(8,128)S(1)}, f32[4,32,288]{2,1,0:T(8,128)}, u32[]{:S(2)}, u32[]{:S(2)}) collective-permute-start(f32[4,32,288]{2,1,0:T(8,128)S(1)} %maximum_select_fusion.4), channel_id=1, source_target_pairs={{0,4},{2,6},{4,0},{6,2},{8,12},{10,14},{12,8},{14,10},{16,20},{18,... | collective-permute-start | bytes 442376 | tf_op jit(solution)/shard_map/ppermute | solution.py:102
  42.2 9.7 %collective-permute-start.5 = (f32[8,32,288]{2,1,0:T(8,128)S(1)}, f32[8,32,288]{2,1,0:T(8,128)S(1)}, u32[]{:S(2)}, u32[]{:S(2)}) collective-permute-start(f32[8,32,288]{2,1,0:T(8,128)S(1)} %maximum_select_fusion.2), channel_id=1, source_target_pairs={{0,2},{2,0},{4,6},{6,4},{8,10},{10,8},{12,14},{14,12},{16,18},{18,... | collective-permute-start | bytes 884744 | tf_op jit(solution)/shard_map/ppermute | solution.py:102
  53.0 39.2 %copy-start.16 = (f32[8,32,128]{2,1,0:T(8,128)S(1)}, f32[8,32,128]{2,1,0:T(8,128)}, u32[]{:S(2)}) copy-start(f32[8,32,128]{2,1,0:T(8,128)} %constant_dynamic-update-slice_fusion.2) | copy-start | bytes 393220
  53.6 23.0 %collective-permute-start.8 = (f32[1,32,288]{2,1,0:T(8,128)S(1)}, f32[1,32,288]{2,1,0:T(8,128)S(1)}, u32[]{:S(2)}, u32[]{:S(2)}) collective-permute-start(f32[1,32,288]{2,1,0:T(8,128)S(1)} %maximum_bitcast_fusion.1), channel_id=1, source_target_pairs={{0,256},{32,288},{64,320},{96,352},{128,384},{160,416},{192,448},{... | collective-permute-start | bytes 110600 | tf_op jit(solution)/shard_map/ppermute | solution.py:102
  70.8 21.5 %collective-permute-start.7 = (f32[11,32,128]{2,1,0:T(8,128)S(1)}, f32[11,32,128]{2,1,0:T(8,128)S(1)}, u32[]{:S(2)}, u32[]{:S(2)}) collective-permute-start(f32[11,32,128]{2,1,0:T(8,128)S(1)} %get-tuple-element.78), channel_id=1, source_target_pairs={{32,0},{64,32},{96,64},{128,96},{160,128},{192,160},{224,192},{256... | collective-permute-start | bytes 540680 | tf_op jit(solution)/shard_map/ppermute | solution.py:131
  72.1 20.1 %collective-permute-start.6 = (f32[11,32,128]{2,1,0:T(8,128)S(1)}, f32[11,32,128]{2,1,0:T(8,128)S(1)}, u32[]{:S(2)}, u32[]{:S(2)}) collective-permute-start(f32[11,32,128]{2,1,0:T(8,128)S(1)} %get-tuple-element.77), channel_id=1, source_target_pairs={{0,32},{32,64},{64,96},{96,128},{128,160},{160,192},{192,224},{224... | collective-permute-start | bytes 540680 | tf_op jit(solution)/shard_map/ppermute | solution.py:130
  76.7 13.6 %collective-permute-start.9 = (f32[2,32,288]{2,1,0:T(8,128)S(1)}, f32[2,32,288]{2,1,0:T(8,128)S(1)}, u32[]{:S(2)}, u32[]{:S(2)}) collective-permute-start(f32[2,32,288]{2,1,0:T(8,128)S(1)} %maximum_select_fusion.7), channel_id=1, source_target_pairs={{0,128},{32,160},{64,192},{96,224},{128,0},{160,32},{192,64},{224,... | collective-permute-start | bytes 221192 | tf_op jit(solution)/shard_map/ppermute | solution.py:102
  90.3 9.4 %collective-permute-start.10 = (f32[4,32,288]{2,1,0:T(8,128)S(1)}, f32[4,32,288]{2,1,0:T(8,128)S(1)}, u32[]{:S(2)}, u32[]{:S(2)}) collective-permute-start(f32[4,32,288]{2,1,0:T(8,128)S(1)} %maximum_select_fusion.5), channel_id=1, source_target_pairs={{0,64},{32,96},{64,0},{96,32},{128,192},{160,224},{192,128},{224,1... | collective-permute-start | bytes 442376 | tf_op jit(solution)/shard_map/ppermute | solution.py:102
  99.7 11.2 %collective-permute-start.11 = (f32[8,32,288]{2,1,0:T(8,128)S(1)}, f32[8,32,288]{2,1,0:T(8,128)S(1)}, u32[]{:S(2)}, u32[]{:S(2)}) collective-permute-start(f32[8,32,288]{2,1,0:T(8,128)S(1)} %maximum_select_fusion.3), channel_id=1, source_target_pairs={{0,32},{32,0},{64,96},{96,64},{128,160},{160,128},{192,224},{224,1... | collective-permute-start | bytes 884744 | tf_op jit(solution)/shard_map/ppermute | solution.py:102
  111.7 2.1 %copy-start.9 = (f32[32,128]{1,0:T(8,128)S(1)}, f32[32,128]{1,0:T(8,128)}, u32[]{:S(2)}) copy-start(f32[32,128]{1,0:T(8,128)} %fusion.49) | copy-start | bytes 49156
  111.7 2.1 %copy-start.15 = (f32[32,64]{1,0:T(8,128)S(1)}, f32[32,64]{1,0:T(8,128)}, u32[]{:S(2)}) copy-start(f32[32,64]{1,0:T(8,128)} %get-tuple-element.30) | copy-start | bytes 24580
  111.7 2.4 %copy-start.8 = (f32[32,128]{1,0:T(8,128)S(1)}, f32[32,128]{1,0:T(8,128)}, u32[]{:S(2)}) copy-start(f32[32,128]{1,0:T(8,128)} %fusion.43) | copy-start | bytes 49156
  111.7 2.4 %copy-start.14 = (f32[32,64]{1,0:T(8,128)S(1)}, f32[32,64]{1,0:T(8,128)}, u32[]{:S(2)}) copy-start(f32[32,64]{1,0:T(8,128)} %get-tuple-element.31) | copy-start | bytes 24580
  111.7 2.7 %copy-start.13 = (f32[32,64]{1,0:T(8,128)S(1)}, f32[32,64]{1,0:T(8,128)}, u32[]{:S(2)}) copy-start(f32[32,64]{1,0:T(8,128)} %get-tuple-element.32) | copy-start | bytes 24580
  111.7 3.0 %copy-start.11 = (f32[32,128]{1,0:T(8,128)S(1)}, f32[32,128]{1,0:T(8,128)}, u32[]{:S(2)}) copy-start(f32[32,128]{1,0:T(8,128)} %convolution_bitcast_fusion.5) | copy-start | bytes 49156
  111.7 3.0 %copy-start.12 = (f32[32,64]{1,0:T(8,128)S(1)}, f32[32,64]{1,0:T(8,128)}, u32[]{:S(2)}) copy-start(f32[32,64]{1,0:T(8,128)} %get-tuple-element.29) | copy-start | bytes 24580
  111.7 3.3 %copy-start.7 = (f32[2,32,128]{2,1,0:T(8,128)S(1)}, f32[2,32,128]{2,1,0:T(8,128)}, u32[]{:S(2)}) copy-start(f32[2,32,128]{2,1,0:T(8,128)} %convolution_bitcast_fusion.4) | copy-start | bytes 98308
  111.7 3.3 %copy-start.10 = (bf16[64,32]{1,0:T(8,128)(2,1)S(1)}, bf16[64,32]{1,0:T(8,128)(2,1)}, u32[]{:S(2)}) copy-start(bf16[64,32]{1,0:T(8,128)(2,1)} %copy.41) | copy-start | bytes 12292
  111.7 3.4 %copy-start.5 = (bf16[1,15,32,64]{3,2,1,0:T(8,128)(2,1)S(1)}, bf16[1,15,32,64]{3,2,1,0:T(8,128)(2,1)}, u32[]{:S(2)}) copy-start(bf16[1,15,32,64]{3,2,1,0:T(8,128)(2,1)} %param.24) | copy-start | bytes 184324
  111.8 3.7 %copy-start.2 = (f32[12,32,128]{2,1,0:T(8,128)S(1)}, f32[12,32,128]{2,1,0:T(8,128)}, u32[]{:S(2)}) copy-start(f32[12,32,128]{2,1,0:T(8,128)} %gather_fusion.4) | copy-start | bytes 589828
  111.8 3.7 %copy-start.6 = (bf16[1,31,32,96]{3,2,1,0:T(8,128)(2,1)S(1)}, bf16[1,31,32,96]{3,2,1,0:T(8,128)(2,1)}, u32[]{:S(2)}) copy-start(bf16[1,31,32,96]{3,2,1,0:T(8,128)(2,1)} %param.25) | copy-start | bytes 571396
  111.9 4.0 %copy-start.1 = (f32[24,32,128]{2,1,0:T(8,128)S(1)}, f32[24,32,128]{2,1,0:T(8,128)}, u32[]{:S(2)}) copy-start(f32[24,32,128]{2,1,0:T(8,128)} %gather_fusion.3) | copy-start | bytes 1179652
  116.2 1.2 %copy-start.3 = (f32[16,64,128,1]{2,1,3,0:T(8,128)S(1)}, f32[16,64,128,1]{2,1,3,0:T(8,128)}, u32[]{:S(2)}) copy-start(f32[16,64,128,1]{2,1,3,0:T(8,128)} %fusion.6) | copy-start | bytes 1572868

commit v7 on v6

--- a/solution.py
+++ b/solution.py
@@ -91,6 +91,12 @@
 def rims(own, left_tail, right_head):
     zeros = jnp.zeros((3 - left_tail.shape[0],) + own.shape[1:], own.dtype)
     return jnp.concatenate([zeros, left_tail, own, right_head, zeros], 0)
+
+
+def spread_gather(block, axis):
+    count = lax.axis_size(axis)
+    copies = jnp.broadcast_to(block[None], (count,) + block.shape)
+    return lax.all_to_all(copies, axis, 0, 0, tiled=True)
 
 
 def doubling_gather(block, axis):
@@ -119,7 +125,7 @@
     seat = lax.axis_index(PLANE)
     matrices = as_float(jnp.concatenate([upper_transfer[0], upper_coupling[0]], 1))
     columns = device_coef.shape[1]
-    plane_held = doubling_gather(jnp.concatenate([device_coef, matrices], 1), PLANE)
+    plane_held = spread_gather(jnp.concatenate([device_coef, matrices], 1), PLANE)
     plane_lift = plane_held[:, :, columns : columns + 2 * RANK]
     plane_mix = plane_held[:, :, columns + 2 * RANK :]
     inner = [plane_held[:, :, :columns]]
@@ -129,7 +135,7 @@
     heads = jnp.concatenate([level[:3] for level in inner[:plane_bits]], 0)
     from_left = lax.ppermute(tails, "z", [(i, i + 1) for i in range(planes - 1)])
     from_right = lax.ppermute(heads, "z", [(i + 1, i) for i in range(planes - 1)])
-    outer_held = doubling_gather(
+    outer_held = spread_gather(
         jnp.concatenate([inner[plane_bits][0], plane_held[0, :, columns:]], 1), "z"
     )
     summary = outer_held[:, :, :columns]

time: 119 us -> 107 us (0.90); the launches traced: 118 us -> 105 us
  starting transfers between devices: 56.6 us -> 39.2 us
  local copies, waits for them, and re-layouts: 12.1 us -> 18.4 us
  waiting for transfers between devices: 29.3 us -> 26.8 us
    ppermute x8 -> x0, starting transfers between devices: 42.8 us -> none  [doubling_gather(): lax.ppermute(gathered, axis, [(i, i ^ step) for i in range(count)])]
    ppermute x8 -> x0, waiting for transfers between devices: 29.3 us -> none  [doubling_gather(): lax.ppermute(gathered, axis, [(i, i ^ step) for i in range(count)])]
    all_to_all x0 -> x2, waiting for transfers between devices: none -> 26.8 us  [spread_gather(): return lax.all_to_all(copies, axis, 0, 0, tiled=True)]
    all_to_all x0 -> x2, starting transfers between devices: none -> 24.7 us  [spread_gather(): return lax.all_to_all(copies, axis, 0, 0, tiled=True)]
    unnamed x58 -> x48, local copies, waits for them, and re-layouts: 0.75 us -> 4.07 us
    broadcast_in_dim x0 -> x2, local copies, waits for them, and re-layouts: none -> 1.94 us  [spread_gather(): copies = jnp.broadcast_to(block[None], (count,) + block.shape)]
    dot_general x1, matrix products: 1.78 us -> 3.17 us  [one_group(): jnp.einsum('gkij,gkjv->giv', blocks, source_leaves[located], preferred_el...]
    gather x2 -> x0, local copies, waits for them, and re-layouts: 1.32 us -> none  [doubling_gather(): return jnp.take(gathered, np.array(order), axis=0)]
  transfers between devices with their start and end apart: 12 -> 6, of which waited for: 6 -> 1; matrix products, arithmetic and copies ran while one was open for 13% -> 23% of each run, Pallas kernels for 0% -> 0%
where the time goes in v7:
time: 107 us; the launch traced here: 105 us
  starting transfers between devices  39.2 us (37%)
  waiting for transfers between devices  26.8 us (25%)
  local copies, waits for them, and re-layouts  18.4 us (17%)
  matrix products  14.7 us (14%)
  other arithmetic  4.49 us (4%)
  between operations  1.08 us (1%)
    all_to_all x2, waiting for transfers between devices, spread_gather(): return lax.all_to_all(copies, axis, 0, 0, tiled=True)  26.8 us
    all_to_all x2, starting transfers between devices, spread_gather(): return lax.all_to_all(copies, axis, 0, 0, tiled=True)  24.7 us
    ppermute x1, starting transfers between devices, upper_tree(): lax.ppermute(tails, 'z', [(i, i + 1) for i in range(planes - 1)])  5.23 us
    ppermute x1, starting transfers between devices, local(): lax.ppermute(tail, SPACE, [(i, i + 1) for i in range(count - 1)])  5.22 us
    dot_general x13, matrix products, product(): return jnp.dot(matrix, operand, precision=HIGHEST)  4.12 us
    unnamed x48, local copies, waits for them, and re-layouts  4.07 us
    dot_general x1, matrix products, one_group(): jnp.einsum('gkij,gkjv->giv', blocks, source_leaves[located], preferred_el...  3.17 us
    gather x4, local copies, waits for them, and re-layouts, local(): extended[partner_table(cluster_count) + 2]  2.97 us
  transfers between devices with their start and end apart: 6, of which 1 were waited for; matrix products, arithmetic and copies ran while one was open for 23% of the time, Pallas kernels for 0%

profile of v7, /device:TPU:6, one launch (start us, length us, event | category | flops | bytes accessed | tf_op | source)
XLA Modules:
  0.0 104.7 jit_solution(9953282429528371261)
XLA Ops:
  0.0 0.8 bitcast_convert_fusion.1
  0.8 0.8 fusion.153
  1.6 1.0 reshape.189
  2.7 1.2 %fusion.154 = (bf16[16,32,128]{2,1,0:T(8,128)(2,1)S(1)}, f32[16,32,128]{2,1,0:T(8,128)S(1)}) fusion(bf16[16,64,128]{2,1,0:T(8,128)(2,1)} %bitcast.262, bf16[32,16,64]{2,1,0:T(8,128)(2,1)S(1)} %reshape.189), kind=kOutput, calls=%fused_computation.254 | convolution fusion | flops 8454144 | bytes 720896 | tf_op jit(solution)/shard_map/rlp,lpv->lrv/dot_general | solution.py:196
  3.8 1.1 %bitcast_convert_fusion.3 = (bf16[8,32,128]{2,1,0:T(8,128)(2,1)S(1)}, f32[8,128,32]{1,2,0:T(8,128)S(1)}) fusion(f32[8,64,128]{2,1,0:T(8,128)S(1)} %bitcast.263, bf16[1,15,32,64]{3,2,1,0:T(8,128)(2,1)} %param.20), kind=kOutput, calls=%fused_computation.241 | convolution fusion | flops 25198592 | bytes 524288 | tf_op jit(solution)/shard_map/cra,cav->crv/dot_general | solution.py:203
  4.9 0.2 bitcast_convert_fusion.2
  5.1 0.2 fusion.106
  5.5 2.7 %collective-permute-start.1 = (f32[41152]{0:T(1024)S(1)}, f32[41152]{0:T(1024)S(1)}, u32[]{:S(2)}, u32[]{:S(2)}) collective-permute-start(f32[41152]{0:T(1024)S(1)} %concatenate.73), channel_id=1, source_target_pairs={{2,0},{4,2},{6,4},{8,6},{10,8},{12,10},{14,12},{16,14},{18,16},{20... | collective-permute-start | bytes 493832 | tf_op jit(solution)/shard_map/ppermute | solution.py:217
  8.5 5.2 %collective-permute-start = (f32[41152]{0:T(1024)S(1)}, f32[41152]{0:T(1024)S(1)}, u32[]{:S(2)}, u32[]{:S(2)}) collective-permute-start(f32[41152]{0:T(1024)S(1)} %concatenate.72), channel_id=1, source_target_pairs={{0,2},{2,4},{4,6},{6,8},{8,10},{10,12},{12,14},{14,16},{16,18},{18... | collective-permute-start | bytes 493832 | tf_op jit(solution)/shard_map/ppermute | solution.py:216
  13.7 0.1 convolution_bitcast_fusion.6
  14.0 1.0 broadcast_in_dim.50
  14.9 9.1 %all-to-all-start = ((f32[16,32,288]{2,1,0:T(8,128)}), f32[16,32,288]{2,1,0:T(8,128)S(1)}, u32[]{:S(2)}, u32[]{:S(2)}) async-start(f32[16,32,288]{2,1,0:T(8,128)} %broadcast_in_dim.50), calls=%async_computation | async-start | bytes 1572864 | tf_op jit(solution)/shard_map/all_to_all | solution.py:99
  24.7 0.6 constant_dynamic-update-slice_fusion.2
  25.7 0.6 gather_fusion
  26.7 1.8 %multiply_reduce_fusion = f32[16,3,64,64]{3,2,1,0:T(8,128)} fusion(f32[3,16,3,64]{3,2,1,0:T(4,128)S(1)} %bitcast.281, f32[3,16,64]{2,1,0:T(8,128)S(1)} %dynamic_slice.147), kind=kLoop, calls=%fused_computation.6 | loop fusion | flops 1572864 | bytes 835584 | tf_op jit(solution)/shard_map/while/body/eval_jaxpr/reduce_sum | solution.py:19
  28.6 0.7 gather_fusion.1
  29.3 0.6 gather_fusion.5
  29.9 1.2 %gather_fusion.4 = f32[12,32,128]{2,1,0:T(8,128)} fusion(f32[8,32,128]{2,1,0:T(8,128)S(1)} %pad_maximum_fusion.8, s32[1024]{0:T(1024)S(1)} %get-tuple-element.95), kind=kCustom, calls=%fused_computation.4 | custom fusion | bytes 393264 | tf_op jit(solution)/shard_map/gather | solution.py:239
  31.1 0.6 gather_fusion.3
  31.7 0.6 gather_fusion.2
  32.3 0.9 convolution_bitcast_fusion.4
  33.2 3.2 %fusion.6 = f32[16,64,128,1]{2,1,3,0:T(8,128)} fusion(bf16[16,3,64,128]{3,2,1,0:T(8,128)(2,1)S(1)} %bitcast.273, f32[16,3,64,64]{3,2,1,0:T(8,128)} %multiply_reduce_fusion, bf16[16,3]{1,0:T(8,128)(2,1)S(1)} %copy.38), kind=kOutput, calls=%fused_computation.27 | convolution fusion | flops 51707904 | bytes 2097248 | tf_op jit(solution)/shard_map/while/body/eval_jaxpr/gkij,gkjv->giv/dot_general | solution.py:39
  36.4 0.3 fusion.13
  36.8 0.2 fusion.27
  37.0 0.2 fusion.78
  37.2 0.8 pad_maximum_fusion.4
  38.0 1.3 %collective-permute-start.3 = (f32[11,32,128]{2,1,0:T(8,128)}, f32[11,32,128]{2,1,0:T(8,128)}, u32[]{:S(2)}, u32[]{:S(2)}) collective-permute-start(f32[11,32,128]{2,1,0:T(8,128)} %get-tuple-element.77), channel_id=1, source_target_pairs={{32,0},{64,32},{96,64},{128,96},{160,128},{192,160},{224,192},{256... | collective-permute-start | bytes 540680 | tf_op jit(solution)/shard_map/ppermute | solution.py:137
  39.3 5.2 %collective-permute-start.2 = (f32[11,32,128]{2,1,0:T(8,128)}, f32[11,32,128]{2,1,0:T(8,128)}, u32[]{:S(2)}, u32[]{:S(2)}) collective-permute-start(f32[11,32,128]{2,1,0:T(8,128)} %get-tuple-element.76), channel_id=1, source_target_pairs={{0,32},{32,64},{64,96},{96,128},{128,160},{160,192},{192,224},{224... | collective-permute-start | bytes 540680 | tf_op jit(solution)/shard_map/ppermute | solution.py:136
  44.5 0.1 fusion.93
  44.7 1.0 broadcast_in_dim.52
  45.7 15.6 %all-to-all-start.1 = ((f32[16,32,288]{2,1,0:T(8,128)}), f32[16,32,288]{2,1,0:T(8,128)S(1)}, u32[]{:S(2)}, u32[]{:S(2)}) async-start(f32[16,32,288]{2,1,0:T(8,128)} %broadcast_in_dim.52), calls=%async_computation.1 | async-start | bytes 1572864 | tf_op jit(solution)/shard_map/all_to_all | solution.py:99
  61.4 1.4 %dynamic-slice_bitcast_fusion.14 = (f32[32,64]{1,0:T(8,128)}, f32[32,64]{1,0:T(8,128)}, f32[32,64]{1,0:T(8,128)}, f32[32,64]{1,0:T(8,128)}) fusion(f32[16,32,64]{2,1,0:T(8,128)} %copy-done.1, s32[]{:T(128)S(6)} %select_n.286, s32[]{:T(128)S(6)} %select_n.319, s32[]{:T(128)S(6)} %select_n.308, s32[]{:T(128)S(6)} %select_n.297), kind=kLoop, calls=%fused_computation.196 | loop fusion | bytes 65552 | tf_op jit(solution)/shard_map/jit(dynamic_index_in_dim)/squeeze | solution.py:83
  62.9 1.4 %slice_dynamic-update-slice_fusion.1 = f32[8,32,128]{2,1,0:T(8,128)} fusion(f32[8,32,128]{2,1,0:T(8,128)} %constant_dynamic-update-slice_fusion.2, f32[11,32,128]{2,1,0:T(8,128)} %collective-permute-done.2), kind=kLoop, calls=%fused_computation.121 | loop fusion | bytes 65536
  64.2 0.6 constant_dynamic-update-slice_fusion.1
  64.8 1.4 %slice_dynamic-update-slice_fusion = f32[8,32,128]{2,1,0:T(8,128)} fusion(f32[8,32,128]{2,1,0:T(8,128)} %constant_dynamic-update-slice_fusion.1, f32[11,32,128]{2,1,0:T(8,128)} %collective-permute-done.3), kind=kLoop, calls=%fused_computation.120 | loop fusion | bytes 65536
  66.2 0.6 constant_dynamic-update-slice_fusion
  66.8 0.9 fusion.148
  67.7 0.9 fusion.147
  68.6 0.1 fusion.37
  68.8 0.1 fusion.43
  68.9 0.8 dynamic-slice_bitcast_fusion.5
  69.7 0.1 fusion.49
  69.9 1.5 %convolution_bitcast_fusion.5 = f32[32,128]{1,0:T(8,128)} fusion(f32[32,128]{1,0:T(8,128)S(1)} %get-tuple-element.24, f32[32,128]{1,0:T(8,128)S(1)} %get-tuple-element.26, f32[32,128]{1,0:T(8,128)S(1)} %get-tuple-element.17, bf16[1,31,32,96]{3,2,1,0:T(8,128)(2,1)} %param.21), kind=kOutput, calls=%fused_computation.24 | convolution fusion | flops 4743168 | bytes 73728 | tf_op jit(solution)/shard_map/dot_general | solution.py:63
  71.4 26.8 %all-to-all-done.1 = f32[16,32,288]{2,1,0:T(8,128)S(1)} async-done(((f32[16,32,288]{2,1,0:T(8,128)}), f32[16,32,288]{2,1,0:T(8,128)S(1)}, u32[]{:S(2)}, u32[]{:S(2)}) %all-to-all-start.1) | async-done | bytes 589856 | tf_op jit(solution)/shard_map/all_to_all | solution.py:99
  98.3 0.3 fusion.11
  98.7 0.2 fusion.25
  99.1 0.2 fusion.61
  99.3 0.2 fusion.67
  99.5 0.3 convolution_add_fusion.5
  99.8 0.2 fusion.55
  100.0 0.3 convolution_add_fusion.4
  100.3 0.3 convolution_add_fusion.3
  100.6 0.3 convolution_add_fusion.2
  100.9 0.3 convolution_add_fusion.1
  101.2 0.3 fusion.4
  101.5 0.1 fusion.3
  101.6 0.2 fusion.104
  101.9 0.2 fusion.2
  102.1 0.3 fusion.74
  102.4 0.3 fusion.1
  102.7 0.3 fusion.21
  103.0 0.5 fusion
  103.5 0.4 fusion.16
  103.9 0.8 fusion.8
  (107 shorter events, 2.3 us)
Async XLA Ops:
  0.0 4.9 %copy-start.6 = (bf16[1,15,32,64]{3,2,1,0:T(8,128)(2,1)S(1)}, bf16[1,15,32,64]{3,2,1,0:T(8,128)(2,1)}, u32[]{:S(2)}) copy-start(bf16[1,15,32,64]{3,2,1,0:T(8,128)(2,1)} %param.20) | copy-start | bytes 184324
  0.0 13.9 %copy-start.16 = (bf16[1,32,96]{2,1,0:T(8,128)(2,1)S(1)}, bf16[1,32,96]{2,1,0:T(8,128)(2,1)}, u32[]{:S(2)}) copy-start(bf16[1,32,96]{2,1,0:T(8,128)(2,1)} %param.23) | copy-start | bytes 18436
  0.0 13.9 %copy-start.17 = (bf16[1,32,64]{2,1,0:T(8,128)(2,1)S(1)}, bf16[1,32,64]{2,1,0:T(8,128)(2,1)}, u32[]{:S(2)}) copy-start(bf16[1,32,64]{2,1,0:T(8,128)(2,1)} %param.22) | copy-start | bytes 12292
  2.6 12.3 %copy-start.2 = (bf16[32,16,64]{2,1,0:T(8,128)(2,1)}, bf16[32,16,64]{2,1,0:T(8,128)(2,1)S(1)}, u32[]{:S(2)}) copy-start(bf16[32,16,64]{2,1,0:T(8,128)(2,1)S(1)} %reshape.189) | copy-start | bytes 196612
  5.4 18.7 %copy-start.15 = (s32[16,3]{0,1:T(4,128)S(1)}, s32[16,3]{0,1:T(4,128)}, u32[]{:S(2)}) copy-start(s32[16,3]{0,1:T(4,128)} %param.18) | copy-start | bytes 580
  5.4 18.9 %copy-start.20 = (s32[6]{0:T(128)S(1)}, s32[6]{0:T(128)}, u32[]{:S(2)}) copy-start(s32[6]{0:T(128)} %constant.263) | copy-start | bytes 76
  5.4 18.9 %copy-start.21 = (s32[12]{0:T(128)S(1)}, s32[12]{0:T(128)}, u32[]{:S(2)}) copy-start(s32[12]{0:T(128)} %constant.262) | copy-start | bytes 148
  5.4 18.9 %copy-start.18 = (s32[24]{0:T(128)S(1)}, s32[24]{0:T(128)}, u32[]{:S(2)}) copy-start(s32[24]{0:T(128)} %constant.261) | copy-start | bytes 292
  5.4 18.9 %copy-start.19 = (s32[48]{0:T(128)S(1)}, s32[48]{0:T(128)}, u32[]{:S(2)}) copy-start(s32[48]{0:T(128)} %constant.260) | copy-start | bytes 580
  5.5 19.9 %collective-permute-start.1 = (f32[41152]{0:T(1024)S(1)}, f32[41152]{0:T(1024)S(1)}, u32[]{:S(2)}, u32[]{:S(2)}) collective-permute-start(f32[41152]{0:T(1024)S(1)} %concatenate.73), channel_id=1, source_target_pairs={{2,0},{4,2},{6,4},{8,6},{10,8},{12,10},{14,12},{16,14},{18,16},{20... | collective-permute-start | bytes 493832 | tf_op jit(solution)/shard_map/ppermute | solution.py:217
  8.5 16.8 %collective-permute-start = (f32[41152]{0:T(1024)S(1)}, f32[41152]{0:T(1024)S(1)}, u32[]{:S(2)}, u32[]{:S(2)}) collective-permute-start(f32[41152]{0:T(1024)S(1)} %concatenate.72), channel_id=1, source_target_pairs={{0,2},{2,4},{4,6},{6,8},{8,10},{10,12},{12,14},{14,16},{16,18},{18... | collective-permute-start | bytes 493832 | tf_op jit(solution)/shard_map/ppermute | solution.py:216
  14.0 11.5 %copy-start.14 = (f32[3,1024]{1,0:T(4,128)S(1)}, f32[3,1024]{1,0:T(4,128)}, u32[]{:S(2)}) copy-start(f32[3,1024]{1,0:T(4,128)} %param.17) | copy-start | bytes 36868
  14.9 21.4 %all-to-all-start = ((f32[16,32,288]{2,1,0:T(8,128)}), f32[16,32,288]{2,1,0:T(8,128)S(1)}, u32[]{:S(2)}, u32[]{:S(2)}) async-start(f32[16,32,288]{2,1,0:T(8,128)} %broadcast_in_dim.50), calls=%async_computation | async-start | bytes 1572864 | tf_op jit(solution)/shard_map/all_to_all | solution.py:99
  24.0 2.6 %copy-start = (bf16[1024,128]{1,0:T(8,128)(2,1)S(1)}, bf16[1024,128]{1,0:T(8,128)(2,1)}, u32[]{:S(2)}) copy-start(bf16[1024,128]{1,0:T(8,128)(2,1)} %param.16) | copy-start | bytes 786436
  36.4 9.3 %copy-start.1 = (f32[16,32,64]{2,1,0:T(8,128)}, f32[16,32,64]{2,1,0:T(8,128)S(1)}, u32[]{:S(2)}) copy-start(f32[16,32,64]{2,1,0:T(8,128)S(1)} %slice.404) | copy-start | bytes 393220
  38.0 26.8 %collective-permute-start.3 = (f32[11,32,128]{2,1,0:T(8,128)}, f32[11,32,128]{2,1,0:T(8,128)}, u32[]{:S(2)}, u32[]{:S(2)}) collective-permute-start(f32[11,32,128]{2,1,0:T(8,128)} %get-tuple-element.77), channel_id=1, source_target_pairs={{32,0},{64,32},{96,64},{128,96},{160,128},{192,160},{224,192},{256... | collective-permute-start | bytes 540680 | tf_op jit(solution)/shard_map/ppermute | solution.py:137
  39.3 23.6 %collective-permute-start.2 = (f32[11,32,128]{2,1,0:T(8,128)}, f32[11,32,128]{2,1,0:T(8,128)}, u32[]{:S(2)}, u32[]{:S(2)}) collective-permute-start(f32[11,32,128]{2,1,0:T(8,128)} %get-tuple-element.76), channel_id=1, source_target_pairs={{0,32},{32,64},{64,96},{96,128},{128,160},{160,192},{192,224},{224... | collective-permute-start | bytes 540680 | tf_op jit(solution)/shard_map/ppermute | solution.py:136
  45.7 52.5 %all-to-all-start.1 = ((f32[16,32,288]{2,1,0:T(8,128)}), f32[16,32,288]{2,1,0:T(8,128)S(1)}, u32[]{:S(2)}, u32[]{:S(2)}) async-start(f32[16,32,288]{2,1,0:T(8,128)} %broadcast_in_dim.52), calls=%async_computation.1 | async-start | bytes 1572864 | tf_op jit(solution)/shard_map/all_to_all | solution.py:99
  98.2 2.1 %copy-start.13 = (f32[32,64]{1,0:T(8,128)S(1)}, f32[32,64]{1,0:T(8,128)}, u32[]{:S(2)}) copy-start(f32[32,64]{1,0:T(8,128)} %get-tuple-element.29) | copy-start | bytes 24580
  98.2 2.4 %copy-start.12 = (f32[32,64]{1,0:T(8,128)S(1)}, f32[32,64]{1,0:T(8,128)}, u32[]{:S(2)}) copy-start(f32[32,64]{1,0:T(8,128)} %get-tuple-element.30) | copy-start | bytes 24580
  98.2 2.7 %copy-start.11 = (f32[32,64]{1,0:T(8,128)S(1)}, f32[32,64]{1,0:T(8,128)}, u32[]{:S(2)}) copy-start(f32[32,64]{1,0:T(8,128)} %get-tuple-element.31) | copy-start | bytes 24580
  98.2 2.9 %copy-start.9 = (f32[32,128]{1,0:T(8,128)S(1)}, f32[32,128]{1,0:T(8,128)}, u32[]{:S(2)}) copy-start(f32[32,128]{1,0:T(8,128)} %convolution_bitcast_fusion.5) | copy-start | bytes 49156
  98.2 2.9 %copy-start.10 = (f32[32,64]{1,0:T(8,128)S(1)}, f32[32,64]{1,0:T(8,128)}, u32[]{:S(2)}) copy-start(f32[32,64]{1,0:T(8,128)} %get-tuple-element.28) | copy-start | bytes 24580
  98.2 3.4 %copy-start.7 = (bf16[1,15,32,64]{3,2,1,0:T(8,128)(2,1)S(1)}, bf16[1,15,32,64]{3,2,1,0:T(8,128)(2,1)}, u32[]{:S(2)}) copy-start(bf16[1,15,32,64]{3,2,1,0:T(8,128)(2,1)} %param.20) | copy-start | bytes 184324
  98.3 3.6 %copy-start.4 = (f32[12,32,128]{2,1,0:T(8,128)S(1)}, f32[12,32,128]{2,1,0:T(8,128)}, u32[]{:S(2)}) copy-start(f32[12,32,128]{2,1,0:T(8,128)} %gather_fusion.4) | copy-start | bytes 589828
  98.3 3.6 %copy-start.8 = (bf16[1,31,32,96]{3,2,1,0:T(8,128)(2,1)S(1)}, bf16[1,31,32,96]{3,2,1,0:T(8,128)(2,1)}, u32[]{:S(2)}) copy-start(bf16[1,31,32,96]{3,2,1,0:T(8,128)(2,1)} %param.21) | copy-start | bytes 571396
  101.9 1.6 %copy-start.3 = (bf16[32,16,64]{2,1,0:T(8,128)(2,1)S(1)}, bf16[32,16,64]{2,1,0:T(8,128)(2,1)}, u32[]{:S(2)}) copy-start(bf16[32,16,64]{2,1,0:T(8,128)(2,1)} %copy-done.2) | copy-start | bytes 196612
  102.7 1.2 %copy-start.5 = (f32[16,64,128,1]{2,1,3,0:T(8,128)S(1)}, f32[16,64,128,1]{2,1,3,0:T(8,128)}, u32[]{:S(2)}) copy-start(f32[16,64,128,1]{2,1,3,0:T(8,128)} %fusion.6) | copy-start | bytes 1572868

commit v8 on v7

--- a/solution.py
+++ b/solution.py
@@ -135,9 +135,8 @@
     heads = jnp.concatenate([level[:3] for level in inner[:plane_bits]], 0)
     from_left = lax.ppermute(tails, "z", [(i, i + 1) for i in range(planes - 1)])
     from_right = lax.ppermute(heads, "z", [(i + 1, i) for i in range(planes - 1)])
-    outer_held = spread_gather(
-        jnp.concatenate([inner[plane_bits][0], plane_held[0, :, columns:]], 1), "z"
-    )
+    outer_unit = jnp.concatenate([inner[plane_bits][0], plane_held[0, :, columns:]], 1)
+    outer_held = as_float(spread_gather(outer_unit.astype(jnp.bfloat16), "z"))
     summary = outer_held[:, :, :columns]
     outer_lift = outer_held[:, :, columns : columns + 2 * RANK]
     outer_mix = outer_held[:, :, columns + 2 * RANK :]

time: 107 us -> 96.4 us (0.901)
  the two profiles are of different devices: /device:TPU:6 before, /device:TPU:24 now
where the time goes in v8:
time: 96.4 us; the launch traced here: 95.4 us
  starting transfers between devices  36.6 us (38%)
  waiting for transfers between devices  21.5 us (22%)
  local copies, waits for them, and re-layouts  16.5 us (17%)
  matrix products  16.2 us (17%)
  other arithmetic  3.71 us (4%)
    all_to_all x2, starting transfers between devices, spread_gather(): return lax.all_to_all(copies, axis, 0, 0, tiled=True)  22.9 us
    ppermute x1, waiting for transfers between devices, upper_tree(): lax.ppermute(heads, 'z', [(i + 1, i) for i in range(planes - 1)])  18.5 us
    ppermute x1, starting transfers between devices, local(): lax.ppermute(head, SPACE, [(i + 1, i) for i in range(count - 1)])  4.57 us
    ppermute x1, starting transfers between devices, upper_tree(): lax.ppermute(tails, 'z', [(i, i + 1) for i in range(planes - 1)])  4.48 us
    dot_general x4, matrix products, local(): jnp.einsum('cra,cav->crv', lift_mats, children, precision=HIGHEST)  3.78 us
    gather x4, local copies, waits for them, and re-layouts, local(): extended[partner_table(cluster_count) + 2]  3.61 us
    dot_general x13, matrix products, product(): return jnp.dot(matrix, operand, precision=HIGHEST)  3.48 us
    ppermute x1, starting transfers between devices, local(): lax.ppermute(tail, SPACE, [(i, i + 1) for i in range(count - 1)])  3.38 us
  transfers between devices with their start and end apart: 6, of which 2 were waited for; matrix products, arithmetic and copies ran while one was open for 23% of the time, Pallas kernels for 0%

profile of v8, /device:TPU:24, one launch (start us, length us, event | category | flops | bytes accessed | tf_op | source)
XLA Modules:
  0.0 95.4 jit_solution(474872611201286430)
XLA Ops:
  0.0 1.0 %reshape.204 = bf16[32,16,64]{2,1,0:T(8,128)(2,1)S(1)} reshape(bf16[32,1024]{1,0:T(8,128)(2,1)} %param.19) | data formatting | bytes 131072 | tf_op jit(solution)/shard_map/reshape | solution.py:192
  1.0 1.1 %fusion.154 = (bf16[16,32,128]{2,1,0:T(8,128)(2,1)S(1)}, f32[16,32,128]{2,1,0:T(8,128)S(1)}) fusion(bf16[16,64,128]{2,1,0:T(8,128)(2,1)} %bitcast.262, bf16[32,16,64]{2,1,0:T(8,128)(2,1)S(1)} %reshape.204), kind=kOutput, calls=%fused_computation.255 | convolution fusion | flops 8454144 | bytes 720896 | tf_op jit(solution)/shard_map/rlp,lpv->lrv/dot_general | solution.py:195
  2.2 1.1 %bitcast_convert_fusion.3 = (bf16[8,32,128]{2,1,0:T(8,128)(2,1)S(1)}, f32[8,128,32]{1,2,0:T(8,128)S(1)}) fusion(f32[8,64,128]{2,1,0:T(8,128)S(1)} %bitcast.263, bf16[1,15,32,64]{3,2,1,0:T(8,128)(2,1)} %param.20), kind=kOutput, calls=%fused_computation.242 | convolution fusion | flops 25198592 | bytes 524288 | tf_op jit(solution)/shard_map/cra,cav->crv/dot_general | solution.py:202
  3.3 1.0 %bitcast_convert_fusion.2 = (bf16[4,32,128]{2,1,0:T(8,128)(2,1)S(1)}, f32[4,128,32]{1,2,0:T(8,128)S(1)}) fusion(f32[4,64,128]{2,1,0:T(8,128)S(1)} %bitcast.269, bf16[1,15,32,64]{3,2,1,0:T(8,128)(2,1)} %param.20), kind=kOutput, calls=%fused_computation.241 | convolution fusion | flops 12599296 | bytes 262144 | tf_op jit(solution)/shard_map/cra,cav->crv/dot_general | solution.py:202
  4.3 0.9 fusion.104
  5.2 0.8 convolution_bitcast_fusion.6
  6.1 1.0 %broadcast_in_dim.50 = f32[16,32,288]{2,1,0:T(8,128)} broadcast(f32[32,288]{1,0:T(8,128)S(1)} %pad_maximum_fusion.12), dimensions={1,2} | broadcast | bytes 626688 | tf_op jit(solution)/shard_map/broadcast_in_dim | solution.py:98
  7.1 9.2 %all-to-all-start = ((f32[16,32,288]{2,1,0:T(8,128)}), f32[16,32,288]{2,1,0:T(8,128)S(1)}, u32[]{:S(2)}, u32[]{:S(2)}) async-start(f32[16,32,288]{2,1,0:T(8,128)} %broadcast_in_dim.50), calls=%async_computation | async-start | bytes 1572864 | tf_op jit(solution)/shard_map/all_to_all | solution.py:99
  16.6 0.1 concatenate.79
  16.7 3.4 %collective-permute-start = (f32[41152]{0:T(1024)S(1)}, f32[41152]{0:T(1024)S(1)}, u32[]{:S(2)}, u32[]{:S(2)}) collective-permute-start(f32[41152]{0:T(1024)S(1)} %concatenate.79), channel_id=1, source_target_pairs={{0,2},{2,4},{4,6},{6,8},{8,10},{10,12},{12,14},{14,16},{16,18},{18... | collective-permute-start | bytes 493832 | tf_op jit(solution)/shard_map/ppermute | solution.py:215
  20.3 4.6 %collective-permute-start.1 = (f32[41152]{0:T(1024)S(1)}, f32[41152]{0:T(1024)S(1)}, u32[]{:S(2)}, u32[]{:S(2)}) collective-permute-start(f32[41152]{0:T(1024)S(1)} %concatenate.80), channel_id=1, source_target_pairs={{2,0},{4,2},{6,4},{8,6},{10,8},{12,10},{14,12},{16,14},{18,16},{20... | collective-permute-start | bytes 493832 | tf_op jit(solution)/shard_map/ppermute | solution.py:216
  24.9 0.7 slice_bitcast_fusion.10
  26.2 0.6 constant_dynamic-update-slice_fusion.2
  26.8 2.9 %collective-permute-done = f32[41152]{0:T(1024)S(1)} collective-permute-done((f32[41152]{0:T(1024)S(1)}, f32[41152]{0:T(1024)S(1)}, u32[]{:S(2)}, u32[]{:S(2)}) %collective-permute-start) | collective-permute-done | bytes 164640 | tf_op jit(solution)/shard_map/ppermute | solution.py:215
  30.1 0.6 gather_fusion
  31.0 1.8 %multiply_reduce_fusion = f32[16,3,64,64]{3,2,1,0:T(8,128)} fusion(f32[3,16,3,64]{3,2,1,0:T(4,128)S(1)} %bitcast.281, f32[3,16,64]{2,1,0:T(8,128)S(1)} %dynamic_slice.147), kind=kLoop, calls=%fused_computation.6 | loop fusion | flops 1572864 | bytes 835584 | tf_op jit(solution)/shard_map/while/body/eval_jaxpr/reduce_sum | solution.py:19
  33.0 0.7 gather_fusion.1
  33.7 1.2 %gather_fusion.5 = f32[6,32,128]{2,1,0:T(8,128)} fusion(f32[6,32,128]{2,1,0:T(8,128)S(1)} %pad_maximum_fusion.9, s32[1024]{0:T(1024)S(1)} %get-tuple-element.94), kind=kCustom, calls=%fused_computation.5 | custom fusion | bytes 196632 | tf_op jit(solution)/shard_map/gather | solution.py:238
  34.9 1.2 %gather_fusion.4 = f32[12,32,128]{2,1,0:T(8,128)} fusion(f32[8,32,128]{2,1,0:T(8,128)S(1)} %pad_maximum_fusion.8, s32[1024]{0:T(1024)S(1)} %get-tuple-element.95), kind=kCustom, calls=%fused_computation.4 | custom fusion | bytes 393264 | tf_op jit(solution)/shard_map/gather | solution.py:238
  36.1 0.6 gather_fusion.3
  36.7 0.6 gather_fusion.2
  37.3 1.1 %convolution_bitcast_fusion.4 = f32[2,32,128]{2,1,0:T(8,128)S(1)} fusion(f32[2,96,128]{2,1,0:T(8,128)} %bitcast.282, bf16[1,31,32,96]{3,2,1,0:T(8,128)(2,1)} %param.21), kind=kOutput, calls=%fused_computation.16 | convolution fusion | flops 9437184 | bytes 147456 | tf_op jit(solution)/shard_map/cra,cav->crv/dot_general | solution.py:242
  38.4 3.2 %fusion.6 = f32[16,64,128,1]{2,1,3,0:T(8,128)} fusion(bf16[16,3,64,128]{3,2,1,0:T(8,128)(2,1)S(1)} %bitcast.272, f32[16,3,64,64]{3,2,1,0:T(8,128)} %multiply_reduce_fusion, bf16[16,3]{1,0:T(8,128)(2,1)S(1)} %copy.38), kind=kOutput, calls=%fused_computation.28 | convolution fusion | flops 51707904 | bytes 2097248 | tf_op jit(solution)/shard_map/while/body/eval_jaxpr/gkij,gkjv->giv/dot_general | solution.py:39
  41.6 0.3 fusion.11
  42.0 0.2 fusion.25
  42.2 0.2 fusion.78
  42.4 0.8 pad_maximum_fusion.4
  43.2 4.5 %collective-permute-start.2 = (f32[11,32,128]{2,1,0:T(8,128)}, f32[11,32,128]{2,1,0:T(8,128)}, u32[]{:S(2)}, u32[]{:S(2)}) collective-permute-start(f32[11,32,128]{2,1,0:T(8,128)} %get-tuple-element.76), channel_id=1, source_target_pairs={{0,32},{32,64},{64,96},{96,128},{128,160},{160,192},{192,224},{224... | collective-permute-start | bytes 540680 | tf_op jit(solution)/shard_map/ppermute | solution.py:136
  47.7 0.1 convolution_convert_fusion
  47.8 0.8 broadcast_in_dim.52
  48.6 13.6 %all-to-all-start.1 = ((bf16[16,32,288]{2,1,0:T(8,128)(2,1)}), bf16[16,32,288]{2,1,0:T(8,128)(2,1)S(1)}, u32[]{:S(2)}, u32[]{:S(2)}) async-start(bf16[16,32,288]{2,1,0:T(8,128)(2,1)} %broadcast_in_dim.52), calls=%async_computation.1 | async-start | bytes 786432 | tf_op jit(solution)/shard_map/all_to_all | solution.py:99
  62.3 1.3 %collective-permute-start.3 = (f32[11,32,128]{2,1,0:T(8,128)}, f32[11,32,128]{2,1,0:T(8,128)S(1)}, u32[]{:S(2)}, u32[]{:S(2)}) collective-permute-start(f32[11,32,128]{2,1,0:T(8,128)} %get-tuple-element.77), channel_id=1, source_target_pairs={{32,0},{64,32},{96,64},{128,96},{160,128},{192,160},{224,192},{256... | collective-permute-start | bytes 540680 | tf_op jit(solution)/shard_map/ppermute | solution.py:137
  63.7 0.6 dynamic-slice_bitcast_fusion.14
  64.3 1.4 %slice_dynamic-update-slice_fusion.1 = f32[8,32,128]{2,1,0:T(8,128)} fusion(f32[8,32,128]{2,1,0:T(8,128)} %constant_dynamic-update-slice_fusion.2, f32[11,32,128]{2,1,0:T(8,128)} %collective-permute-done.2), kind=kLoop, calls=%fused_computation.119 | loop fusion | bytes 65536
  65.7 0.6 constant_dynamic-update-slice_fusion.1
  66.3 18.5 %collective-permute-done.3 = f32[11,32,128]{2,1,0:T(8,128)S(1)} collective-permute-done((f32[11,32,128]{2,1,0:T(8,128)}, f32[11,32,128]{2,1,0:T(8,128)S(1)}, u32[]{:S(2)}, u32[]{:S(2)}) %collective-permute-start.3) | collective-permute-done | bytes 180256 | tf_op jit(solution)/shard_map/ppermute | solution.py:137
  84.8 0.6 slice_dynamic-update-slice_fusion
  85.4 0.6 constant_dynamic-update-slice_fusion
  86.0 0.9 fusion.147
  86.9 0.8 dynamic-slice_bitcast_fusion.5
  87.7 0.1 fusion.47
  87.9 0.1 fusion.41
  88.1 0.1 fusion.35
  88.3 0.8 convolution_bitcast_fusion.5
  89.3 0.1 fusion.23
  89.4 0.2 fusion.76
  89.8 0.1 fusion.65
  90.0 0.1 fusion.59
  90.1 0.3 convolution_add_fusion.5
  90.5 0.2 fusion.53
  90.7 0.3 convolution_add_fusion.4
  91.0 0.3 convolution_add_fusion.3
  91.3 0.3 convolution_add_fusion.2
  91.6 0.3 convolution_add_fusion.1
  91.9 0.3 fusion.4
  92.2 0.1 fusion.3
  92.4 0.2 fusion.102
  92.6 0.2 fusion.2
  92.8 0.3 fusion.72
  93.1 0.3 fusion.1
  93.4 0.3 fusion.19
  93.7 0.5 fusion
  94.2 0.4 fusion.14
  94.6 0.8 fusion.8
  (99 shorter events, 2.3 us)
Async XLA Ops:
  0.0 6.0 %copy-start.12 = (bf16[1,32,64]{2,1,0:T(8,128)(2,1)S(1)}, bf16[1,32,64]{2,1,0:T(8,128)(2,1)}, u32[]{:S(2)}) copy-start(bf16[1,32,64]{2,1,0:T(8,128)(2,1)} %param.22) | copy-start | bytes 12292
  0.0 6.0 %copy-start.11 = (bf16[1,32,96]{2,1,0:T(8,128)(2,1)S(1)}, bf16[1,32,96]{2,1,0:T(8,128)(2,1)}, u32[]{:S(2)}) copy-start(bf16[1,32,96]{2,1,0:T(8,128)(2,1)} %param.23) | copy-start | bytes 18436
  3.3 13.1 %copy-start = (bf16[1024,128]{1,0:T(8,128)(2,1)S(1)}, bf16[1024,128]{1,0:T(8,128)(2,1)}, u32[]{:S(2)}) copy-start(bf16[1024,128]{1,0:T(8,128)(2,1)} %param.16) | copy-start | bytes 786436
  3.3 13.1 %copy-start.9 = (f32[3,1024]{1,0:T(4,128)S(1)}, f32[3,1024]{1,0:T(4,128)}, u32[]{:S(2)}) copy-start(f32[3,1024]{1,0:T(4,128)} %param.17) | copy-start | bytes 36868
  7.1 18.5 %copy-start.10 = (s32[16,3]{0,1:T(4,128)S(1)}, s32[16,3]{0,1:T(4,128)}, u32[]{:S(2)}) copy-start(s32[16,3]{0,1:T(4,128)} %param.18) | copy-start | bytes 580
  7.1 18.7 %copy-start.15 = (s32[12]{0:T(128)S(1)}, s32[12]{0:T(128)}, u32[]{:S(2)}) copy-start(s32[12]{0:T(128)} %constant.262) | copy-start | bytes 148
  7.1 18.7 %copy-start.16 = (s32[6]{0:T(128)S(1)}, s32[6]{0:T(128)}, u32[]{:S(2)}) copy-start(s32[6]{0:T(128)} %constant.263) | copy-start | bytes 76
  7.1 18.7 %copy-start.13 = (s32[48]{0:T(128)S(1)}, s32[48]{0:T(128)}, u32[]{:S(2)}) copy-start(s32[48]{0:T(128)} %constant.260) | copy-start | bytes 580
  7.1 18.7 %copy-start.14 = (s32[24]{0:T(128)S(1)}, s32[24]{0:T(128)}, u32[]{:S(2)}) copy-start(s32[24]{0:T(128)} %constant.261) | copy-start | bytes 292
  7.1 34.5 %all-to-all-start = ((f32[16,32,288]{2,1,0:T(8,128)}), f32[16,32,288]{2,1,0:T(8,128)S(1)}, u32[]{:S(2)}, u32[]{:S(2)}) async-start(f32[16,32,288]{2,1,0:T(8,128)} %broadcast_in_dim.50), calls=%async_computation | async-start | bytes 1572864 | tf_op jit(solution)/shard_map/all_to_all | solution.py:99
  16.7 13.0 %collective-permute-start = (f32[41152]{0:T(1024)S(1)}, f32[41152]{0:T(1024)S(1)}, u32[]{:S(2)}, u32[]{:S(2)}) collective-permute-start(f32[41152]{0:T(1024)S(1)} %concatenate.79), channel_id=1, source_target_pairs={{0,2},{2,4},{4,6},{6,8},{8,10},{10,12},{12,14},{14,16},{16,18},{18... | collective-permute-start | bytes 493832 | tf_op jit(solution)/shard_map/ppermute | solution.py:215
  20.3 9.5 %collective-permute-start.1 = (f32[41152]{0:T(1024)S(1)}, f32[41152]{0:T(1024)S(1)}, u32[]{:S(2)}, u32[]{:S(2)}) collective-permute-start(f32[41152]{0:T(1024)S(1)} %concatenate.80), channel_id=1, source_target_pairs={{2,0},{4,2},{6,4},{8,6},{10,8},{12,10},{14,12},{16,14},{18,16},{20... | collective-permute-start | bytes 493832 | tf_op jit(solution)/shard_map/ppermute | solution.py:216
  43.2 21.2 %collective-permute-start.2 = (f32[11,32,128]{2,1,0:T(8,128)}, f32[11,32,128]{2,1,0:T(8,128)}, u32[]{:S(2)}, u32[]{:S(2)}) collective-permute-start(f32[11,32,128]{2,1,0:T(8,128)} %get-tuple-element.76), channel_id=1, source_target_pairs={{0,32},{32,64},{64,96},{96,128},{128,160},{160,192},{192,224},{224... | collective-permute-start | bytes 540680 | tf_op jit(solution)/shard_map/ppermute | solution.py:136
  48.6 40.5 %all-to-all-start.1 = ((bf16[16,32,288]{2,1,0:T(8,128)(2,1)}), bf16[16,32,288]{2,1,0:T(8,128)(2,1)S(1)}, u32[]{:S(2)}, u32[]{:S(2)}) async-start(bf16[16,32,288]{2,1,0:T(8,128)(2,1)} %broadcast_in_dim.52), calls=%async_computation.1 | async-start | bytes 786432 | tf_op jit(solution)/shard_map/all_to_all | solution.py:99
  62.3 22.6 %collective-permute-start.3 = (f32[11,32,128]{2,1,0:T(8,128)}, f32[11,32,128]{2,1,0:T(8,128)S(1)}, u32[]{:S(2)}, u32[]{:S(2)}) collective-permute-start(f32[11,32,128]{2,1,0:T(8,128)} %get-tuple-element.77), channel_id=1, source_target_pairs={{32,0},{64,32},{96,64},{128,96},{160,128},{192,160},{224,192},{256... | collective-permute-start | bytes 540680 | tf_op jit(solution)/shard_map/ppermute | solution.py:137
  89.2 1.8 %copy-start.8 = (f32[32,64]{1,0:T(8,128)S(1)}, f32[32,64]{1,0:T(8,128)}, u32[]{:S(2)}) copy-start(f32[32,64]{1,0:T(8,128)} %get-tuple-element.29) | copy-start | bytes 24580
  89.2 2.1 %copy-start.7 = (f32[32,64]{1,0:T(8,128)S(1)}, f32[32,64]{1,0:T(8,128)}, u32[]{:S(2)}) copy-start(f32[32,64]{1,0:T(8,128)} %get-tuple-element.30) | copy-start | bytes 24580
  89.2 2.4 %copy-start.6 = (f32[32,64]{1,0:T(8,128)S(1)}, f32[32,64]{1,0:T(8,128)}, u32[]{:S(2)}) copy-start(f32[32,64]{1,0:T(8,128)} %get-tuple-element.31) | copy-start | bytes 24580
  89.3 2.7 %copy-start.5 = (f32[32,64]{1,0:T(8,128)S(1)}, f32[32,64]{1,0:T(8,128)}, u32[]{:S(2)}) copy-start(f32[32,64]{1,0:T(8,128)} %get-tuple-element.28) | copy-start | bytes 24580
  89.3 3.1 %copy-start.3 = (bf16[1,15,32,64]{3,2,1,0:T(8,128)(2,1)S(1)}, bf16[1,15,32,64]{3,2,1,0:T(8,128)(2,1)}, u32[]{:S(2)}) copy-start(bf16[1,15,32,64]{3,2,1,0:T(8,128)(2,1)} %param.20) | copy-start | bytes 184324
  89.4 3.2 %copy-start.1 = (f32[12,32,128]{2,1,0:T(8,128)S(1)}, f32[12,32,128]{2,1,0:T(8,128)}, u32[]{:S(2)}) copy-start(f32[12,32,128]{2,1,0:T(8,128)} %gather_fusion.4) | copy-start | bytes 589828
  89.4 3.2 %copy-start.4 = (bf16[1,31,32,96]{3,2,1,0:T(8,128)(2,1)S(1)}, bf16[1,31,32,96]{3,2,1,0:T(8,128)(2,1)}, u32[]{:S(2)}) copy-start(bf16[1,31,32,96]{3,2,1,0:T(8,128)(2,1)} %param.21) | copy-start | bytes 571396
  93.4 1.2 %copy-start.2 = (f32[16,64,128,1]{2,1,3,0:T(8,128)S(1)}, f32[16,64,128,1]{2,1,3,0:T(8,128)}, u32[]{:S(2)}) copy-start(f32[16,64,128,1]{2,1,3,0:T(8,128)} %fusion.6) | copy-start | bytes 1572868

commit v9 on v8

--- a/solution.py
+++ b/solution.py
@@ -118,7 +118,7 @@
     return jnp.take(gathered, np.array(order), axis=0)
 
 
-def upper_tree(device_coef, device_coupling, upper_transfer, upper_coupling):
+def upper_tree(device_coef, device_coupling, upper_transfer, upper_coupling, held, late):
     planes = lax.axis_size("z")
     plane_bits = lax.axis_size(PLANE).bit_length() - 1
     plane = lax.axis_index("z")
@@ -136,7 +136,9 @@
     from_left = lax.ppermute(tails, "z", [(i, i + 1) for i in range(planes - 1)])
     from_right = lax.ppermute(heads, "z", [(i + 1, i) for i in range(planes - 1)])
     outer_unit = jnp.concatenate([inner[plane_bits][0], plane_held[0, :, columns:]], 1)
-    outer_held = as_float(spread_gather(outer_unit.astype(jnp.bfloat16), "z"))
+    outer_unit, held = lax.optimization_barrier((outer_unit.astype(jnp.bfloat16), held))
+    outer_held = as_float(spread_gather(outer_unit, "z"))
+    late_result = late(held)
     summary = outer_held[:, :, :columns]
     outer_lift = outer_held[:, :, columns : columns + 2 * RANK]
     outer_mix = outer_held[:, :, columns + 2 * RANK :]
@@ -178,7 +180,7 @@
         cluster, lift = lifts[height]
         half = jnp.where(cluster % 2 == 1, lift[:, RANK:], lift[:, :RANK])
         downward = fields[height] + product(half.T, downward)
-    return downward
+    return downward, late_result
 
 
 def local(
@@ -223,26 +225,32 @@
             done += size
         return pieces
 
-    left_vectors, left_points, left_edges = unpack(from_left)
-    right_vectors, right_points, right_edges = unpack(from_right)
-    vector_rims = jnp.concatenate(
-        [left_vectors.astype(vectors.dtype), vectors, right_vectors.astype(vectors.dtype)], 0
-    )
-    point_rims = jnp.concatenate([left_points, points, right_points], 1)
-    nearby = near_field(vector_rims, point_rims, near_index, 0, leaf_zero, leaf_count)
-    fields = []
-    for height in range(depth_local):
-        cluster_count = leaf_count >> height
-        first_slot = 2 * leaf_count - (2 * leaf_count >> height)
-        extended = jnp.concatenate([left_edges[height], coefficients[height], right_edges[height]], 0)
-        stacked = extended[partner_table(cluster_count) + 2].reshape(
-            cluster_count, 3 * RANK, columns
-        )
-        mixers = as_float(coupling[0, first_slot : first_slot + cluster_count])
-        fields.append(jnp.einsum("cra,cav->crv", mixers, stacked, precision=HIGHEST))
+    def late(held):
+        from_left, from_right = held
+        left_vectors, left_points, left_edges = unpack(from_left)
+        right_vectors, right_points, right_edges = unpack(from_right)
+        vector_rims = jnp.concatenate(
+            [left_vectors.astype(vectors.dtype), vectors, right_vectors.astype(vectors.dtype)], 0
+        )
+        point_rims = jnp.concatenate([left_points, points, right_points], 1)
+        nearby = near_field(vector_rims, point_rims, near_index, 0, leaf_zero, leaf_count)
+        fields = []
+        for height in range(depth_local):
+            cluster_count = leaf_count >> height
+            first_slot = 2 * leaf_count - (2 * leaf_count >> height)
+            extended = jnp.concatenate([left_edges[height], coefficients[height], right_edges[height]], 0)
+            stacked = extended[partner_table(cluster_count) + 2].reshape(
+                cluster_count, 3 * RANK, columns
+            )
+            mixers = as_float(coupling[0, first_slot : first_slot + cluster_count])
+            fields.append(jnp.einsum("cra,cav->crv", mixers, stacked, precision=HIGHEST))
+        return nearby, fields
+
     device_coupling = as_float(coupling[0, 2 * leaf_count - 2])
     device_coef = coefficients[depth_local][0]
-    downward = upper_tree(device_coef, device_coupling, upper_transfer, upper_coupling)
+    downward, (nearby, fields) = upper_tree(
+        device_coef, device_coupling, upper_transfer, upper_coupling, (from_left, from_right), late
+    )
     downward = downward[None]
     for height in range(depth_local - 1, -1, -1):
         cluster_count = leaf_count >> height + 1

time: 96.4 us -> 95.5 us (level)
  the two profiles are of different devices: /device:TPU:24 before, /device:TPU:64 now
where the time goes in v9:
time: 95.5 us; the launch traced here: 94.4 us
  starting transfers between devices  38.6 us (40%)
  local copies, waits for them, and re-layouts  21.2 us (22%)
  matrix products  14.3 us (15%)
  waiting for transfers between devices  12.9 us (14%)
  other arithmetic  6.35 us (7%)
  between operations  1.18 us (1%)
    all_to_all x2, starting transfers between devices, spread_gather(): return lax.all_to_all(copies, axis, 0, 0, tiled=True)  23.1 us
    all_to_all x2, waiting for transfers between devices, spread_gather(): return lax.all_to_all(copies, axis, 0, 0, tiled=True)  12.8 us
    ppermute x1, starting transfers between devices, local(): lax.ppermute(head, SPACE, [(i + 1, i) for i in range(count - 1)])  6.66 us
    ppermute x1, starting transfers between devices, upper_tree(): lax.ppermute(tails, 'z', [(i, i + 1) for i in range(planes - 1)])  5.03 us
    dot_general x13, matrix products, product(): return jnp.dot(matrix, operand, precision=HIGHEST)  4.72 us
    gather x4, local copies, waits for them, and re-layouts, late(): extended[partner_table(cluster_count) + 2]  3.76 us
    dot_general x4, matrix products, late(): jnp.einsum('cra,cav->crv', mixers, stacked, precision=HIGHEST)  2.5 us
    unnamed x78, local copies, waits for them, and re-layouts  2.3 us
  transfers between devices with their start and end apart: 6, of which 2 were waited for; matrix products, arithmetic and copies ran while one was open for 27% of the time, Pallas kernels for 0%

profile of v9, /device:TPU:64, one launch (start us, length us, event | category | flops | bytes accessed | tf_op | source)
XLA Modules:
  0.0 94.4 jit_solution(17197316779698190519)
XLA Ops:
  0.0 0.8 fusion.153
  0.9 0.7 bitcast_convert_fusion
  1.6 1.0 %reshape.186 = bf16[32,16,64]{2,1,0:T(8,128)(2,1)S(1)} reshape(bf16[32,1024]{1,0:T(8,128)(2,1)} %param.19) | data formatting | bytes 131072 | tf_op jit(solution)/shard_map/reshape | solution.py:194
  2.6 1.1 %fusion.154 = (bf16[16,32,128]{2,1,0:T(8,128)(2,1)S(1)}, f32[16,32,128]{2,1,0:T(8,128)S(1)}) fusion(bf16[16,64,128]{2,1,0:T(8,128)(2,1)} %bitcast.262, bf16[32,16,64]{2,1,0:T(8,128)(2,1)S(1)} %reshape.186), kind=kOutput, calls=%fused_computation.255 | convolution fusion | flops 8454144 | bytes 720896 | tf_op jit(solution)/shard_map/rlp,lpv->lrv/dot_general | solution.py:197
  3.8 1.1 %bitcast_convert_fusion.3 = (bf16[8,32,128]{2,1,0:T(8,128)(2,1)S(1)}, f32[8,128,32]{1,2,0:T(8,128)S(1)}) fusion(f32[8,64,128]{2,1,0:T(8,128)S(1)} %bitcast.263, bf16[1,15,32,64]{3,2,1,0:T(8,128)(2,1)} %param.20), kind=kOutput, calls=%fused_computation.242 | convolution fusion | flops 25198592 | bytes 524288 | tf_op jit(solution)/shard_map/cra,cav->crv/dot_general | solution.py:204
  4.9 0.2 bitcast_convert_fusion.2
  5.1 0.2 fusion.104
  5.4 6.7 %collective-permute-start.1 = (f32[41152]{0:T(1024)S(1)}, f32[41152]{0:T(1024)S(1)}, u32[]{:S(2)}, u32[]{:S(2)}) collective-permute-start(f32[41152]{0:T(1024)S(1)} %concatenate.77), channel_id=1, source_target_pairs={{2,0},{4,2},{6,4},{8,6},{10,8},{12,10},{14,12},{16,14},{18,16},{20... | collective-permute-start | bytes 493832 | tf_op jit(solution)/shard_map/ppermute | solution.py:218
  12.3 1.9 %collective-permute-start = (f32[41152]{0:T(1024)S(1)}, f32[41152]{0:T(1024)S(1)}, u32[]{:S(2)}, u32[]{:S(2)}) collective-permute-start(f32[41152]{0:T(1024)S(1)} %concatenate.76), channel_id=1, source_target_pairs={{0,2},{2,4},{4,6},{6,8},{8,10},{10,12},{12,14},{14,16},{16,18},{18... | collective-permute-start | bytes 493832 | tf_op jit(solution)/shard_map/ppermute | solution.py:217
  14.5 1.0 %broadcast_in_dim.45 = f32[16,32,288]{2,1,0:T(8,128)} broadcast(f32[32,288]{1,0:T(8,128)S(1)} %pad_maximum_fusion.12), dimensions={1,2} | broadcast | bytes 626688 | tf_op jit(solution)/shard_map/broadcast_in_dim | solution.py:98
  15.5 8.1 %all-to-all-start = ((f32[16,32,288]{2,1,0:T(8,128)}), f32[16,32,288]{2,1,0:T(8,128)S(1)}, u32[]{:S(2)}, u32[]{:S(2)}) async-start(f32[16,32,288]{2,1,0:T(8,128)} %broadcast_in_dim.45), calls=%async_computation | async-start | bytes 1572864 | tf_op jit(solution)/shard_map/all_to_all | solution.py:99
  23.8 0.7 copy.38
  24.7 0.7 copy.39
  25.4 0.6 pad_clamp_fusion.2
  26.0 0.6 pad_clamp_fusion
  26.6 0.6 constant_dynamic-update-slice_fusion.2
  27.2 10.2 %all-to-all-done = f32[16,32,288]{2,1,0:T(8,128)S(1)} async-done(((f32[16,32,288]{2,1,0:T(8,128)}), f32[16,32,288]{2,1,0:T(8,128)S(1)}, u32[]{:S(2)}, u32[]{:S(2)}) %all-to-all-start) | async-done | bytes 589856 | tf_op jit(solution)/shard_map/all_to_all | solution.py:99
  37.4 0.3 fusion.12
  37.8 0.2 fusion.26
  38.0 0.2 fusion.79
  38.4 0.7 fusion.149
  39.2 0.6 fusion.85
  39.8 0.7 fusion.150
  40.8 0.6 dynamic_slice.147
  41.5 0.6 gather_fusion
  42.1 0.7 copy.50
  42.8 0.8 pad_maximum_fusion.4
  43.6 5.0 %collective-permute-start.2 = (f32[11,32,128]{2,1,0:T(8,128)}, f32[11,32,128]{2,1,0:T(8,128)}, u32[]{:S(2)}, u32[]{:S(2)}) collective-permute-start(f32[11,32,128]{2,1,0:T(8,128)} %get-tuple-element.82), channel_id=1, source_target_pairs={{0,32},{32,64},{64,96},{96,128},{128,160},{160,192},{192,224},{224... | collective-permute-start | bytes 540680 | tf_op jit(solution)/shard_map/ppermute | solution.py:136
  48.6 1.9 %collective-permute-start.3 = (f32[11,32,128]{2,1,0:T(8,128)}, f32[11,32,128]{2,1,0:T(8,128)}, u32[]{:S(2)}, u32[]{:S(2)}) collective-permute-start(f32[11,32,128]{2,1,0:T(8,128)} %get-tuple-element.83), channel_id=1, source_target_pairs={{32,0},{64,32},{96,64},{128,96},{160,128},{192,160},{224,192},{256... | collective-permute-start | bytes 540680 | tf_op jit(solution)/shard_map/ppermute | solution.py:137
  50.6 0.8 broadcast_in_dim.52
  51.4 15.0 %all-to-all-start.1 = ((bf16[16,32,288]{2,1,0:T(8,128)(2,1)}), bf16[16,32,288]{2,1,0:T(8,128)(2,1)S(1)}, u32[]{:S(2)}, u32[]{:S(2)}) async-start(bf16[16,32,288]{2,1,0:T(8,128)(2,1)} %broadcast_in_dim.52), calls=%async_computation.1 | async-start | bytes 786432 | tf_op jit(solution)/shard_map/all_to_all | solution.py:99
  66.4 0.8 pad_maximum_fusion.2
  67.2 1.6 %gather_fusion.1 = bf16[48,64,128]{2,1,0:T(8,128)(2,1)} fusion(bf16[18,64,128]{2,1,0:T(8,128)(2,1)S(1)} %bitcast.260, s32[1024]{0:T(1024)S(1)} %pad_clamp_fusion.4), kind=kCustom, calls=%fused_computation.1 | custom fusion | bytes 1573056 | tf_op jit(solution)/shard_map/while/body/eval_jaxpr/gather | solution.py:40
  68.9 1.3 %gather_fusion.5 = f32[6,32,128]{2,1,0:T(8,128)} fusion(f32[6,32,128]{2,1,0:T(8,128)S(1)} %pad_maximum_fusion.9, s32[1024]{0:T(1024)} %get-tuple-element.100), kind=kCustom, calls=%fused_computation.5 | custom fusion | bytes 196632 | tf_op jit(solution)/shard_map/gather | solution.py:242
  70.2 1.2 %gather_fusion.4 = f32[12,32,128]{2,1,0:T(8,128)} fusion(f32[8,32,128]{2,1,0:T(8,128)S(1)} %pad_maximum_fusion.8, s32[1024]{0:T(1024)S(1)} %copy-done.28), kind=kCustom, calls=%fused_computation.4 | custom fusion | bytes 393264 | tf_op jit(solution)/shard_map/gather | solution.py:242
  71.5 0.6 gather_fusion.3
  72.1 0.6 gather_fusion.2
  72.7 1.8 %multiply_reduce_fusion = f32[16,3,64,64]{3,2,1,0:T(8,128)S(1)} fusion(f32[3,16,3,64]{3,2,1,0:T(4,128)} %bitcast.281, f32[3,16,64]{2,1,0:T(8,128)} %dynamic_slice.147), kind=kLoop, calls=%fused_computation.6 | loop fusion | flops 1572864 | bytes 835584 | tf_op jit(solution)/shard_map/while/body/eval_jaxpr/reduce_sum | solution.py:19
  74.6 1.8 %fusion.6 = f32[16,64,128,1]{2,1,3,0:T(8,128)} fusion(bf16[16,3,64,128]{3,2,1,0:T(8,128)(2,1)S(1)} %bitcast.272, f32[16,3,64,64]{3,2,1,0:T(8,128)S(1)} %multiply_reduce_fusion, bf16[16,3]{1,0:T(8,128)(2,1)S(1)} %copy-done.32), kind=kOutput, calls=%fused_computation.28 | convolution fusion | flops 51707904 | bytes 2097248 | tf_op jit(solution)/shard_map/while/body/eval_jaxpr/gkij,gkjv->giv/dot_general | solution.py:39
  76.4 1.4 %dynamic-slice_bitcast_fusion.14 = (f32[32,64]{1,0:T(8,128)}, f32[32,64]{1,0:T(8,128)}, f32[32,64]{1,0:T(8,128)}, f32[32,64]{1,0:T(8,128)}) fusion(f32[16,32,64]{2,1,0:T(8,128)} %copy-done.1, s32[]{:T(128)S(6)} %select_n.286, s32[]{:T(128)S(6)} %select_n.319, s32[]{:T(128)S(6)} %select_n.308, s32[]{:T(128)S(6)} %select_n.297), kind=kLoop, calls=%fused_computation.193 | loop fusion | bytes 65552 | tf_op jit(solution)/shard_map/jit(dynamic_index_in_dim)/squeeze | solution.py:83
  77.9 1.5 %convolution_bitcast_fusion.4 = f32[2,32,128]{2,1,0:T(8,128)} fusion(f32[2,96,128]{2,1,0:T(8,128)S(1)} %bitcast.282, bf16[1,31,32,96]{3,2,1,0:T(8,128)(2,1)} %param.21), kind=kOutput, calls=%fused_computation.16 | convolution fusion | flops 9437184 | bytes 147456 | tf_op jit(solution)/shard_map/cra,cav->crv/dot_general | solution.py:246
  79.4 0.8 slice_dynamic-update-slice_fusion.1
  80.2 0.8 slice_dynamic-update-slice_fusion
  81.0 0.9 fusion.147
  81.8 0.9 fusion.148
  82.9 0.8 fusion.47
  83.9 1.5 %convolution_bitcast_fusion.5 = f32[32,128]{1,0:T(8,128)} fusion(f32[32,128]{1,0:T(8,128)S(1)} %get-tuple-element.32, f32[32,128]{1,0:T(8,128)S(1)} %get-tuple-element.33, f32[32,128]{1,0:T(8,128)S(1)} %get-tuple-element.31, bf16[1,31,32,96]{3,2,1,0:T(8,128)(2,1)} %param.21), kind=kOutput, calls=%fused_computation.24 | convolution fusion | flops 4743168 | bytes 73728 | tf_op jit(solution)/shard_map/dot_general | solution.py:63
  85.4 2.7 %all-to-all-done.1 = bf16[16,32,288]{2,1,0:T(8,128)(2,1)S(1)} async-done(((bf16[16,32,288]{2,1,0:T(8,128)(2,1)}), bf16[16,32,288]{2,1,0:T(8,128)(2,1)S(1)}, u32[]{:S(2)}, u32[]{:S(2)}) %all-to-all-start.1) | async-done | bytes 294944 | tf_op jit(solution)/shard_map/all_to_all | solution.py:99
  88.4 0.2 fusion.76
  89.1 0.3 convolution_add_fusion.5
  89.4 0.2 fusion.53
  89.6 0.3 convolution_add_fusion.4
  90.0 0.3 convolution_add_fusion.3
  90.3 0.3 convolution_add_fusion.2
  90.6 0.3 convolution_add_fusion.1
  90.9 0.3 fusion.4
  91.3 0.2 fusion.102
  91.6 0.2 fusion.2
  91.8 0.3 fusion.72
  92.1 0.3 fusion.1
  92.4 0.3 fusion.19
  92.7 0.5 fusion
  93.2 0.4 fusion.14
  93.6 0.8 fusion.8
  (139 shorter events, 3.1 us)
Async XLA Ops:
  0.0 4.9 %copy-start.7 = (bf16[1,15,32,64]{3,2,1,0:T(8,128)(2,1)S(1)}, bf16[1,15,32,64]{3,2,1,0:T(8,128)(2,1)}, u32[]{:S(2)}) copy-start(bf16[1,15,32,64]{3,2,1,0:T(8,128)(2,1)} %param.20) | copy-start | bytes 184324
  0.0 14.4 %copy-start.30 = (bf16[1,32,96]{2,1,0:T(8,128)(2,1)S(1)}, bf16[1,32,96]{2,1,0:T(8,128)(2,1)}, u32[]{:S(2)}) copy-start(bf16[1,32,96]{2,1,0:T(8,128)(2,1)} %param.23) | copy-start | bytes 18436
  0.0 14.4 %copy-start.31 = (bf16[1,32,64]{2,1,0:T(8,128)(2,1)S(1)}, bf16[1,32,64]{2,1,0:T(8,128)(2,1)}, u32[]{:S(2)}) copy-start(bf16[1,32,64]{2,1,0:T(8,128)(2,1)} %param.22) | copy-start | bytes 12292
  5.3 18.3 %copy-start.29 = (s32[16,3]{0,1:T(4,128)S(1)}, s32[16,3]{0,1:T(4,128)}, u32[]{:S(2)}) copy-start(s32[16,3]{0,1:T(4,128)} %param.18) | copy-start | bytes 580
  5.4 33.0 %collective-permute-start.1 = (f32[41152]{0:T(1024)S(1)}, f32[41152]{0:T(1024)S(1)}, u32[]{:S(2)}, u32[]{:S(2)}) collective-permute-start(f32[41152]{0:T(1024)S(1)} %concatenate.77), channel_id=1, source_target_pairs={{2,0},{4,2},{6,4},{8,6},{10,8},{12,10},{14,12},{16,14},{18,16},{20... | collective-permute-start | bytes 493832 | tf_op jit(solution)/shard_map/ppermute | solution.py:218
  12.3 26.1 %collective-permute-start = (f32[41152]{0:T(1024)S(1)}, f32[41152]{0:T(1024)S(1)}, u32[]{:S(2)}, u32[]{:S(2)}) collective-permute-start(f32[41152]{0:T(1024)S(1)} %concatenate.76), channel_id=1, source_target_pairs={{0,2},{2,4},{4,6},{6,8},{8,10},{10,12},{12,14},{14,16},{16,18},{18... | collective-permute-start | bytes 493832 | tf_op jit(solution)/shard_map/ppermute | solution.py:217
  14.5 10.9 %copy-start.35 = (s32[24]{0:T(128)S(1)}, s32[24]{0:T(128)}, u32[]{:S(2)}) copy-start(s32[24]{0:T(128)} %constant.261) | copy-start | bytes 292
  14.5 10.9 %copy-start.36 = (s32[48]{0:T(128)S(1)}, s32[48]{0:T(128)}, u32[]{:S(2)}) copy-start(s32[48]{0:T(128)} %constant.260) | copy-start | bytes 580
  14.5 11.5 %copy-start.33 = (s32[6]{0:T(128)S(1)}, s32[6]{0:T(128)}, u32[]{:S(2)}) copy-start(s32[6]{0:T(128)} %constant.263) | copy-start | bytes 76
  14.5 11.5 %copy-start.34 = (s32[12]{0:T(128)S(1)}, s32[12]{0:T(128)}, u32[]{:S(2)}) copy-start(s32[12]{0:T(128)} %constant.262) | copy-start | bytes 148
  15.5 21.9 %all-to-all-start = ((f32[16,32,288]{2,1,0:T(8,128)}), f32[16,32,288]{2,1,0:T(8,128)S(1)}, u32[]{:S(2)}, u32[]{:S(2)}) async-start(f32[16,32,288]{2,1,0:T(8,128)} %broadcast_in_dim.45), calls=%async_computation | async-start | bytes 1572864 | tf_op jit(solution)/shard_map/all_to_all | solution.py:99
  23.7 16.9 %copy-start.26 = (f32[3,1024]{1,0:T(4,128)S(1)}, f32[3,1024]{1,0:T(4,128)}, u32[]{:S(2)}) copy-start(f32[3,1024]{1,0:T(4,128)} %param.17) | copy-start | bytes 36868
  37.4 5.4 %copy-start.1 = (f32[16,32,64]{2,1,0:T(8,128)}, f32[16,32,64]{2,1,0:T(8,128)S(1)}, u32[]{:S(2)}) copy-start(f32[16,32,64]{2,1,0:T(8,128)S(1)} %slice.393) | copy-start | bytes 393220
  38.2 13.2 %copy-start.5 = (f32[2,32,128]{2,1,0:T(8,128)}, f32[2,32,128]{2,1,0:T(8,128)S(1)}, u32[]{:S(2)}) copy-start(f32[2,32,128]{2,1,0:T(8,128)S(1)} %fusion.79) | copy-start | bytes 98308
  40.5 25.9 %copy-start = (bf16[1024,128]{1,0:T(8,128)(2,1)S(1)}, bf16[1024,128]{1,0:T(8,128)(2,1)}, u32[]{:S(2)}) copy-start(bf16[1024,128]{1,0:T(8,128)(2,1)} %param.16) | copy-start | bytes 786436
  43.6 35.8 %collective-permute-start.2 = (f32[11,32,128]{2,1,0:T(8,128)}, f32[11,32,128]{2,1,0:T(8,128)}, u32[]{:S(2)}, u32[]{:S(2)}) collective-permute-start(f32[11,32,128]{2,1,0:T(8,128)} %get-tuple-element.82), channel_id=1, source_target_pairs={{0,32},{32,64},{64,96},{96,128},{128,160},{160,192},{192,224},{224... | collective-permute-start | bytes 540680 | tf_op jit(solution)/shard_map/ppermute | solution.py:136
  48.6 31.5 %collective-permute-start.3 = (f32[11,32,128]{2,1,0:T(8,128)}, f32[11,32,128]{2,1,0:T(8,128)}, u32[]{:S(2)}, u32[]{:S(2)}) collective-permute-start(f32[11,32,128]{2,1,0:T(8,128)} %get-tuple-element.83), channel_id=1, source_target_pairs={{32,0},{64,32},{96,64},{128,96},{160,128},{192,160},{224,192},{256... | collective-permute-start | bytes 540680 | tf_op jit(solution)/shard_map/ppermute | solution.py:137
  51.4 17.4 %copy-start.12 = (f32[8192]{0:T(1024)S(1)}, f32[8192]{0:T(1024)}, u32[]{:S(2)}) copy-start(f32[8192]{0:T(1024)} %get-tuple-element.58) | copy-start | bytes 98308
  51.4 36.7 %all-to-all-start.1 = ((bf16[16,32,288]{2,1,0:T(8,128)(2,1)}), bf16[16,32,288]{2,1,0:T(8,128)(2,1)S(1)}, u32[]{:S(2)}, u32[]{:S(2)}) async-start(bf16[16,32,288]{2,1,0:T(8,128)(2,1)} %broadcast_in_dim.52), calls=%async_computation.1 | async-start | bytes 786432 | tf_op jit(solution)/shard_map/all_to_all | solution.py:99
  66.4 2.4 %copy-start.13 = (f32[8192]{0:T(1024)S(1)}, f32[8192]{0:T(1024)}, u32[]{:S(2)}) copy-start(f32[8192]{0:T(1024)} %get-tuple-element.55) | copy-start | bytes 98308
  66.4 2.4 %copy-start.14 = (f32[8192]{0:T(1024)S(1)}, f32[8192]{0:T(1024)}, u32[]{:S(2)}) copy-start(f32[8192]{0:T(1024)} %get-tuple-element.59) | copy-start | bytes 98308
  66.4 3.8 %copy-start.15 = (f32[8192]{0:T(1024)S(1)}, f32[8192]{0:T(1024)}, u32[]{:S(2)}) copy-start(f32[8192]{0:T(1024)} %get-tuple-element.56) | copy-start | bytes 98308
  66.4 3.8 %copy-start.16 = (f32[8192]{0:T(1024)S(1)}, f32[8192]{0:T(1024)}, u32[]{:S(2)}) copy-start(f32[8192]{0:T(1024)} %get-tuple-element.60) | copy-start | bytes 98308
  67.2 3.0 %copy-start.28 = (s32[1024]{0:T(1024)S(1)}, s32[1024]{0:T(1024)}, u32[]{:S(2)}) copy-start(s32[1024]{0:T(1024)} %get-tuple-element.101) | copy-start | bytes 12292
  67.2 4.3 %copy-start.27 = (s32[1024]{0:T(1024)S(1)}, s32[1024]{0:T(1024)}, u32[]{:S(2)}) copy-start(s32[1024]{0:T(1024)} %get-tuple-element.102) | copy-start | bytes 12292
  68.8 3.3 %copy-start.24 = (s32[1024]{0:T(1024)S(1)}, s32[1024]{0:T(1024)}, u32[]{:S(2)}) copy-start(s32[1024]{0:T(1024)} %get-tuple-element.103) | copy-start | bytes 12292
  72.1 2.5 %copy-start.32 = (bf16[16,3]{1,0:T(8,128)(2,1)S(1)}, bf16[16,3]{1,0:T(8,128)(2,1)}, u32[]{:S(2)}) copy-start(bf16[16,3]{1,0:T(8,128)(2,1)} %copy.38) | copy-start | bytes 292
  72.7 1.8 %copy-start.2 = (bf16[48,64,128]{2,1,0:T(8,128)(2,1)S(1)}, bf16[48,64,128]{2,1,0:T(8,128)(2,1)}, u32[]{:S(2)}) copy-start(bf16[48,64,128]{2,1,0:T(8,128)(2,1)} %gather_fusion.1) | copy-start | bytes 2359300
  74.6 3.3 %copy-start.9 = (f32[6,32,128]{2,1,0:T(8,128)S(1)}, f32[6,32,128]{2,1,0:T(8,128)}, u32[]{:S(2)}) copy-start(f32[6,32,128]{2,1,0:T(8,128)} %gather_fusion.5) | copy-start | bytes 294916
  74.6 4.8 %copy-start.25 = (f32[8,32,128]{2,1,0:T(8,128)S(1)}, f32[8,32,128]{2,1,0:T(8,128)}, u32[]{:S(2)}) copy-start(f32[8,32,128]{2,1,0:T(8,128)} %constant_dynamic-update-slice_fusion.2) | copy-start | bytes 393220
  74.6 5.6 %copy-start.6 = (f32[2,32,128]{2,1,0:T(8,128)S(1)}, f32[2,32,128]{2,1,0:T(8,128)}, u32[]{:S(2)}) copy-start(f32[2,32,128]{2,1,0:T(8,128)} %copy-done.5) | copy-start | bytes 98308
  88.1 1.9 %copy-start.17 = (f32[32,128]{1,0:T(8,128)S(1)}, f32[32,128]{1,0:T(8,128)}, u32[]{:S(2)}) copy-start(f32[32,128]{1,0:T(8,128)} %fusion.47) | copy-start | bytes 49156
  88.1 1.9 %copy-start.23 = (f32[32,64]{1,0:T(8,128)S(1)}, f32[32,64]{1,0:T(8,128)}, u32[]{:S(2)}) copy-start(f32[32,64]{1,0:T(8,128)} %get-tuple-element.35) | copy-start | bytes 24580
  88.1 2.1 %copy-start.22 = (f32[32,64]{1,0:T(8,128)S(1)}, f32[32,64]{1,0:T(8,128)}, u32[]{:S(2)}) copy-start(f32[32,64]{1,0:T(8,128)} %get-tuple-element.36) | copy-start | bytes 24580
  88.1 2.4 %copy-start.21 = (f32[32,64]{1,0:T(8,128)S(1)}, f32[32,64]{1,0:T(8,128)}, u32[]{:S(2)}) copy-start(f32[32,64]{1,0:T(8,128)} %get-tuple-element.37) | copy-start | bytes 24580
  88.2 2.7 %copy-start.19 = (f32[32,128]{1,0:T(8,128)S(1)}, f32[32,128]{1,0:T(8,128)}, u32[]{:S(2)}) copy-start(f32[32,128]{1,0:T(8,128)} %convolution_bitcast_fusion.5) | copy-start | bytes 49156
  88.2 2.7 %copy-start.20 = (f32[32,64]{1,0:T(8,128)S(1)}, f32[32,64]{1,0:T(8,128)}, u32[]{:S(2)}) copy-start(f32[32,64]{1,0:T(8,128)} %get-tuple-element.34) | copy-start | bytes 24580
  88.2 3.0 %copy-start.11 = (f32[2,32,128]{2,1,0:T(8,128)S(1)}, f32[2,32,128]{2,1,0:T(8,128)}, u32[]{:S(2)}) copy-start(f32[2,32,128]{2,1,0:T(8,128)} %convolution_bitcast_fusion.4) | copy-start | bytes 98308
  88.2 3.0 %copy-start.18 = (bf16[64,32]{1,0:T(8,128)(2,1)S(1)}, bf16[64,32]{1,0:T(8,128)(2,1)}, u32[]{:S(2)}) copy-start(bf16[64,32]{1,0:T(8,128)(2,1)} %copy.39) | copy-start | bytes 12292
  88.2 3.1 %copy-start.8 = (bf16[1,15,32,64]{3,2,1,0:T(8,128)(2,1)S(1)}, bf16[1,15,32,64]{3,2,1,0:T(8,128)(2,1)}, u32[]{:S(2)}) copy-start(bf16[1,15,32,64]{3,2,1,0:T(8,128)(2,1)} %param.20) | copy-start | bytes 184324
  88.4 3.2 %copy-start.3 = (f32[12,32,128]{2,1,0:T(8,128)S(1)}, f32[12,32,128]{2,1,0:T(8,128)}, u32[]{:S(2)}) copy-start(f32[12,32,128]{2,1,0:T(8,128)} %gather_fusion.4) | copy-start | bytes 589828
  88.4 3.2 %copy-start.10 = (bf16[1,31,32,96]{3,2,1,0:T(8,128)(2,1)S(1)}, bf16[1,31,32,96]{3,2,1,0:T(8,128)(2,1)}, u32[]{:S(2)}) copy-start(bf16[1,31,32,96]{3,2,1,0:T(8,128)(2,1)} %param.21) | copy-start | bytes 571396
  92.4 1.2 %copy-start.4 = (f32[16,64,128,1]{2,1,3,0:T(8,128)S(1)}, f32[16,64,128,1]{2,1,3,0:T(8,128)}, u32[]{:S(2)}) copy-start(f32[16,64,128,1]{2,1,3,0:T(8,128)} %fusion.6) | copy-start | bytes 1572868

commit v10 on v9

--- a/solution.py
+++ b/solution.py
@@ -63,9 +63,10 @@
     return jnp.dot(matrix, operand, precision=HIGHEST)
 
 
-SPACE = ("z", "y", "x")
+SPACE = ("zh", "zl", "y", "x")
+DEPTH = ("zh", "zl")
 PLANE = ("y", "x")
-CUTS = (16, 4, 4)
+CUTS = (4, 4, 4, 4)
 
 
 def neighbours(padded, cluster):
@@ -119,9 +120,9 @@
 
 
 def upper_tree(device_coef, device_coupling, upper_transfer, upper_coupling, held, late):
-    planes = lax.axis_size("z")
+    planes = lax.axis_size(DEPTH)
     plane_bits = lax.axis_size(PLANE).bit_length() - 1
-    plane = lax.axis_index("z")
+    plane = lax.axis_index(DEPTH)
     seat = lax.axis_index(PLANE)
     matrices = as_float(jnp.concatenate([upper_transfer[0], upper_coupling[0]], 1))
     columns = device_coef.shape[1]
@@ -133,11 +134,12 @@
         inner.append(lift_up(plane_lift[2 ** (height - 1) :: 2**height], inner[-1]))
     tails = jnp.concatenate([level[-3:] for level in inner[:plane_bits]], 0)
     heads = jnp.concatenate([level[:3] for level in inner[:plane_bits]], 0)
-    from_left = lax.ppermute(tails, "z", [(i, i + 1) for i in range(planes - 1)])
-    from_right = lax.ppermute(heads, "z", [(i + 1, i) for i in range(planes - 1)])
+    from_left = lax.ppermute(tails, DEPTH, [(i, i + 1) for i in range(planes - 1)])
+    from_right = lax.ppermute(heads, DEPTH, [(i + 1, i) for i in range(planes - 1)])
     outer_unit = jnp.concatenate([inner[plane_bits][0], plane_held[0, :, columns:]], 1)
     outer_unit, held = lax.optimization_barrier((outer_unit.astype(jnp.bfloat16), held))
-    outer_held = as_float(spread_gather(outer_unit, "z"))
+    nearby_planes = spread_gather(outer_unit, "zl")
+    outer_held = as_float(spread_gather(nearby_planes, "zh").reshape((planes,) + outer_unit.shape))
     late_result = late(held)
     summary = outer_held[:, :, :columns]
     outer_lift = outer_held[:, :, columns : columns + 2 * RANK]

time: 95.5 us -> 113 us (1.18)
  the two profiles are of different devices: /device:TPU:64 before, /device:TPU:56 now
where the time goes in v10:
time: 113 us; the launch traced here: 112 us
  starting transfers between devices  40.7 us (36%)
  waiting for transfers between devices  26.6 us (24%)
  local copies, waits for them, and re-layouts  23 us (20%)
  matrix products  16.5 us (15%)
  other arithmetic  3.76 us (3%)
    all_to_all x3, starting transfers between devices, spread_gather(): return lax.all_to_all(copies, axis, 0, 0, tiled=True)  26.9 us
    all_to_all x3, waiting for transfers between devices, spread_gather(): return lax.all_to_all(copies, axis, 0, 0, tiled=True)  26.5 us
    dot_general x13, matrix products, product(): return jnp.dot(matrix, operand, precision=HIGHEST)  4.72 us
    ppermute x1, starting transfers between devices, local(): lax.ppermute(head, SPACE, [(i + 1, i) for i in range(count - 1)])  4.58 us
    unnamed x60, local copies, waits for them, and re-layouts  4.09 us
    ppermute x1, starting transfers between devices, upper_tree(): lax.ppermute(tails, DEPTH, [(i, i + 1) for i in range(planes - 1)])  3.92 us
    dot_general x4, matrix products, local(): jnp.einsum('cra,cav->crv', lift_mats, children, precision=HIGHEST)  3.78 us
    gather x4, local copies, waits for them, and re-layouts, late(): extended[partner_table(cluster_count) + 2]  3.61 us
  transfers between devices with their start and end apart: 7, of which 2 were waited for; matrix products, arithmetic and copies ran while one was open for 24% of the time, Pallas kernels for 0%

profile of v10, /device:TPU:56, one launch (start us, length us, event | category | flops | bytes accessed | tf_op | source)
XLA Modules:
  0.0 111.6 jit_solution(17547257543907877649)
XLA Ops:
  0.0 1.0 reshape.190
  1.0 1.2 %fusion.154 = (bf16[16,32,128]{2,1,0:T(8,128)(2,1)S(1)}, f32[16,32,128]{2,1,0:T(8,128)S(1)}) fusion(bf16[16,64,128]{2,1,0:T(8,128)(2,1)} %bitcast.267, bf16[32,16,64]{2,1,0:T(8,128)(2,1)S(1)} %reshape.190), kind=kOutput, calls=%fused_computation.256 | convolution fusion | flops 8454144 | bytes 720896 | tf_op jit(solution)/shard_map/rlp,lpv->lrv/dot_general | solution.py:199
  2.2 1.1 bitcast_convert_fusion.4
  3.4 1.0 bitcast_convert_fusion.3
  4.3 0.9 fusion.104
  5.2 0.8 convolution_bitcast_fusion.6
  6.2 1.0 broadcast_in_dim.32
  7.2 7.3 %all-to-all-start = ((f32[16,32,288]{2,1,0:T(8,128)}), f32[16,32,288]{2,1,0:T(8,128)S(1)}, u32[]{:S(2)}, u32[]{:S(2)}) async-start(f32[16,32,288]{2,1,0:T(8,128)} %broadcast_in_dim.32), calls=%async_computation | async-start | bytes 1572864 | tf_op jit(solution)/shard_map/all_to_all | solution.py:100
  14.9 3.4 %collective-permute-start = (f32[41152]{0:T(1024)S(1)}, f32[41152]{0:T(1024)S(1)}, u32[]{:S(2)}, u32[]{:S(2)}) collective-permute-start(f32[41152]{0:T(1024)S(1)} %concatenate.76), channel_id=1, source_target_pairs={{0,2},{2,4},{4,6},{6,8},{8,10},{10,12},{12,14},{14,16},{16,18},{18... | collective-permute-start | bytes 493832 | tf_op jit(solution)/shard_map/ppermute | solution.py:219
  18.5 4.6 %collective-permute-start.1 = (f32[41152]{0:T(1024)S(1)}, f32[41152]{0:T(1024)S(1)}, u32[]{:S(2)}, u32[]{:S(2)}) collective-permute-start(f32[41152]{0:T(1024)S(1)} %concatenate.77), channel_id=1, source_target_pairs={{2,0},{4,2},{6,4},{8,6},{10,8},{12,10},{14,12},{16,14},{18,16},{20... | collective-permute-start | bytes 493832 | tf_op jit(solution)/shard_map/ppermute | solution.py:220
  23.1 0.7 slice_bitcast_fusion.10
  23.9 0.7 copy.39
  25.0 0.6 constant_dynamic-update-slice_fusion.2
  25.6 5.4 %all-to-all-done = f32[16,32,288]{2,1,0:T(8,128)S(1)} async-done(((f32[16,32,288]{2,1,0:T(8,128)}), f32[16,32,288]{2,1,0:T(8,128)S(1)}, u32[]{:S(2)}, u32[]{:S(2)}) %all-to-all-start) | async-done | bytes 589856 | tf_op jit(solution)/shard_map/all_to_all | solution.py:100
  31.1 0.3 fusion.12
  31.4 0.2 fusion.26
  31.7 0.2 fusion.79
  32.7 0.6 dynamic_slice.147
  33.3 0.8 pad_maximum_fusion.4
  34.1 1.9 %collective-permute-start.3 = (f32[11,32,128]{2,1,0:T(8,128)}, f32[11,32,128]{2,1,0:T(8,128)}, u32[]{:S(2)}, u32[]{:S(2)}) collective-permute-start(f32[11,32,128]{2,1,0:T(8,128)} %get-tuple-element.83), channel_id=1, source_target_pairs={{32,0},{64,32},{96,64},{128,96},{160,128},{192,160},{224,192},{256... | collective-permute-start | bytes 540680 | tf_op jit(solution)/shard_map/ppermute | solution.py:138
  36.0 3.9 %collective-permute-start.2 = (f32[11,32,128]{2,1,0:T(8,128)}, f32[11,32,128]{2,1,0:T(8,128)}, u32[]{:S(2)}, u32[]{:S(2)}) collective-permute-start(f32[11,32,128]{2,1,0:T(8,128)} %get-tuple-element.82), channel_id=1, source_target_pairs={{0,32},{32,64},{64,96},{96,128},{128,160},{160,192},{192,224},{224... | collective-permute-start | bytes 540680 | tf_op jit(solution)/shard_map/ppermute | solution.py:137
  39.9 0.6 broadcast_in_dim.58
  40.5 7.2 %all-to-all-start.1 = ((bf16[4,32,288]{2,1,0:T(8,128)(2,1)}), bf16[4,32,288]{2,1,0:T(8,128)(2,1)}, u32[]{:S(2)}, u32[]{:S(2)}) async-start(bf16[4,32,288]{2,1,0:T(8,128)(2,1)} %broadcast_in_dim.58), calls=%async_computation.1 | async-start | bytes 196608 | tf_op jit(solution)/shard_map/all_to_all | solution.py:100
  47.8 1.6 %gather_fusion.1 = bf16[48,64,128]{2,1,0:T(8,128)(2,1)} fusion(bf16[18,64,128]{2,1,0:T(8,128)(2,1)S(1)} %bitcast.262, s32[1024]{0:T(1024)S(1)} %pad_clamp_fusion.4), kind=kCustom, calls=%fused_computation.1 | custom fusion | bytes 1573056 | tf_op jit(solution)/shard_map/while/body/eval_jaxpr/gather | solution.py:40
  49.4 0.6 gather_fusion
  50.0 0.7 copy.50
  50.7 1.2 %gather_fusion.5 = f32[6,32,128]{2,1,0:T(8,128)} fusion(f32[6,32,128]{2,1,0:T(8,128)S(1)} %pad_maximum_fusion.9, s32[1024]{0:T(1024)S(1)} %get-tuple-element.100), kind=kCustom, calls=%fused_computation.5 | custom fusion | bytes 196632 | tf_op jit(solution)/shard_map/gather | solution.py:244
  51.9 1.2 %gather_fusion.4 = f32[12,32,128]{2,1,0:T(8,128)} fusion(f32[8,32,128]{2,1,0:T(8,128)S(1)} %pad_maximum_fusion.8, s32[1024]{0:T(1024)S(1)} %get-tuple-element.101), kind=kCustom, calls=%fused_computation.4 | custom fusion | bytes 393264 | tf_op jit(solution)/shard_map/gather | solution.py:244
  53.1 0.6 gather_fusion.3
  53.7 0.6 gather_fusion.2
  54.4 1.8 %multiply_reduce_fusion = f32[16,3,64,64]{3,2,1,0:T(8,128)S(1)} fusion(f32[3,16,3,64]{3,2,1,0:T(4,128)} %bitcast.287, f32[3,16,64]{2,1,0:T(8,128)} %dynamic_slice.147), kind=kLoop, calls=%fused_computation.6 | loop fusion | flops 1572864 | bytes 835584 | tf_op jit(solution)/shard_map/while/body/eval_jaxpr/reduce_sum | solution.py:19
  56.2 1.8 %fusion.6 = f32[16,64,128,1]{2,1,3,0:T(8,128)} fusion(bf16[16,3,64,128]{3,2,1,0:T(8,128)(2,1)S(1)} %bitcast.277, f32[16,3,64,64]{3,2,1,0:T(8,128)S(1)} %multiply_reduce_fusion, bf16[16,3]{1,0:T(8,128)(2,1)S(1)} %copy.38), kind=kOutput, calls=%fused_computation.28 | convolution fusion | flops 51707904 | bytes 2097248 | tf_op jit(solution)/shard_map/while/body/eval_jaxpr/gkij,gkjv->giv/dot_general | solution.py:39
  58.0 0.6 dynamic-slice_bitcast_fusion.14
  58.8 1.5 %convolution_bitcast_fusion.4 = f32[2,32,128]{2,1,0:T(8,128)} fusion(f32[2,96,128]{2,1,0:T(8,128)S(1)} %bitcast.286, bf16[1,31,32,96]{3,2,1,0:T(8,128)(2,1)} %param.21), kind=kOutput, calls=%fused_computation.16 | convolution fusion | flops 9437184 | bytes 147456 | tf_op jit(solution)/shard_map/cra,cav->crv/dot_general | solution.py:248
  60.3 1.4 %slice_dynamic-update-slice_fusion.1 = f32[8,32,128]{2,1,0:T(8,128)} fusion(f32[8,32,128]{2,1,0:T(8,128)} %constant_dynamic-update-slice_fusion.2, f32[11,32,128]{2,1,0:T(8,128)} %collective-permute-done.2), kind=kLoop, calls=%fused_computation.118 | loop fusion | bytes 65536
  61.6 0.6 constant_dynamic-update-slice_fusion.1
  62.3 0.9 fusion.147
  63.1 1.5 %fusion.148 = (f32[3,32,128]{2,1,0:T(8,128)S(1)}, f32[3,32,128]{2,1,0:T(8,128)S(1)}, f32[3,32,128]{2,1,0:T(8,128)}) fusion(f32[11,32,128]{2,1,0:T(8,128)} %collective-permute-done.3), kind=kLoop, calls=%fused_computation.250 | loop fusion | bytes 294912 | tf_op jit(solution)/shard_map/slice | solution.py:157
  64.7 1.4 %slice_dynamic-update-slice_fusion = f32[8,32,128]{2,1,0:T(8,128)} fusion(f32[8,32,128]{2,1,0:T(8,128)} %constant_dynamic-update-slice_fusion.1, f32[11,32,128]{2,1,0:T(8,128)} %collective-permute-done.3), kind=kLoop, calls=%fused_computation.117 | loop fusion | bytes 65536
  66.0 0.6 constant_dynamic-update-slice_fusion
  66.7 1.7 %broadcast_in_dim.59 = bf16[4,4,32,288]{3,2,1,0:T(8,128)(2,1)} broadcast(bf16[4,32,288]{2,1,0:T(8,128)(2,1)} %all-to-all-done.1), dimensions={1,2,3} | broadcast | bytes 368640 | tf_op jit(solution)/shard_map/broadcast_in_dim | solution.py:99
  68.3 12.4 %all-to-all-start.2 = ((bf16[4,4,32,288]{3,2,1,0:T(8,128)(2,1)}), bf16[4,4,32,288]{3,2,1,0:T(8,128)(2,1)S(1)}, u32[]{:S(2)}, u32[]{:S(2)}) async-start(bf16[4,4,32,288]{3,2,1,0:T(8,128)(2,1)} %broadcast_in_dim.59), calls=%async_computation.2 | async-start | bytes 786432 | tf_op jit(solution)/shard_map/all_to_all | solution.py:100
  80.9 0.8 fusion.41
  81.6 0.8 dynamic-slice_bitcast_fusion.5
  82.4 0.8 fusion.47
  83.2 0.8 convolution_bitcast_fusion.5
  84.0 21.1 %all-to-all-done.2 = bf16[4,4,32,288]{3,2,1,0:T(8,128)(2,1)S(1)} async-done(((bf16[4,4,32,288]{3,2,1,0:T(8,128)(2,1)}), bf16[4,4,32,288]{3,2,1,0:T(8,128)(2,1)S(1)}, u32[]{:S(2)}, u32[]{:S(2)}) %all-to-all-start.2) | async-done | bytes 294944 | tf_op jit(solution)/shard_map/all_to_all | solution.py:100
  105.6 0.2 fusion.23
  105.8 0.2 fusion.76
  106.3 0.3 convolution_add_fusion.5
  106.7 0.2 fusion.53
  106.9 0.3 convolution_add_fusion.4
  107.2 0.3 convolution_add_fusion.3
  107.5 0.3 convolution_add_fusion.2
  107.8 0.3 convolution_add_fusion.1
  108.1 0.3 fusion.4
  108.6 0.2 fusion.102
  108.8 0.2 fusion.2
  109.0 0.3 fusion.72
  109.3 0.3 fusion.1
  109.6 0.3 fusion.19
  109.9 0.5 fusion
  110.4 0.4 fusion.14
  110.9 0.8 fusion.8
  (125 shorter events, 3.1 us)
Async XLA Ops:
  0.0 6.1 %copy-start.22 = (bf16[1,32,96]{2,1,0:T(8,128)(2,1)S(1)}, bf16[1,32,96]{2,1,0:T(8,128)(2,1)}, u32[]{:S(2)}) copy-start(bf16[1,32,96]{2,1,0:T(8,128)(2,1)} %param.23) | copy-start | bytes 18436
  0.0 6.1 %copy-start.23 = (bf16[1,32,64]{2,1,0:T(8,128)(2,1)S(1)}, bf16[1,32,64]{2,1,0:T(8,128)(2,1)}, u32[]{:S(2)}) copy-start(bf16[1,32,64]{2,1,0:T(8,128)(2,1)} %param.22) | copy-start | bytes 12292
  1.0 1.2 %copy-start.1 = (bf16[32,16,64]{2,1,0:T(8,128)(2,1)}, bf16[32,16,64]{2,1,0:T(8,128)(2,1)S(1)}, u32[]{:S(2)}) copy-start(bf16[32,16,64]{2,1,0:T(8,128)(2,1)S(1)} %reshape.190) | copy-start | bytes 196612
  3.3 11.2 %copy-start = (bf16[1024,128]{1,0:T(8,128)(2,1)S(1)}, bf16[1024,128]{1,0:T(8,128)(2,1)}, u32[]{:S(2)}) copy-start(bf16[1024,128]{1,0:T(8,128)(2,1)} %param.16) | copy-start | bytes 786436
  3.3 11.2 %copy-start.20 = (f32[3,1024]{1,0:T(4,128)S(1)}, f32[3,1024]{1,0:T(4,128)}, u32[]{:S(2)}) copy-start(f32[3,1024]{1,0:T(4,128)} %param.17) | copy-start | bytes 36868
  7.2 16.6 %copy-start.21 = (s32[16,3]{0,1:T(4,128)S(1)}, s32[16,3]{0,1:T(4,128)}, u32[]{:S(2)}) copy-start(s32[16,3]{0,1:T(4,128)} %param.18) | copy-start | bytes 580
  7.2 17.7 %copy-start.26 = (s32[6]{0:T(128)S(1)}, s32[6]{0:T(128)}, u32[]{:S(2)}) copy-start(s32[6]{0:T(128)} %constant.267) | copy-start | bytes 76
  7.2 17.7 %copy-start.27 = (s32[12]{0:T(128)S(1)}, s32[12]{0:T(128)}, u32[]{:S(2)}) copy-start(s32[12]{0:T(128)} %constant.266) | copy-start | bytes 148
  7.2 17.8 %copy-start.24 = (s32[24]{0:T(128)S(1)}, s32[24]{0:T(128)}, u32[]{:S(2)}) copy-start(s32[24]{0:T(128)} %constant.265) | copy-start | bytes 292
  7.2 17.8 %copy-start.25 = (s32[48]{0:T(128)S(1)}, s32[48]{0:T(128)}, u32[]{:S(2)}) copy-start(s32[48]{0:T(128)} %constant.264) | copy-start | bytes 580
  7.2 23.8 %all-to-all-start = ((f32[16,32,288]{2,1,0:T(8,128)}), f32[16,32,288]{2,1,0:T(8,128)S(1)}, u32[]{:S(2)}, u32[]{:S(2)}) async-start(f32[16,32,288]{2,1,0:T(8,128)} %broadcast_in_dim.32), calls=%async_computation | async-start | bytes 1572864 | tf_op jit(solution)/shard_map/all_to_all | solution.py:100
  14.9 17.2 %collective-permute-start = (f32[41152]{0:T(1024)S(1)}, f32[41152]{0:T(1024)S(1)}, u32[]{:S(2)}, u32[]{:S(2)}) collective-permute-start(f32[41152]{0:T(1024)S(1)} %concatenate.76), channel_id=1, source_target_pairs={{0,2},{2,4},{4,6},{6,8},{8,10},{10,12},{12,14},{14,16},{16,18},{18... | collective-permute-start | bytes 493832 | tf_op jit(solution)/shard_map/ppermute | solution.py:219
  18.5 13.6 %collective-permute-start.1 = (f32[41152]{0:T(1024)S(1)}, f32[41152]{0:T(1024)S(1)}, u32[]{:S(2)}, u32[]{:S(2)}) collective-permute-start(f32[41152]{0:T(1024)S(1)} %concatenate.77), channel_id=1, source_target_pairs={{2,0},{4,2},{6,4},{8,6},{10,8},{12,10},{14,12},{16,14},{18,16},{20... | collective-permute-start | bytes 493832 | tf_op jit(solution)/shard_map/ppermute | solution.py:220
  31.8 17.5 %copy-start.6 = (f32[2,32,128]{2,1,0:T(8,128)}, f32[2,32,128]{2,1,0:T(8,128)S(1)}, u32[]{:S(2)}) copy-start(f32[2,32,128]{2,1,0:T(8,128)S(1)} %fusion.79) | copy-start | bytes 98308
  34.1 29.1 %collective-permute-start.3 = (f32[11,32,128]{2,1,0:T(8,128)}, f32[11,32,128]{2,1,0:T(8,128)}, u32[]{:S(2)}, u32[]{:S(2)}) collective-permute-start(f32[11,32,128]{2,1,0:T(8,128)} %get-tuple-element.83), channel_id=1, source_target_pairs={{32,0},{64,32},{96,64},{128,96},{160,128},{192,160},{224,192},{256... | collective-permute-start | bytes 540680 | tf_op jit(solution)/shard_map/ppermute | solution.py:138
  36.0 24.3 %collective-permute-start.2 = (f32[11,32,128]{2,1,0:T(8,128)}, f32[11,32,128]{2,1,0:T(8,128)}, u32[]{:S(2)}, u32[]{:S(2)}) collective-permute-start(f32[11,32,128]{2,1,0:T(8,128)} %get-tuple-element.82), channel_id=1, source_target_pairs={{0,32},{32,64},{64,96},{96,128},{128,160},{160,192},{192,224},{224... | collective-permute-start | bytes 540680 | tf_op jit(solution)/shard_map/ppermute | solution.py:137
  40.5 26.1 %all-to-all-start.1 = ((bf16[4,32,288]{2,1,0:T(8,128)(2,1)}), bf16[4,32,288]{2,1,0:T(8,128)(2,1)}, u32[]{:S(2)}, u32[]{:S(2)}) async-start(bf16[4,32,288]{2,1,0:T(8,128)(2,1)} %broadcast_in_dim.58), calls=%async_computation.1 | async-start | bytes 196608 | tf_op jit(solution)/shard_map/all_to_all | solution.py:100
  54.4 1.8 %copy-start.3 = (bf16[48,64,128]{2,1,0:T(8,128)(2,1)S(1)}, bf16[48,64,128]{2,1,0:T(8,128)(2,1)}, u32[]{:S(2)}) copy-start(bf16[48,64,128]{2,1,0:T(8,128)(2,1)} %gather_fusion.1) | copy-start | bytes 2359300
  56.2 2.6 %copy-start.9 = (f32[6,32,128]{2,1,0:T(8,128)S(1)}, f32[6,32,128]{2,1,0:T(8,128)}, u32[]{:S(2)}) copy-start(f32[6,32,128]{2,1,0:T(8,128)} %gather_fusion.5) | copy-start | bytes 294916
  56.2 5.4 %copy-start.7 = (f32[2,32,128]{2,1,0:T(8,128)S(1)}, f32[2,32,128]{2,1,0:T(8,128)}, u32[]{:S(2)}) copy-start(f32[2,32,128]{2,1,0:T(8,128)} %copy-done.6) | copy-start | bytes 98308
  64.6 18.5 %copy-start.11 = (f32[3,32,128]{2,1,0:T(8,128)S(1)}, f32[3,32,128]{2,1,0:T(8,128)}, u32[]{:S(2)}) copy-start(f32[3,32,128]{2,1,0:T(8,128)} %get-tuple-element.53) | copy-start | bytes 147460
  68.3 36.8 %all-to-all-start.2 = ((bf16[4,4,32,288]{3,2,1,0:T(8,128)(2,1)}), bf16[4,4,32,288]{3,2,1,0:T(8,128)(2,1)S(1)}, u32[]{:S(2)}, u32[]{:S(2)}) async-start(bf16[4,4,32,288]{3,2,1,0:T(8,128)(2,1)} %broadcast_in_dim.59), calls=%async_computation.2 | async-start | bytes 786432 | tf_op jit(solution)/shard_map/all_to_all | solution.py:100
  105.4 1.7 %copy-start.14 = (f32[32,128]{1,0:T(8,128)S(1)}, f32[32,128]{1,0:T(8,128)}, u32[]{:S(2)}) copy-start(f32[32,128]{1,0:T(8,128)} %fusion.47) | copy-start | bytes 49156
  105.4 1.7 %copy-start.19 = (f32[32,64]{1,0:T(8,128)S(1)}, f32[32,64]{1,0:T(8,128)}, u32[]{:S(2)}) copy-start(f32[32,64]{1,0:T(8,128)} %get-tuple-element.35) | copy-start | bytes 24580
  105.5 2.0 %copy-start.13 = (f32[32,128]{1,0:T(8,128)S(1)}, f32[32,128]{1,0:T(8,128)}, u32[]{:S(2)}) copy-start(f32[32,128]{1,0:T(8,128)} %fusion.41) | copy-start | bytes 49156
  105.5 2.0 %copy-start.18 = (f32[32,64]{1,0:T(8,128)S(1)}, f32[32,64]{1,0:T(8,128)}, u32[]{:S(2)}) copy-start(f32[32,64]{1,0:T(8,128)} %get-tuple-element.36) | copy-start | bytes 24580
  105.5 2.3 %copy-start.17 = (f32[32,64]{1,0:T(8,128)S(1)}, f32[32,64]{1,0:T(8,128)}, u32[]{:S(2)}) copy-start(f32[32,64]{1,0:T(8,128)} %get-tuple-element.37) | copy-start | bytes 24580
  105.5 2.6 %copy-start.16 = (f32[32,64]{1,0:T(8,128)S(1)}, f32[32,64]{1,0:T(8,128)}, u32[]{:S(2)}) copy-start(f32[32,64]{1,0:T(8,128)} %get-tuple-element.34) | copy-start | bytes 24580
  105.5 2.9 %copy-start.12 = (f32[2,32,128]{2,1,0:T(8,128)S(1)}, f32[2,32,128]{2,1,0:T(8,128)}, u32[]{:S(2)}) copy-start(f32[2,32,128]{2,1,0:T(8,128)} %convolution_bitcast_fusion.4) | copy-start | bytes 98308
  105.5 2.9 %copy-start.15 = (bf16[64,32]{1,0:T(8,128)(2,1)S(1)}, bf16[64,32]{1,0:T(8,128)(2,1)}, u32[]{:S(2)}) copy-start(bf16[64,32]{1,0:T(8,128)(2,1)} %copy.39) | copy-start | bytes 12292
  105.5 3.0 %copy-start.8 = (bf16[1,15,32,64]{3,2,1,0:T(8,128)(2,1)S(1)}, bf16[1,15,32,64]{3,2,1,0:T(8,128)(2,1)}, u32[]{:S(2)}) copy-start(bf16[1,15,32,64]{3,2,1,0:T(8,128)(2,1)} %param.20) | copy-start | bytes 184324
  105.5 3.3 %copy-start.4 = (f32[12,32,128]{2,1,0:T(8,128)S(1)}, f32[12,32,128]{2,1,0:T(8,128)}, u32[]{:S(2)}) copy-start(f32[12,32,128]{2,1,0:T(8,128)} %gather_fusion.4) | copy-start | bytes 589828
  105.5 3.3 %copy-start.10 = (bf16[1,31,32,96]{3,2,1,0:T(8,128)(2,1)S(1)}, bf16[1,31,32,96]{3,2,1,0:T(8,128)(2,1)}, u32[]{:S(2)}) copy-start(bf16[1,31,32,96]{3,2,1,0:T(8,128)(2,1)} %param.21) | copy-start | bytes 571396
  108.8 1.6 %copy-start.2 = (bf16[32,16,64]{2,1,0:T(8,128)(2,1)S(1)}, bf16[32,16,64]{2,1,0:T(8,128)(2,1)}, u32[]{:S(2)}) copy-start(bf16[32,16,64]{2,1,0:T(8,128)(2,1)} %copy-done.1) | copy-start | bytes 196612
  109.6 1.2 %copy-start.5 = (f32[16,64,128,1]{2,1,3,0:T(8,128)S(1)}, f32[16,64,128,1]{2,1,3,0:T(8,128)}, u32[]{:S(2)}) copy-start(f32[16,64,128,1]{2,1,3,0:T(8,128)} %fusion.6) | copy-start | bytes 1572868

commit v11 on v9

--- a/solution.py
+++ b/solution.py
@@ -123,12 +123,15 @@
     plane_bits = lax.axis_size(PLANE).bit_length() - 1
     plane = lax.axis_index("z")
     seat = lax.axis_index(PLANE)
-    matrices = as_float(jnp.concatenate([upper_transfer[0], upper_coupling[0]], 1))
     columns = device_coef.shape[1]
-    plane_held = spread_gather(jnp.concatenate([device_coef, matrices], 1), PLANE)
+    high = device_coef.astype(jnp.bfloat16)
+    low = (device_coef - high.astype(jnp.float32)).astype(jnp.bfloat16)
+    plane_unit = jnp.concatenate([high, low, upper_transfer[0], upper_coupling[0]], 1)
+    plane_sent = spread_gather(plane_unit, PLANE)
+    plane_held = as_float(plane_sent[:, :, columns:])
     plane_lift = plane_held[:, :, columns : columns + 2 * RANK]
     plane_mix = plane_held[:, :, columns + 2 * RANK :]
-    inner = [plane_held[:, :, :columns]]
+    inner = [as_float(plane_sent[:, :, :columns]) + plane_held[:, :, :columns]]
     for height in range(1, plane_bits + 1):
         inner.append(lift_up(plane_lift[2 ** (height - 1) :: 2**height], inner[-1]))
     tails = jnp.concatenate([level[-3:] for level in inner[:plane_bits]], 0)

time: 95.5 us -> 93.8 us (0.982)
  waiting for transfers between devices: 12.9 us -> 14.9 us
  local copies, waits for them, and re-layouts: 21.2 us -> 19.5 us
  matrix products: 14.3 us -> 12.8 us
    all_to_all x2, waiting for transfers between devices: 12.8 us -> 14.9 us  [spread_gather(): return lax.all_to_all(copies, axis, 0, 0, tiled=True)]
    dot_general x13, matrix products: 4.72 us -> 3.43 us  [product(): return jnp.dot(matrix, operand, precision=HIGHEST)]
    gather x4, local copies, waits for them, and re-layouts: 3.76 us -> 2.55 us  [late(): extended[partner_table(cluster_count) + 2]]
    unnamed x78 -> x76, local copies, waits for them, and re-layouts: 2.3 us -> 2.29 us
  transfers between devices with their start and end apart: 6 -> 6, of which waited for: 2 -> 2; matrix products, arithmetic and copies ran while one was open for 27% -> 22% of each run, Pallas kernels for 0% -> 0%
where the time goes in v11:
time: 93.8 us; the launch traced here: 92.6 us
  starting transfers between devices  38.6 us (41%)
  local copies, waits for them, and re-layouts  19.5 us (21%)
  waiting for transfers between devices  14.9 us (16%)
  matrix products  12.8 us (14%)
  other arithmetic  5.57 us (6%)
  between operations  1.23 us (1%)
    all_to_all x2, starting transfers between devices, spread_gather(): return lax.all_to_all(copies, axis, 0, 0, tiled=True)  23.1 us
    all_to_all x2, waiting for transfers between devices, spread_gather(): return lax.all_to_all(copies, axis, 0, 0, tiled=True)  14.9 us
    ppermute x1, starting transfers between devices, local(): lax.ppermute(head, SPACE, [(i + 1, i) for i in range(count - 1)])  6.66 us
    ppermute x1, starting transfers between devices, upper_tree(): lax.ppermute(tails, 'z', [(i, i + 1) for i in range(planes - 1)])  5.03 us
    dot_general x13, matrix products, product(): return jnp.dot(matrix, operand, precision=HIGHEST)  3.43 us
    gather x4, local copies, waits for them, and re-layouts, late(): extended[partner_table(cluster_count) + 2]  2.55 us
    dot_general x4, matrix products, late(): jnp.einsum('cra,cav->crv', mixers, stacked, precision=HIGHEST)  2.5 us
    unnamed x76, local copies, waits for them, and re-layouts  2.29 us
  transfers between devices with their start and end apart: 6, of which 2 were waited for; matrix products, arithmetic and copies ran while one was open for 22% of the time, Pallas kernels for 0%

profile of v11, /device:TPU:64, one launch (start us, length us, event | category | flops | bytes accessed | tf_op | source)
XLA Modules:
  0.0 92.6 jit_solution(67383670722328827)
XLA Ops:
  0.0 0.8 fusion.152
  0.9 0.7 bitcast_convert_fusion
  1.6 1.0 %reshape.186 = bf16[32,16,64]{2,1,0:T(8,128)(2,1)S(1)} reshape(bf16[32,1024]{1,0:T(8,128)(2,1)} %param.19) | data formatting | bytes 131072 | tf_op jit(solution)/shard_map/reshape | solution.py:197
  2.7 1.2 %fusion.153 = (bf16[16,32,128]{2,1,0:T(8,128)(2,1)S(1)}, f32[16,32,128]{2,1,0:T(8,128)S(1)}) fusion(bf16[16,64,128]{2,1,0:T(8,128)(2,1)} %bitcast.265, bf16[32,16,64]{2,1,0:T(8,128)(2,1)S(1)} %reshape.186), kind=kOutput, calls=%fused_computation.256 | convolution fusion | flops 8454144 | bytes 720896 | tf_op jit(solution)/shard_map/rlp,lpv->lrv/dot_general | solution.py:200
  3.9 1.1 %bitcast_convert_fusion.3 = (bf16[8,32,128]{2,1,0:T(8,128)(2,1)S(1)}, f32[8,128,32]{1,2,0:T(8,128)S(1)}) fusion(f32[8,64,128]{2,1,0:T(8,128)S(1)} %bitcast.266, bf16[1,15,32,64]{3,2,1,0:T(8,128)(2,1)} %param.20), kind=kOutput, calls=%fused_computation.243 | convolution fusion | flops 25198592 | bytes 524288 | tf_op jit(solution)/shard_map/cra,cav->crv/dot_general | solution.py:207
  5.0 0.2 bitcast_convert_fusion.2
  5.1 0.2 fusion.98
  5.5 6.7 %collective-permute-start.1 = (f32[41152]{0:T(1024)S(1)}, f32[41152]{0:T(1024)S(1)}, u32[]{:S(2)}, u32[]{:S(2)}) collective-permute-start(f32[41152]{0:T(1024)S(1)} %concatenate.73), channel_id=1, source_target_pairs={{2,0},{4,2},{6,4},{8,6},{10,8},{12,10},{14,12},{16,14},{18,16},{20... | collective-permute-start | bytes 493832 | tf_op jit(solution)/shard_map/ppermute | solution.py:221
  12.4 1.9 %collective-permute-start = (f32[41152]{0:T(1024)S(1)}, f32[41152]{0:T(1024)}, u32[]{:S(2)}, u32[]{:S(2)}) collective-permute-start(f32[41152]{0:T(1024)S(1)} %concatenate.72), channel_id=1, source_target_pairs={{0,2},{2,4},{4,6},{6,8},{8,10},{10,12},{12,14},{14,16},{16,18},{18... | collective-permute-start | bytes 493832 | tf_op jit(solution)/shard_map/ppermute | solution.py:220
  14.6 0.9 broadcast_in_dim.45
  15.5 8.1 %all-to-all-start = ((bf16[16,32,416]{2,1,0:T(8,128)(2,1)}), bf16[16,32,416]{2,1,0:T(8,128)(2,1)S(1)}, u32[]{:S(2)}, u32[]{:S(2)}) async-start(bf16[16,32,416]{2,1,0:T(8,128)(2,1)} %broadcast_in_dim.45), calls=%async_computation | async-start | bytes 1048576 | tf_op jit(solution)/shard_map/all_to_all | solution.py:99
  23.8 0.7 copy.38
  24.8 0.6 pad_clamp_fusion.2
  25.4 0.6 pad_clamp_fusion
  26.0 0.6 constant_dynamic-update-slice_fusion.2
  26.6 8.0 %all-to-all-done = bf16[16,32,416]{2,1,0:T(8,128)(2,1)S(1)} async-done(((bf16[16,32,416]{2,1,0:T(8,128)(2,1)}), bf16[16,32,416]{2,1,0:T(8,128)(2,1)S(1)}, u32[]{:S(2)}, u32[]{:S(2)}) %all-to-all-start) | async-done | bytes 426016 | tf_op jit(solution)/shard_map/all_to_all | solution.py:99
  34.7 0.3 fusion.24
  34.9 0.2 fusion.77
  35.1 0.2 fusion.101
  35.5 0.7 slice.332
  36.1 0.8 fusion.81
  36.9 1.6 %fusion.148 = (f32[8192]{0:T(1024)}, f32[8192]{0:T(1024)}, f32[8192]{0:T(1024)}, f32[8192]{0:T(1024)}) fusion(f32[41152]{0:T(1024)} %collective-permute-done), kind=kLoop, calls=%fused_computation.251 | loop fusion | bytes 262144 | tf_op jit(solution)/shard_map/slice | solution.py:244
  38.5 0.7 fusion.149
  39.6 0.6 dynamic_slice.147
  40.3 0.6 gather_fusion
  40.9 0.8 pad_maximum_fusion.4
  41.7 5.0 %collective-permute-start.2 = (f32[11,32,128]{2,1,0:T(8,128)}, f32[11,32,128]{2,1,0:T(8,128)}, u32[]{:S(2)}, u32[]{:S(2)}) collective-permute-start(f32[11,32,128]{2,1,0:T(8,128)} %get-tuple-element.84), channel_id=1, source_target_pairs={{0,32},{32,64},{64,96},{96,128},{128,160},{160,192},{192,224},{224... | collective-permute-start | bytes 540680 | tf_op jit(solution)/shard_map/ppermute | solution.py:139
  46.7 1.9 %collective-permute-start.3 = (f32[11,32,128]{2,1,0:T(8,128)}, f32[11,32,128]{2,1,0:T(8,128)}, u32[]{:S(2)}, u32[]{:S(2)}) collective-permute-start(f32[11,32,128]{2,1,0:T(8,128)} %get-tuple-element.85), channel_id=1, source_target_pairs={{32,0},{64,32},{96,64},{128,96},{160,128},{192,160},{224,192},{256... | collective-permute-start | bytes 540680 | tf_op jit(solution)/shard_map/ppermute | solution.py:140
  48.7 0.8 broadcast_in_dim.52
  49.5 15.0 %all-to-all-start.1 = ((bf16[16,32,288]{2,1,0:T(8,128)(2,1)}), bf16[16,32,288]{2,1,0:T(8,128)(2,1)S(1)}, u32[]{:S(2)}, u32[]{:S(2)}) async-start(bf16[16,32,288]{2,1,0:T(8,128)(2,1)} %broadcast_in_dim.52), calls=%async_computation.1 | async-start | bytes 786432 | tf_op jit(solution)/shard_map/all_to_all | solution.py:99
  64.6 1.6 %gather_fusion.1 = bf16[48,64,128]{2,1,0:T(8,128)(2,1)} fusion(bf16[18,64,128]{2,1,0:T(8,128)(2,1)S(1)} %bitcast.262, s32[1024]{0:T(1024)S(1)} %pad_clamp_fusion.4), kind=kCustom, calls=%fused_computation.1 | custom fusion | bytes 1573056 | tf_op jit(solution)/shard_map/while/body/eval_jaxpr/gather | solution.py:40
  66.2 0.7 gather_fusion.5
  66.9 0.6 gather_fusion.4
  67.6 0.6 gather_fusion.3
  68.1 0.7 gather_fusion.2
  68.9 1.7 %multiply_reduce_fusion = f32[16,3,64,64]{3,2,1,0:T(8,128)S(1)} fusion(f32[3,16,3,64]{3,2,1,0:T(4,128)S(1)} %bitcast.283, f32[3,16,64]{2,1,0:T(8,128)} %dynamic_slice.147), kind=kLoop, calls=%fused_computation.6 | loop fusion | flops 1572864 | bytes 835584 | tf_op jit(solution)/shard_map/while/body/eval_jaxpr/reduce_sum | solution.py:19
  70.6 1.8 %fusion.6 = f32[16,64,128,1]{2,1,3,0:T(8,128)} fusion(bf16[16,3,64,128]{3,2,1,0:T(8,128)(2,1)S(1)} %bitcast.274, f32[16,3,64,64]{3,2,1,0:T(8,128)S(1)} %multiply_reduce_fusion, bf16[16,3]{1,0:T(8,128)(2,1)S(1)} %copy-done.31), kind=kOutput, calls=%fused_computation.28 | convolution fusion | flops 51707904 | bytes 2097248 | tf_op jit(solution)/shard_map/while/body/eval_jaxpr/gkij,gkjv->giv/dot_general | solution.py:39
  72.4 0.6 dynamic-slice_bitcast_fusion.14
  73.1 1.5 %convolution_bitcast_fusion.4 = f32[2,32,128]{2,1,0:T(8,128)} fusion(f32[2,96,128]{2,1,0:T(8,128)S(1)} %bitcast.284, bf16[1,31,32,96]{3,2,1,0:T(8,128)(2,1)} %param.21), kind=kOutput, calls=%fused_computation.16 | convolution fusion | flops 9437184 | bytes 147456 | tf_op jit(solution)/shard_map/cra,cav->crv/dot_general | solution.py:249
  74.7 0.8 slice_dynamic-update-slice_fusion.1
  75.4 0.8 slice_dynamic-update-slice_fusion
  76.2 0.9 fusion.146
  77.1 0.9 fusion.147
  78.5 0.8 convolution_bitcast_fusion.5
  79.4 7.0 %all-to-all-done.1 = bf16[16,32,288]{2,1,0:T(8,128)(2,1)S(1)} async-done(((bf16[16,32,288]{2,1,0:T(8,128)(2,1)}), bf16[16,32,288]{2,1,0:T(8,128)(2,1)S(1)}, u32[]{:S(2)}, u32[]{:S(2)}) %all-to-all-start.1) | async-done | bytes 294944 | tf_op jit(solution)/shard_map/all_to_all | solution.py:99
  86.5 0.2 fusion.21
  86.6 0.2 fusion.74
  87.2 0.1 fusion.57
  87.3 0.3 convolution_add_fusion.5
  87.7 0.2 fusion.51
  87.9 0.3 convolution_add_fusion.4
  88.2 0.3 convolution_add_fusion.3
  88.5 0.3 convolution_add_fusion.2
  88.8 0.3 convolution_add_fusion.1
  89.1 0.3 fusion.4
  89.4 0.1 fusion.3
  89.5 0.2 fusion.96
  89.8 0.2 fusion.2
  90.0 0.3 fusion.70
  90.3 0.3 fusion.1
  90.6 0.3 fusion.17
  90.9 0.5 fusion
  91.4 0.4 fusion.12
  91.8 0.8 fusion.8
  (139 shorter events, 3.0 us)
Async XLA Ops:
  0.0 4.9 %copy-start.8 = (bf16[1,15,32,64]{3,2,1,0:T(8,128)(2,1)S(1)}, bf16[1,15,32,64]{3,2,1,0:T(8,128)(2,1)}, u32[]{:S(2)}) copy-start(bf16[1,15,32,64]{3,2,1,0:T(8,128)(2,1)} %param.20) | copy-start | bytes 184324
  0.0 14.5 %copy-start.29 = (bf16[1,32,96]{2,1,0:T(8,128)(2,1)S(1)}, bf16[1,32,96]{2,1,0:T(8,128)(2,1)}, u32[]{:S(2)}) copy-start(bf16[1,32,96]{2,1,0:T(8,128)(2,1)} %param.23) | copy-start | bytes 18436
  0.0 14.5 %copy-start.30 = (bf16[1,32,64]{2,1,0:T(8,128)(2,1)S(1)}, bf16[1,32,64]{2,1,0:T(8,128)(2,1)}, u32[]{:S(2)}) copy-start(bf16[1,32,64]{2,1,0:T(8,128)(2,1)} %param.22) | copy-start | bytes 12292
  2.6 12.8 %copy-start.2 = (bf16[32,16,64]{2,1,0:T(8,128)(2,1)}, bf16[32,16,64]{2,1,0:T(8,128)(2,1)S(1)}, u32[]{:S(2)}) copy-start(bf16[32,16,64]{2,1,0:T(8,128)(2,1)S(1)} %reshape.186) | copy-start | bytes 196612
  5.3 18.4 %copy-start.28 = (s32[16,3]{0,1:T(4,128)S(1)}, s32[16,3]{0,1:T(4,128)}, u32[]{:S(2)}) copy-start(s32[16,3]{0,1:T(4,128)} %param.18) | copy-start | bytes 580
  5.3 19.4 %copy-start.34 = (s32[24]{0:T(128)S(1)}, s32[24]{0:T(128)}, u32[]{:S(2)}) copy-start(s32[24]{0:T(128)} %constant.261) | copy-start | bytes 292
  5.3 19.4 %copy-start.35 = (s32[48]{0:T(128)S(1)}, s32[48]{0:T(128)}, u32[]{:S(2)}) copy-start(s32[48]{0:T(128)} %constant.260) | copy-start | bytes 580
  5.4 20.0 %copy-start.32 = (s32[6]{0:T(128)S(1)}, s32[6]{0:T(128)}, u32[]{:S(2)}) copy-start(s32[6]{0:T(128)} %constant.263) | copy-start | bytes 76
  5.4 20.0 %copy-start.33 = (s32[12]{0:T(128)S(1)}, s32[12]{0:T(128)}, u32[]{:S(2)}) copy-start(s32[12]{0:T(128)} %constant.262) | copy-start | bytes 148
  5.5 29.9 %collective-permute-start.1 = (f32[41152]{0:T(1024)S(1)}, f32[41152]{0:T(1024)S(1)}, u32[]{:S(2)}, u32[]{:S(2)}) collective-permute-start(f32[41152]{0:T(1024)S(1)} %concatenate.73), channel_id=1, source_target_pairs={{2,0},{4,2},{6,4},{8,6},{10,8},{12,10},{14,12},{16,14},{18,16},{20... | collective-permute-start | bytes 493832 | tf_op jit(solution)/shard_map/ppermute | solution.py:221
  12.4 23.0 %collective-permute-start = (f32[41152]{0:T(1024)S(1)}, f32[41152]{0:T(1024)}, u32[]{:S(2)}, u32[]{:S(2)}) collective-permute-start(f32[41152]{0:T(1024)S(1)} %concatenate.72), channel_id=1, source_target_pairs={{0,2},{2,4},{4,6},{6,8},{8,10},{10,12},{12,14},{14,16},{16,18},{18... | collective-permute-start | bytes 493832 | tf_op jit(solution)/shard_map/ppermute | solution.py:220
  15.5 19.1 %all-to-all-start = ((bf16[16,32,416]{2,1,0:T(8,128)(2,1)}), bf16[16,32,416]{2,1,0:T(8,128)(2,1)S(1)}, u32[]{:S(2)}, u32[]{:S(2)}) async-start(bf16[16,32,416]{2,1,0:T(8,128)(2,1)} %broadcast_in_dim.45), calls=%async_computation | async-start | bytes 1048576 | tf_op jit(solution)/shard_map/all_to_all | solution.py:99
  34.6 5.6 %copy-start.1 = (f32[16,32,288]{2,1,0:T(8,128)}, f32[16,32,288]{2,1,0:T(8,128)S(1)}, u32[]{:S(2)}) copy-start(f32[16,32,288]{2,1,0:T(8,128)S(1)} %slice_convert_fusion) | copy-start | bytes 1769476
  34.6 4.8 %copy-start.25 = (f32[3,1024]{1,0:T(4,128)S(1)}, f32[3,1024]{1,0:T(4,128)}, u32[]{:S(2)}) copy-start(f32[3,1024]{1,0:T(4,128)} %param.17) | copy-start | bytes 36868
  35.3 6.4 %copy-start.6 = (f32[2,32,128]{2,1,0:T(8,128)}, f32[2,32,128]{2,1,0:T(8,128)S(1)}, u32[]{:S(2)}) copy-start(f32[2,32,128]{2,1,0:T(8,128)S(1)} %fusion.101) | copy-start | bytes 98308
  39.2 25.2 %copy-start = (bf16[1024,128]{1,0:T(8,128)(2,1)S(1)}, bf16[1024,128]{1,0:T(8,128)(2,1)}, u32[]{:S(2)}) copy-start(bf16[1024,128]{1,0:T(8,128)(2,1)} %param.16) | copy-start | bytes 786436
  41.7 32.9 %collective-permute-start.2 = (f32[11,32,128]{2,1,0:T(8,128)}, f32[11,32,128]{2,1,0:T(8,128)}, u32[]{:S(2)}, u32[]{:S(2)}) collective-permute-start(f32[11,32,128]{2,1,0:T(8,128)} %get-tuple-element.84), channel_id=1, source_target_pairs={{0,32},{32,64},{64,96},{96,128},{128,160},{160,192},{192,224},{224... | collective-permute-start | bytes 540680 | tf_op jit(solution)/shard_map/ppermute | solution.py:139
  46.7 28.7 %collective-permute-start.3 = (f32[11,32,128]{2,1,0:T(8,128)}, f32[11,32,128]{2,1,0:T(8,128)}, u32[]{:S(2)}, u32[]{:S(2)}) collective-permute-start(f32[11,32,128]{2,1,0:T(8,128)} %get-tuple-element.85), channel_id=1, source_target_pairs={{32,0},{64,32},{96,64},{128,96},{160,128},{192,160},{224,192},{256... | collective-permute-start | bytes 540680 | tf_op jit(solution)/shard_map/ppermute | solution.py:140
  49.5 16.7 %copy-start.14 = (f32[8192]{0:T(1024)S(1)}, f32[8192]{0:T(1024)}, u32[]{:S(2)}) copy-start(f32[8192]{0:T(1024)} %get-tuple-element.56) | copy-start | bytes 98308
  49.5 16.7 %copy-start.15 = (f32[8192]{0:T(1024)S(1)}, f32[8192]{0:T(1024)}, u32[]{:S(2)}) copy-start(f32[8192]{0:T(1024)} %get-tuple-element.60) | copy-start | bytes 98308
  49.5 36.9 %all-to-all-start.1 = ((bf16[16,32,288]{2,1,0:T(8,128)(2,1)}), bf16[16,32,288]{2,1,0:T(8,128)(2,1)S(1)}, u32[]{:S(2)}, u32[]{:S(2)}) async-start(bf16[16,32,288]{2,1,0:T(8,128)(2,1)} %broadcast_in_dim.52), calls=%async_computation.1 | async-start | bytes 786432 | tf_op jit(solution)/shard_map/all_to_all | solution.py:99
  64.5 1.7 %copy-start.16 = (f32[8192]{0:T(1024)S(1)}, f32[8192]{0:T(1024)}, u32[]{:S(2)}) copy-start(f32[8192]{0:T(1024)} %get-tuple-element.57) | copy-start | bytes 98308
  64.5 1.7 %copy-start.17 = (f32[8192]{0:T(1024)S(1)}, f32[8192]{0:T(1024)}, u32[]{:S(2)}) copy-start(f32[8192]{0:T(1024)} %get-tuple-element.61) | copy-start | bytes 98308
  64.5 2.4 %copy-start.18 = (f32[8192]{0:T(1024)S(1)}, f32[8192]{0:T(1024)}, u32[]{:S(2)}) copy-start(f32[8192]{0:T(1024)} %get-tuple-element.58) | copy-start | bytes 98308
  64.5 2.4 %copy-start.19 = (f32[8192]{0:T(1024)S(1)}, f32[8192]{0:T(1024)}, u32[]{:S(2)}) copy-start(f32[8192]{0:T(1024)} %get-tuple-element.62) | copy-start | bytes 98308
  64.5 2.4 %copy-start.27 = (s32[1024]{0:T(1024)S(1)}, s32[1024]{0:T(1024)}, u32[]{:S(2)}) copy-start(s32[1024]{0:T(1024)} %get-tuple-element.103) | copy-start | bytes 12292
  64.5 3.0 %copy-start.12 = (f32[8192]{0:T(1024)S(1)}, f32[8192]{0:T(1024)}, u32[]{:S(2)}) copy-start(f32[8192]{0:T(1024)} %get-tuple-element.59) | copy-start | bytes 98308
  64.6 3.0 %copy-start.13 = (f32[8192]{0:T(1024)S(1)}, f32[8192]{0:T(1024)}, u32[]{:S(2)}) copy-start(f32[8192]{0:T(1024)} %get-tuple-element.63) | copy-start | bytes 98308
  64.6 3.0 %copy-start.26 = (s32[1024]{0:T(1024)S(1)}, s32[1024]{0:T(1024)}, u32[]{:S(2)}) copy-start(s32[1024]{0:T(1024)} %get-tuple-element.104) | copy-start | bytes 12292
  68.9 1.7 %copy-start.4 = (bf16[48,64,128]{2,1,0:T(8,128)(2,1)S(1)}, bf16[48,64,128]{2,1,0:T(8,128)(2,1)}, u32[]{:S(2)}) copy-start(bf16[48,64,128]{2,1,0:T(8,128)(2,1)} %gather_fusion.1) | copy-start | bytes 2359300
  68.9 1.7 %copy-start.31 = (bf16[16,3]{1,0:T(8,128)(2,1)S(1)}, bf16[16,3]{1,0:T(8,128)(2,1)}, u32[]{:S(2)}) copy-start(bf16[16,3]{1,0:T(8,128)(2,1)} %copy.38) | copy-start | bytes 292
  70.6 1.8 %slice-start = ((f32[16,32,288]{2,1,0:T(8,128)}), f32[16,32,64]{2,1,0:T(8,128)S(1)}, s32[]{:S(2)}) async-start(f32[16,32,288]{2,1,0:T(8,128)} %copy-done.1), calls=%async_computation.2 | async-start | bytes 524288 | tf_op jit(solution)/shard_map/slice | solution.py:132
  70.6 4.1 %copy-start.24 = (f32[8,32,128]{2,1,0:T(8,128)S(1)}, f32[8,32,128]{2,1,0:T(8,128)}, u32[]{:S(2)}) copy-start(f32[8,32,128]{2,1,0:T(8,128)} %constant_dynamic-update-slice_fusion.2) | copy-start | bytes 393220
  70.6 4.8 %copy-start.7 = (f32[2,32,128]{2,1,0:T(8,128)S(1)}, f32[2,32,128]{2,1,0:T(8,128)}, u32[]{:S(2)}) copy-start(f32[2,32,128]{2,1,0:T(8,128)} %copy-done.6) | copy-start | bytes 98308
  86.4 1.8 %copy-start.23 = (f32[32,64]{1,0:T(8,128)S(1)}, f32[32,64]{1,0:T(8,128)}, u32[]{:S(2)}) copy-start(f32[32,64]{1,0:T(8,128)} %get-tuple-element.35) | copy-start | bytes 24580
  86.4 2.1 %copy-start.22 = (f32[32,64]{1,0:T(8,128)S(1)}, f32[32,64]{1,0:T(8,128)}, u32[]{:S(2)}) copy-start(f32[32,64]{1,0:T(8,128)} %get-tuple-element.36) | copy-start | bytes 24580
  86.4 2.4 %copy-start.21 = (f32[32,64]{1,0:T(8,128)S(1)}, f32[32,64]{1,0:T(8,128)}, u32[]{:S(2)}) copy-start(f32[32,64]{1,0:T(8,128)} %get-tuple-element.37) | copy-start | bytes 24580
  86.4 2.6 %copy-start.20 = (f32[32,64]{1,0:T(8,128)S(1)}, f32[32,64]{1,0:T(8,128)}, u32[]{:S(2)}) copy-start(f32[32,64]{1,0:T(8,128)} %get-tuple-element.34) | copy-start | bytes 24580
  86.4 2.9 %copy-start.11 = (f32[2,32,128]{2,1,0:T(8,128)S(1)}, f32[2,32,128]{2,1,0:T(8,128)}, u32[]{:S(2)}) copy-start(f32[2,32,128]{2,1,0:T(8,128)} %convolution_bitcast_fusion.4) | copy-start | bytes 98308
  86.5 3.1 %copy-start.9 = (bf16[1,15,32,64]{3,2,1,0:T(8,128)(2,1)S(1)}, bf16[1,15,32,64]{3,2,1,0:T(8,128)(2,1)}, u32[]{:S(2)}) copy-start(bf16[1,15,32,64]{3,2,1,0:T(8,128)(2,1)} %param.20) | copy-start | bytes 184324
  86.6 3.2 %copy-start.10 = (bf16[1,31,32,96]{3,2,1,0:T(8,128)(2,1)S(1)}, bf16[1,31,32,96]{3,2,1,0:T(8,128)(2,1)}, u32[]{:S(2)}) copy-start(bf16[1,31,32,96]{3,2,1,0:T(8,128)(2,1)} %param.21) | copy-start | bytes 571396
  89.8 1.6 %copy-start.3 = (bf16[32,16,64]{2,1,0:T(8,128)(2,1)S(1)}, bf16[32,16,64]{2,1,0:T(8,128)(2,1)}, u32[]{:S(2)}) copy-start(bf16[32,16,64]{2,1,0:T(8,128)(2,1)} %copy-done.2) | copy-start | bytes 196612
  90.6 1.2 %copy-start.5 = (f32[16,64,128,1]{2,1,3,0:T(8,128)S(1)}, f32[16,64,128,1]{2,1,3,0:T(8,128)}, u32[]{:S(2)}) copy-start(f32[16,64,128,1]{2,1,3,0:T(8,128)} %fusion.6) | copy-start | bytes 1572868

commit v12 on v11

--- a/solution.py
+++ b/solution.py
@@ -124,8 +124,9 @@
     plane = lax.axis_index("z")
     seat = lax.axis_index(PLANE)
     columns = device_coef.shape[1]
-    high = device_coef.astype(jnp.bfloat16)
-    low = (device_coef - high.astype(jnp.float32)).astype(jnp.bfloat16)
+    rounded = lax.reduce_precision(device_coef, exponent_bits=8, mantissa_bits=7)
+    high = rounded.astype(jnp.bfloat16)
+    low = (device_coef - rounded).astype(jnp.bfloat16)
     plane_unit = jnp.concatenate([high, low, upper_transfer[0], upper_coupling[0]], 1)
     plane_sent = spread_gather(plane_unit, PLANE)
     plane_held = as_float(plane_sent[:, :, columns:])

time: 93.8 us -> 93.8 us (level)
  no operation moved by 1% of the time
where the time goes in v12:
time: 93.8 us; the launch traced here: 92.6 us
  starting transfers between devices  38.6 us (41%)
  local copies, waits for them, and re-layouts  19.5 us (21%)
  waiting for transfers between devices  14.9 us (16%)
  matrix products  12.8 us (14%)
  other arithmetic  5.57 us (6%)
  between operations  1.23 us (1%)
    all_to_all x2, starting transfers between devices, spread_gather(): return lax.all_to_all(copies, axis, 0, 0, tiled=True)  23.1 us
    all_to_all x2, waiting for transfers between devices, spread_gather(): return lax.all_to_all(copies, axis, 0, 0, tiled=True)  14.9 us
    ppermute x1, starting transfers between devices, local(): lax.ppermute(head, SPACE, [(i + 1, i) for i in range(count - 1)])  6.66 us
    ppermute x1, starting transfers between devices, upper_tree(): lax.ppermute(tails, 'z', [(i, i + 1) for i in range(planes - 1)])  5.03 us
    dot_general x13, matrix products, product(): return jnp.dot(matrix, operand, precision=HIGHEST)  3.43 us
    gather x4, local copies, waits for them, and re-layouts, late(): extended[partner_table(cluster_count) + 2]  2.55 us
    dot_general x4, matrix products, late(): jnp.einsum('cra,cav->crv', mixers, stacked, precision=HIGHEST)  2.5 us
    unnamed x76, local copies, waits for them, and re-layouts  2.29 us
  transfers between devices with their start and end apart: 6, of which 2 were waited for; matrix products, arithmetic and copies ran while one was open for 22% of the time, Pallas kernels for 0%

profile of v12, /device:TPU:64, one launch (start us, length us, event | category | flops | bytes accessed | tf_op | source)
XLA Modules:
  0.0 92.6 jit_solution(1710970807553938650)
XLA Ops:
  0.0 0.8 fusion.153
  0.9 0.7 bitcast_convert_fusion
  1.6 1.0 %reshape.186 = bf16[32,16,64]{2,1,0:T(8,128)(2,1)S(1)} reshape(bf16[32,1024]{1,0:T(8,128)(2,1)} %param.19) | data formatting | bytes 131072 | tf_op jit(solution)/shard_map/reshape | solution.py:198
  2.7 1.2 %fusion.154 = (bf16[16,32,128]{2,1,0:T(8,128)(2,1)S(1)}, f32[16,32,128]{2,1,0:T(8,128)S(1)}) fusion(bf16[16,64,128]{2,1,0:T(8,128)(2,1)} %bitcast.265, bf16[32,16,64]{2,1,0:T(8,128)(2,1)S(1)} %reshape.186), kind=kOutput, calls=%fused_computation.258 | convolution fusion | flops 8454144 | bytes 720896 | tf_op jit(solution)/shard_map/rlp,lpv->lrv/dot_general | solution.py:201
  3.9 1.1 %bitcast_convert_fusion.3 = (bf16[8,32,128]{2,1,0:T(8,128)(2,1)S(1)}, f32[8,128,32]{1,2,0:T(8,128)S(1)}) fusion(f32[8,64,128]{2,1,0:T(8,128)S(1)} %bitcast.266, bf16[1,15,32,64]{3,2,1,0:T(8,128)(2,1)} %param.20), kind=kOutput, calls=%fused_computation.245 | convolution fusion | flops 25198592 | bytes 524288 | tf_op jit(solution)/shard_map/cra,cav->crv/dot_general | solution.py:208
  5.0 0.2 bitcast_convert_fusion.2
  5.1 0.2 fusion.99
  5.5 6.7 %collective-permute-start.1 = (f32[41152]{0:T(1024)S(1)}, f32[41152]{0:T(1024)S(1)}, u32[]{:S(2)}, u32[]{:S(2)}) collective-permute-start(f32[41152]{0:T(1024)S(1)} %concatenate.73), channel_id=1, source_target_pairs={{2,0},{4,2},{6,4},{8,6},{10,8},{12,10},{14,12},{16,14},{18,16},{20... | collective-permute-start | bytes 493832 | tf_op jit(solution)/shard_map/ppermute | solution.py:222
  12.4 1.9 %collective-permute-start = (f32[41152]{0:T(1024)S(1)}, f32[41152]{0:T(1024)}, u32[]{:S(2)}, u32[]{:S(2)}) collective-permute-start(f32[41152]{0:T(1024)S(1)} %concatenate.72), channel_id=1, source_target_pairs={{0,2},{2,4},{4,6},{6,8},{8,10},{10,12},{12,14},{14,16},{16,18},{18... | collective-permute-start | bytes 493832 | tf_op jit(solution)/shard_map/ppermute | solution.py:221
  14.6 0.9 broadcast_in_dim.45
  15.5 8.1 %all-to-all-start = ((bf16[16,32,416]{2,1,0:T(8,128)(2,1)}), bf16[16,32,416]{2,1,0:T(8,128)(2,1)S(1)}, u32[]{:S(2)}, u32[]{:S(2)}) async-start(bf16[16,32,416]{2,1,0:T(8,128)(2,1)} %broadcast_in_dim.45), calls=%async_computation | async-start | bytes 1048576 | tf_op jit(solution)/shard_map/all_to_all | solution.py:99
  23.8 0.7 copy.38
  24.8 0.6 pad_clamp_fusion.2
  25.4 0.6 pad_clamp_fusion
  26.0 0.6 constant_dynamic-update-slice_fusion.2
  26.6 8.0 %all-to-all-done = bf16[16,32,416]{2,1,0:T(8,128)(2,1)S(1)} async-done(((bf16[16,32,416]{2,1,0:T(8,128)(2,1)}), bf16[16,32,416]{2,1,0:T(8,128)(2,1)S(1)}, u32[]{:S(2)}, u32[]{:S(2)}) %all-to-all-start) | async-done | bytes 426016 | tf_op jit(solution)/shard_map/all_to_all | solution.py:99
  34.7 0.3 fusion.24
  34.9 0.2 fusion.77
  35.1 0.2 fusion.102
  35.5 0.7 slice.332
  36.1 0.8 fusion.82
  36.9 1.6 %fusion.149 = (f32[8192]{0:T(1024)}, f32[8192]{0:T(1024)}, f32[8192]{0:T(1024)}, f32[8192]{0:T(1024)}) fusion(f32[41152]{0:T(1024)} %collective-permute-done), kind=kLoop, calls=%fused_computation.253 | loop fusion | bytes 262144 | tf_op jit(solution)/shard_map/slice | solution.py:245
  38.5 0.7 fusion.150
  39.6 0.6 dynamic_slice.147
  40.3 0.6 gather_fusion
  40.9 0.8 pad_maximum_fusion.4
  41.7 5.0 %collective-permute-start.2 = (f32[11,32,128]{2,1,0:T(8,128)}, f32[11,32,128]{2,1,0:T(8,128)}, u32[]{:S(2)}, u32[]{:S(2)}) collective-permute-start(f32[11,32,128]{2,1,0:T(8,128)} %get-tuple-element.82), channel_id=1, source_target_pairs={{0,32},{32,64},{64,96},{96,128},{128,160},{160,192},{192,224},{224... | collective-permute-start | bytes 540680 | tf_op jit(solution)/shard_map/ppermute | solution.py:140
  46.8 1.9 %collective-permute-start.3 = (f32[11,32,128]{2,1,0:T(8,128)}, f32[11,32,128]{2,1,0:T(8,128)}, u32[]{:S(2)}, u32[]{:S(2)}) collective-permute-start(f32[11,32,128]{2,1,0:T(8,128)} %get-tuple-element.83), channel_id=1, source_target_pairs={{32,0},{64,32},{96,64},{128,96},{160,128},{192,160},{224,192},{256... | collective-permute-start | bytes 540680 | tf_op jit(solution)/shard_map/ppermute | solution.py:141
  48.7 0.8 broadcast_in_dim.52
  49.5 15.0 %all-to-all-start.1 = ((bf16[16,32,288]{2,1,0:T(8,128)(2,1)}), bf16[16,32,288]{2,1,0:T(8,128)(2,1)S(1)}, u32[]{:S(2)}, u32[]{:S(2)}) async-start(bf16[16,32,288]{2,1,0:T(8,128)(2,1)} %broadcast_in_dim.52), calls=%async_computation.1 | async-start | bytes 786432 | tf_op jit(solution)/shard_map/all_to_all | solution.py:99
  64.6 1.6 %gather_fusion.1 = bf16[48,64,128]{2,1,0:T(8,128)(2,1)} fusion(bf16[18,64,128]{2,1,0:T(8,128)(2,1)S(1)} %bitcast.262, s32[1024]{0:T(1024)S(1)} %pad_clamp_fusion.4), kind=kCustom, calls=%fused_computation.1 | custom fusion | bytes 1573056 | tf_op jit(solution)/shard_map/while/body/eval_jaxpr/gather | solution.py:40
  66.2 0.7 gather_fusion.5
  66.9 0.6 gather_fusion.4
  67.6 0.6 gather_fusion.3
  68.2 0.7 gather_fusion.2
  68.9 1.7 %multiply_reduce_fusion = f32[16,3,64,64]{3,2,1,0:T(8,128)S(1)} fusion(f32[3,16,3,64]{3,2,1,0:T(4,128)S(1)} %bitcast.283, f32[3,16,64]{2,1,0:T(8,128)} %dynamic_slice.147), kind=kLoop, calls=%fused_computation.6 | loop fusion | flops 1572864 | bytes 835584 | tf_op jit(solution)/shard_map/while/body/eval_jaxpr/reduce_sum | solution.py:19
  70.6 1.8 %fusion.6 = f32[16,64,128,1]{2,1,3,0:T(8,128)} fusion(bf16[16,3,64,128]{3,2,1,0:T(8,128)(2,1)S(1)} %bitcast.274, f32[16,3,64,64]{3,2,1,0:T(8,128)S(1)} %multiply_reduce_fusion, bf16[16,3]{1,0:T(8,128)(2,1)S(1)} %copy-done.31), kind=kOutput, calls=%fused_computation.28 | convolution fusion | flops 51707904 | bytes 2097248 | tf_op jit(solution)/shard_map/while/body/eval_jaxpr/gkij,gkjv->giv/dot_general | solution.py:39
  72.4 0.6 dynamic-slice_bitcast_fusion.14
  73.1 1.5 %convolution_bitcast_fusion.4 = f32[2,32,128]{2,1,0:T(8,128)} fusion(f32[2,96,128]{2,1,0:T(8,128)S(1)} %bitcast.284, bf16[1,31,32,96]{3,2,1,0:T(8,128)(2,1)} %param.21), kind=kOutput, calls=%fused_computation.16 | convolution fusion | flops 9437184 | bytes 147456 | tf_op jit(solution)/shard_map/cra,cav->crv/dot_general | solution.py:250
  74.7 0.8 slice_dynamic-update-slice_fusion.1
  75.4 0.8 slice_dynamic-update-slice_fusion
  76.2 0.9 fusion.147
  77.1 0.9 fusion.148
  78.5 0.8 convolution_bitcast_fusion.5
  79.4 7.0 %all-to-all-done.1 = bf16[16,32,288]{2,1,0:T(8,128)(2,1)S(1)} async-done(((bf16[16,32,288]{2,1,0:T(8,128)(2,1)}), bf16[16,32,288]{2,1,0:T(8,128)(2,1)S(1)}, u32[]{:S(2)}, u32[]{:S(2)}) %all-to-all-start.1) | async-done | bytes 294944 | tf_op jit(solution)/shard_map/all_to_all | solution.py:99
  86.5 0.2 fusion.21
  86.6 0.2 fusion.74
  87.2 0.1 fusion.57
  87.3 0.3 convolution_add_fusion.5
  87.7 0.2 fusion.51
  87.9 0.3 convolution_add_fusion.4
  88.2 0.3 convolution_add_fusion.3
  88.5 0.3 convolution_add_fusion.2
  88.8 0.3 convolution_add_fusion.1
  89.1 0.3 fusion.4
  89.4 0.1 fusion.3
  89.6 0.2 fusion.97
  89.8 0.2 fusion.2
  90.0 0.3 fusion.70
  90.3 0.3 fusion.1
  90.6 0.3 fusion.17
  90.9 0.5 fusion
  91.4 0.4 fusion.12
  91.8 0.8 fusion.8
  (139 shorter events, 3.0 us)
Async XLA Ops:
  0.0 4.9 %copy-start.8 = (bf16[1,15,32,64]{3,2,1,0:T(8,128)(2,1)S(1)}, bf16[1,15,32,64]{3,2,1,0:T(8,128)(2,1)}, u32[]{:S(2)}) copy-start(bf16[1,15,32,64]{3,2,1,0:T(8,128)(2,1)} %param.20) | copy-start | bytes 184324
  0.0 14.5 %copy-start.29 = (bf16[1,32,96]{2,1,0:T(8,128)(2,1)S(1)}, bf16[1,32,96]{2,1,0:T(8,128)(2,1)}, u32[]{:S(2)}) copy-start(bf16[1,32,96]{2,1,0:T(8,128)(2,1)} %param.23) | copy-start | bytes 18436
  0.0 14.5 %copy-start.30 = (bf16[1,32,64]{2,1,0:T(8,128)(2,1)S(1)}, bf16[1,32,64]{2,1,0:T(8,128)(2,1)}, u32[]{:S(2)}) copy-start(bf16[1,32,64]{2,1,0:T(8,128)(2,1)} %param.22) | copy-start | bytes 12292
  2.6 12.8 %copy-start.2 = (bf16[32,16,64]{2,1,0:T(8,128)(2,1)}, bf16[32,16,64]{2,1,0:T(8,128)(2,1)S(1)}, u32[]{:S(2)}) copy-start(bf16[32,16,64]{2,1,0:T(8,128)(2,1)S(1)} %reshape.186) | copy-start | bytes 196612
  5.3 18.4 %copy-start.28 = (s32[16,3]{0,1:T(4,128)S(1)}, s32[16,3]{0,1:T(4,128)}, u32[]{:S(2)}) copy-start(s32[16,3]{0,1:T(4,128)} %param.18) | copy-start | bytes 580
  5.3 19.4 %copy-start.34 = (s32[24]{0:T(128)S(1)}, s32[24]{0:T(128)}, u32[]{:S(2)}) copy-start(s32[24]{0:T(128)} %constant.261) | copy-start | bytes 292
  5.3 19.4 %copy-start.35 = (s32[48]{0:T(128)S(1)}, s32[48]{0:T(128)}, u32[]{:S(2)}) copy-start(s32[48]{0:T(128)} %constant.260) | copy-start | bytes 580
  5.4 20.0 %copy-start.32 = (s32[6]{0:T(128)S(1)}, s32[6]{0:T(128)}, u32[]{:S(2)}) copy-start(s32[6]{0:T(128)} %constant.263) | copy-start | bytes 76
  5.4 20.0 %copy-start.33 = (s32[12]{0:T(128)S(1)}, s32[12]{0:T(128)}, u32[]{:S(2)}) copy-start(s32[12]{0:T(128)} %constant.262) | copy-start | bytes 148
  5.5 29.9 %collective-permute-start.1 = (f32[41152]{0:T(1024)S(1)}, f32[41152]{0:T(1024)S(1)}, u32[]{:S(2)}, u32[]{:S(2)}) collective-permute-start(f32[41152]{0:T(1024)S(1)} %concatenate.73), channel_id=1, source_target_pairs={{2,0},{4,2},{6,4},{8,6},{10,8},{12,10},{14,12},{16,14},{18,16},{20... | collective-permute-start | bytes 493832 | tf_op jit(solution)/shard_map/ppermute | solution.py:222
  12.4 23.0 %collective-permute-start = (f32[41152]{0:T(1024)S(1)}, f32[41152]{0:T(1024)}, u32[]{:S(2)}, u32[]{:S(2)}) collective-permute-start(f32[41152]{0:T(1024)S(1)} %concatenate.72), channel_id=1, source_target_pairs={{0,2},{2,4},{4,6},{6,8},{8,10},{10,12},{12,14},{14,16},{16,18},{18... | collective-permute-start | bytes 493832 | tf_op jit(solution)/shard_map/ppermute | solution.py:221
  15.5 19.1 %all-to-all-start = ((bf16[16,32,416]{2,1,0:T(8,128)(2,1)}), bf16[16,32,416]{2,1,0:T(8,128)(2,1)S(1)}, u32[]{:S(2)}, u32[]{:S(2)}) async-start(bf16[16,32,416]{2,1,0:T(8,128)(2,1)} %broadcast_in_dim.45), calls=%async_computation | async-start | bytes 1048576 | tf_op jit(solution)/shard_map/all_to_all | solution.py:99
  34.6 5.6 %copy-start.1 = (f32[16,32,288]{2,1,0:T(8,128)}, f32[16,32,288]{2,1,0:T(8,128)S(1)}, u32[]{:S(2)}) copy-start(f32[16,32,288]{2,1,0:T(8,128)S(1)} %slice_convert_fusion) | copy-start | bytes 1769476
  34.6 4.8 %copy-start.25 = (f32[3,1024]{1,0:T(4,128)S(1)}, f32[3,1024]{1,0:T(4,128)}, u32[]{:S(2)}) copy-start(f32[3,1024]{1,0:T(4,128)} %param.17) | copy-start | bytes 36868
  35.3 6.4 %copy-start.6 = (f32[2,32,128]{2,1,0:T(8,128)}, f32[2,32,128]{2,1,0:T(8,128)S(1)}, u32[]{:S(2)}) copy-start(f32[2,32,128]{2,1,0:T(8,128)S(1)} %fusion.102) | copy-start | bytes 98308
  39.2 25.2 %copy-start = (bf16[1024,128]{1,0:T(8,128)(2,1)S(1)}, bf16[1024,128]{1,0:T(8,128)(2,1)}, u32[]{:S(2)}) copy-start(bf16[1024,128]{1,0:T(8,128)(2,1)} %param.16) | copy-start | bytes 786436
  41.7 32.9 %collective-permute-start.2 = (f32[11,32,128]{2,1,0:T(8,128)}, f32[11,32,128]{2,1,0:T(8,128)}, u32[]{:S(2)}, u32[]{:S(2)}) collective-permute-start(f32[11,32,128]{2,1,0:T(8,128)} %get-tuple-element.82), channel_id=1, source_target_pairs={{0,32},{32,64},{64,96},{96,128},{128,160},{160,192},{192,224},{224... | collective-permute-start | bytes 540680 | tf_op jit(solution)/shard_map/ppermute | solution.py:140
  46.8 28.7 %collective-permute-start.3 = (f32[11,32,128]{2,1,0:T(8,128)}, f32[11,32,128]{2,1,0:T(8,128)}, u32[]{:S(2)}, u32[]{:S(2)}) collective-permute-start(f32[11,32,128]{2,1,0:T(8,128)} %get-tuple-element.83), channel_id=1, source_target_pairs={{32,0},{64,32},{96,64},{128,96},{160,128},{192,160},{224,192},{256... | collective-permute-start | bytes 540680 | tf_op jit(solution)/shard_map/ppermute | solution.py:141
  49.5 16.7 %copy-start.14 = (f32[8192]{0:T(1024)S(1)}, f32[8192]{0:T(1024)}, u32[]{:S(2)}) copy-start(f32[8192]{0:T(1024)} %get-tuple-element.54) | copy-start | bytes 98308
  49.5 16.7 %copy-start.15 = (f32[8192]{0:T(1024)S(1)}, f32[8192]{0:T(1024)}, u32[]{:S(2)}) copy-start(f32[8192]{0:T(1024)} %get-tuple-element.58) | copy-start | bytes 98308
  49.5 36.9 %all-to-all-start.1 = ((bf16[16,32,288]{2,1,0:T(8,128)(2,1)}), bf16[16,32,288]{2,1,0:T(8,128)(2,1)S(1)}, u32[]{:S(2)}, u32[]{:S(2)}) async-start(bf16[16,32,288]{2,1,0:T(8,128)(2,1)} %broadcast_in_dim.52), calls=%async_computation.1 | async-start | bytes 786432 | tf_op jit(solution)/shard_map/all_to_all | solution.py:99
  64.5 1.7 %copy-start.16 = (f32[8192]{0:T(1024)S(1)}, f32[8192]{0:T(1024)}, u32[]{:S(2)}) copy-start(f32[8192]{0:T(1024)} %get-tuple-element.55) | copy-start | bytes 98308
  64.5 1.7 %copy-start.17 = (f32[8192]{0:T(1024)S(1)}, f32[8192]{0:T(1024)}, u32[]{:S(2)}) copy-start(f32[8192]{0:T(1024)} %get-tuple-element.59) | copy-start | bytes 98308
  64.5 2.4 %copy-start.18 = (f32[8192]{0:T(1024)S(1)}, f32[8192]{0:T(1024)}, u32[]{:S(2)}) copy-start(f32[8192]{0:T(1024)} %get-tuple-element.56) | copy-start | bytes 98308
  64.5 2.4 %copy-start.19 = (f32[8192]{0:T(1024)S(1)}, f32[8192]{0:T(1024)}, u32[]{:S(2)}) copy-start(f32[8192]{0:T(1024)} %get-tuple-element.60) | copy-start | bytes 98308
  64.5 2.4 %copy-start.27 = (s32[1024]{0:T(1024)S(1)}, s32[1024]{0:T(1024)}, u32[]{:S(2)}) copy-start(s32[1024]{0:T(1024)} %get-tuple-element.103) | copy-start | bytes 12292
  64.5 3.0 %copy-start.12 = (f32[8192]{0:T(1024)S(1)}, f32[8192]{0:T(1024)}, u32[]{:S(2)}) copy-start(f32[8192]{0:T(1024)} %get-tuple-element.57) | copy-start | bytes 98308
  64.6 3.0 %copy-start.13 = (f32[8192]{0:T(1024)S(1)}, f32[8192]{0:T(1024)}, u32[]{:S(2)}) copy-start(f32[8192]{0:T(1024)} %get-tuple-element.61) | copy-start | bytes 98308
  64.6 3.0 %copy-start.26 = (s32[1024]{0:T(1024)S(1)}, s32[1024]{0:T(1024)}, u32[]{:S(2)}) copy-start(s32[1024]{0:T(1024)} %get-tuple-element.104) | copy-start | bytes 12292
  68.9 1.7 %copy-start.4 = (bf16[48,64,128]{2,1,0:T(8,128)(2,1)S(1)}, bf16[48,64,128]{2,1,0:T(8,128)(2,1)}, u32[]{:S(2)}) copy-start(bf16[48,64,128]{2,1,0:T(8,128)(2,1)} %gather_fusion.1) | copy-start | bytes 2359300
  68.9 1.7 %copy-start.31 = (bf16[16,3]{1,0:T(8,128)(2,1)S(1)}, bf16[16,3]{1,0:T(8,128)(2,1)}, u32[]{:S(2)}) copy-start(bf16[16,3]{1,0:T(8,128)(2,1)} %copy.38) | copy-start | bytes 292
  70.6 1.8 %slice-start = ((f32[16,32,288]{2,1,0:T(8,128)}), f32[16,32,64]{2,1,0:T(8,128)S(1)}, s32[]{:S(2)}) async-start(f32[16,32,288]{2,1,0:T(8,128)} %copy-done.1), calls=%async_computation.2 | async-start | bytes 524288 | tf_op jit(solution)/shard_map/slice | solution.py:133
  70.6 4.1 %copy-start.24 = (f32[8,32,128]{2,1,0:T(8,128)S(1)}, f32[8,32,128]{2,1,0:T(8,128)}, u32[]{:S(2)}) copy-start(f32[8,32,128]{2,1,0:T(8,128)} %constant_dynamic-update-slice_fusion.2) | copy-start | bytes 393220
  70.6 4.8 %copy-start.7 = (f32[2,32,128]{2,1,0:T(8,128)S(1)}, f32[2,32,128]{2,1,0:T(8,128)}, u32[]{:S(2)}) copy-start(f32[2,32,128]{2,1,0:T(8,128)} %copy-done.6) | copy-start | bytes 98308
  86.4 1.8 %copy-start.23 = (f32[32,64]{1,0:T(8,128)S(1)}, f32[32,64]{1,0:T(8,128)}, u32[]{:S(2)}) copy-start(f32[32,64]{1,0:T(8,128)} %get-tuple-element.33) | copy-start | bytes 24580
  86.4 2.1 %copy-start.22 = (f32[32,64]{1,0:T(8,128)S(1)}, f32[32,64]{1,0:T(8,128)}, u32[]{:S(2)}) copy-start(f32[32,64]{1,0:T(8,128)} %get-tuple-element.34) | copy-start | bytes 24580
  86.4 2.4 %copy-start.21 = (f32[32,64]{1,0:T(8,128)S(1)}, f32[32,64]{1,0:T(8,128)}, u32[]{:S(2)}) copy-start(f32[32,64]{1,0:T(8,128)} %get-tuple-element.35) | copy-start | bytes 24580
  86.4 2.6 %copy-start.20 = (f32[32,64]{1,0:T(8,128)S(1)}, f32[32,64]{1,0:T(8,128)}, u32[]{:S(2)}) copy-start(f32[32,64]{1,0:T(8,128)} %get-tuple-element.32) | copy-start | bytes 24580
  86.4 2.9 %copy-start.11 = (f32[2,32,128]{2,1,0:T(8,128)S(1)}, f32[2,32,128]{2,1,0:T(8,128)}, u32[]{:S(2)}) copy-start(f32[2,32,128]{2,1,0:T(8,128)} %convolution_bitcast_fusion.4) | copy-start | bytes 98308
  86.5 3.1 %copy-start.9 = (bf16[1,15,32,64]{3,2,1,0:T(8,128)(2,1)S(1)}, bf16[1,15,32,64]{3,2,1,0:T(8,128)(2,1)}, u32[]{:S(2)}) copy-start(bf16[1,15,32,64]{3,2,1,0:T(8,128)(2,1)} %param.20) | copy-start | bytes 184324
  86.6 3.2 %copy-start.10 = (bf16[1,31,32,96]{3,2,1,0:T(8,128)(2,1)S(1)}, bf16[1,31,32,96]{3,2,1,0:T(8,128)(2,1)}, u32[]{:S(2)}) copy-start(bf16[1,31,32,96]{3,2,1,0:T(8,128)(2,1)} %param.21) | copy-start | bytes 571396
  89.8 1.6 %copy-start.3 = (bf16[32,16,64]{2,1,0:T(8,128)(2,1)S(1)}, bf16[32,16,64]{2,1,0:T(8,128)(2,1)}, u32[]{:S(2)}) copy-start(bf16[32,16,64]{2,1,0:T(8,128)(2,1)} %copy-done.2) | copy-start | bytes 196612
  90.6 1.2 %copy-start.5 = (f32[16,64,128,1]{2,1,3,0:T(8,128)S(1)}, f32[16,64,128,1]{2,1,3,0:T(8,128)}, u32[]{:S(2)}) copy-start(f32[16,64,128,1]{2,1,3,0:T(8,128)} %fusion.6) | copy-start | bytes 1572868

commit v13 on v12

--- a/solution.py
+++ b/solution.py
@@ -179,11 +179,13 @@
         if height < summit:
             parent = cluster >> 1
             lifts.append((cluster, pick(outer_lift, parent * 2 ** (level + 1) + 2**level)))
-    downward = fields[summit]
-    for height in range(summit - 1, -1, -1):
-        cluster, lift = lifts[height]
-        half = jnp.where(cluster % 2 == 1, lift[:, RANK:], lift[:, :RANK])
-        downward = fields[height] + product(half.T, downward)
+    prefix = None
+    downward = fields[0]
+    for height in range(1, summit + 1):
+        cluster, lift = lifts[height - 1]
+        half = jnp.where(cluster % 2 == 1, lift[:, RANK:], lift[:, :RANK]).T
+        prefix = half if prefix is None else product(prefix, half)
+        downward = downward + product(prefix, fields[height])
     return downward, late_result
 
 
@@ -255,15 +257,24 @@
     downward, (nearby, fields) = upper_tree(
         device_coef, device_coupling, upper_transfer, upper_coupling, (from_left, from_right), late
     )
-    downward = downward[None]
+    local_down = None
+    reach = jnp.eye(RANK, dtype=jnp.float32)[None]
     for height in range(depth_local - 1, -1, -1):
         cluster_count = leaf_count >> height + 1
         first_slot = leaf_count - (2 * leaf_count >> height + 1)
         lift_mats = as_float(transfer[0, first_slot : first_slot + cluster_count])
-        spread = jnp.einsum("cra,crv->cav", lift_mats, downward, precision=HIGHEST)
-        downward = fields[height] + spread.reshape(2 * cluster_count, RANK, columns)
-    far_field = jnp.einsum(
-        "rlp,lrv->lpv", as_float(basis_leaves), downward, precision=HIGHEST
+        reach = jnp.einsum("cra,crk->cak", lift_mats, reach, precision=HIGHEST)
+        reach = reach.reshape(2 * cluster_count, RANK, RANK)
+        if local_down is None:
+            local_down = fields[height]
+        else:
+            spread = jnp.einsum("cra,crv->cav", lift_mats, local_down, precision=HIGHEST)
+            local_down = fields[height] + spread.reshape(2 * cluster_count, RANK, columns)
+    basis_float = as_float(basis_leaves)
+    reach_rows = jnp.einsum("rlp,lrk->lpk", basis_float, reach, precision=HIGHEST)
+    far_field = (
+        jnp.einsum("rlp,lrv->lpv", basis_float, local_down, precision=HIGHEST)
+        + jnp.einsum("lpk,kv->lpv", reach_rows, downward, precision=HIGHEST)
     ).reshape(row_count, columns)
     return (nearby + NUGGET * vectors.astype(jnp.float32) + far_field).astype(jnp.bfloat16)
 

time: 93.8 us -> 102 us (1.087)
  matrix products: 12.8 us -> 16.9 us
  waiting for transfers between devices: 14.9 us -> 18.2 us
  local copies, waits for them, and re-layouts: 19.5 us -> 22.2 us
  other arithmetic: 5.57 us -> 3.97 us
    all_to_all x2, waiting for transfers between devices: 14.9 us -> 18.2 us  [spread_gather(): return lax.all_to_all(copies, axis, 0, 0, tiled=True)]
    dot_general x5 -> x10, matrix products: 1.33 us -> 3.92 us  [the longest x1 1.05 us: local(): jnp.einsum('rlp,lrk->lpk', basis_float, reach, precision=HIGHEST)]
    convert_element_type x1, local copies, waits for them, and re-layouts: 0.01 us -> 1.35 us  [late(): right_vectors.astype(vectors.dtype)]
    gather x2, other arithmetic: 1.21 us -> 0.01 us  [late(): extended[partner_table(cluster_count) + 2]]
    dot_general x13 -> x18, matrix products: 3.43 us -> 3.89 us  [product(): return jnp.dot(matrix, operand, precision=HIGHEST)]
    unnamed x76 -> x56, local copies, waits for them, and re-layouts: 2.29 us -> 2.24 us
  transfers between devices with their start and end apart: 6 -> 6, of which waited for: 2 -> 2; matrix products, arithmetic and copies ran while one was open for 22% -> 18% of each run, Pallas kernels for 0% -> 0%
where the time goes in v13:
time: 102 us; the launch traced here: 101 us
  starting transfers between devices  38.6 us (38%)
  local copies, waits for them, and re-layouts  22.2 us (22%)
  waiting for transfers between devices  18.2 us (18%)
  matrix products  16.9 us (17%)
  other arithmetic  3.97 us (4%)
  between operations  1.18 us (1%)
    all_to_all x2, starting transfers between devices, spread_gather(): return lax.all_to_all(copies, axis, 0, 0, tiled=True)  23.1 us
    all_to_all x2, waiting for transfers between devices, spread_gather(): return lax.all_to_all(copies, axis, 0, 0, tiled=True)  18.2 us
    ppermute x1, starting transfers between devices, local(): lax.ppermute(head, SPACE, [(i + 1, i) for i in range(count - 1)])  6.66 us
    ppermute x1, starting transfers between devices, upper_tree(): lax.ppermute(tails, 'z', [(i, i + 1) for i in range(planes - 1)])  5.03 us
    dot_general x18, matrix products, product(): return jnp.dot(matrix, operand, precision=HIGHEST)  3.89 us
    dot_general x4, matrix products, late(): jnp.einsum('cra,cav->crv', mixers, stacked, precision=HIGHEST)  3.5 us
    gather x4, local copies, waits for them, and re-layouts, late(): extended[partner_table(cluster_count) + 2]  2.3 us
    unnamed x56, local copies, waits for them, and re-layouts  2.24 us
  transfers between devices with their start and end apart: 6, of which 2 were waited for; matrix products, arithmetic and copies ran while one was open for 18% of the time, Pallas kernels for 0%

profile of v13, /device:TPU:64, one launch (start us, length us, event | category | flops | bytes accessed | tf_op | source)
XLA Modules:
  0.0 101.0 jit_solution(14534708434162249097)
XLA Ops:
  0.0 0.8 fusion.168
  0.9 0.7 bitcast_convert_fusion
  1.6 1.0 reshape.196
  2.6 1.1 %fusion.169 = (bf16[16,32,128]{2,1,0:T(8,128)(2,1)S(1)}, f32[16,32,128]{2,1,0:T(8,128)S(1)}) fusion(bf16[16,64,128]{2,1,0:T(8,128)(2,1)} %bitcast.295, bf16[32,16,64]{2,1,0:T(8,128)(2,1)S(1)} %reshape.196), kind=kOutput, calls=%fused_computation.277 | convolution fusion | flops 8454144 | bytes 720896 | tf_op jit(solution)/shard_map/rlp,lpv->lrv/dot_general | solution.py:203
  3.8 1.1 %bitcast_convert_fusion.3 = (bf16[8,32,128]{2,1,0:T(8,128)(2,1)S(1)}, f32[8,128,32]{1,2,0:T(8,128)S(1)}) fusion(f32[8,64,128]{2,1,0:T(8,128)S(1)} %bitcast.296, bf16[1,15,32,64]{3,2,1,0:T(8,128)(2,1)} %param.20), kind=kOutput, calls=%fused_computation.264 | convolution fusion | flops 25198592 | bytes 524288 | tf_op jit(solution)/shard_map/cra,cav->crv/dot_general | solution.py:210
  4.9 0.2 bitcast_convert_fusion.2
  5.4 6.7 %collective-permute-start.1 = (f32[41152]{0:T(1024)S(1)}, f32[41152]{0:T(1024)}, u32[]{:S(2)}, u32[]{:S(2)}) collective-permute-start(f32[41152]{0:T(1024)S(1)} %concatenate.73), channel_id=1, source_target_pairs={{2,0},{4,2},{6,4},{8,6},{10,8},{12,10},{14,12},{16,14},{18,16},{20... | collective-permute-start | bytes 493832 | tf_op jit(solution)/shard_map/ppermute | solution.py:224
  12.2 0.8 concatenate.72
  13.0 1.9 %collective-permute-start = (f32[41152]{0:T(1024)}, f32[41152]{0:T(1024)}, u32[]{:S(2)}, u32[]{:S(2)}) collective-permute-start(f32[41152]{0:T(1024)} %concatenate.72), channel_id=1, source_target_pairs={{0,2},{2,4},{4,6},{6,8},{8,10},{10,12},{12,14},{14,16},{16,18},{18... | collective-permute-start | bytes 493832 | tf_op jit(solution)/shard_map/ppermute | solution.py:223
  15.1 0.8 broadcast_in_dim.45
  16.0 8.1 %all-to-all-start = ((bf16[16,32,416]{2,1,0:T(8,128)(2,1)}), bf16[16,32,416]{2,1,0:T(8,128)(2,1)S(1)}, u32[]{:S(2)}, u32[]{:S(2)}) async-start(bf16[16,32,416]{2,1,0:T(8,128)(2,1)} %broadcast_in_dim.45), calls=%async_computation | async-start | bytes 1048576 | tf_op jit(solution)/shard_map/all_to_all | solution.py:99
  24.5 0.2 convolution_bitcast_fusion.7
  25.2 0.2 convolution_bitcast_fusion.4
  25.9 0.6 constant_dynamic-update-slice_fusion.2
  26.5 1.1 %convolution_bitcast_fusion.1 = f32[16,64,32]{1,2,0:T(8,128)} fusion(f32[16,32,32]{1,0,2:T(8,128)S(1)} %reshape.228, bf16[32,16,64]{2,1,0:T(8,128)(2,1)S(1)} %reshape.196), kind=kOutput, calls=%fused_computation.10 | convolution fusion | flops 12582912 | bytes 262144 | tf_op jit(solution)/shard_map/rlp,lrk->lpk/dot_general | solution.py:274
  27.6 7.5 %all-to-all-done = bf16[16,32,416]{2,1,0:T(8,128)(2,1)S(1)} async-done(((bf16[16,32,416]{2,1,0:T(8,128)(2,1)}), bf16[16,32,416]{2,1,0:T(8,128)(2,1)S(1)}, u32[]{:S(2)}, u32[]{:S(2)}) %all-to-all-start) | async-done | bytes 426016 | tf_op jit(solution)/shard_map/all_to_all | solution.py:99
  35.2 0.3 fusion.28
  35.5 0.2 fusion.83
  36.0 0.6 pad_maximum_fusion.13
  36.6 0.7 slice.332
  37.3 1.4 %fusion.89 = bf16[64,128]{1,0:T(8,128)(2,1)} fusion(f32[41152]{0:T(1024)} %collective-permute-done), kind=kLoop, calls=%fused_computation.148 | loop fusion | bytes 32768 | tf_op jit(solution)/shard_map/convert_element_type | solution.py:239
  38.6 1.5 %fusion.164 = (f32[8192]{0:T(1024)}, f32[8192]{0:T(1024)S(1)}, f32[8192]{0:T(1024)S(1)}, f32[8192]{0:T(1024)S(1)}) fusion(f32[41152]{0:T(1024)} %collective-permute-done), kind=kLoop, calls=%fused_computation.272 | loop fusion | bytes 262144 | tf_op jit(solution)/shard_map/slice | solution.py:247
  40.1 0.7 slice.333
  40.8 1.4 %fusion.90 = bf16[64,128]{1,0:T(8,128)(2,1)} fusion(f32[41152]{0:T(1024)} %collective-permute-done.1), kind=kLoop, calls=%fused_computation.149 | loop fusion | bytes 32768 | tf_op jit(solution)/shard_map/convert_element_type | solution.py:239
  42.2 1.5 %fusion.165 = (f32[8192]{0:T(1024)}, f32[8192]{0:T(1024)S(1)}, f32[8192]{0:T(1024)S(1)}, f32[8192]{0:T(1024)S(1)}) fusion(f32[41152]{0:T(1024)} %collective-permute-done.1), kind=kLoop, calls=%fused_computation.273 | loop fusion | bytes 262144 | tf_op jit(solution)/shard_map/slice | solution.py:247
  44.1 0.6 dynamic_slice.147
  44.8 0.6 gather_fusion.5
  45.3 0.9 fusion.107
  46.2 0.2 fusion.110
  46.4 0.6 gather_fusion
  47.1 0.7 copy.77
  47.7 0.6 gather_fusion.4
  48.3 1.0 fusion.2
  49.3 0.3 fusion.76
  49.6 0.6 gather_fusion.3
  50.2 1.1 %fusion.1 = f32[8,32,128]{2,1,0:T(8,128)S(1)} fusion(f32[8,32,128]{2,1,0:T(8,128)S(1)} %bitcast.308, f32[8,96,128]{2,1,0:T(8,128)S(1)} %bitcast.298, bf16[1,31,32,96]{3,2,1,0:T(8,128)(2,1)} %param.21), kind=kOutput, calls=%fused_computation.14 | convolution fusion | flops 37781504 | bytes 720896 | tf_op jit(solution)/shard_map/cra,cav->crv/dot_general | solution.py:252
  51.4 0.3 fusion.20
  51.7 0.8 pad_maximum_fusion.4
  52.5 5.0 %collective-permute-start.2 = (f32[11,32,128]{2,1,0:T(8,128)}, f32[11,32,128]{2,1,0:T(8,128)}, u32[]{:S(2)}, u32[]{:S(2)}) collective-permute-start(f32[11,32,128]{2,1,0:T(8,128)} %get-tuple-element.82), channel_id=1, source_target_pairs={{0,32},{32,64},{64,96},{96,128},{128,160},{160,192},{192,224},{224... | collective-permute-start | bytes 540680 | tf_op jit(solution)/shard_map/ppermute | solution.py:140
  57.5 1.9 %collective-permute-start.3 = (f32[11,32,128]{2,1,0:T(8,128)}, f32[11,32,128]{2,1,0:T(8,128)}, u32[]{:S(2)}, u32[]{:S(2)}) collective-permute-start(f32[11,32,128]{2,1,0:T(8,128)} %get-tuple-element.83), channel_id=1, source_target_pairs={{32,0},{64,32},{96,64},{128,96},{160,128},{192,160},{224,192},{256... | collective-permute-start | bytes 540680 | tf_op jit(solution)/shard_map/ppermute | solution.py:141
  59.4 0.8 broadcast_in_dim.52
  60.2 15.0 %all-to-all-start.1 = ((bf16[16,32,288]{2,1,0:T(8,128)(2,1)}), bf16[16,32,288]{2,1,0:T(8,128)(2,1)S(1)}, u32[]{:S(2)}, u32[]{:S(2)}) async-start(bf16[16,32,288]{2,1,0:T(8,128)(2,1)} %broadcast_in_dim.52), calls=%async_computation.1 | async-start | bytes 786432 | tf_op jit(solution)/shard_map/all_to_all | solution.py:99
  75.3 0.6 gather_fusion.2
  75.9 0.5 fusion
  76.4 0.4 convolution_bitcast_fusion
  76.9 0.7 gather_fusion.1
  77.7 0.3 fusion.105
  77.9 0.2 fusion.103
  78.2 0.7 multiply_reduce_fusion
  78.9 1.8 %fusion.5 = f32[16,64,128,1]{2,1,3,0:T(8,128)} fusion(bf16[16,3,64,128]{3,2,1,0:T(8,128)(2,1)S(1)} %bitcast.304, f32[16,3,64,64]{3,2,1,0:T(8,128)S(1)} %multiply_reduce_fusion, bf16[16,3]{1,0:T(8,128)(2,1)S(1)} %copy.50), kind=kOutput, calls=%fused_computation.32 | convolution fusion | flops 51707904 | bytes 2097248 | tf_op jit(solution)/shard_map/while/body/eval_jaxpr/gkij,gkjv->giv/dot_general | solution.py:39
  80.8 0.2 fusion.101
  81.1 0.8 slice_dynamic-update-slice_fusion.1
  81.8 0.8 slice_dynamic-update-slice_fusion
  82.6 0.9 fusion.162
  83.5 0.9 fusion.163
  84.9 0.8 convolution_bitcast_fusion.9
  85.8 0.3 convolution_add_fusion.6
  86.4 10.7 %all-to-all-done.1 = bf16[16,32,288]{2,1,0:T(8,128)(2,1)S(1)} async-done(((bf16[16,32,288]{2,1,0:T(8,128)(2,1)}), bf16[16,32,288]{2,1,0:T(8,128)(2,1)S(1)}, u32[]{:S(2)}, u32[]{:S(2)}) %all-to-all-start.1) | async-done | bytes 294944 | tf_op jit(solution)/shard_map/all_to_all | solution.py:99
  97.3 0.2 fusion.80
  97.6 0.2 fusion.99
  97.9 0.2 fusion.56
  98.2 0.2 fusion.97
  99.2 1.0 %convolution_add_fusion = f32[16,64,128]{2,1,0:T(8,128)S(1)} fusion(f32[16,64,128]{2,1,0:T(8,128)S(1)} %convolution_bitcast_fusion, f32[16,64,32]{1,2,0:T(8,128)S(1)} %copy-done.5, f32[32,128,1]{1,0,2:T(8,128)S(1)} %fusion.3), kind=kOutput, calls=%fused_computation.8 | convolution fusion | flops 50462720 | bytes 1196032 | tf_op jit(solution)/shard_map/lpk,kv->lpv/dot_general | solution.py:277
  100.3 0.8 fusion.8
  (135 shorter events, 5.0 us)
Async XLA Ops:
  0.0 4.9 %copy-start.4 = (bf16[1,15,32,64]{3,2,1,0:T(8,128)(2,1)S(1)}, bf16[1,15,32,64]{3,2,1,0:T(8,128)(2,1)}, u32[]{:S(2)}) copy-start(bf16[1,15,32,64]{3,2,1,0:T(8,128)(2,1)} %param.20) | copy-start | bytes 184324
  0.0 15.0 %copy-start.20 = (bf16[1,32,96]{2,1,0:T(8,128)(2,1)S(1)}, bf16[1,32,96]{2,1,0:T(8,128)(2,1)}, u32[]{:S(2)}) copy-start(bf16[1,32,96]{2,1,0:T(8,128)(2,1)} %param.23) | copy-start | bytes 18436
  0.0 15.0 %copy-start.21 = (bf16[1,32,64]{2,1,0:T(8,128)(2,1)S(1)}, bf16[1,32,64]{2,1,0:T(8,128)(2,1)}, u32[]{:S(2)}) copy-start(bf16[1,32,64]{2,1,0:T(8,128)(2,1)} %param.22) | copy-start | bytes 12292
  4.9 19.2 %copy-start.19 = (s32[16,3]{0,1:T(4,128)S(1)}, s32[16,3]{0,1:T(4,128)}, u32[]{:S(2)}) copy-start(s32[16,3]{0,1:T(4,128)} %param.18) | copy-start | bytes 580
  5.4 31.1 %collective-permute-start.1 = (f32[41152]{0:T(1024)S(1)}, f32[41152]{0:T(1024)}, u32[]{:S(2)}, u32[]{:S(2)}) collective-permute-start(f32[41152]{0:T(1024)S(1)} %concatenate.73), channel_id=1, source_target_pairs={{2,0},{4,2},{6,4},{8,6},{10,8},{12,10},{14,12},{16,14},{18,16},{20... | collective-permute-start | bytes 493832 | tf_op jit(solution)/shard_map/ppermute | solution.py:224
  12.2 13.2 %copy-start.24 = (s32[24]{0:T(128)S(1)}, s32[24]{0:T(128)}, u32[]{:S(2)}) copy-start(s32[24]{0:T(128)} %constant.261) | copy-start | bytes 292
  12.2 13.2 %copy-start.25 = (s32[48]{0:T(128)S(1)}, s32[48]{0:T(128)}, u32[]{:S(2)}) copy-start(s32[48]{0:T(128)} %constant.260) | copy-start | bytes 580
  12.2 13.2 %copy-start.22 = (s32[6]{0:T(128)S(1)}, s32[6]{0:T(128)}, u32[]{:S(2)}) copy-start(s32[6]{0:T(128)} %constant.263) | copy-start | bytes 76
  12.2 13.2 %copy-start.23 = (s32[12]{0:T(128)S(1)}, s32[12]{0:T(128)}, u32[]{:S(2)}) copy-start(s32[12]{0:T(128)} %constant.262) | copy-start | bytes 148
  13.0 23.6 %collective-permute-start = (f32[41152]{0:T(1024)}, f32[41152]{0:T(1024)}, u32[]{:S(2)}, u32[]{:S(2)}) collective-permute-start(f32[41152]{0:T(1024)} %concatenate.72), channel_id=1, source_target_pairs={{0,2},{2,4},{4,6},{6,8},{8,10},{10,12},{12,14},{14,16},{16,18},{18... | collective-permute-start | bytes 493832 | tf_op jit(solution)/shard_map/ppermute | solution.py:223
  16.0 19.0 %all-to-all-start = ((bf16[16,32,416]{2,1,0:T(8,128)(2,1)}), bf16[16,32,416]{2,1,0:T(8,128)(2,1)S(1)}, u32[]{:S(2)}, u32[]{:S(2)}) async-start(bf16[16,32,416]{2,1,0:T(8,128)(2,1)} %broadcast_in_dim.45), calls=%async_computation | async-start | bytes 1048576 | tf_op jit(solution)/shard_map/all_to_all | solution.py:99
  35.1 9.6 %copy-start.1 = (f32[16,32,288]{2,1,0:T(8,128)}, f32[16,32,288]{2,1,0:T(8,128)S(1)}, u32[]{:S(2)}) copy-start(f32[16,32,288]{2,1,0:T(8,128)S(1)} %slice_convert_fusion) | copy-start | bytes 1769476
  35.1 8.7 %copy-start.18 = (f32[3,1024]{1,0:T(4,128)S(1)}, f32[3,1024]{1,0:T(4,128)}, u32[]{:S(2)}) copy-start(f32[3,1024]{1,0:T(4,128)} %param.17) | copy-start | bytes 36868
  35.5 11.6 %copy-start.2 = (f32[8,32,128]{2,1,0:T(8,128)}, f32[8,32,128]{2,1,0:T(8,128)S(1)}, u32[]{:S(2)}) copy-start(f32[8,32,128]{2,1,0:T(8,128)S(1)} %fusion.28) | copy-start | bytes 393220
  35.8 15.9 %copy-start.7 = (f32[2,32,128]{2,1,0:T(8,128)}, f32[2,32,128]{2,1,0:T(8,128)S(1)}, u32[]{:S(2)}) copy-start(f32[2,32,128]{2,1,0:T(8,128)S(1)} %fusion.115) | copy-start | bytes 98308
  49.6 9.9 %copy-start.13 = (bf16[32,288]{1,0:T(8,128)(2,1)S(1)}, bf16[32,288]{1,0:T(8,128)(2,1)}, u32[]{:S(2)}) copy-start(bf16[32,288]{1,0:T(8,128)(2,1)} %pad_maximum_fusion.13) | copy-start | bytes 55300
  50.2 25.1 %copy-start.11 = (f32[8192]{0:T(1024)S(1)}, f32[8192]{0:T(1024)}, u32[]{:S(2)}) copy-start(f32[8192]{0:T(1024)} %get-tuple-element.54) | copy-start | bytes 98308
  50.2 25.1 %copy-start.12 = (f32[8192]{0:T(1024)S(1)}, f32[8192]{0:T(1024)}, u32[]{:S(2)}) copy-start(f32[8192]{0:T(1024)} %get-tuple-element.58) | copy-start | bytes 98308
  52.5 28.6 %collective-permute-start.2 = (f32[11,32,128]{2,1,0:T(8,128)}, f32[11,32,128]{2,1,0:T(8,128)}, u32[]{:S(2)}, u32[]{:S(2)}) collective-permute-start(f32[11,32,128]{2,1,0:T(8,128)} %get-tuple-element.82), channel_id=1, source_target_pairs={{0,32},{32,64},{64,96},{96,128},{128,160},{160,192},{192,224},{224... | collective-permute-start | bytes 540680 | tf_op jit(solution)/shard_map/ppermute | solution.py:140
  57.5 24.4 %collective-permute-start.3 = (f32[11,32,128]{2,1,0:T(8,128)}, f32[11,32,128]{2,1,0:T(8,128)}, u32[]{:S(2)}, u32[]{:S(2)}) collective-permute-start(f32[11,32,128]{2,1,0:T(8,128)} %get-tuple-element.83), channel_id=1, source_target_pairs={{32,0},{64,32},{96,64},{128,96},{160,128},{192,160},{224,192},{256... | collective-permute-start | bytes 540680 | tf_op jit(solution)/shard_map/ppermute | solution.py:141
  60.2 15.7 %copy-start.10 = (bf16[1,31,32,96]{3,2,1,0:T(8,128)(2,1)S(1)}, bf16[1,31,32,96]{3,2,1,0:T(8,128)(2,1)}, u32[]{:S(2)}) copy-start(bf16[1,31,32,96]{3,2,1,0:T(8,128)(2,1)} %param.21) | copy-start | bytes 571396
  60.2 36.9 %all-to-all-start.1 = ((bf16[16,32,288]{2,1,0:T(8,128)(2,1)}), bf16[16,32,288]{2,1,0:T(8,128)(2,1)S(1)}, u32[]{:S(2)}, u32[]{:S(2)}) async-start(bf16[16,32,288]{2,1,0:T(8,128)(2,1)} %broadcast_in_dim.52), calls=%async_computation.1 | async-start | bytes 786432 | tf_op jit(solution)/shard_map/all_to_all | solution.py:99
  75.9 1.0 copy-start
  75.9 1.0 copy-start.15
  75.9 1.0 copy-start.16
  76.4 1.2 %slice-start = ((f32[16,32,288]{2,1,0:T(8,128)}), f32[16,32,64]{2,1,0:T(8,128)S(1)}, s32[]{:S(2)}) async-start(f32[16,32,288]{2,1,0:T(8,128)} %copy-done.1), calls=%async_computation.2 | async-start | bytes 524288 | tf_op jit(solution)/shard_map/slice | solution.py:133
  76.4 1.7 %copy-start.14 = (f32[3,16,64]{2,1,0:T(8,128)S(1)}, f32[3,16,64]{2,1,0:T(8,128)}, u32[]{:S(2)}) copy-start(f32[3,16,64]{2,1,0:T(8,128)} %dynamic_slice.147) | copy-start | bytes 36868
  76.9 1.3 %copy-start.9 = (f32[16,3,3,64]{3,1,0,2:T(4,128)S(1)}, f32[16,3,3,64]{3,1,0,2:T(4,128)}, u32[]{:S(2)}) copy-start(f32[16,3,3,64]{3,1,0,2:T(4,128)} %copy.77) | copy-start | bytes 110596
  78.9 2.2 %copy-start.17 = (f32[8,32,128]{2,1,0:T(8,128)S(1)}, f32[8,32,128]{2,1,0:T(8,128)}, u32[]{:S(2)}) copy-start(f32[8,32,128]{2,1,0:T(8,128)} %constant_dynamic-update-slice_fusion.2) | copy-start | bytes 393220
  78.9 2.9 %copy-start.8 = (f32[2,32,128]{2,1,0:T(8,128)S(1)}, f32[2,32,128]{2,1,0:T(8,128)}, u32[]{:S(2)}) copy-start(f32[2,32,128]{2,1,0:T(8,128)} %copy-done.7) | copy-start | bytes 98308
  78.9 5.5 %copy-start.3 = (f32[8,32,128]{2,1,0:T(8,128)S(1)}, f32[8,32,128]{2,1,0:T(8,128)}, u32[]{:S(2)}) copy-start(f32[8,32,128]{2,1,0:T(8,128)} %copy-done.2) | copy-start | bytes 393220
  97.2 2.0 %copy-start.5 = (f32[16,64,32]{1,2,0:T(8,128)S(1)}, f32[16,64,32]{1,2,0:T(8,128)}, u32[]{:S(2)}) copy-start(f32[16,64,32]{1,2,0:T(8,128)} %convolution_bitcast_fusion.1) | copy-start | bytes 393220
  97.8 2.5 %copy-start.6 = (f32[16,64,128,1]{2,1,3,0:T(8,128)S(1)}, f32[16,64,128,1]{2,1,3,0:T(8,128)}, u32[]{:S(2)}) copy-start(f32[16,64,128,1]{2,1,3,0:T(8,128)} %fusion.5) | copy-start | bytes 1572868

commit v14 on v13

--- a/solution.py
+++ b/solution.py
@@ -140,7 +140,9 @@
     from_left = lax.ppermute(tails, "z", [(i, i + 1) for i in range(planes - 1)])
     from_right = lax.ppermute(heads, "z", [(i + 1, i) for i in range(planes - 1)])
     outer_unit = jnp.concatenate([inner[plane_bits][0], plane_held[0, :, columns:]], 1)
-    outer_unit, held = lax.optimization_barrier((outer_unit.astype(jnp.bfloat16), held))
+    outer_unit, held, plane_lift, plane_mix = lax.optimization_barrier(
+        (outer_unit.astype(jnp.bfloat16), held, plane_lift, plane_mix)
+    )
     outer_held = as_float(spread_gather(outer_unit, "z"))
     late_result = late(held)
     summary = outer_held[:, :, :columns]
@@ -232,7 +234,15 @@
         return pieces
 
     def late(held):
-        from_left, from_right = held
+        (from_left, from_right), lift_stack, basis_float = held
+        reach = jnp.eye(RANK, dtype=jnp.float32)[None]
+        for height in range(depth_local - 1, -1, -1):
+            cluster_count = leaf_count >> height + 1
+            first_slot = leaf_count - (2 * leaf_count >> height + 1)
+            lift_mats = lift_stack[first_slot : first_slot + cluster_count]
+            reach = jnp.einsum("cra,crk->cak", lift_mats, reach, precision=HIGHEST)
+            reach = reach.reshape(2 * cluster_count, RANK, RANK)
+        reach_rows = jnp.einsum("rlp,lrk->lpk", basis_float, reach, precision=HIGHEST)
         left_vectors, left_points, left_edges = unpack(from_left)
         right_vectors, right_points, right_edges = unpack(from_right)
         vector_rims = jnp.concatenate(
@@ -250,28 +260,24 @@
             )
             mixers = as_float(coupling[0, first_slot : first_slot + cluster_count])
             fields.append(jnp.einsum("cra,cav->crv", mixers, stacked, precision=HIGHEST))
-        return nearby, fields
+        return nearby, fields, reach_rows
 
     device_coupling = as_float(coupling[0, 2 * leaf_count - 2])
     device_coef = coefficients[depth_local][0]
-    downward, (nearby, fields) = upper_tree(
-        device_coef, device_coupling, upper_transfer, upper_coupling, (from_left, from_right), late
+    downward, (nearby, fields, reach_rows) = upper_tree(
+        device_coef, device_coupling, upper_transfer, upper_coupling, ((from_left, from_right), as_float(transfer[0]), as_float(basis_leaves)), late
     )
     local_down = None
-    reach = jnp.eye(RANK, dtype=jnp.float32)[None]
     for height in range(depth_local - 1, -1, -1):
         cluster_count = leaf_count >> height + 1
         first_slot = leaf_count - (2 * leaf_count >> height + 1)
         lift_mats = as_float(transfer[0, first_slot : first_slot + cluster_count])
-        reach = jnp.einsum("cra,crk->cak", lift_mats, reach, precision=HIGHEST)
-        reach = reach.reshape(2 * cluster_count, RANK, RANK)
         if local_down is None:
             local_down = fields[height]
         else:
             spread = jnp.einsum("cra,crv->cav", lift_mats, local_down, precision=HIGHEST)
             local_down = fields[height] + spread.reshape(2 * cluster_count, RANK, columns)
     basis_float = as_float(basis_leaves)
-    reach_rows = jnp.einsum("rlp,lrk->lpk", basis_float, reach, precision=HIGHEST)
     far_field = (
         jnp.einsum("rlp,lrv->lpv", basis_float, local_down, precision=HIGHEST)
         + jnp.einsum("lpk,kv->lpv", reach_rows, downward, precision=HIGHEST)

time: 102 us -> 97 us (0.951)
  the two profiles are of different devices: /device:TPU:64 before, /device:TPU:32 now
where the time goes in v14:
time: 97 us; the launch traced here: 95.3 us
  starting transfers between devices  38.5 us (40%)
  local copies, waits for them, and re-layouts  26.3 us (27%)
  matrix products  20.9 us (22%)
  other arithmetic  4.63 us (5%)
  waiting for transfers between devices  3.96 us (4%)
  between operations  1 us (1%)
    all_to_all x2, starting transfers between devices, spread_gather(): return lax.all_to_all(copies, axis, 0, 0, tiled=True)  21.6 us
    ppermute x1, starting transfers between devices, local(): lax.ppermute(head, SPACE, [(i + 1, i) for i in range(count - 1)])  8.57 us
    dot_general x18, matrix products, product(): return jnp.dot(matrix, operand, precision=HIGHEST)  6.77 us
    dot_general x4, matrix products, late(): jnp.einsum('cra,cav->crv', mixers, stacked, precision=HIGHEST)  4.39 us
    ppermute x1, waiting for transfers between devices, local(): lax.ppermute(tail, SPACE, [(i, i + 1) for i in range(count - 1)])  3.94 us
    ppermute x1, starting transfers between devices, upper_tree(): lax.ppermute(tails, 'z', [(i, i + 1) for i in range(planes - 1)])  3.36 us
    ppermute x1, starting transfers between devices, upper_tree(): lax.ppermute(heads, 'z', [(i + 1, i) for i in range(planes - 1)])  3.13 us
    unnamed x54, local copies, waits for them, and re-layouts  2.53 us
  transfers between devices with their start and end apart: 6, of which 1 were waited for; matrix products, arithmetic and copies ran while one was open for 34% of the time, Pallas kernels for 0%

profile of v14, /device:TPU:32, one launch (start us, length us, event | category | flops | bytes accessed | tf_op | source)
XLA Modules:
  0.0 95.3 jit_solution(10707755774397079079)
XLA Ops:
  0.0 1.0 %reshape.199 = bf16[32,16,64]{2,1,0:T(8,128)(2,1)S(1)} reshape(bf16[32,1024]{1,0:T(8,128)(2,1)} %param.19) | data formatting | bytes 131072 | tf_op jit(solution)/shard_map/reshape | solution.py:202
  1.1 1.2 %fusion.168 = (bf16[16,32,128]{2,1,0:T(8,128)(2,1)S(1)}, f32[16,32,128]{2,1,0:T(8,128)S(1)}) fusion(bf16[16,64,128]{2,1,0:T(8,128)(2,1)} %bitcast.287, bf16[32,16,64]{2,1,0:T(8,128)(2,1)S(1)} %reshape.199), kind=kOutput, calls=%fused_computation.272 | convolution fusion | flops 8454144 | bytes 720896 | tf_op jit(solution)/shard_map/rlp,lpv->lrv/dot_general | solution.py:205
  2.3 1.1 %bitcast_convert_fusion.4 = (bf16[8,32,128]{2,1,0:T(8,128)(2,1)S(1)}, f32[8,128,32]{1,2,0:T(8,128)S(1)}) fusion(f32[8,64,128]{2,1,0:T(8,128)S(1)} %bitcast.288, bf16[1,15,32,64]{3,2,1,0:T(8,128)(2,1)} %param.20), kind=kOutput, calls=%fused_computation.259 | convolution fusion | flops 25198592 | bytes 524288 | tf_op jit(solution)/shard_map/cra,cav->crv/dot_general | solution.py:212
  3.4 0.9 bitcast_convert_fusion.3
  4.8 0.9 broadcast_in_dim.45
  5.6 7.0 %all-to-all-start = ((bf16[16,32,416]{2,1,0:T(8,128)(2,1)}), bf16[16,32,416]{2,1,0:T(8,128)(2,1)S(1)}, u32[]{:S(2)}, u32[]{:S(2)}) async-start(bf16[16,32,416]{2,1,0:T(8,128)(2,1)} %broadcast_in_dim.45), calls=%async_computation | async-start | bytes 1048576 | tf_op jit(solution)/shard_map/all_to_all | solution.py:99
  12.7 0.8 fusion.167
  13.6 0.8 concatenate.73
  14.4 8.6 %collective-permute-start.1 = (f32[41152]{0:T(1024)}, f32[41152]{0:T(1024)}, u32[]{:S(2)}, u32[]{:S(2)}) collective-permute-start(f32[41152]{0:T(1024)} %concatenate.73), channel_id=1, source_target_pairs={{2,0},{4,2},{6,4},{8,6},{10,8},{12,10},{14,12},{16,14},{18,16},{20... | collective-permute-start | bytes 493832 | tf_op jit(solution)/shard_map/ppermute | solution.py:226
  23.0 0.8 concatenate.72
  23.8 1.9 %collective-permute-start = (f32[41152]{0:T(1024)}, f32[41152]{0:T(1024)}, u32[]{:S(2)}, u32[]{:S(2)}) collective-permute-start(f32[41152]{0:T(1024)} %concatenate.72), channel_id=1, source_target_pairs={{0,2},{2,4},{4,6},{6,8},{8,10},{10,12},{12,14},{14,16},{16,18},{18... | collective-permute-start | bytes 493832 | tf_op jit(solution)/shard_map/ppermute | solution.py:225
  26.0 0.6 pad_clamp_fusion.2
  26.6 0.6 pad_clamp_fusion
  27.2 0.7 copy.52
  27.9 0.6 constant_dynamic-update-slice_fusion.2
  28.7 0.3 fusion.29
  29.0 0.7 fusion.160
  29.8 0.6 fusion.166
  30.8 0.9 slice.430
  31.7 3.9 %collective-permute-done = f32[41152]{0:T(1024)} collective-permute-done((f32[41152]{0:T(1024)}, f32[41152]{0:T(1024)}, u32[]{:S(2)}, u32[]{:S(2)}) %collective-permute-start) | collective-permute-done | bytes 164640 | tf_op jit(solution)/shard_map/ppermute | solution.py:225
  35.6 0.9 fusion.163
  36.6 0.7 slice.343
  37.2 0.9 fusion.164
  38.2 0.7 slice.344
  39.0 0.8 concatenate.74
  39.9 0.6 copy.50
  40.6 0.6 dynamic_slice.147
  41.2 1.4 %fusion.87 = bf16[64,128]{1,0:T(8,128)(2,1)} fusion(f32[41152]{0:T(1024)} %collective-permute-done), kind=kLoop, calls=%fused_computation.143 | loop fusion | bytes 32768 | tf_op jit(solution)/shard_map/convert_element_type | solution.py:249
  42.5 1.4 %fusion.88 = bf16[64,128]{1,0:T(8,128)(2,1)} fusion(f32[41152]{0:T(1024)} %collective-permute-done.1), kind=kLoop, calls=%fused_computation.144 | loop fusion | bytes 32768 | tf_op jit(solution)/shard_map/convert_element_type | solution.py:249
  43.9 0.8 broadcast_in_dim.52
  44.7 14.5 %all-to-all-start.1 = ((bf16[16,32,288]{2,1,0:T(8,128)(2,1)}), bf16[16,32,288]{2,1,0:T(8,128)(2,1)S(1)}, u32[]{:S(2)}, u32[]{:S(2)}) async-start(bf16[16,32,288]{2,1,0:T(8,128)(2,1)} %broadcast_in_dim.52), calls=%async_computation.1 | async-start | bytes 786432 | tf_op jit(solution)/shard_map/all_to_all | solution.py:99
  59.2 1.6 %pad_maximum_fusion.4 = (f32[11,32,128]{2,1,0:T(8,128)}, f32[11,32,128]{2,1,0:T(8,128)}) fusion(f32[2,32,128]{2,1,0:T(8,128)S(1)} %fusion.120, f32[3,32,128]{2,1,0:T(8,128)S(1)} %copy-done.10, f32[3,32,128]{2,1,0:T(8,128)S(1)} %copy-done.9, f32[3,32,128]{2,1,0:T(8,128)S(1)} %get-tuple-element.49, f32[3,32,128]{2,1,0:T(8,128)} %get-tuple-element.87, ...), kind=kLoop, calls=%fused_computation.46 | loop fusion | flops 270336 | bytes 688128 | tf_op jit(solution)/shard_map/concatenate | solution.py:138
  60.8 3.4 %collective-permute-start.2 = (f32[11,32,128]{2,1,0:T(8,128)}, f32[11,32,128]{2,1,0:T(8,128)}, u32[]{:S(2)}, u32[]{:S(2)}) collective-permute-start(f32[11,32,128]{2,1,0:T(8,128)} %get-tuple-element.90), channel_id=1, source_target_pairs={{0,32},{32,64},{64,96},{96,128},{128,160},{160,192},{192,224},{224... | collective-permute-start | bytes 540680 | tf_op jit(solution)/shard_map/ppermute | solution.py:140
  64.2 3.1 %collective-permute-start.3 = (f32[11,32,128]{2,1,0:T(8,128)}, f32[11,32,128]{2,1,0:T(8,128)}, u32[]{:S(2)}, u32[]{:S(2)}) collective-permute-start(f32[11,32,128]{2,1,0:T(8,128)} %get-tuple-element.91), channel_id=1, source_target_pairs={{32,0},{64,32},{96,64},{128,96},{160,128},{192,160},{224,192},{256... | collective-permute-start | bytes 540680 | tf_op jit(solution)/shard_map/ppermute | solution.py:141
  68.3 0.3 fusion.13
  68.8 0.7 gather_fusion.5
  69.5 0.9 fusion.109
  70.6 0.6 gather_fusion.4
  71.2 1.0 %fusion.2 = f32[4,32,128]{2,1,0:T(8,128)S(1)} fusion(f32[4,32,128]{2,1,0:T(8,128)S(1)} %bitcast.308, f32[4,96,128]{2,1,0:T(8,128)S(1)} %bitcast.297, bf16[1,31,32,96]{3,2,1,0:T(8,128)(2,1)} %param.21), kind=kOutput, calls=%fused_computation.15 | convolution fusion | flops 18890752 | bytes 360448 | tf_op jit(solution)/shard_map/cra,cav->crv/dot_general | solution.py:262
  72.5 0.6 gather_fusion.3
  73.0 1.1 %fusion.1 = f32[8,32,128]{2,1,0:T(8,128)S(1)} fusion(f32[8,32,128]{2,1,0:T(8,128)S(1)} %bitcast.300, f32[8,96,128]{2,1,0:T(8,128)S(1)} %bitcast.290, bf16[1,31,32,96]{3,2,1,0:T(8,128)(2,1)} %param.21), kind=kOutput, calls=%fused_computation.13 | convolution fusion | flops 37781504 | bytes 720896 | tf_op jit(solution)/shard_map/cra,cav->crv/dot_general | solution.py:262
  74.2 1.0 %fusion.20 = f32[8,128,64]{1,2,0:T(8,128)} fusion(f32[8,32,128]{2,1,0:T(8,128)S(1)} %fusion.1, bf16[1,15,32,64]{3,2,1,0:T(8,128)(2,1)S(1)} %copy-done.2), kind=kOutput, calls=%fused_computation.68 | convolution fusion | flops 25165824 | bytes 458752 | tf_op jit(solution)/shard_map/cra,crv->cav/dot_general | solution.py:278
  75.2 0.6 gather_fusion.2
  75.9 0.3 copy-done.3
  76.2 1.4 %fusion = f32[16,32,128]{2,1,0:T(8,128)S(1)} fusion(f32[16,32,128]{2,1,0:T(8,128)S(1)} %bitcast.295, f32[16,96,128]{2,1,0:T(8,128)S(1)} %bitcast.285, bf16[1,31,32,96]{3,2,1,0:T(8,128)(2,1)} %param.21), kind=kOutput, calls=%fused_computation.11 | convolution fusion | flops 75563008 | bytes 1441792 | tf_op jit(solution)/shard_map/cra,cav->crv/dot_general | solution.py:262
  77.6 0.4 convolution_bitcast_fusion
  78.0 0.6 gather_fusion
  78.7 1.5 %gather_fusion.1 = bf16[48,64,128]{2,1,0:T(8,128)(2,1)} fusion(bf16[18,64,128]{2,1,0:T(8,128)(2,1)S(1)} %bitcast.284, s32[1024]{0:T(1024)S(1)} %pad_clamp_fusion.4), kind=kCustom, calls=%fused_computation.1 | custom fusion | bytes 1573056 | tf_op jit(solution)/shard_map/while/body/eval_jaxpr/gather | solution.py:40
  80.3 0.3 fusion.103
  80.8 0.4 fusion.10
  81.3 0.7 multiply_reduce_fusion
  82.0 1.0 %fusion.5 = f32[16,64,128,1]{2,1,3,0:T(8,128)S(1)} fusion(bf16[16,3,64,128]{3,2,1,0:T(8,128)(2,1)S(1)} %bitcast.296, f32[16,3,64,64]{3,2,1,0:T(8,128)S(1)} %multiply_reduce_fusion, bf16[16,3]{1,0:T(8,128)(2,1)S(1)} %copy-done.20), kind=kOutput, calls=%fused_computation.27 | convolution fusion | flops 51707904 | bytes 2097248 | tf_op jit(solution)/shard_map/while/body/eval_jaxpr/gkij,gkjv->giv/dot_general | solution.py:39
  83.2 0.8 slice_dynamic-update-slice_fusion.1
  84.0 0.8 slice_dynamic-update-slice_fusion
  84.7 0.9 fusion.161
  85.6 0.9 fusion.162
  86.6 0.9 fusion.50
  87.5 0.9 fusion.44
  88.4 0.9 fusion.38
  89.3 0.8 convolution_bitcast_fusion.4
  90.1 0.3 convolution_add_fusion.6
  91.7 0.9 fusion.56
  93.5 1.0 %convolution_add_fusion = f32[16,64,128]{2,1,0:T(8,128)S(1)} fusion(f32[16,64,128]{2,1,0:T(8,128)S(1)} %convolution_bitcast_fusion, f32[16,64,32]{1,2,0:T(8,128)S(1)} %fusion.10, f32[32,128,1]{1,0,2:T(8,128)S(1)} %fusion.3), kind=kOutput, calls=%fused_computation.8 | convolution fusion | flops 50462720 | bytes 1196032 | tf_op jit(solution)/shard_map/lpk,kv->lpv/dot_general | solution.py:283
  94.5 0.8 fusion.8
  (135 shorter events, 6.2 us)
Async XLA Ops:
  0.0 4.3 %copy-start.2 = (bf16[1,15,32,64]{3,2,1,0:T(8,128)(2,1)S(1)}, bf16[1,15,32,64]{3,2,1,0:T(8,128)(2,1)}, u32[]{:S(2)}) copy-start(bf16[1,15,32,64]{3,2,1,0:T(8,128)(2,1)} %param.20) | copy-start | bytes 184324
  0.0 4.6 %copy-start.19 = (bf16[1,32,64]{2,1,0:T(8,128)(2,1)S(1)}, bf16[1,32,64]{2,1,0:T(8,128)(2,1)}, u32[]{:S(2)}) copy-start(bf16[1,32,64]{2,1,0:T(8,128)(2,1)} %param.22) | copy-start | bytes 12292
  0.0 4.6 %copy-start.18 = (bf16[1,32,96]{2,1,0:T(8,128)(2,1)S(1)}, bf16[1,32,96]{2,1,0:T(8,128)(2,1)}, u32[]{:S(2)}) copy-start(bf16[1,32,96]{2,1,0:T(8,128)(2,1)} %param.23) | copy-start | bytes 18436
  1.0 11.6 %copy-start.1 = (bf16[1024,128]{1,0:T(8,128)(2,1)S(1)}, bf16[1024,128]{1,0:T(8,128)(2,1)}, u32[]{:S(2)}) copy-start(bf16[1024,128]{1,0:T(8,128)(2,1)} %param.16) | copy-start | bytes 786436
  4.7 21.1 %copy-start.17 = (s32[16,3]{0,1:T(4,128)S(1)}, s32[16,3]{0,1:T(4,128)}, u32[]{:S(2)}) copy-start(s32[16,3]{0,1:T(4,128)} %param.18) | copy-start | bytes 580
  4.7 21.3 %copy-start.23 = (s32[48]{0:T(128)S(1)}, s32[48]{0:T(128)}, u32[]{:S(2)}) copy-start(s32[48]{0:T(128)} %constant.260) | copy-start | bytes 580
  4.7 21.3 %copy-start.24 = (s32[24]{0:T(128)S(1)}, s32[24]{0:T(128)}, u32[]{:S(2)}) copy-start(s32[24]{0:T(128)} %constant.261) | copy-start | bytes 292
  4.7 21.9 %copy-start.21 = (s32[12]{0:T(128)S(1)}, s32[12]{0:T(128)}, u32[]{:S(2)}) copy-start(s32[12]{0:T(128)} %constant.262) | copy-start | bytes 148
  4.7 21.9 %copy-start.22 = (s32[6]{0:T(128)S(1)}, s32[6]{0:T(128)}, u32[]{:S(2)}) copy-start(s32[6]{0:T(128)} %constant.263) | copy-start | bytes 76
  5.6 22.9 %all-to-all-start = ((bf16[16,32,416]{2,1,0:T(8,128)(2,1)}), bf16[16,32,416]{2,1,0:T(8,128)(2,1)S(1)}, u32[]{:S(2)}, u32[]{:S(2)}) async-start(bf16[16,32,416]{2,1,0:T(8,128)(2,1)} %broadcast_in_dim.45), calls=%async_computation | async-start | bytes 1048576 | tf_op jit(solution)/shard_map/all_to_all | solution.py:99
  14.4 17.3 %collective-permute-start.1 = (f32[41152]{0:T(1024)}, f32[41152]{0:T(1024)}, u32[]{:S(2)}, u32[]{:S(2)}) collective-permute-start(f32[41152]{0:T(1024)} %concatenate.73), channel_id=1, source_target_pairs={{2,0},{4,2},{6,4},{8,6},{10,8},{12,10},{14,12},{16,14},{18,16},{20... | collective-permute-start | bytes 493832 | tf_op jit(solution)/shard_map/ppermute | solution.py:226
  23.8 11.8 %collective-permute-start = (f32[41152]{0:T(1024)}, f32[41152]{0:T(1024)}, u32[]{:S(2)}, u32[]{:S(2)}) collective-permute-start(f32[41152]{0:T(1024)} %concatenate.72), channel_id=1, source_target_pairs={{0,2},{2,4},{4,6},{6,8},{8,10},{10,12},{12,14},{14,16},{16,18},{18... | collective-permute-start | bytes 493832 | tf_op jit(solution)/shard_map/ppermute | solution.py:225
  28.6 3.0 %copy-start = (f32[16,32,288]{2,1,0:T(8,128)}, f32[16,32,288]{2,1,0:T(8,128)S(1)}, u32[]{:S(2)}) copy-start(f32[16,32,288]{2,1,0:T(8,128)S(1)} %slice_convert_fusion) | copy-start | bytes 1769476
  30.6 28.6 %copy-start.5 = (f32[2,32,128]{2,1,0:T(8,128)}, f32[2,32,128]{2,1,0:T(8,128)S(1)}, u32[]{:S(2)}) copy-start(f32[2,32,128]{2,1,0:T(8,128)S(1)} %fusion.120) | copy-start | bytes 98308
  30.7 28.5 %copy-start.8 = (f32[3,32,128]{2,1,0:T(8,128)S(1)}, f32[3,32,128]{2,1,0:T(8,128)}, u32[]{:S(2)}) copy-start(f32[3,32,128]{2,1,0:T(8,128)} %get-tuple-element.108) | copy-start | bytes 147460
  30.8 28.5 %copy-start.9 = (f32[3,32,128]{2,1,0:T(8,128)S(1)}, f32[3,32,128]{2,1,0:T(8,128)}, u32[]{:S(2)}) copy-start(f32[3,32,128]{2,1,0:T(8,128)} %get-tuple-element.109) | copy-start | bytes 147460
  30.8 28.5 %copy-start.10 = (f32[3,32,128]{2,1,0:T(8,128)S(1)}, f32[3,32,128]{2,1,0:T(8,128)}, u32[]{:S(2)}) copy-start(f32[3,32,128]{2,1,0:T(8,128)} %get-tuple-element.86) | copy-start | bytes 147460
  44.7 46.0 %all-to-all-start.1 = ((bf16[16,32,288]{2,1,0:T(8,128)(2,1)}), bf16[16,32,288]{2,1,0:T(8,128)(2,1)S(1)}, u32[]{:S(2)}, u32[]{:S(2)}) async-start(bf16[16,32,288]{2,1,0:T(8,128)(2,1)} %broadcast_in_dim.52), calls=%async_computation.1 | async-start | bytes 786432 | tf_op jit(solution)/shard_map/all_to_all | solution.py:99
  60.8 22.4 %collective-permute-start.2 = (f32[11,32,128]{2,1,0:T(8,128)}, f32[11,32,128]{2,1,0:T(8,128)}, u32[]{:S(2)}, u32[]{:S(2)}) collective-permute-start(f32[11,32,128]{2,1,0:T(8,128)} %get-tuple-element.90), channel_id=1, source_target_pairs={{0,32},{32,64},{64,96},{96,128},{128,160},{160,192},{192,224},{224... | collective-permute-start | bytes 540680 | tf_op jit(solution)/shard_map/ppermute | solution.py:140
  64.2 19.8 %collective-permute-start.3 = (f32[11,32,128]{2,1,0:T(8,128)}, f32[11,32,128]{2,1,0:T(8,128)}, u32[]{:S(2)}, u32[]{:S(2)}) collective-permute-start(f32[11,32,128]{2,1,0:T(8,128)} %get-tuple-element.91), channel_id=1, source_target_pairs={{32,0},{64,32},{96,64},{128,96},{160,128},{192,160},{224,192},{256... | collective-permute-start | bytes 540680 | tf_op jit(solution)/shard_map/ppermute | solution.py:141
  67.4 3.2 %copy-start.16 = (s32[1024]{0:T(1024)S(1)}, s32[1024]{0:T(1024)}, u32[]{:S(2)}) copy-start(s32[1024]{0:T(1024)} %get-tuple-element.111) | copy-start | bytes 12292
  68.6 3.9 %copy-start.15 = (s32[1024]{0:T(1024)S(1)}, s32[1024]{0:T(1024)}, u32[]{:S(2)}) copy-start(s32[1024]{0:T(1024)} %get-tuple-element.112) | copy-start | bytes 12292
  75.2 1.0 %copy-start.3 = (f32[8,128,64]{1,2,0:T(8,128)S(1)}, f32[8,128,64]{1,2,0:T(8,128)}, u32[]{:S(2)}) copy-start(f32[8,128,64]{1,2,0:T(8,128)} %fusion.20) | copy-start | bytes 786436
  75.9 2.1 %copy-start.7 = (f32[3,18,64]{2,0,1:T(4,128)S(1)}, f32[3,18,64]{2,0,1:T(4,128)}, u32[]{:S(2)}) copy-start(f32[3,18,64]{2,0,1:T(4,128)} %copy.50) | copy-start | bytes 41476
  75.9 2.8 %copy-start.12 = (bf16[64,128]{1,0:T(8,128)(2,1)S(1)}, bf16[64,128]{1,0:T(8,128)(2,1)}, u32[]{:S(2)}) copy-start(bf16[64,128]{1,0:T(8,128)(2,1)} %fusion.87) | copy-start | bytes 49156
  75.9 2.8 %copy-start.13 = (bf16[64,128]{1,0:T(8,128)(2,1)S(1)}, bf16[64,128]{1,0:T(8,128)(2,1)}, u32[]{:S(2)}) copy-start(bf16[64,128]{1,0:T(8,128)(2,1)} %fusion.88) | copy-start | bytes 49156
  77.6 2.7 %slice-start = ((f32[16,32,288]{2,1,0:T(8,128)}), f32[16,32,64]{2,1,0:T(8,128)S(1)}, s32[]{:S(2)}) async-start(f32[16,32,288]{2,1,0:T(8,128)} %copy-done), calls=%async_computation.2 | async-start | bytes 524288 | tf_op jit(solution)/shard_map/slice | solution.py:133
  78.7 2.5 %copy-start.11 = (f32[3,16,64]{2,1,0:T(8,128)S(1)}, f32[3,16,64]{2,1,0:T(8,128)}, u32[]{:S(2)}) copy-start(f32[3,16,64]{2,1,0:T(8,128)} %dynamic_slice.147) | copy-start | bytes 36868
  80.3 1.6 %copy-start.4 = (bf16[48,64,128]{2,1,0:T(8,128)(2,1)S(1)}, bf16[48,64,128]{2,1,0:T(8,128)(2,1)}, u32[]{:S(2)}) copy-start(bf16[48,64,128]{2,1,0:T(8,128)(2,1)} %gather_fusion.1) | copy-start | bytes 2359300
  80.3 1.7 %copy-start.20 = (bf16[16,3]{1,0:T(8,128)(2,1)S(1)}, bf16[16,3]{1,0:T(8,128)(2,1)}, u32[]{:S(2)}) copy-start(bf16[16,3]{1,0:T(8,128)(2,1)} %copy.52) | copy-start | bytes 292
  82.0 1.2 %copy-start.14 = (f32[8,32,128]{2,1,0:T(8,128)S(1)}, f32[8,32,128]{2,1,0:T(8,128)}, u32[]{:S(2)}) copy-start(f32[8,32,128]{2,1,0:T(8,128)} %constant_dynamic-update-slice_fusion.2) | copy-start | bytes 393220
  82.0 2.0 %copy-start.6 = (f32[2,32,128]{2,1,0:T(8,128)S(1)}, f32[2,32,128]{2,1,0:T(8,128)}, u32[]{:S(2)}) copy-start(f32[2,32,128]{2,1,0:T(8,128)} %copy-done.5) | copy-start | bytes 98308

commit v15 on v14

--- a/solution.py
+++ b/solution.py
@@ -243,13 +243,8 @@
             reach = jnp.einsum("cra,crk->cak", lift_mats, reach, precision=HIGHEST)
             reach = reach.reshape(2 * cluster_count, RANK, RANK)
         reach_rows = jnp.einsum("rlp,lrk->lpk", basis_float, reach, precision=HIGHEST)
-        left_vectors, left_points, left_edges = unpack(from_left)
-        right_vectors, right_points, right_edges = unpack(from_right)
-        vector_rims = jnp.concatenate(
-            [left_vectors.astype(vectors.dtype), vectors, right_vectors.astype(vectors.dtype)], 0
-        )
-        point_rims = jnp.concatenate([left_points, points, right_points], 1)
-        nearby = near_field(vector_rims, point_rims, near_index, 0, leaf_zero, leaf_count)
+        left_edges = unpack(from_left)[2]
+        right_edges = unpack(from_right)[2]
         fields = []
         for height in range(depth_local):
             cluster_count = leaf_count >> height
@@ -260,11 +255,18 @@
             )
             mixers = as_float(coupling[0, first_slot : first_slot + cluster_count])
             fields.append(jnp.einsum("cra,cav->crv", mixers, stacked, precision=HIGHEST))
-        return nearby, fields, reach_rows
-
+        return fields, reach_rows
+
+    left_vectors, left_points, _ = unpack(from_left)
+    right_vectors, right_points, _ = unpack(from_right)
+    vector_rims = jnp.concatenate(
+        [left_vectors.astype(vectors.dtype), vectors, right_vectors.astype(vectors.dtype)], 0
+    )
+    point_rims = jnp.concatenate([left_points, points, right_points], 1)
+    nearby = near_field(vector_rims, point_rims, near_index, 0, leaf_zero, leaf_count)
     device_coupling = as_float(coupling[0, 2 * leaf_count - 2])
     device_coef = coefficients[depth_local][0]
-    downward, (nearby, fields, reach_rows) = upper_tree(
+    downward, (fields, reach_rows) = upper_tree(
         device_coef, device_coupling, upper_transfer, upper_coupling, ((from_left, from_right), as_float(transfer[0]), as_float(basis_leaves)), late
     )
     local_down = None

time: 97 us -> 85.9 us (0.89)
  the two profiles are of different devices: /device:TPU:32 before, /device:TPU:30 now
where the time goes in v15:
time: 85.9 us; the launch traced here: 84.7 us
  starting transfers between devices  35.4 us (41%)
  matrix products  20.1 us (23%)
  local copies, waits for them, and re-layouts  15.6 us (18%)
  waiting for transfers between devices  8.07 us (9%)
  other arithmetic  4.33 us (5%)
  between operations  1.14 us (1%)
    all_to_all x2, starting transfers between devices, spread_gather(): return lax.all_to_all(copies, axis, 0, 0, tiled=True)  23.8 us
    dot_general x18, matrix products, product(): return jnp.dot(matrix, operand, precision=HIGHEST)  6.8 us
    ppermute x1, waiting for transfers between devices, local(): lax.ppermute(head, SPACE, [(i + 1, i) for i in range(count - 1)])  5.24 us
    ppermute x1, starting transfers between devices, upper_tree(): lax.ppermute(tails, 'z', [(i, i + 1) for i in range(planes - 1)])  4.49 us
    ppermute x1, starting transfers between devices, local(): lax.ppermute(head, SPACE, [(i + 1, i) for i in range(count - 1)])  3.92 us
    dot_general x4, matrix products, late(): jnp.einsum('cra,cav->crv', mixers, stacked, precision=HIGHEST)  3.49 us
    dot_general x4, matrix products, local(): jnp.einsum('cra,cav->crv', lift_mats, children, precision=HIGHEST)  2.34 us
    gather x4, local copies, waits for them, and re-layouts, late(): extended[partner_table(cluster_count) + 2]  2.3 us
  transfers between devices with their start and end apart: 6, of which 4 were waited for; matrix products, arithmetic and copies ran while one was open for 31% of the time, Pallas kernels for 0%

profile of v15, /device:TPU:30, one launch (start us, length us, event | category | flops | bytes accessed | tf_op | source)
XLA Modules:
  0.0 84.7 jit_solution(13650343195202844842)
XLA Ops:
  0.0 1.0 %reshape.202 = bf16[32,16,64]{2,1,0:T(8,128)(2,1)S(1)} reshape(bf16[32,1024]{1,0:T(8,128)(2,1)} %param.19) | data formatting | bytes 131072 | tf_op jit(solution)/shard_map/reshape | solution.py:202
  1.1 1.2 %fusion.168 = (bf16[16,32,128]{2,1,0:T(8,128)(2,1)S(1)}, f32[16,32,128]{2,1,0:T(8,128)S(1)}) fusion(bf16[16,64,128]{2,1,0:T(8,128)(2,1)} %bitcast.287, bf16[32,16,64]{2,1,0:T(8,128)(2,1)S(1)} %reshape.202), kind=kOutput, calls=%fused_computation.272 | convolution fusion | flops 8454144 | bytes 720896 | tf_op jit(solution)/shard_map/rlp,lpv->lrv/dot_general | solution.py:205
  2.3 1.1 %bitcast_convert_fusion.4 = (bf16[8,32,128]{2,1,0:T(8,128)(2,1)S(1)}, f32[8,128,32]{1,2,0:T(8,128)S(1)}) fusion(f32[8,64,128]{2,1,0:T(8,128)S(1)} %bitcast.288, bf16[1,15,32,64]{3,2,1,0:T(8,128)(2,1)} %param.20), kind=kOutput, calls=%fused_computation.259 | convolution fusion | flops 25198592 | bytes 524288 | tf_op jit(solution)/shard_map/cra,cav->crv/dot_general | solution.py:212
  3.4 0.9 %bitcast_convert_fusion.3 = (bf16[4,32,128]{2,1,0:T(8,128)(2,1)S(1)}, f32[4,128,32]{1,2,0:T(8,128)S(1)}) fusion(f32[4,64,128]{2,1,0:T(8,128)S(1)} %bitcast.293, bf16[1,15,32,64]{3,2,1,0:T(8,128)(2,1)} %param.20), kind=kOutput, calls=%fused_computation.258 | convolution fusion | flops 12599296 | bytes 262144 | tf_op jit(solution)/shard_map/cra,cav->crv/dot_general | solution.py:212
  4.7 0.9 %broadcast_in_dim.46 = bf16[16,32,416]{2,1,0:T(8,128)(2,1)} broadcast(bf16[32,416]{1,0:T(8,128)(2,1)S(1)} %pad_maximum_fusion.12), dimensions={1,2} | broadcast | bytes 452608 | tf_op jit(solution)/shard_map/broadcast_in_dim | solution.py:98
  5.6 9.1 %all-to-all-start = ((bf16[16,32,416]{2,1,0:T(8,128)(2,1)}), bf16[16,32,416]{2,1,0:T(8,128)(2,1)S(1)}, u32[]{:S(2)}, u32[]{:S(2)}) async-start(bf16[16,32,416]{2,1,0:T(8,128)(2,1)} %broadcast_in_dim.46), calls=%async_computation | async-start | bytes 1048576 | tf_op jit(solution)/shard_map/all_to_all | solution.py:99
  15.1 1.9 %collective-permute-start = (f32[41152]{0:T(1024)S(1)}, f32[41152]{0:T(1024)S(1)}, u32[]{:S(2)}, u32[]{:S(2)}) collective-permute-start(f32[41152]{0:T(1024)S(1)} %concatenate.70), channel_id=1, source_target_pairs={{0,2},{2,4},{4,6},{6,8},{8,10},{10,12},{12,14},{14,16},{16,18},{18... | collective-permute-start | bytes 493832 | tf_op jit(solution)/shard_map/ppermute | solution.py:225
  17.2 3.9 %collective-permute-start.1 = (f32[41152]{0:T(1024)S(1)}, f32[41152]{0:T(1024)S(1)}, u32[]{:S(2)}, u32[]{:S(2)}) collective-permute-start(f32[41152]{0:T(1024)S(1)} %concatenate.71), channel_id=1, source_target_pairs={{2,0},{4,2},{6,4},{8,6},{10,8},{12,10},{14,12},{16,14},{18,16},{20... | collective-permute-start | bytes 493832 | tf_op jit(solution)/shard_map/ppermute | solution.py:226
  21.2 0.7 copy_convert_fusion
  22.5 0.6 constant_dynamic-update-slice_fusion.2
  23.1 0.3 collective-permute-done
  23.5 5.2 %collective-permute-done.1 = f32[41152]{0:T(1024)S(1)} collective-permute-done((f32[41152]{0:T(1024)S(1)}, f32[41152]{0:T(1024)S(1)}, u32[]{:S(2)}, u32[]{:S(2)}) %collective-permute-start.1) | collective-permute-done | bytes 164640 | tf_op jit(solution)/shard_map/ppermute | solution.py:226
  29.0 0.6 gather_fusion
  29.8 0.7 gather_fusion.1
  30.5 0.7 multiply_reduce_fusion
  31.1 1.8 %fusion.5 = f32[16,64,128,1]{2,1,3,0:T(8,128)} fusion(bf16[16,3,64,128]{3,2,1,0:T(8,128)(2,1)S(1)} %bitcast.296, f32[16,3,64,64]{3,2,1,0:T(8,128)S(1)} %multiply_reduce_fusion, bf16[16,3]{1,0:T(8,128)(2,1)S(1)} %copy.51), kind=kOutput, calls=%fused_computation.27 | convolution fusion | flops 51707904 | bytes 2097248 | tf_op jit(solution)/shard_map/while/body/eval_jaxpr/gkij,gkjv->giv/dot_general | solution.py:39
  33.0 1.0 %slice.434 = f32[16,32,96]{2,1,0:T(8,128)} slice(f32[16,32,288]{2,1,0:T(8,128)S(1)} %slice_convert_fusion), slice={[0:16], [0:32], [192:288]} | slice | bytes 393216 | tf_op jit(solution)/shard_map/slice | solution.py:134
  34.1 0.3 fusion.29
  34.3 0.7 fusion.160
  35.0 0.2 fusion.82
  35.2 0.6 fusion.166
  36.1 0.8 broadcast_in_dim.52
  36.9 14.7 %all-to-all-start.1 = ((bf16[16,32,288]{2,1,0:T(8,128)(2,1)}), bf16[16,32,288]{2,1,0:T(8,128)(2,1)S(1)}, u32[]{:S(2)}, u32[]{:S(2)}) async-start(bf16[16,32,288]{2,1,0:T(8,128)(2,1)} %broadcast_in_dim.52), calls=%async_computation.1 | async-start | bytes 786432 | tf_op jit(solution)/shard_map/all_to_all | solution.py:99
  51.7 1.7 %pad_maximum_fusion.4 = (f32[11,32,128]{2,1,0:T(8,128)}, f32[11,32,128]{2,1,0:T(8,128)}) fusion(f32[2,32,128]{2,1,0:T(8,128)S(1)} %fusion.120, f32[3,32,128]{2,1,0:T(8,128)} %get-tuple-element.86, f32[3,32,128]{2,1,0:T(8,128)} %get-tuple-element.109, f32[3,32,128]{2,1,0:T(8,128)S(1)} %get-tuple-element.49, f32[3,32,128]{2,1,0:T(8,128)} %get-tuple-element.87, ...), kind=kLoop, calls=%fused_computation.46 | loop fusion | flops 270336 | bytes 688128 | tf_op jit(solution)/shard_map/concatenate | solution.py:138
  53.4 4.5 %collective-permute-start.2 = (f32[11,32,128]{2,1,0:T(8,128)}, f32[11,32,128]{2,1,0:T(8,128)}, u32[]{:S(2)}, u32[]{:S(2)}) collective-permute-start(f32[11,32,128]{2,1,0:T(8,128)} %get-tuple-element.90), channel_id=1, source_target_pairs={{0,32},{32,64},{64,96},{96,128},{128,160},{160,192},{192,224},{224... | collective-permute-start | bytes 540680 | tf_op jit(solution)/shard_map/ppermute | solution.py:140
  57.9 1.3 %collective-permute-start.3 = (f32[11,32,128]{2,1,0:T(8,128)}, f32[11,32,128]{2,1,0:T(8,128)}, u32[]{:S(2)}, u32[]{:S(2)}) collective-permute-start(f32[11,32,128]{2,1,0:T(8,128)} %get-tuple-element.91), channel_id=1, source_target_pairs={{32,0},{64,32},{96,64},{128,96},{160,128},{192,160},{224,192},{256... | collective-permute-start | bytes 540680 | tf_op jit(solution)/shard_map/ppermute | solution.py:141
  59.3 0.2 fusion.126
  59.5 0.2 fusion.169
  59.8 0.2 fusion.24
  60.2 0.3 fusion.13
  60.5 0.8 reshape.232
  61.6 0.6 gather_fusion.5
  62.1 0.9 %fusion.109 = f32[2,128,32]{1,2,0:T(8,128)S(1)} fusion(f32[2,96,128]{2,1,0:T(8,128)S(1)} %bitcast.306, bf16[1,31,32,96]{3,2,1,0:T(8,128)(2,1)} %param.21), kind=kOutput, calls=%fused_computation.180 | convolution fusion | flops 9437184 | bytes 147456 | tf_op jit(solution)/shard_map/cra,cav->crv/dot_general | solution.py:257
  63.0 0.2 fusion.111
  63.3 0.6 gather_fusion.4
  63.8 1.0 %fusion.2 = f32[4,32,128]{2,1,0:T(8,128)S(1)} fusion(f32[4,32,128]{2,1,0:T(8,128)S(1)} %bitcast.308, f32[4,96,128]{2,1,0:T(8,128)S(1)} %bitcast.297, bf16[1,31,32,96]{3,2,1,0:T(8,128)(2,1)} %param.21), kind=kOutput, calls=%fused_computation.15 | convolution fusion | flops 18890752 | bytes 360448 | tf_op jit(solution)/shard_map/cra,cav->crv/dot_general | solution.py:257
  64.8 0.3 fusion.75
  65.1 0.6 gather_fusion.3
  65.7 1.1 %fusion.1 = f32[8,32,128]{2,1,0:T(8,128)S(1)} fusion(f32[8,32,128]{2,1,0:T(8,128)S(1)} %bitcast.300, f32[8,96,128]{2,1,0:T(8,128)S(1)} %bitcast.290, bf16[1,31,32,96]{3,2,1,0:T(8,128)(2,1)} %param.21), kind=kOutput, calls=%fused_computation.13 | convolution fusion | flops 37781504 | bytes 720896 | tf_op jit(solution)/shard_map/cra,cav->crv/dot_general | solution.py:257
  66.9 0.3 fusion.20
  67.2 0.6 gather_fusion.2
  67.9 0.5 fusion
  68.4 0.4 convolution_bitcast_fusion
  68.8 0.3 fusion.103
  69.1 0.2 fusion.101
  69.3 0.4 fusion.10
  69.8 0.2 fusion.99
  70.0 0.8 collective-permute-done.2
  70.8 0.8 slice_dynamic-update-slice_fusion.1
  71.5 1.8 %collective-permute-done.3 = f32[11,32,128]{2,1,0:T(8,128)} collective-permute-done((f32[11,32,128]{2,1,0:T(8,128)}, f32[11,32,128]{2,1,0:T(8,128)}, u32[]{:S(2)}, u32[]{:S(2)}) %collective-permute-start.3) | collective-permute-done | bytes 180256 | tf_op jit(solution)/shard_map/ppermute | solution.py:141
  73.3 0.8 slice_dynamic-update-slice_fusion
  74.1 0.9 %fusion.161 = (f32[3,32,128]{2,1,0:T(8,128)S(1)}, f32[3,32,128]{2,1,0:T(8,128)S(1)}, f32[3,32,128]{2,1,0:T(8,128)S(1)}) fusion(f32[11,32,128]{2,1,0:T(8,128)} %collective-permute-done.2), kind=kLoop, calls=%fused_computation.265 | loop fusion | bytes 294912 | tf_op jit(solution)/shard_map/slice | solution.py:161
  74.9 0.9 %fusion.162 = (f32[3,32,128]{2,1,0:T(8,128)S(1)}, f32[3,32,128]{2,1,0:T(8,128)S(1)}, f32[3,32,128]{2,1,0:T(8,128)S(1)}) fusion(f32[11,32,128]{2,1,0:T(8,128)} %collective-permute-done.3), kind=kLoop, calls=%fused_computation.266 | loop fusion | bytes 294912 | tf_op jit(solution)/shard_map/slice | solution.py:161
  75.9 0.9 %fusion.50 = f32[32,128]{1,0:T(8,128)S(1)} fusion(f32[32,128]{1,0:T(8,128)S(1)} %get-tuple-element.77, f32[32,128]{1,0:T(8,128)S(1)} %get-tuple-element.78, f32[32,128]{1,0:T(8,128)S(1)} %get-tuple-element.76, f32[16,32,96]{2,1,0:T(8,128)} %slice.434, s32[]{:T(128)S(6)} %select_n.310), kind=kOutput, calls=%fused_computation.98 | convolution fusion | flops 4743168 | bytes 81924 | tf_op jit(solution)/shard_map/dot_general | solution.py:63
  76.8 0.9 %fusion.44 = f32[32,128]{1,0:T(8,128)S(1)} fusion(f32[32,128]{1,0:T(8,128)S(1)} %get-tuple-element.71, f32[32,128]{1,0:T(8,128)S(1)} %get-tuple-element.72, f32[32,128]{1,0:T(8,128)S(1)} %get-tuple-element.70, f32[16,32,96]{2,1,0:T(8,128)} %slice.434, s32[]{:T(128)S(6)} %select_n.299), kind=kOutput, calls=%fused_computation.92 | convolution fusion | flops 4743168 | bytes 81924 | tf_op jit(solution)/shard_map/dot_general | solution.py:63
  77.7 0.9 %fusion.38 = f32[32,128]{1,0:T(8,128)S(1)} fusion(f32[32,128]{1,0:T(8,128)S(1)} %get-tuple-element.54, f32[32,128]{1,0:T(8,128)S(1)} %get-tuple-element.55, f32[32,128]{1,0:T(8,128)S(1)} %get-tuple-element.53, f32[16,32,96]{2,1,0:T(8,128)} %slice.434, s32[]{:T(128)S(6)} %select_n.288), kind=kOutput, calls=%fused_computation.86 | convolution fusion | flops 4743168 | bytes 81924 | tf_op jit(solution)/shard_map/dot_general | solution.py:63
  78.6 0.8 convolution_bitcast_fusion.4
  79.4 0.3 convolution_add_fusion.6
  80.2 0.2 fusion.79
  80.5 0.2 fusion.97
  80.7 0.2 fusion.95
  81.0 0.9 %fusion.56 = f32[32,128]{1,0:T(8,128)S(1)} fusion(f32[32,128]{1,0:T(8,128)S(1)} %get-tuple-element.44, f32[32,128]{1,0:T(8,128)S(1)} %get-tuple-element.43, f32[32,128]{1,0:T(8,128)S(1)} %get-tuple-element.42, f32[16,32,96]{2,1,0:T(8,128)} %slice.434), kind=kOutput, calls=%fused_computation.104 | convolution fusion | flops 4743168 | bytes 81920 | tf_op jit(solution)/shard_map/dot_general | solution.py:63
  82.8 1.0 %convolution_add_fusion = f32[16,64,128]{2,1,0:T(8,128)S(1)} fusion(f32[16,64,128]{2,1,0:T(8,128)S(1)} %convolution_bitcast_fusion, f32[16,64,32]{1,2,0:T(8,128)S(1)} %fusion.10, f32[32,128,1]{1,0,2:T(8,128)S(1)} %fusion.3), kind=kOutput, calls=%fused_computation.8 | convolution fusion | flops 50462720 | bytes 1196032 | tf_op jit(solution)/shard_map/lpk,kv->lpv/dot_general | solution.py:285
  83.9 0.8 fusion.8
  (125 shorter events, 4.5 us)
Async XLA Ops:
  0.0 4.3 %copy-start.2 = (bf16[1,15,32,64]{3,2,1,0:T(8,128)(2,1)S(1)}, bf16[1,15,32,64]{3,2,1,0:T(8,128)(2,1)}, u32[]{:S(2)}) copy-start(bf16[1,15,32,64]{3,2,1,0:T(8,128)(2,1)} %param.20) | copy-start | bytes 184324
  0.0 4.6 %copy-start.15 = (bf16[1,32,64]{2,1,0:T(8,128)(2,1)S(1)}, bf16[1,32,64]{2,1,0:T(8,128)(2,1)}, u32[]{:S(2)}) copy-start(bf16[1,32,64]{2,1,0:T(8,128)(2,1)} %param.22) | copy-start | bytes 12292
  0.0 4.6 %copy-start.14 = (bf16[1,32,96]{2,1,0:T(8,128)(2,1)S(1)}, bf16[1,32,96]{2,1,0:T(8,128)(2,1)}, u32[]{:S(2)}) copy-start(bf16[1,32,96]{2,1,0:T(8,128)(2,1)} %param.23) | copy-start | bytes 18436
  1.0 13.7 %copy-start.1 = (bf16[1024,128]{1,0:T(8,128)(2,1)S(1)}, bf16[1024,128]{1,0:T(8,128)(2,1)}, u32[]{:S(2)}) copy-start(bf16[1024,128]{1,0:T(8,128)(2,1)} %param.16) | copy-start | bytes 786436
  2.3 12.5 %copy-start.12 = (f32[3,1024]{1,0:T(4,128)S(1)}, f32[3,1024]{1,0:T(4,128)}, u32[]{:S(2)}) copy-start(f32[3,1024]{1,0:T(4,128)} %param.17) | copy-start | bytes 36868
  5.6 16.4 %copy-start.13 = (s32[16,3]{0,1:T(4,128)S(1)}, s32[16,3]{0,1:T(4,128)}, u32[]{:S(2)}) copy-start(s32[16,3]{0,1:T(4,128)} %param.18) | copy-start | bytes 580
  5.6 16.6 %copy-start.18 = (s32[48]{0:T(128)S(1)}, s32[48]{0:T(128)}, u32[]{:S(2)}) copy-start(s32[48]{0:T(128)} %constant.260) | copy-start | bytes 580
  5.6 16.6 %copy-start.19 = (s32[24]{0:T(128)S(1)}, s32[24]{0:T(128)}, u32[]{:S(2)}) copy-start(s32[24]{0:T(128)} %constant.261) | copy-start | bytes 292
  5.6 16.6 %copy-start.16 = (s32[12]{0:T(128)S(1)}, s32[12]{0:T(128)}, u32[]{:S(2)}) copy-start(s32[12]{0:T(128)} %constant.262) | copy-start | bytes 148
  5.6 16.6 %copy-start.17 = (s32[6]{0:T(128)S(1)}, s32[6]{0:T(128)}, u32[]{:S(2)}) copy-start(s32[6]{0:T(128)} %constant.263) | copy-start | bytes 76
  5.6 27.3 %all-to-all-start = ((bf16[16,32,416]{2,1,0:T(8,128)(2,1)}), bf16[16,32,416]{2,1,0:T(8,128)(2,1)S(1)}, u32[]{:S(2)}, u32[]{:S(2)}) async-start(bf16[16,32,416]{2,1,0:T(8,128)(2,1)} %broadcast_in_dim.46), calls=%async_computation | async-start | bytes 1048576 | tf_op jit(solution)/shard_map/all_to_all | solution.py:99
  15.1 8.3 %collective-permute-start = (f32[41152]{0:T(1024)S(1)}, f32[41152]{0:T(1024)S(1)}, u32[]{:S(2)}, u32[]{:S(2)}) collective-permute-start(f32[41152]{0:T(1024)S(1)} %concatenate.70), channel_id=1, source_target_pairs={{0,2},{2,4},{4,6},{6,8},{8,10},{10,12},{12,14},{14,16},{16,18},{18... | collective-permute-start | bytes 493832 | tf_op jit(solution)/shard_map/ppermute | solution.py:225
  17.2 11.5 %collective-permute-start.1 = (f32[41152]{0:T(1024)S(1)}, f32[41152]{0:T(1024)S(1)}, u32[]{:S(2)}, u32[]{:S(2)}) collective-permute-start(f32[41152]{0:T(1024)S(1)} %concatenate.71), channel_id=1, source_target_pairs={{2,0},{4,2},{6,4},{8,6},{10,8},{12,10},{14,12},{16,14},{18,16},{20... | collective-permute-start | bytes 493832 | tf_op jit(solution)/shard_map/ppermute | solution.py:226
  23.4 6.4 %copy-start.7 = (f32[41152]{0:T(1024)}, f32[41152]{0:T(1024)S(1)}, u32[]{:S(2)}) copy-start(f32[41152]{0:T(1024)S(1)} %collective-permute-done) | copy-start | bytes 493828
  28.7 1.0 %copy-start.9 = (f32[41152]{0:T(1024)}, f32[41152]{0:T(1024)S(1)}, u32[]{:S(2)}) copy-start(f32[41152]{0:T(1024)S(1)} %collective-permute-done.1) | copy-start | bytes 493828
  33.0 2.8 %copy-start = (f32[16,32,288]{2,1,0:T(8,128)}, f32[16,32,288]{2,1,0:T(8,128)S(1)}, u32[]{:S(2)}) copy-start(f32[16,32,288]{2,1,0:T(8,128)S(1)} %slice_convert_fusion) | copy-start | bytes 1769476
  36.9 43.1 %all-to-all-start.1 = ((bf16[16,32,288]{2,1,0:T(8,128)(2,1)}), bf16[16,32,288]{2,1,0:T(8,128)(2,1)S(1)}, u32[]{:S(2)}, u32[]{:S(2)}) async-start(bf16[16,32,288]{2,1,0:T(8,128)(2,1)} %broadcast_in_dim.52), calls=%async_computation.1 | async-start | bytes 786432 | tf_op jit(solution)/shard_map/all_to_all | solution.py:99
  51.7 9.7 %copy-start.8 = (f32[41152]{0:T(1024)S(1)}, f32[41152]{0:T(1024)}, u32[]{:S(2)}) copy-start(f32[41152]{0:T(1024)} %copy-done.7) | copy-start | bytes 493828
  51.7 9.8 %copy-start.10 = (f32[41152]{0:T(1024)S(1)}, f32[41152]{0:T(1024)}, u32[]{:S(2)}) copy-start(f32[41152]{0:T(1024)} %copy-done.9) | copy-start | bytes 493828
  53.4 17.4 %collective-permute-start.2 = (f32[11,32,128]{2,1,0:T(8,128)}, f32[11,32,128]{2,1,0:T(8,128)}, u32[]{:S(2)}, u32[]{:S(2)}) collective-permute-start(f32[11,32,128]{2,1,0:T(8,128)} %get-tuple-element.90), channel_id=1, source_target_pairs={{0,32},{32,64},{64,96},{96,128},{128,160},{160,192},{192,224},{224... | collective-permute-start | bytes 540680 | tf_op jit(solution)/shard_map/ppermute | solution.py:140
  57.9 15.4 %collective-permute-start.3 = (f32[11,32,128]{2,1,0:T(8,128)}, f32[11,32,128]{2,1,0:T(8,128)}, u32[]{:S(2)}, u32[]{:S(2)}) collective-permute-start(f32[11,32,128]{2,1,0:T(8,128)} %get-tuple-element.91), channel_id=1, source_target_pairs={{32,0},{64,32},{96,64},{128,96},{160,128},{192,160},{224,192},{256... | collective-permute-start | bytes 540680 | tf_op jit(solution)/shard_map/ppermute | solution.py:141
  66.8 1.0 %copy-start.6 = (bf16[1,31,32,96]{3,2,1,0:T(8,128)(2,1)S(1)}, bf16[1,31,32,96]{3,2,1,0:T(8,128)(2,1)}, u32[]{:S(2)}) copy-start(bf16[1,31,32,96]{3,2,1,0:T(8,128)(2,1)} %param.21) | copy-start | bytes 571396
  67.8 1.0 %slice-start = ((f32[16,32,288]{2,1,0:T(8,128)}), f32[16,32,64]{2,1,0:T(8,128)S(1)}, s32[]{:S(2)}) async-start(f32[16,32,288]{2,1,0:T(8,128)} %copy-done), calls=%async_computation.2 | async-start | bytes 524288 | tf_op jit(solution)/shard_map/slice | solution.py:133
  67.8 1.5 %copy-start.3 = (f32[32,16,64]{2,0,1:T(8,128)S(1)}, f32[32,16,64]{2,0,1:T(8,128)}, u32[]{:S(2)}) copy-start(f32[32,16,64]{2,0,1:T(8,128)} %copy_convert_fusion) | copy-start | bytes 393220
  67.8 1.5 %copy-start.4 = (f32[16,32,32]{1,0,2:T(8,128)S(1)}, f32[16,32,32]{1,0,2:T(8,128)}, u32[]{:S(2)}) copy-start(f32[16,32,32]{1,0,2:T(8,128)} %reshape.232) | copy-start | bytes 196612
  67.9 2.9 %copy-start.11 = (f32[8,32,128]{2,1,0:T(8,128)S(1)}, f32[8,32,128]{2,1,0:T(8,128)}, u32[]{:S(2)}) copy-start(f32[8,32,128]{2,1,0:T(8,128)} %constant_dynamic-update-slice_fusion.2) | copy-start | bytes 393220
  80.9 2.9 %copy-start.5 = (f32[16,64,128,1]{2,1,3,0:T(8,128)S(1)}, f32[16,64,128,1]{2,1,3,0:T(8,128)}, u32[]{:S(2)}) copy-start(f32[16,64,128,1]{2,1,3,0:T(8,128)} %fusion.5) | copy-start | bytes 1572868

commit v16 on v15

--- a/solution.py
+++ b/solution.py
@@ -233,7 +233,7 @@
             done += size
         return pieces
 
-    def late(held):
+    def early(held):
         (from_left, from_right), lift_stack, basis_float = held
         reach = jnp.eye(RANK, dtype=jnp.float32)[None]
         for height in range(depth_local - 1, -1, -1):
@@ -266,9 +266,14 @@
     nearby = near_field(vector_rims, point_rims, near_index, 0, leaf_zero, leaf_count)
     device_coupling = as_float(coupling[0, 2 * leaf_count - 2])
     device_coef = coefficients[depth_local][0]
-    downward, (fields, reach_rows) = upper_tree(
-        device_coef, device_coupling, upper_transfer, upper_coupling, ((from_left, from_right), as_float(transfer[0]), as_float(basis_leaves)), late
-    )
+    fields, reach_rows = early(
+        ((from_left, from_right), as_float(transfer[0]), as_float(basis_leaves))
+    )
+    downward, _ = upper_tree(
+        device_coef, device_coupling, upper_transfer, upper_coupling, (), lambda held: None
+    )
+
+
     local_down = None
     for height in range(depth_local - 1, -1, -1):
         cluster_count = leaf_count >> height + 1

time: 85.9 us -> 87.8 us (1.022)
  the two profiles are of different devices: /device:TPU:30 before, /device:TPU:1 now
where the time goes in v16:
time: 87.8 us; the launch traced here: 87.1 us
  starting transfers between devices  35.3 us (40%)
  waiting for transfers between devices  17.5 us (20%)
  local copies, waits for them, and re-layouts  15.8 us (18%)
  matrix products  14.6 us (17%)
  other arithmetic  2.79 us (3%)
  between operations  1.13 us (1%)
    all_to_all x2, starting transfers between devices, spread_gather(): return lax.all_to_all(copies, axis, 0, 0, tiled=True)  26.2 us
    ppermute x1, waiting for transfers between devices, upper_tree(): lax.ppermute(tails, 'z', [(i, i + 1) for i in range(planes - 1)])  12 us
    dot_general x18, matrix products, product(): return jnp.dot(matrix, operand, precision=HIGHEST)  3.89 us
    ppermute x1, starting transfers between devices, upper_tree(): lax.ppermute(tails, 'z', [(i, i + 1) for i in range(planes - 1)])  3.28 us
    ppermute x1, starting transfers between devices, local(): lax.ppermute(tail, SPACE, [(i, i + 1) for i in range(count - 1)])  3.27 us
    ppermute x1, waiting for transfers between devices, upper_tree(): lax.ppermute(heads, 'z', [(i + 1, i) for i in range(planes - 1)])  2.95 us
    unnamed x36, local copies, waits for them, and re-layouts  2.54 us
    ppermute x1, waiting for transfers between devices, local(): lax.ppermute(head, SPACE, [(i + 1, i) for i in range(count - 1)])  2.46 us
  transfers between devices with their start and end apart: 6, of which 3 were waited for; matrix products, arithmetic and copies ran while one was open for 24% of the time, Pallas kernels for 0%

profile of v16, /device:TPU:1, one launch (start us, length us, event | category | flops | bytes accessed | tf_op | source)
XLA Modules:
  0.0 87.1 jit_solution(9349528085960874184)
XLA Ops:
  0.0 1.0 %reshape.203 = bf16[32,16,64]{2,1,0:T(8,128)(2,1)S(1)} reshape(bf16[32,1024]{1,0:T(8,128)(2,1)} %param.19) | data formatting | bytes 131072 | tf_op jit(solution)/shard_map/reshape | solution.py:202
  1.1 1.2 %fusion.171 = (bf16[16,32,128]{2,1,0:T(8,128)(2,1)S(1)}, f32[16,32,128]{2,1,0:T(8,128)S(1)}) fusion(bf16[16,64,128]{2,1,0:T(8,128)(2,1)} %bitcast.295, bf16[32,16,64]{2,1,0:T(8,128)(2,1)S(1)} %reshape.203), kind=kOutput, calls=%fused_computation.278 | convolution fusion | flops 8454144 | bytes 720896 | tf_op jit(solution)/shard_map/rlp,lpv->lrv/dot_general | solution.py:205
  2.3 1.1 %bitcast_convert_fusion.3 = (bf16[8,32,128]{2,1,0:T(8,128)(2,1)S(1)}, f32[8,128,32]{1,2,0:T(8,128)S(1)}) fusion(f32[8,64,128]{2,1,0:T(8,128)S(1)} %bitcast.296, bf16[1,15,32,64]{3,2,1,0:T(8,128)(2,1)} %param.20), kind=kOutput, calls=%fused_computation.265 | convolution fusion | flops 25198592 | bytes 524288 | tf_op jit(solution)/shard_map/cra,cav->crv/dot_general | solution.py:212
  3.4 0.9 %bitcast_convert_fusion.2 = (bf16[4,32,128]{2,1,0:T(8,128)(2,1)S(1)}, f32[4,128,32]{1,2,0:T(8,128)S(1)}) fusion(f32[4,64,128]{2,1,0:T(8,128)S(1)} %bitcast.301, bf16[1,15,32,64]{3,2,1,0:T(8,128)(2,1)} %param.20), kind=kOutput, calls=%fused_computation.264 | convolution fusion | flops 12599296 | bytes 262144 | tf_op jit(solution)/shard_map/cra,cav->crv/dot_general | solution.py:212
  4.3 0.2 fusion.116
  4.7 0.9 broadcast_in_dim.50
  5.6 7.6 %all-to-all-start = ((bf16[16,32,416]{2,1,0:T(8,128)(2,1)}), bf16[16,32,416]{2,1,0:T(8,128)(2,1)S(1)}, u32[]{:S(2)}, u32[]{:S(2)}) async-start(bf16[16,32,416]{2,1,0:T(8,128)(2,1)} %broadcast_in_dim.50), calls=%async_computation | async-start | bytes 1048576 | tf_op jit(solution)/shard_map/all_to_all | solution.py:99
  13.6 3.3 %collective-permute-start = (f32[41152]{0:T(1024)S(1)}, f32[41152]{0:T(1024)S(1)}, u32[]{:S(2)}, u32[]{:S(2)}) collective-permute-start(f32[41152]{0:T(1024)S(1)} %concatenate.70), channel_id=1, source_target_pairs={{0,2},{2,4},{4,6},{6,8},{8,10},{10,12},{12,14},{14,16},{16,18},{18... | collective-permute-start | bytes 493832 | tf_op jit(solution)/shard_map/ppermute | solution.py:225
  17.1 1.3 %collective-permute-start.1 = (f32[41152]{0:T(1024)S(1)}, f32[41152]{0:T(1024)S(1)}, u32[]{:S(2)}, u32[]{:S(2)}) collective-permute-start(f32[41152]{0:T(1024)S(1)} %concatenate.71), channel_id=1, source_target_pairs={{2,0},{4,2},{6,4},{8,6},{10,8},{12,10},{14,12},{16,14},{18,16},{20... | collective-permute-start | bytes 493832 | tf_op jit(solution)/shard_map/ppermute | solution.py:226
  18.7 0.2 convolution_bitcast_fusion.7
  19.0 0.2 convolution_bitcast_fusion.5
  19.3 0.2 convolution_bitcast_fusion.4
  19.7 0.3 convolution_bitcast_fusion.1
  20.6 0.6 constant_dynamic-update-slice_fusion.2
  21.3 2.5 %collective-permute-done.1 = f32[41152]{0:T(1024)S(1)} collective-permute-done((f32[41152]{0:T(1024)S(1)}, f32[41152]{0:T(1024)S(1)}, u32[]{:S(2)}, u32[]{:S(2)}) %collective-permute-start.1) | collective-permute-done | bytes 164640 | tf_op jit(solution)/shard_map/ppermute | solution.py:226
  24.1 0.6 dynamic_slice.147
  24.7 0.7 fusion.166
  25.4 0.7 fusion.167
  26.1 0.6 gather_fusion.5
  26.7 0.2 fusion.111
  26.8 0.2 fusion.114
  27.1 0.6 gather_fusion.4
  27.7 0.2 fusion.2
  27.9 0.3 fusion.76
  28.2 0.6 gather_fusion.3
  28.8 0.3 fusion.1
  29.1 0.3 fusion.20
  29.4 0.6 gather_fusion.2
  30.1 0.5 fusion
  30.6 0.4 convolution_bitcast_fusion
  31.0 0.6 gather_fusion
  31.7 0.7 gather_fusion.1
  32.4 0.7 multiply_reduce_fusion
  33.1 1.8 %fusion.5 = f32[16,64,128,1]{2,1,3,0:T(8,128)} fusion(bf16[16,3,64,128]{3,2,1,0:T(8,128)(2,1)S(1)} %bitcast.304, f32[16,3,64,64]{3,2,1,0:T(8,128)S(1)} %multiply_reduce_fusion, bf16[16,3]{1,0:T(8,128)(2,1)S(1)} %copy.50), kind=kOutput, calls=%fused_computation.32 | convolution fusion | flops 51707904 | bytes 2097248 | tf_op jit(solution)/shard_map/while/body/eval_jaxpr/gkij,gkjv->giv/dot_general | solution.py:39
  35.2 0.3 fusion.27
  35.4 0.7 fusion.163
  36.1 0.2 fusion.82
  36.3 0.7 fusion.169
  36.9 0.2 fusion.122
  37.2 0.8 broadcast_in_dim.52
  38.0 18.6 %all-to-all-start.1 = ((bf16[16,32,288]{2,1,0:T(8,128)(2,1)}), bf16[16,32,288]{2,1,0:T(8,128)(2,1)S(1)}, u32[]{:S(2)}, u32[]{:S(2)}) async-start(bf16[16,32,288]{2,1,0:T(8,128)(2,1)} %broadcast_in_dim.52), calls=%async_computation.1 | async-start | bytes 786432 | tf_op jit(solution)/shard_map/all_to_all | solution.py:99
  56.6 0.9 %pad_maximum_fusion.4 = (f32[11,32,128]{2,1,0:T(8,128)S(1)}, f32[11,32,128]{2,1,0:T(8,128)S(1)}) fusion(f32[2,32,128]{2,1,0:T(8,128)S(1)} %fusion.122, f32[3,32,128]{2,1,0:T(8,128)} %get-tuple-element.78, f32[3,32,128]{2,1,0:T(8,128)} %get-tuple-element.101, f32[3,32,128]{2,1,0:T(8,128)S(1)} %get-tuple-element.41, f32[3,32,128]{2,1,0:T(8,128)} %get-tuple-element.79, ...), kind=kLoop, calls=%fused_computation.50 | loop fusion | flops 270336 | bytes 688128 | tf_op jit(solution)/shard_map/concatenate | solution.py:138
  57.6 3.3 %collective-permute-start.2 = (f32[11,32,128]{2,1,0:T(8,128)S(1)}, f32[11,32,128]{2,1,0:T(8,128)S(1)}, u32[]{:S(2)}, u32[]{:S(2)}) collective-permute-start(f32[11,32,128]{2,1,0:T(8,128)S(1)} %get-tuple-element.82), channel_id=1, source_target_pairs={{0,32},{32,64},{64,96},{96,128},{128,160},{160,192},{192,224},{224... | collective-permute-start | bytes 540680 | tf_op jit(solution)/shard_map/ppermute | solution.py:140
  60.9 1.3 %collective-permute-start.3 = (f32[11,32,128]{2,1,0:T(8,128)S(1)}, f32[11,32,128]{2,1,0:T(8,128)S(1)}, u32[]{:S(2)}, u32[]{:S(2)}) collective-permute-start(f32[11,32,128]{2,1,0:T(8,128)S(1)} %get-tuple-element.83), channel_id=1, source_target_pairs={{32,0},{64,32},{96,64},{128,96},{160,128},{192,160},{224,192},{256... | collective-permute-start | bytes 540680 | tf_op jit(solution)/shard_map/ppermute | solution.py:141
  62.2 0.3 fusion.105
  62.5 0.2 fusion.103
  62.7 0.2 fusion.101
  62.9 12.0 %collective-permute-done.2 = f32[11,32,128]{2,1,0:T(8,128)S(1)} collective-permute-done((f32[11,32,128]{2,1,0:T(8,128)S(1)}, f32[11,32,128]{2,1,0:T(8,128)S(1)}, u32[]{:S(2)}, u32[]{:S(2)}) %collective-permute-start.2) | collective-permute-done | bytes 180256 | tf_op jit(solution)/shard_map/ppermute | solution.py:140
  75.0 0.6 slice_dynamic-update-slice_fusion.1
  75.6 0.6 constant_dynamic-update-slice_fusion.1
  76.2 3.0 %collective-permute-done.3 = f32[11,32,128]{2,1,0:T(8,128)S(1)} collective-permute-done((f32[11,32,128]{2,1,0:T(8,128)S(1)}, f32[11,32,128]{2,1,0:T(8,128)S(1)}, u32[]{:S(2)}, u32[]{:S(2)}) %collective-permute-start.3) | collective-permute-done | bytes 180256 | tf_op jit(solution)/shard_map/ppermute | solution.py:141
  79.1 0.6 slice_dynamic-update-slice_fusion
  79.8 0.6 constant_dynamic-update-slice_fusion
  80.5 0.8 dynamic-slice_bitcast_fusion.5
  81.4 0.2 fusion.44
  81.8 0.8 convolution_bitcast_fusion.9
  82.6 0.3 convolution_add_fusion.6
  83.4 0.2 fusion.80
  83.7 0.2 fusion.99
  83.9 0.2 fusion.97
  84.8 0.2 convolution_add_fusion.2
  85.1 0.2 fusion.3
  85.3 1.0 %convolution_add_fusion = f32[16,64,128]{2,1,0:T(8,128)S(1)} fusion(f32[16,64,128]{2,1,0:T(8,128)S(1)} %convolution_bitcast_fusion, f32[16,64,32]{1,2,0:T(8,128)S(1)} %convolution_bitcast_fusion.1, f32[32,128,1]{1,0,2:T(8,128)S(1)} %fusion.3), kind=kOutput, calls=%fused_computation.8 | convolution fusion | flops 50462720 | bytes 1196032 | tf_op jit(solution)/shard_map/lpk,kv->lpv/dot_general | solution.py:290
  86.3 0.8 fusion.8
  (115 shorter events, 4.4 us)
Async XLA Ops:
  0.0 4.3 %copy-start.2 = (bf16[1,15,32,64]{3,2,1,0:T(8,128)(2,1)S(1)}, bf16[1,15,32,64]{3,2,1,0:T(8,128)(2,1)}, u32[]{:S(2)}) copy-start(bf16[1,15,32,64]{3,2,1,0:T(8,128)(2,1)} %param.20) | copy-start | bytes 184324
  0.0 4.6 %copy-start.11 = (bf16[1,32,64]{2,1,0:T(8,128)(2,1)S(1)}, bf16[1,32,64]{2,1,0:T(8,128)(2,1)}, u32[]{:S(2)}) copy-start(bf16[1,32,64]{2,1,0:T(8,128)(2,1)} %param.22) | copy-start | bytes 12292
  0.0 4.6 %copy-start.10 = (bf16[1,32,96]{2,1,0:T(8,128)(2,1)S(1)}, bf16[1,32,96]{2,1,0:T(8,128)(2,1)}, u32[]{:S(2)}) copy-start(bf16[1,32,96]{2,1,0:T(8,128)(2,1)} %param.23) | copy-start | bytes 18436
  1.0 12.2 %copy-start.1 = (bf16[1024,128]{1,0:T(8,128)(2,1)S(1)}, bf16[1024,128]{1,0:T(8,128)(2,1)}, u32[]{:S(2)}) copy-start(bf16[1024,128]{1,0:T(8,128)(2,1)} %param.16) | copy-start | bytes 786436
  2.3 11.0 %copy-start.8 = (f32[3,1024]{1,0:T(4,128)S(1)}, f32[3,1024]{1,0:T(4,128)}, u32[]{:S(2)}) copy-start(f32[3,1024]{1,0:T(4,128)} %param.17) | copy-start | bytes 36868
  5.6 29.3 %all-to-all-start = ((bf16[16,32,416]{2,1,0:T(8,128)(2,1)}), bf16[16,32,416]{2,1,0:T(8,128)(2,1)S(1)}, u32[]{:S(2)}, u32[]{:S(2)}) async-start(bf16[16,32,416]{2,1,0:T(8,128)(2,1)} %broadcast_in_dim.50), calls=%async_computation | async-start | bytes 1048576 | tf_op jit(solution)/shard_map/all_to_all | solution.py:99
  13.4 6.7 %copy-start.9 = (s32[16,3]{0,1:T(4,128)S(1)}, s32[16,3]{0,1:T(4,128)}, u32[]{:S(2)}) copy-start(s32[16,3]{0,1:T(4,128)} %param.18) | copy-start | bytes 580
  13.4 6.9 %copy-start.14 = (s32[12]{0:T(128)S(1)}, s32[12]{0:T(128)}, u32[]{:S(2)}) copy-start(s32[12]{0:T(128)} %constant.262) | copy-start | bytes 148
  13.5 6.9 %copy-start.15 = (s32[6]{0:T(128)S(1)}, s32[6]{0:T(128)}, u32[]{:S(2)}) copy-start(s32[6]{0:T(128)} %constant.263) | copy-start | bytes 76
  13.5 6.9 %copy-start.12 = (s32[48]{0:T(128)S(1)}, s32[48]{0:T(128)}, u32[]{:S(2)}) copy-start(s32[48]{0:T(128)} %constant.260) | copy-start | bytes 580
  13.5 6.9 %copy-start.13 = (s32[24]{0:T(128)S(1)}, s32[24]{0:T(128)}, u32[]{:S(2)}) copy-start(s32[24]{0:T(128)} %constant.261) | copy-start | bytes 292
  13.6 7.6 %collective-permute-start = (f32[41152]{0:T(1024)S(1)}, f32[41152]{0:T(1024)S(1)}, u32[]{:S(2)}, u32[]{:S(2)}) collective-permute-start(f32[41152]{0:T(1024)S(1)} %concatenate.70), channel_id=1, source_target_pairs={{0,2},{2,4},{4,6},{6,8},{8,10},{10,12},{12,14},{14,16},{16,18},{18... | collective-permute-start | bytes 493832 | tf_op jit(solution)/shard_map/ppermute | solution.py:225
  17.1 6.7 %collective-permute-start.1 = (f32[41152]{0:T(1024)S(1)}, f32[41152]{0:T(1024)S(1)}, u32[]{:S(2)}, u32[]{:S(2)}) collective-permute-start(f32[41152]{0:T(1024)S(1)} %concatenate.71), channel_id=1, source_target_pairs={{2,0},{4,2},{6,4},{8,6},{10,8},{12,10},{14,12},{16,14},{18,16},{20... | collective-permute-start | bytes 493832 | tf_op jit(solution)/shard_map/ppermute | solution.py:226
  19.5 7.1 %copy-start.4 = (bf16[1,31,32,96]{3,2,1,0:T(8,128)(2,1)S(1)}, bf16[1,31,32,96]{3,2,1,0:T(8,128)(2,1)}, u32[]{:S(2)}) copy-start(bf16[1,31,32,96]{3,2,1,0:T(8,128)(2,1)} %param.21) | copy-start | bytes 571396
  27.7 1.7 %copy-start.5 = (f32[8192]{0:T(1024)S(1)}, f32[8192]{0:T(1024)}, u32[]{:S(2)}) copy-start(f32[8192]{0:T(1024)} %get-tuple-element.54) | copy-start | bytes 98308
  27.7 1.7 %copy-start.6 = (f32[8192]{0:T(1024)S(1)}, f32[8192]{0:T(1024)}, u32[]{:S(2)}) copy-start(f32[8192]{0:T(1024)} %get-tuple-element.58) | copy-start | bytes 98308
  30.5 1.9 %copy-start.7 = (f32[3,16,64]{2,1,0:T(8,128)S(1)}, f32[3,16,64]{2,1,0:T(8,128)}, u32[]{:S(2)}) copy-start(f32[3,16,64]{2,1,0:T(8,128)} %dynamic_slice.147) | copy-start | bytes 36868
  34.9 2.0 %copy-start = (f32[16,32,288]{2,1,0:T(8,128)}, f32[16,32,288]{2,1,0:T(8,128)S(1)}, u32[]{:S(2)}) copy-start(f32[16,32,288]{2,1,0:T(8,128)S(1)} %slice_convert_fusion) | copy-start | bytes 1769476
  36.9 25.2 %slice-start = ((f32[16,32,288]{2,1,0:T(8,128)}), f32[16,32,64]{2,1,0:T(8,128)S(1)}, s32[]{:S(2)}) async-start(f32[16,32,288]{2,1,0:T(8,128)} %copy-done), calls=%async_computation.2 | async-start | bytes 524288 | tf_op jit(solution)/shard_map/slice | solution.py:133
  38.0 45.2 %all-to-all-start.1 = ((bf16[16,32,288]{2,1,0:T(8,128)(2,1)}), bf16[16,32,288]{2,1,0:T(8,128)(2,1)S(1)}, u32[]{:S(2)}, u32[]{:S(2)}) async-start(bf16[16,32,288]{2,1,0:T(8,128)(2,1)} %broadcast_in_dim.52), calls=%async_computation.1 | async-start | bytes 786432 | tf_op jit(solution)/shard_map/all_to_all | solution.py:99
  57.6 17.4 %collective-permute-start.2 = (f32[11,32,128]{2,1,0:T(8,128)S(1)}, f32[11,32,128]{2,1,0:T(8,128)S(1)}, u32[]{:S(2)}, u32[]{:S(2)}) collective-permute-start(f32[11,32,128]{2,1,0:T(8,128)S(1)} %get-tuple-element.82), channel_id=1, source_target_pairs={{0,32},{32,64},{64,96},{96,128},{128,160},{160,192},{192,224},{224... | collective-permute-start | bytes 540680 | tf_op jit(solution)/shard_map/ppermute | solution.py:140
  60.9 18.3 %collective-permute-start.3 = (f32[11,32,128]{2,1,0:T(8,128)S(1)}, f32[11,32,128]{2,1,0:T(8,128)S(1)}, u32[]{:S(2)}, u32[]{:S(2)}) collective-permute-start(f32[11,32,128]{2,1,0:T(8,128)S(1)} %get-tuple-element.83), channel_id=1, source_target_pairs={{32,0},{64,32},{96,64},{128,96},{160,128},{192,160},{224,192},{256... | collective-permute-start | bytes 540680 | tf_op jit(solution)/shard_map/ppermute | solution.py:141
  84.1 2.2 %copy-start.3 = (f32[16,64,128,1]{2,1,3,0:T(8,128)S(1)}, f32[16,64,128,1]{2,1,3,0:T(8,128)}, u32[]{:S(2)}) copy-start(f32[16,64,128,1]{2,1,3,0:T(8,128)} %fusion.5) | copy-start | bytes 1572868

commit v17 on v15

--- a/solution.py
+++ b/solution.py
@@ -137,8 +137,12 @@
         inner.append(lift_up(plane_lift[2 ** (height - 1) :: 2**height], inner[-1]))
     tails = jnp.concatenate([level[-3:] for level in inner[:plane_bits]], 0)
     heads = jnp.concatenate([level[:3] for level in inner[:plane_bits]], 0)
-    from_left = lax.ppermute(tails, "z", [(i, i + 1) for i in range(planes - 1)])
-    from_right = lax.ppermute(heads, "z", [(i + 1, i) for i in range(planes - 1)])
+    from_left = as_float(
+        lax.ppermute(tails.astype(jnp.bfloat16), "z", [(i, i + 1) for i in range(planes - 1)])
+    )
+    from_right = as_float(
+        lax.ppermute(heads.astype(jnp.bfloat16), "z", [(i + 1, i) for i in range(planes - 1)])
+    )
     outer_unit = jnp.concatenate([inner[plane_bits][0], plane_held[0, :, columns:]], 1)
     outer_unit, held, plane_lift, plane_mix = lax.optimization_barrier(
         (outer_unit.astype(jnp.bfloat16), held, plane_lift, plane_mix)
@@ -235,6 +239,8 @@
 
     def late(held):
         (from_left, from_right), lift_stack, basis_float = held
+        lift_stack = as_float(lift_stack)
+        basis_float = as_float(basis_float)
         reach = jnp.eye(RANK, dtype=jnp.float32)[None]
         for height in range(depth_local - 1, -1, -1):
             cluster_count = leaf_count >> height + 1
@@ -267,7 +273,7 @@
     device_coupling = as_float(coupling[0, 2 * leaf_count - 2])
     device_coef = coefficients[depth_local][0]
     downward, (fields, reach_rows) = upper_tree(
-        device_coef, device_coupling, upper_transfer, upper_coupling, ((from_left, from_right), as_float(transfer[0]), as_float(basis_leaves)), late
+        device_coef, device_coupling, upper_transfer, upper_coupling, ((from_left, from_right), transfer[0], basis_leaves), late
     )
     local_down = None
     for height in range(depth_local - 1, -1, -1):

time: 85.9 us -> 82.1 us (0.956)
  local copies, waits for them, and re-layouts: 15.6 us -> 11.7 us
    slice x2, local copies, waits for them, and re-layouts: 1.32 us -> 0.02 us  [upper_tree(): tails = jnp.concatenate([level[-3:] for level in inner[:plane_bits]], 0)]
    unnamed x44 -> x46, local copies, waits for them, and re-layouts: 2.22 us -> 1.16 us
    concatenate x1, other arithmetic: 1.72 us -> 0.7 us  [upper_tree(): tails = jnp.concatenate([level[-3:] for level in inner[:plane_bits]], 0)]
    dot_general x4, matrix products: 3.49 us -> 4.44 us  [late(): jnp.einsum('cra,cav->crv', mixers, stacked, precision=HIGHEST)]
  transfers between devices with their start and end apart: 6 -> 6, of which waited for: 4 -> 4; matrix products, arithmetic and copies ran while one was open for 31% -> 29% of each run, Pallas kernels for 0% -> 0%
where the time goes in v17:
time: 82.1 us; the launch traced here: 81 us
  starting transfers between devices  34.8 us (42%)
  matrix products  20.8 us (25%)
  local copies, waits for them, and re-layouts  11.7 us (14%)
  waiting for transfers between devices  8.42 us (10%)
  other arithmetic  4.07 us (5%)
  between operations  1.19 us (1%)
    all_to_all x2, starting transfers between devices, spread_gather(): return lax.all_to_all(copies, axis, 0, 0, tiled=True)  23.8 us
    dot_general x18, matrix products, product(): return jnp.dot(matrix, operand, precision=HIGHEST)  6.8 us
    ppermute x1, waiting for transfers between devices, local(): lax.ppermute(head, SPACE, [(i + 1, i) for i in range(count - 1)])  5.23 us
    dot_general x4, matrix products, late(): jnp.einsum('cra,cav->crv', mixers, stacked, precision=HIGHEST)  4.44 us
    ppermute x1, starting transfers between devices, local(): lax.ppermute(head, SPACE, [(i + 1, i) for i in range(count - 1)])  3.92 us
    ppermute x1, starting transfers between devices, upper_tree(): lax.ppermute(tails.astype(jnp.bfloat16), 'z', [(i, i + 1) for i in range(...  3.82 us
    ppermute x1, waiting for transfers between devices, upper_tree(): lax.ppermute(heads.astype(jnp.bfloat16), 'z', [(i + 1, i) for i in range(...  2.61 us
    gather x4, local copies, waits for them, and re-layouts, late(): extended[partner_table(cluster_count) + 2]  2.42 us
  transfers between devices with their start and end apart: 6, of which 4 were waited for; matrix products, arithmetic and copies ran while one was open for 29% of the time, Pallas kernels for 0%

profile of v17, /device:TPU:30, one launch (start us, length us, event | category | flops | bytes accessed | tf_op | source)
XLA Modules:
  0.0 81.0 jit_solution(18405918135100028240)
XLA Ops:
  0.0 1.0 %reshape.200 = bf16[32,16,64]{2,1,0:T(8,128)(2,1)S(1)} reshape(bf16[32,1024]{1,0:T(8,128)(2,1)} %param.19) | data formatting | bytes 131072 | tf_op jit(solution)/shard_map/reshape | solution.py:206
  1.1 1.2 %fusion.170 = (bf16[16,32,128]{2,1,0:T(8,128)(2,1)S(1)}, f32[16,32,128]{2,1,0:T(8,128)S(1)}) fusion(bf16[16,64,128]{2,1,0:T(8,128)(2,1)} %bitcast.283, bf16[32,16,64]{2,1,0:T(8,128)(2,1)S(1)} %reshape.200), kind=kOutput, calls=%fused_computation.272 | convolution fusion | flops 8454144 | bytes 720896 | tf_op jit(solution)/shard_map/rlp,lpv->lrv/dot_general | solution.py:209
  2.3 1.1 %bitcast_convert_fusion.3 = (bf16[8,32,128]{2,1,0:T(8,128)(2,1)S(1)}, f32[8,128,32]{1,2,0:T(8,128)S(1)}) fusion(f32[8,64,128]{2,1,0:T(8,128)S(1)} %bitcast.284, bf16[1,15,32,64]{3,2,1,0:T(8,128)(2,1)} %param.20), kind=kOutput, calls=%fused_computation.258 | convolution fusion | flops 25198592 | bytes 524288 | tf_op jit(solution)/shard_map/cra,cav->crv/dot_general | solution.py:216
  3.4 0.9 %bitcast_convert_fusion.2 = (bf16[4,32,128]{2,1,0:T(8,128)(2,1)S(1)}, f32[4,128,32]{1,2,0:T(8,128)S(1)}) fusion(f32[4,64,128]{2,1,0:T(8,128)S(1)} %bitcast.288, bf16[1,15,32,64]{3,2,1,0:T(8,128)(2,1)} %param.20), kind=kOutput, calls=%fused_computation.257 | convolution fusion | flops 12599296 | bytes 262144 | tf_op jit(solution)/shard_map/cra,cav->crv/dot_general | solution.py:216
  4.4 0.2 fusion.114
  4.8 0.9 %broadcast_in_dim.46 = bf16[16,32,416]{2,1,0:T(8,128)(2,1)} broadcast(bf16[32,416]{1,0:T(8,128)(2,1)S(1)} %pad_maximum_fusion.12), dimensions={1,2} | broadcast | bytes 452608 | tf_op jit(solution)/shard_map/broadcast_in_dim | solution.py:98
  5.7 9.0 %all-to-all-start = ((bf16[16,32,416]{2,1,0:T(8,128)(2,1)}), bf16[16,32,416]{2,1,0:T(8,128)(2,1)S(1)}, u32[]{:S(2)}, u32[]{:S(2)}) async-start(bf16[16,32,416]{2,1,0:T(8,128)(2,1)} %broadcast_in_dim.46), calls=%async_computation | async-start | bytes 1048576 | tf_op jit(solution)/shard_map/all_to_all | solution.py:99
  15.0 1.9 %collective-permute-start = (f32[41152]{0:T(1024)S(1)}, f32[41152]{0:T(1024)S(1)}, u32[]{:S(2)}, u32[]{:S(2)}) collective-permute-start(f32[41152]{0:T(1024)S(1)} %concatenate.72), channel_id=1, source_target_pairs={{0,2},{2,4},{4,6},{6,8},{8,10},{10,12},{12,14},{14,16},{16,18},{18... | collective-permute-start | bytes 493832 | tf_op jit(solution)/shard_map/ppermute | solution.py:229
  17.1 3.9 %collective-permute-start.1 = (f32[41152]{0:T(1024)S(1)}, f32[41152]{0:T(1024)S(1)}, u32[]{:S(2)}, u32[]{:S(2)}) collective-permute-start(f32[41152]{0:T(1024)S(1)} %concatenate.73), channel_id=1, source_target_pairs={{2,0},{4,2},{6,4},{8,6},{10,8},{12,10},{14,12},{16,14},{18,16},{20... | collective-permute-start | bytes 493832 | tf_op jit(solution)/shard_map/ppermute | solution.py:230
  21.3 0.6 pad_clamp_fusion.2
  22.2 0.6 constant_dynamic-update-slice_fusion.2
  22.8 0.5 collective-permute-done
  23.4 5.2 %collective-permute-done.1 = f32[41152]{0:T(1024)S(1)} collective-permute-done((f32[41152]{0:T(1024)S(1)}, f32[41152]{0:T(1024)S(1)}, u32[]{:S(2)}, u32[]{:S(2)}) %collective-permute-start.1) | collective-permute-done | bytes 164640 | tf_op jit(solution)/shard_map/ppermute | solution.py:230
  28.9 0.6 gather_fusion
  29.7 0.7 gather_fusion.1
  30.4 0.7 multiply_reduce_fusion
  31.0 1.8 %fusion.5 = f32[16,64,128,1]{2,1,3,0:T(8,128)} fusion(bf16[16,3,64,128]{3,2,1,0:T(8,128)(2,1)S(1)} %bitcast.296, f32[16,3,64,64]{3,2,1,0:T(8,128)S(1)} %multiply_reduce_fusion, bf16[16,3]{1,0:T(8,128)(2,1)S(1)} %copy.51), kind=kOutput, calls=%fused_computation.27 | convolution fusion | flops 51707904 | bytes 2097248 | tf_op jit(solution)/shard_map/while/body/eval_jaxpr/gkij,gkjv->giv/dot_general | solution.py:39
  32.9 1.0 %slice.440 = f32[16,32,96]{2,1,0:T(8,128)} slice(f32[16,32,288]{2,1,0:T(8,128)S(1)} %slice_convert_fusion), slice={[0:16], [0:32], [192:288]} | slice | bytes 393216 | tf_op jit(solution)/shard_map/slice | solution.py:134
  33.9 0.3 fusion.173
  34.2 0.2 fusion.172
  34.4 0.2 fusion.171
  34.7 0.3 copy-done.3
  35.2 0.8 broadcast_in_dim.52
  35.9 14.9 %all-to-all-start.1 = ((bf16[16,32,288]{2,1,0:T(8,128)(2,1)}), bf16[16,32,288]{2,1,0:T(8,128)(2,1)S(1)}, u32[]{:S(2)}, u32[]{:S(2)}) async-start(bf16[16,32,288]{2,1,0:T(8,128)(2,1)} %broadcast_in_dim.52), calls=%async_computation.1 | async-start | bytes 786432 | tf_op jit(solution)/shard_map/all_to_all | solution.py:99
  50.9 0.7 pad_maximum_fusion.8
  51.6 3.8 %collective-permute-start.2 = (bf16[11,32,128]{2,1,0:T(8,128)(2,1)}, bf16[11,32,128]{2,1,0:T(8,128)(2,1)S(1)}, u32[]{:S(2)}, u32[]{:S(2)}) collective-permute-start(bf16[11,32,128]{2,1,0:T(8,128)(2,1)} %get-tuple-element.94), channel_id=1, source_target_pairs={{0,32},{32,64},{64,96},{96,128},{128,160},{160,192},{192,224},{224... | collective-permute-start | bytes 270344 | tf_op jit(solution)/shard_map/ppermute | solution.py:141
  55.4 1.3 %collective-permute-start.3 = (bf16[11,32,128]{2,1,0:T(8,128)(2,1)}, bf16[11,32,128]{2,1,0:T(8,128)(2,1)}, u32[]{:S(2)}, u32[]{:S(2)}) collective-permute-start(bf16[11,32,128]{2,1,0:T(8,128)(2,1)} %get-tuple-element.95), channel_id=1, source_target_pairs={{32,0},{64,32},{96,64},{128,96},{160,128},{192,160},{224,192},{256... | collective-permute-start | bytes 270344 | tf_op jit(solution)/shard_map/ppermute | solution.py:144
  56.8 0.2 fusion.127
  57.3 0.1 fusion.25
  57.6 0.2 fusion.14
  58.2 0.6 gather_fusion.5
  58.8 0.9 %fusion.110 = f32[2,128,32]{1,2,0:T(8,128)S(1)} fusion(f32[2,96,128]{2,1,0:T(8,128)S(1)} %bitcast.306, bf16[1,31,32,96]{3,2,1,0:T(8,128)(2,1)} %param.21), kind=kOutput, calls=%fused_computation.179 | convolution fusion | flops 9437184 | bytes 147456 | tf_op jit(solution)/shard_map/cra,cav->crv/dot_general | solution.py:263
  59.7 0.2 fusion.112
  59.9 0.6 gather_fusion.4
  60.5 1.0 %fusion.2 = f32[4,32,128]{2,1,0:T(8,128)S(1)} fusion(f32[4,32,128]{2,1,0:T(8,128)S(1)} %bitcast.309, f32[4,96,128]{2,1,0:T(8,128)S(1)} %bitcast.297, bf16[1,31,32,96]{3,2,1,0:T(8,128)(2,1)} %param.21), kind=kOutput, calls=%fused_computation.15 | convolution fusion | flops 18890752 | bytes 360448 | tf_op jit(solution)/shard_map/cra,cav->crv/dot_general | solution.py:263
  61.5 0.3 fusion.76
  61.8 0.6 gather_fusion.3
  62.3 1.1 %fusion.1 = f32[8,32,128]{2,1,0:T(8,128)S(1)} fusion(f32[8,32,128]{2,1,0:T(8,128)S(1)} %bitcast.301, f32[8,96,128]{2,1,0:T(8,128)S(1)} %bitcast.286, bf16[1,31,32,96]{3,2,1,0:T(8,128)(2,1)} %param.21), kind=kOutput, calls=%fused_computation.13 | convolution fusion | flops 37781504 | bytes 720896 | tf_op jit(solution)/shard_map/cra,cav->crv/dot_general | solution.py:263
  63.5 0.3 fusion.21
  63.8 0.7 gather_fusion.2
  64.6 1.4 %fusion = f32[16,32,128]{2,1,0:T(8,128)S(1)} fusion(f32[16,32,128]{2,1,0:T(8,128)S(1)} %bitcast.295, f32[16,96,128]{2,1,0:T(8,128)S(1)} %bitcast.282, bf16[1,31,32,96]{3,2,1,0:T(8,128)(2,1)} %param.21), kind=kOutput, calls=%fused_computation.11 | convolution fusion | flops 75563008 | bytes 1441792 | tf_op jit(solution)/shard_map/cra,cav->crv/dot_general | solution.py:263
  66.1 0.4 convolution_bitcast_fusion
  66.5 0.3 fusion.104
  66.8 0.2 fusion.102
  67.0 0.4 fusion.10
  67.4 0.2 fusion.100
  67.7 2.6 %collective-permute-done.3 = bf16[11,32,128]{2,1,0:T(8,128)(2,1)} collective-permute-done((bf16[11,32,128]{2,1,0:T(8,128)(2,1)}, bf16[11,32,128]{2,1,0:T(8,128)(2,1)}, u32[]{:S(2)}, u32[]{:S(2)}) %collective-permute-start.3) | collective-permute-done | bytes 90144 | tf_op jit(solution)/shard_map/ppermute | solution.py:144
  70.4 0.9 %convert_element_type.103 = f32[11,32,128]{2,1,0:T(8,128)S(1)} convert(bf16[11,32,128]{2,1,0:T(8,128)(2,1)} %collective-permute-done.3) | non-fusion elementwise | flops 45056 | bytes 270336 | tf_op jit(solution)/shard_map/convert_element_type | solution.py:59
  71.3 0.8 fusion.166
  72.2 0.9 %fusion.51 = f32[32,128]{1,0:T(8,128)S(1)} fusion(f32[32,128]{1,0:T(8,128)S(1)} %get-tuple-element.71, f32[32,128]{1,0:T(8,128)S(1)} %get-tuple-element.72, f32[32,128]{1,0:T(8,128)S(1)} %get-tuple-element.70, f32[16,32,96]{2,1,0:T(8,128)} %slice.440, s32[]{:T(128)S(6)} %select_n.310), kind=kOutput, calls=%fused_computation.97 | convolution fusion | flops 4743168 | bytes 81924 | tf_op jit(solution)/shard_map/dot_general | solution.py:63
  73.1 0.9 %fusion.45 = f32[32,128]{1,0:T(8,128)S(1)} fusion(f32[32,128]{1,0:T(8,128)S(1)} %get-tuple-element.65, f32[32,128]{1,0:T(8,128)S(1)} %get-tuple-element.66, f32[32,128]{1,0:T(8,128)S(1)} %get-tuple-element.64, f32[16,32,96]{2,1,0:T(8,128)} %slice.440, s32[]{:T(128)S(6)} %select_n.299), kind=kOutput, calls=%fused_computation.91 | convolution fusion | flops 4743168 | bytes 81924 | tf_op jit(solution)/shard_map/dot_general | solution.py:63
  74.0 0.9 %fusion.39 = f32[32,128]{1,0:T(8,128)S(1)} fusion(f32[32,128]{1,0:T(8,128)S(1)} %get-tuple-element.54, f32[32,128]{1,0:T(8,128)S(1)} %get-tuple-element.55, f32[32,128]{1,0:T(8,128)S(1)} %get-tuple-element.53, f32[16,32,96]{2,1,0:T(8,128)} %slice.440, s32[]{:T(128)S(6)} %select_n.288), kind=kOutput, calls=%fused_computation.85 | convolution fusion | flops 4743168 | bytes 81924 | tf_op jit(solution)/shard_map/dot_general | solution.py:63
  74.9 0.8 %convolution_bitcast_fusion.4 = f32[32,128]{1,0:T(8,128)S(1)} fusion(f32[32,128]{1,0:T(8,128)S(1)} %get-tuple-element.40, f32[32,128]{1,0:T(8,128)S(1)} %get-tuple-element.41, f32[32,128]{1,0:T(8,128)S(1)} %get-tuple-element.39, bf16[1,31,32,96]{3,2,1,0:T(8,128)(2,1)} %param.21), kind=kOutput, calls=%fused_computation.23 | convolution fusion | flops 4743168 | bytes 73728 | tf_op jit(solution)/shard_map/dot_general | solution.py:63
  75.7 0.3 convolution_add_fusion.6
  76.4 0.1 fusion.27
  76.6 0.2 fusion.80
  76.8 0.2 fusion.98
  77.0 0.2 fusion.96
  77.3 0.9 %fusion.57 = f32[32,128]{1,0:T(8,128)S(1)} fusion(f32[32,128]{1,0:T(8,128)S(1)} %get-tuple-element.46, f32[32,128]{1,0:T(8,128)S(1)} %get-tuple-element.45, f32[32,128]{1,0:T(8,128)S(1)} %get-tuple-element.44, f32[16,32,96]{2,1,0:T(8,128)} %slice.440), kind=kOutput, calls=%fused_computation.103 | convolution fusion | flops 4743168 | bytes 81920 | tf_op jit(solution)/shard_map/dot_general | solution.py:63
  78.2 0.1 convolution_add_fusion.3
  78.7 0.2 convolution_add_fusion.2
  79.0 0.2 fusion.3
  79.2 1.0 %convolution_add_fusion = f32[16,64,128]{2,1,0:T(8,128)S(1)} fusion(f32[16,64,128]{2,1,0:T(8,128)S(1)} %convolution_bitcast_fusion, f32[16,64,32]{1,2,0:T(8,128)S(1)} %fusion.10, f32[32,128,1]{1,0,2:T(8,128)S(1)} %fusion.3), kind=kOutput, calls=%fused_computation.8 | convolution fusion | flops 50462720 | bytes 1196032 | tf_op jit(solution)/shard_map/lpk,kv->lpv/dot_general | solution.py:291
  80.2 0.8 fusion.8
  (127 shorter events, 4.1 us)
Async XLA Ops:
  0.0 4.4 %copy-start.2 = (bf16[1,15,32,64]{3,2,1,0:T(8,128)(2,1)S(1)}, bf16[1,15,32,64]{3,2,1,0:T(8,128)(2,1)}, u32[]{:S(2)}) copy-start(bf16[1,15,32,64]{3,2,1,0:T(8,128)(2,1)} %param.20) | copy-start | bytes 184324
  0.0 4.7 %copy-start.16 = (bf16[1,32,64]{2,1,0:T(8,128)(2,1)S(1)}, bf16[1,32,64]{2,1,0:T(8,128)(2,1)}, u32[]{:S(2)}) copy-start(bf16[1,32,64]{2,1,0:T(8,128)(2,1)} %param.22) | copy-start | bytes 12292
  0.0 4.7 %copy-start.15 = (bf16[1,32,96]{2,1,0:T(8,128)(2,1)S(1)}, bf16[1,32,96]{2,1,0:T(8,128)(2,1)}, u32[]{:S(2)}) copy-start(bf16[1,32,96]{2,1,0:T(8,128)(2,1)} %param.23) | copy-start | bytes 18436
  1.0 13.6 %copy-start.1 = (bf16[1024,128]{1,0:T(8,128)(2,1)S(1)}, bf16[1024,128]{1,0:T(8,128)(2,1)}, u32[]{:S(2)}) copy-start(bf16[1024,128]{1,0:T(8,128)(2,1)} %param.16) | copy-start | bytes 786436
  2.3 12.4 %copy-start.13 = (f32[3,1024]{1,0:T(4,128)S(1)}, f32[3,1024]{1,0:T(4,128)}, u32[]{:S(2)}) copy-start(f32[3,1024]{1,0:T(4,128)} %param.17) | copy-start | bytes 36868
  4.3 16.8 %copy-start.14 = (s32[16,3]{0,1:T(4,128)S(1)}, s32[16,3]{0,1:T(4,128)}, u32[]{:S(2)}) copy-start(s32[16,3]{0,1:T(4,128)} %param.18) | copy-start | bytes 580
  4.3 17.0 %copy-start.19 = (s32[48]{0:T(128)S(1)}, s32[48]{0:T(128)}, u32[]{:S(2)}) copy-start(s32[48]{0:T(128)} %constant.260) | copy-start | bytes 580
  4.3 17.0 %copy-start.20 = (s32[24]{0:T(128)S(1)}, s32[24]{0:T(128)}, u32[]{:S(2)}) copy-start(s32[24]{0:T(128)} %constant.261) | copy-start | bytes 292
  4.4 17.5 %copy-start.17 = (s32[12]{0:T(128)S(1)}, s32[12]{0:T(128)}, u32[]{:S(2)}) copy-start(s32[12]{0:T(128)} %constant.262) | copy-start | bytes 148
  4.4 17.5 %copy-start.18 = (s32[6]{0:T(128)S(1)}, s32[6]{0:T(128)}, u32[]{:S(2)}) copy-start(s32[6]{0:T(128)} %constant.263) | copy-start | bytes 76
  5.7 27.2 %all-to-all-start = ((bf16[16,32,416]{2,1,0:T(8,128)(2,1)}), bf16[16,32,416]{2,1,0:T(8,128)(2,1)S(1)}, u32[]{:S(2)}, u32[]{:S(2)}) async-start(bf16[16,32,416]{2,1,0:T(8,128)(2,1)} %broadcast_in_dim.46), calls=%async_computation | async-start | bytes 1048576 | tf_op jit(solution)/shard_map/all_to_all | solution.py:99
  15.0 8.3 %collective-permute-start = (f32[41152]{0:T(1024)S(1)}, f32[41152]{0:T(1024)S(1)}, u32[]{:S(2)}, u32[]{:S(2)}) collective-permute-start(f32[41152]{0:T(1024)S(1)} %concatenate.72), channel_id=1, source_target_pairs={{0,2},{2,4},{4,6},{6,8},{8,10},{10,12},{12,14},{14,16},{16,18},{18... | collective-permute-start | bytes 493832 | tf_op jit(solution)/shard_map/ppermute | solution.py:229
  17.1 11.5 %collective-permute-start.1 = (f32[41152]{0:T(1024)S(1)}, f32[41152]{0:T(1024)S(1)}, u32[]{:S(2)}, u32[]{:S(2)}) collective-permute-start(f32[41152]{0:T(1024)S(1)} %concatenate.73), channel_id=1, source_target_pairs={{2,0},{4,2},{6,4},{8,6},{10,8},{12,10},{14,12},{16,14},{18,16},{20... | collective-permute-start | bytes 493832 | tf_op jit(solution)/shard_map/ppermute | solution.py:230
  23.3 6.3 %copy-start.8 = (f32[41152]{0:T(1024)}, f32[41152]{0:T(1024)S(1)}, u32[]{:S(2)}) copy-start(f32[41152]{0:T(1024)S(1)} %collective-permute-done) | copy-start | bytes 493828
  28.6 2.4 %copy-start.10 = (f32[41152]{0:T(1024)}, f32[41152]{0:T(1024)S(1)}, u32[]{:S(2)}) copy-start(f32[41152]{0:T(1024)S(1)} %collective-permute-done.1) | copy-start | bytes 493828
  32.9 2.1 %copy-start = (f32[16,32,288]{2,1,0:T(8,128)}, f32[16,32,288]{2,1,0:T(8,128)S(1)}, u32[]{:S(2)}) copy-start(f32[16,32,288]{2,1,0:T(8,128)S(1)} %slice_convert_fusion) | copy-start | bytes 1769476
  34.4 0.6 copy-start.3
  34.6 0.6 copy-start.6
  35.9 22.0 %copy-start.9 = (f32[41152]{0:T(1024)S(1)}, f32[41152]{0:T(1024)}, u32[]{:S(2)}) copy-start(f32[41152]{0:T(1024)} %copy-done.8) | copy-start | bytes 493828
  35.9 40.4 %all-to-all-start.1 = ((bf16[16,32,288]{2,1,0:T(8,128)(2,1)}), bf16[16,32,288]{2,1,0:T(8,128)(2,1)S(1)}, u32[]{:S(2)}, u32[]{:S(2)}) async-start(bf16[16,32,288]{2,1,0:T(8,128)(2,1)} %broadcast_in_dim.52), calls=%async_computation.1 | async-start | bytes 786432 | tf_op jit(solution)/shard_map/all_to_all | solution.py:99
  50.8 7.3 %copy-start.11 = (f32[41152]{0:T(1024)S(1)}, f32[41152]{0:T(1024)}, u32[]{:S(2)}) copy-start(f32[41152]{0:T(1024)} %copy-done.10) | copy-start | bytes 493828
  51.6 16.1 %collective-permute-start.2 = (bf16[11,32,128]{2,1,0:T(8,128)(2,1)}, bf16[11,32,128]{2,1,0:T(8,128)(2,1)S(1)}, u32[]{:S(2)}, u32[]{:S(2)}) collective-permute-start(bf16[11,32,128]{2,1,0:T(8,128)(2,1)} %get-tuple-element.94), channel_id=1, source_target_pairs={{0,32},{32,64},{64,96},{96,128},{128,160},{160,192},{192,224},{224... | collective-permute-start | bytes 270344 | tf_op jit(solution)/shard_map/ppermute | solution.py:141
  55.4 15.0 %collective-permute-start.3 = (bf16[11,32,128]{2,1,0:T(8,128)(2,1)}, bf16[11,32,128]{2,1,0:T(8,128)(2,1)}, u32[]{:S(2)}, u32[]{:S(2)}) collective-permute-start(bf16[11,32,128]{2,1,0:T(8,128)(2,1)} %get-tuple-element.95), channel_id=1, source_target_pairs={{32,0},{64,32},{96,64},{128,96},{160,128},{192,160},{224,192},{256... | collective-permute-start | bytes 270344 | tf_op jit(solution)/shard_map/ppermute | solution.py:144
  64.6 1.9 %slice-start = ((f32[16,32,288]{2,1,0:T(8,128)}), f32[16,32,64]{2,1,0:T(8,128)S(1)}, s32[]{:S(2)}) async-start(f32[16,32,288]{2,1,0:T(8,128)} %copy-done), calls=%async_computation.2 | async-start | bytes 524288 | tf_op jit(solution)/shard_map/slice | solution.py:133
  64.6 3.1 %copy-start.12 = (f32[8,32,128]{2,1,0:T(8,128)S(1)}, f32[8,32,128]{2,1,0:T(8,128)}, u32[]{:S(2)}) copy-start(f32[8,32,128]{2,1,0:T(8,128)} %constant_dynamic-update-slice_fusion.2) | copy-start | bytes 393220
  64.6 3.1 %copy-start.7 = (f32[2,32,128]{2,1,0:T(8,128)S(1)}, f32[2,32,128]{2,1,0:T(8,128)}, u32[]{:S(2)}) copy-start(f32[2,32,128]{2,1,0:T(8,128)} %copy-done.6) | copy-start | bytes 98308
  66.0 6.0 %copy-start.4 = (f32[4,32,128]{2,1,0:T(8,128)S(1)}, f32[4,32,128]{2,1,0:T(8,128)}, u32[]{:S(2)}) copy-start(f32[4,32,128]{2,1,0:T(8,128)} %copy-done.3) | copy-start | bytes 196612
  77.3 2.9 %copy-start.5 = (f32[16,64,128,1]{2,1,3,0:T(8,128)S(1)}, f32[16,64,128,1]{2,1,3,0:T(8,128)}, u32[]{:S(2)}) copy-start(f32[16,64,128,1]{2,1,3,0:T(8,128)} %fusion.5) | copy-start | bytes 1572868

commit v18 on v17

--- a/solution.py
+++ b/solution.py
@@ -216,11 +216,11 @@
         coefficients.append(jnp.einsum("cra,cav->crv", lift_mats, children, precision=HIGHEST))
     def rim(rows, clusters):
         edges = jnp.stack([coefficients[height][clusters] for height in range(depth_local)], 0)
-        parts = [
-            vectors[rows].astype(jnp.float32),
-            points[:, rows],
-            edges.astype(jnp.bfloat16).astype(jnp.float32),
-        ]
+        coords = points[:, rows]
+        high = lax.reduce_precision(coords, exponent_bits=8, mantissa_bits=7)
+        middle = lax.reduce_precision(coords - high, exponent_bits=8, mantissa_bits=7)
+        pieces = jnp.stack([high, middle, coords - high - middle], 0).astype(jnp.bfloat16)
+        parts = [vectors[rows], pieces, edges.astype(jnp.bfloat16)]
         return jnp.concatenate([part.reshape(-1) for part in parts]), [p.shape for p in parts]
 
     head, shapes = rim(slice(0, LEAF), slice(0, 2))
@@ -235,7 +235,8 @@
             size = int(np.prod(shape))
             pieces.append(flat[done : done + size].reshape(shape))
             done += size
-        return pieces
+        coords = as_float(pieces[1])
+        return pieces[0], (coords[0] + coords[1]) + coords[2], as_float(pieces[2])
 
     def late(held):
         (from_left, from_right), lift_stack, basis_float = held

time: 82.1 us -> 81.2 us (0.989)
  the two profiles are of different devices: /device:TPU:30 before, /device:TPU:96 now
where the time goes in v18:
time: 81.2 us; the launch traced here: 80.1 us
  starting transfers between devices  39.1 us (48%)
  matrix products  20.9 us (26%)
  local copies, waits for them, and re-layouts  11.6 us (14%)
  other arithmetic  5.12 us (6%)
  waiting for transfers between devices  2.34 us (3%)
  between operations  1.09 us (1%)
    all_to_all x2, starting transfers between devices, spread_gather(): return lax.all_to_all(copies, axis, 0, 0, tiled=True)  22.5 us
    dot_general x18, matrix products, product(): return jnp.dot(matrix, operand, precision=HIGHEST)  6.8 us
    ppermute x1, starting transfers between devices, local(): lax.ppermute(head, SPACE, [(i + 1, i) for i in range(count - 1)])  6.23 us
    ppermute x1, starting transfers between devices, upper_tree(): lax.ppermute(tails.astype(jnp.bfloat16), 'z', [(i, i + 1) for i in range(...  4.57 us
    dot_general x4, matrix products, late(): jnp.einsum('cra,cav->crv', mixers, stacked, precision=HIGHEST)  4.44 us
    ppermute x1, starting transfers between devices, local(): lax.ppermute(tail, SPACE, [(i, i + 1) for i in range(count - 1)])  3.83 us
    gather x4, local copies, waits for them, and re-layouts, late(): extended[partner_table(cluster_count) + 2]  2.55 us
    dot_general x4, matrix products, local(): jnp.einsum('cra,cav->crv', lift_mats, children, precision=HIGHEST)  2.34 us
  transfers between devices with their start and end apart: 6, of which 2 were waited for; matrix products, arithmetic and copies ran while one was open for 31% of the time, Pallas kernels for 0%

profile of v18, /device:TPU:96, one launch (start us, length us, event | category | flops | bytes accessed | tf_op | source)
XLA Modules:
  0.0 80.1 jit_solution(1183014944251538359)
XLA Ops:
  0.0 1.0 %reshape.174 = bf16[32,16,64]{2,1,0:T(8,128)(2,1)S(1)} reshape(bf16[32,1024]{1,0:T(8,128)(2,1)} %param.19) | data formatting | bytes 131072 | tf_op jit(solution)/shard_map/reshape | solution.py:206
  1.1 1.2 %fusion.175 = (bf16[16,32,128]{2,1,0:T(8,128)(2,1)S(1)}, f32[16,32,128]{2,1,0:T(8,128)S(1)}) fusion(bf16[16,64,128]{2,1,0:T(8,128)(2,1)} %bitcast.291, bf16[32,16,64]{2,1,0:T(8,128)(2,1)S(1)} %reshape.174), kind=kOutput, calls=%fused_computation.293 | convolution fusion | flops 8454144 | bytes 720896 | tf_op jit(solution)/shard_map/rlp,lpv->lrv/dot_general | solution.py:209
  2.3 1.1 %bitcast_convert_fusion.1 = (bf16[8,32,128]{2,1,0:T(8,128)(2,1)S(1)}, f32[8,128,32]{1,2,0:T(8,128)S(1)}) fusion(f32[8,64,128]{2,1,0:T(8,128)S(1)} %bitcast.292, bf16[1,15,32,64]{3,2,1,0:T(8,128)(2,1)} %param.20), kind=kOutput, calls=%fused_computation.280 | convolution fusion | flops 25198592 | bytes 524288 | tf_op jit(solution)/shard_map/cra,cav->crv/dot_general | solution.py:216
  3.4 0.9 %bitcast_convert_fusion = (bf16[4,32,128]{2,1,0:T(8,128)(2,1)S(1)}, f32[4,128,32]{1,2,0:T(8,128)S(1)}) fusion(f32[4,64,128]{2,1,0:T(8,128)S(1)} %bitcast.296, bf16[1,15,32,64]{3,2,1,0:T(8,128)(2,1)} %param.20), kind=kOutput, calls=%fused_computation.279 | convolution fusion | flops 12599296 | bytes 262144 | tf_op jit(solution)/shard_map/cra,cav->crv/dot_general | solution.py:216
  4.3 0.2 fusion.112
  4.8 0.9 %broadcast_in_dim.46 = bf16[16,32,416]{2,1,0:T(8,128)(2,1)} broadcast(bf16[32,416]{1,0:T(8,128)(2,1)S(1)} %pad_maximum_fusion.12), dimensions={1,2} | broadcast | bytes 452608 | tf_op jit(solution)/shard_map/broadcast_in_dim | solution.py:98
  5.6 7.0 %all-to-all-start = ((bf16[16,32,416]{2,1,0:T(8,128)(2,1)}), bf16[16,32,416]{2,1,0:T(8,128)(2,1)S(1)}, u32[]{:S(2)}, u32[]{:S(2)}) async-start(bf16[16,32,416]{2,1,0:T(8,128)(2,1)} %broadcast_in_dim.46), calls=%async_computation | async-start | bytes 1048576 | tf_op jit(solution)/shard_map/all_to_all | solution.py:99
  12.9 0.2 concatenate.72
  13.1 3.8 %collective-permute-start = (bf16[41536]{0:T(1024)(128)(2,1)S(1)}, bf16[41536]{0:T(1024)(128)(2,1)S(1)}, u32[]{:S(2)}, u32[]{:S(2)}) collective-permute-start(bf16[41536]{0:T(1024)(128)(2,1)S(1)} %concatenate.72), channel_id=1, source_target_pairs={{0,2},{2,4},{4,6},{6,8},{8,10},{10,12},{12,14},{14,16},{16,18},{18... | collective-permute-start | bytes 249224 | tf_op jit(solution)/shard_map/ppermute | solution.py:229
  17.0 0.2 concatenate.73
  17.2 6.2 %collective-permute-start.1 = (bf16[41536]{0:T(1024)(128)(2,1)S(1)}, bf16[41536]{0:T(1024)(128)(2,1)S(1)}, u32[]{:S(2)}, u32[]{:S(2)}) collective-permute-start(bf16[41536]{0:T(1024)(128)(2,1)S(1)} %concatenate.73), channel_id=1, source_target_pairs={{2,0},{4,2},{6,4},{8,6},{10,8},{12,10},{14,12},{16,14},{18,16},{20... | collective-permute-start | bytes 249224 | tf_op jit(solution)/shard_map/ppermute | solution.py:230
  23.5 0.6 constant_dynamic-update-slice_fusion.2
  24.4 0.6 pad_clamp_fusion.2
  25.0 0.6 pad_clamp_fusion
  26.2 0.6 gather_fusion
  26.9 0.7 gather_fusion.1
  27.6 0.7 multiply_reduce_fusion
  28.3 1.8 %fusion.5 = f32[16,64,128,1]{2,1,3,0:T(8,128)} fusion(bf16[16,3,64,128]{3,2,1,0:T(8,128)(2,1)S(1)} %bitcast.304, f32[16,3,64,64]{3,2,1,0:T(8,128)S(1)} %multiply_reduce_fusion, bf16[16,3]{1,0:T(8,128)(2,1)S(1)} %copy.51), kind=kOutput, calls=%fused_computation.27 | convolution fusion | flops 51707904 | bytes 2097248 | tf_op jit(solution)/shard_map/while/body/eval_jaxpr/gkij,gkjv->giv/dot_general | solution.py:39
  30.2 1.0 %slice.410 = f32[16,32,96]{2,1,0:T(8,128)} slice(f32[16,32,288]{2,1,0:T(8,128)S(1)} %slice_convert_fusion), slice={[0:16], [0:32], [192:288]} | slice | bytes 393216 | tf_op jit(solution)/shard_map/slice | solution.py:134
  31.2 0.3 fusion.178
  31.5 0.2 fusion.177
  31.7 0.2 fusion.176
  32.0 0.3 copy-done.3
  32.4 0.8 broadcast_in_dim.52
  33.2 15.5 %all-to-all-start.1 = ((bf16[16,32,288]{2,1,0:T(8,128)(2,1)}), bf16[16,32,288]{2,1,0:T(8,128)(2,1)S(1)}, u32[]{:S(2)}, u32[]{:S(2)}) async-start(bf16[16,32,288]{2,1,0:T(8,128)(2,1)} %broadcast_in_dim.52), calls=%async_computation.1 | async-start | bytes 786432 | tf_op jit(solution)/shard_map/all_to_all | solution.py:99
  48.8 0.7 pad_maximum_fusion.8
  49.5 4.6 %collective-permute-start.2 = (bf16[11,32,128]{2,1,0:T(8,128)(2,1)}, bf16[11,32,128]{2,1,0:T(8,128)(2,1)S(1)}, u32[]{:S(2)}, u32[]{:S(2)}) collective-permute-start(bf16[11,32,128]{2,1,0:T(8,128)(2,1)} %get-tuple-element.94), channel_id=1, source_target_pairs={{0,32},{32,64},{64,96},{96,128},{128,160},{160,192},{192,224},{224... | collective-permute-start | bytes 270344 | tf_op jit(solution)/shard_map/ppermute | solution.py:141
  54.1 1.9 %collective-permute-start.3 = (bf16[11,32,128]{2,1,0:T(8,128)(2,1)}, bf16[11,32,128]{2,1,0:T(8,128)(2,1)}, u32[]{:S(2)}, u32[]{:S(2)}) collective-permute-start(bf16[11,32,128]{2,1,0:T(8,128)(2,1)} %get-tuple-element.95), channel_id=1, source_target_pairs={{32,0},{64,32},{96,64},{128,96},{160,128},{192,160},{224,192},{256... | collective-permute-start | bytes 270344 | tf_op jit(solution)/shard_map/ppermute | solution.py:144
  56.1 0.2 fusion.125
  56.3 0.1 fusion.179
  56.6 0.1 fusion.25
  56.9 0.2 fusion.14
  57.6 0.7 gather_fusion.5
  58.3 0.9 %fusion.108 = f32[2,128,32]{1,2,0:T(8,128)S(1)} fusion(f32[2,96,128]{2,1,0:T(8,128)S(1)} %bitcast.314, bf16[1,31,32,96]{3,2,1,0:T(8,128)(2,1)} %param.21), kind=kOutput, calls=%fused_computation.177 | convolution fusion | flops 9437184 | bytes 147456 | tf_op jit(solution)/shard_map/cra,cav->crv/dot_general | solution.py:264
  59.2 0.2 fusion.110
  59.4 0.6 gather_fusion.4
  60.0 1.0 %fusion.2 = f32[4,32,128]{2,1,0:T(8,128)S(1)} fusion(f32[4,32,128]{2,1,0:T(8,128)S(1)} %bitcast.317, f32[4,96,128]{2,1,0:T(8,128)S(1)} %bitcast.305, bf16[1,31,32,96]{3,2,1,0:T(8,128)(2,1)} %param.21), kind=kOutput, calls=%fused_computation.15 | convolution fusion | flops 18890752 | bytes 360448 | tf_op jit(solution)/shard_map/cra,cav->crv/dot_general | solution.py:264
  61.0 0.3 fusion.76
  61.2 0.6 gather_fusion.3
  61.8 1.1 %fusion.1 = f32[8,32,128]{2,1,0:T(8,128)S(1)} fusion(f32[8,32,128]{2,1,0:T(8,128)S(1)} %bitcast.309, f32[8,96,128]{2,1,0:T(8,128)S(1)} %bitcast.294, bf16[1,31,32,96]{3,2,1,0:T(8,128)(2,1)} %param.21), kind=kOutput, calls=%fused_computation.13 | convolution fusion | flops 37781504 | bytes 720896 | tf_op jit(solution)/shard_map/cra,cav->crv/dot_general | solution.py:264
  63.0 0.3 fusion.21
  63.3 0.7 gather_fusion.2
  64.1 1.4 %fusion = f32[16,32,128]{2,1,0:T(8,128)S(1)} fusion(f32[16,32,128]{2,1,0:T(8,128)S(1)} %bitcast.303, f32[16,96,128]{2,1,0:T(8,128)S(1)} %bitcast.290, bf16[1,31,32,96]{3,2,1,0:T(8,128)(2,1)} %param.21), kind=kOutput, calls=%fused_computation.11 | convolution fusion | flops 75563008 | bytes 1441792 | tf_op jit(solution)/shard_map/cra,cav->crv/dot_general | solution.py:264
  65.5 0.4 convolution_bitcast_fusion
  66.0 0.3 fusion.102
  66.3 0.2 fusion.100
  66.5 0.4 fusion.10
  66.9 0.2 fusion.98
  67.2 2.3 %collective-permute-done.3 = bf16[11,32,128]{2,1,0:T(8,128)(2,1)} collective-permute-done((bf16[11,32,128]{2,1,0:T(8,128)(2,1)}, bf16[11,32,128]{2,1,0:T(8,128)(2,1)}, u32[]{:S(2)}, u32[]{:S(2)}) %collective-permute-start.3) | collective-permute-done | bytes 90144 | tf_op jit(solution)/shard_map/ppermute | solution.py:144
  69.5 0.9 %convert_element_type.111 = f32[11,32,128]{2,1,0:T(8,128)S(1)} convert(bf16[11,32,128]{2,1,0:T(8,128)(2,1)} %collective-permute-done.3) | non-fusion elementwise | flops 45056 | bytes 270336 | tf_op jit(solution)/shard_map/convert_element_type | solution.py:59
  70.4 0.8 fusion.172
  71.4 0.9 %fusion.51 = f32[32,128]{1,0:T(8,128)S(1)} fusion(f32[32,128]{1,0:T(8,128)S(1)} %get-tuple-element.63, f32[32,128]{1,0:T(8,128)S(1)} %get-tuple-element.64, f32[32,128]{1,0:T(8,128)S(1)} %get-tuple-element.62, f32[16,32,96]{2,1,0:T(8,128)} %slice.410, s32[]{:T(128)S(6)} %select_n.310), kind=kOutput, calls=%fused_computation.99 | convolution fusion | flops 4743168 | bytes 81924 | tf_op jit(solution)/shard_map/dot_general | solution.py:63
  72.2 0.9 %fusion.45 = f32[32,128]{1,0:T(8,128)S(1)} fusion(f32[32,128]{1,0:T(8,128)S(1)} %get-tuple-element.57, f32[32,128]{1,0:T(8,128)S(1)} %get-tuple-element.58, f32[32,128]{1,0:T(8,128)S(1)} %get-tuple-element.56, f32[16,32,96]{2,1,0:T(8,128)} %slice.410, s32[]{:T(128)S(6)} %select_n.299), kind=kOutput, calls=%fused_computation.93 | convolution fusion | flops 4743168 | bytes 81924 | tf_op jit(solution)/shard_map/dot_general | solution.py:63
  73.1 0.9 %fusion.39 = f32[32,128]{1,0:T(8,128)S(1)} fusion(f32[32,128]{1,0:T(8,128)S(1)} %get-tuple-element.54, f32[32,128]{1,0:T(8,128)S(1)} %get-tuple-element.55, f32[32,128]{1,0:T(8,128)S(1)} %get-tuple-element.53, f32[16,32,96]{2,1,0:T(8,128)} %slice.410, s32[]{:T(128)S(6)} %select_n.288), kind=kOutput, calls=%fused_computation.87 | convolution fusion | flops 4743168 | bytes 81924 | tf_op jit(solution)/shard_map/dot_general | solution.py:63
  74.0 0.8 %convolution_bitcast_fusion.4 = f32[32,128]{1,0:T(8,128)S(1)} fusion(f32[32,128]{1,0:T(8,128)S(1)} %get-tuple-element.40, f32[32,128]{1,0:T(8,128)S(1)} %get-tuple-element.41, f32[32,128]{1,0:T(8,128)S(1)} %get-tuple-element.39, bf16[1,31,32,96]{3,2,1,0:T(8,128)(2,1)} %param.21), kind=kOutput, calls=%fused_computation.23 | convolution fusion | flops 4743168 | bytes 73728 | tf_op jit(solution)/shard_map/dot_general | solution.py:63
  74.9 0.3 convolution_add_fusion.6
  75.7 0.2 fusion.80
  75.9 0.2 fusion.96
  76.2 0.2 fusion.94
  76.4 0.9 %fusion.57 = f32[32,128]{1,0:T(8,128)S(1)} fusion(f32[32,128]{1,0:T(8,128)S(1)} %get-tuple-element.46, f32[32,128]{1,0:T(8,128)S(1)} %get-tuple-element.45, f32[32,128]{1,0:T(8,128)S(1)} %get-tuple-element.44, f32[16,32,96]{2,1,0:T(8,128)} %slice.410), kind=kOutput, calls=%fused_computation.105 | convolution fusion | flops 4743168 | bytes 81920 | tf_op jit(solution)/shard_map/dot_general | solution.py:63
  77.8 0.2 convolution_add_fusion.2
  78.1 0.2 fusion.3
  78.3 1.0 %convolution_add_fusion = f32[16,64,128]{2,1,0:T(8,128)S(1)} fusion(f32[16,64,128]{2,1,0:T(8,128)S(1)} %convolution_bitcast_fusion, f32[16,64,32]{1,2,0:T(8,128)S(1)} %fusion.10, f32[32,128,1]{1,0,2:T(8,128)S(1)} %fusion.3), kind=kOutput, calls=%fused_computation.8 | convolution fusion | flops 50462720 | bytes 1196032 | tf_op jit(solution)/shard_map/lpk,kv->lpv/dot_general | solution.py:292
  79.3 0.8 fusion.8
  (130 shorter events, 4.1 us)
Async XLA Ops:
  0.0 4.3 %copy-start.2 = (bf16[1,15,32,64]{3,2,1,0:T(8,128)(2,1)S(1)}, bf16[1,15,32,64]{3,2,1,0:T(8,128)(2,1)}, u32[]{:S(2)}) copy-start(bf16[1,15,32,64]{3,2,1,0:T(8,128)(2,1)} %param.20) | copy-start | bytes 184324
  0.0 4.6 %copy-start.15 = (bf16[1,32,64]{2,1,0:T(8,128)(2,1)S(1)}, bf16[1,32,64]{2,1,0:T(8,128)(2,1)}, u32[]{:S(2)}) copy-start(bf16[1,32,64]{2,1,0:T(8,128)(2,1)} %param.22) | copy-start | bytes 12292
  0.0 4.7 %copy-start.14 = (bf16[1,32,96]{2,1,0:T(8,128)(2,1)S(1)}, bf16[1,32,96]{2,1,0:T(8,128)(2,1)}, u32[]{:S(2)}) copy-start(bf16[1,32,96]{2,1,0:T(8,128)(2,1)} %param.23) | copy-start | bytes 18436
  1.0 11.6 %copy-start.1 = (bf16[1024,128]{1,0:T(8,128)(2,1)S(1)}, bf16[1024,128]{1,0:T(8,128)(2,1)}, u32[]{:S(2)}) copy-start(bf16[1024,128]{1,0:T(8,128)(2,1)} %param.16) | copy-start | bytes 786436
  2.3 10.5 %copy-start.11 = (f32[3,1024]{1,0:T(4,128)S(1)}, f32[3,1024]{1,0:T(4,128)}, u32[]{:S(2)}) copy-start(f32[3,1024]{1,0:T(4,128)} %param.17) | copy-start | bytes 36868
  4.6 19.5 %copy-start.13 = (s32[16,3]{0,1:T(4,128)S(1)}, s32[16,3]{0,1:T(4,128)}, u32[]{:S(2)}) copy-start(s32[16,3]{0,1:T(4,128)} %param.18) | copy-start | bytes 580
  4.7 19.7 %copy-start.18 = (s32[48]{0:T(128)S(1)}, s32[48]{0:T(128)}, u32[]{:S(2)}) copy-start(s32[48]{0:T(128)} %constant.260) | copy-start | bytes 580
  4.8 19.7 %copy-start.19 = (s32[24]{0:T(128)S(1)}, s32[24]{0:T(128)}, u32[]{:S(2)}) copy-start(s32[24]{0:T(128)} %constant.261) | copy-start | bytes 292
  4.8 20.3 %copy-start.16 = (s32[12]{0:T(128)S(1)}, s32[12]{0:T(128)}, u32[]{:S(2)}) copy-start(s32[12]{0:T(128)} %constant.262) | copy-start | bytes 148
  4.8 20.3 %copy-start.17 = (s32[6]{0:T(128)S(1)}, s32[6]{0:T(128)}, u32[]{:S(2)}) copy-start(s32[6]{0:T(128)} %constant.263) | copy-start | bytes 76
  5.6 24.5 %all-to-all-start = ((bf16[16,32,416]{2,1,0:T(8,128)(2,1)}), bf16[16,32,416]{2,1,0:T(8,128)(2,1)S(1)}, u32[]{:S(2)}, u32[]{:S(2)}) async-start(bf16[16,32,416]{2,1,0:T(8,128)(2,1)} %broadcast_in_dim.46), calls=%async_computation | async-start | bytes 1048576 | tf_op jit(solution)/shard_map/all_to_all | solution.py:99
  13.1 12.5 %collective-permute-start = (bf16[41536]{0:T(1024)(128)(2,1)S(1)}, bf16[41536]{0:T(1024)(128)(2,1)S(1)}, u32[]{:S(2)}, u32[]{:S(2)}) collective-permute-start(bf16[41536]{0:T(1024)(128)(2,1)S(1)} %concatenate.72), channel_id=1, source_target_pairs={{0,2},{2,4},{4,6},{6,8},{8,10},{10,12},{12,14},{14,16},{16,18},{18... | collective-permute-start | bytes 249224 | tf_op jit(solution)/shard_map/ppermute | solution.py:229
  17.2 8.6 %collective-permute-start.1 = (bf16[41536]{0:T(1024)(128)(2,1)S(1)}, bf16[41536]{0:T(1024)(128)(2,1)S(1)}, u32[]{:S(2)}, u32[]{:S(2)}) collective-permute-start(bf16[41536]{0:T(1024)(128)(2,1)S(1)} %concatenate.73), channel_id=1, source_target_pairs={{2,0},{4,2},{6,4},{8,6},{10,8},{12,10},{14,12},{16,14},{18,16},{20... | collective-permute-start | bytes 249224 | tf_op jit(solution)/shard_map/ppermute | solution.py:230
  25.8 2.5 %copy-start.8 = (bf16[41536]{0:T(1024)(128)(2,1)}, bf16[41536]{0:T(1024)(128)(2,1)S(1)}, u32[]{:S(2)}) copy-start(bf16[41536]{0:T(1024)(128)(2,1)S(1)} %collective-permute-done.1) | copy-start | bytes 249220
  30.2 2.1 %copy-start = (f32[16,32,288]{2,1,0:T(8,128)}, f32[16,32,288]{2,1,0:T(8,128)S(1)}, u32[]{:S(2)}) copy-start(f32[16,32,288]{2,1,0:T(8,128)S(1)} %slice_convert_fusion) | copy-start | bytes 1769476
  31.7 0.6 copy-start.3
  31.8 0.6 copy-start.6
  33.2 42.3 %all-to-all-start.1 = ((bf16[16,32,288]{2,1,0:T(8,128)(2,1)}), bf16[16,32,288]{2,1,0:T(8,128)(2,1)S(1)}, u32[]{:S(2)}, u32[]{:S(2)}) async-start(bf16[16,32,288]{2,1,0:T(8,128)(2,1)} %broadcast_in_dim.52), calls=%async_computation.1 | async-start | bytes 786432 | tf_op jit(solution)/shard_map/all_to_all | solution.py:99
  48.7 8.7 %copy-start.9 = (bf16[41536]{0:T(1024)(128)(2,1)S(1)}, bf16[41536]{0:T(1024)(128)(2,1)}, u32[]{:S(2)}) copy-start(bf16[41536]{0:T(1024)(128)(2,1)} %copy-done.8) | copy-start | bytes 249220
  49.5 17.6 %collective-permute-start.2 = (bf16[11,32,128]{2,1,0:T(8,128)(2,1)}, bf16[11,32,128]{2,1,0:T(8,128)(2,1)S(1)}, u32[]{:S(2)}, u32[]{:S(2)}) collective-permute-start(bf16[11,32,128]{2,1,0:T(8,128)(2,1)} %get-tuple-element.94), channel_id=1, source_target_pairs={{0,32},{32,64},{64,96},{96,128},{128,160},{160,192},{192,224},{224... | collective-permute-start | bytes 270344 | tf_op jit(solution)/shard_map/ppermute | solution.py:141
  54.1 15.4 %collective-permute-start.3 = (bf16[11,32,128]{2,1,0:T(8,128)(2,1)}, bf16[11,32,128]{2,1,0:T(8,128)(2,1)}, u32[]{:S(2)}, u32[]{:S(2)}) collective-permute-start(bf16[11,32,128]{2,1,0:T(8,128)(2,1)} %get-tuple-element.95), channel_id=1, source_target_pairs={{32,0},{64,32},{96,64},{128,96},{160,128},{192,160},{224,192},{256... | collective-permute-start | bytes 270344 | tf_op jit(solution)/shard_map/ppermute | solution.py:144
  56.8 2.6 %copy-start.12 = (s32[1024]{0:T(1024)S(1)}, s32[1024]{0:T(1024)}, u32[]{:S(2)}) copy-start(s32[1024]{0:T(1024)} %get-tuple-element.125) | copy-start | bytes 12292
  64.1 1.9 %slice-start = ((f32[16,32,288]{2,1,0:T(8,128)}), f32[16,32,64]{2,1,0:T(8,128)S(1)}, s32[]{:S(2)}) async-start(f32[16,32,288]{2,1,0:T(8,128)} %copy-done), calls=%async_computation.2 | async-start | bytes 524288 | tf_op jit(solution)/shard_map/slice | solution.py:133
  64.1 3.1 %copy-start.10 = (f32[8,32,128]{2,1,0:T(8,128)S(1)}, f32[8,32,128]{2,1,0:T(8,128)}, u32[]{:S(2)}) copy-start(f32[8,32,128]{2,1,0:T(8,128)} %constant_dynamic-update-slice_fusion.2) | copy-start | bytes 393220
  64.1 3.1 %copy-start.7 = (f32[2,32,128]{2,1,0:T(8,128)S(1)}, f32[2,32,128]{2,1,0:T(8,128)}, u32[]{:S(2)}) copy-start(f32[2,32,128]{2,1,0:T(8,128)} %copy-done.6) | copy-start | bytes 98308
  65.5 5.7 %copy-start.4 = (f32[4,32,128]{2,1,0:T(8,128)S(1)}, f32[4,32,128]{2,1,0:T(8,128)}, u32[]{:S(2)}) copy-start(f32[4,32,128]{2,1,0:T(8,128)} %copy-done.3) | copy-start | bytes 196612
  76.4 2.9 %copy-start.5 = (f32[16,64,128,1]{2,1,3,0:T(8,128)S(1)}, f32[16,64,128,1]{2,1,3,0:T(8,128)}, u32[]{:S(2)}) copy-start(f32[16,64,128,1]{2,1,3,0:T(8,128)} %fusion.5) | copy-start | bytes 1572868
